TPU v7x, 32 devices: a whole 2x2x4 slice. The times are simulated.
32 devices in a mesh: ctx: 8 (over z, core), tp: 4 (over y, x).
Axes of the slice: x: 2, y: 2, z: 4, core: 2. Of those that a mesh axis runs over, the one named last changes fastest.
Arguments:
- x_in: bfloat16 [4096, 8192], P(('ctx', 'tp')), may hold values from -6 to 6
- bc_in: bfloat16 [4096, 2048], P(('ctx', 'tp')), may hold values from -6 to 6
- dt_in: bfloat16 [4096, 128], P(('ctx', 'tp')), may hold values from -3 to 3
- conv_x_weight: float32 [4, 8192], replicated, may hold values from -3 to 3
- conv_x_bias: float32 [8192], replicated, may hold values from -0.8 to -0.2
- conv_bc_weight: float32 [4, 2048], replicated, may hold values from -3 to 3
- conv_bc_bias: float32 [2048], replicated, may hold values from -0.8 to -0.2
- dt_bias: float32 [128], replicated, as said below
- a_log: float32 [128], replicated, as said below
- skip: float32 [128], replicated, may hold values from 0.5 to 1.5
Outputs:
- scan_out: bfloat16 [4096, 8192], P(('ctx', 'tp'))
Inputs may be any that keep to these rules, and one draw needn't show every extreme that they name: `dt_bias`: one value for each head. `a_log`: one value for each head.
All inputs are finite; a program needn't handle non-finite values.
Results may differ from a plain program's by a relative error of at most 0.0051.
Values may be sent and summed in bfloat16 or wider, within the bound.
No kernel may reach another device: no remote copies, remote signals or barrier semaphores. Data moves between devices by JAX's collectives and lax.ppermute only.
A program may use at most 128 MiB of HBM per device.

v0:
```python
import jax
import jax.numpy as jnp
from jax import lax
from jax.sharding import PartitionSpec as P

H = 128
P_SIZE = 64
N = 256
G = 4
CONV = 4
BLOCK = 512


def from_behind(value, axis, steps):
    count = lax.axis_size(axis)
    initial, last = (max(0, -steps), min(count, count - steps))
    return lax.ppermute(value, axis, [(source, source + steps) for source in range(initial, last)])


def entering(part, axis, combine, identity):
    place = lax.axis_index(axis)
    gathered = jax.tree.map(lambda a: lax.all_gather(a, axis), part)
    state = jax.tree.map(lambda a, e: jnp.zeros_like(a) + jnp.asarray(e, a.dtype), part, identity)

    def one(lap, state):
        return combine(
            state, jax.tree.map(lambda a: lax.dynamic_index_in_dim(a, lap, 0, False), gathered)
        )

    return lax.fori_loop(0, place, one, state)


def conv_silu(raw, prior, weight, bias):
    rows = raw.shape[0]
    full = jnp.concatenate([prior, raw], axis=0).astype(jnp.float32)
    total = bias[None, :] + weight[0][None, :] * full[0:rows]
    for k in range(1, CONV):
        total = total + weight[k][None, :] * full[k : k + rows]
    return jax.nn.silu(total).astype(jnp.bfloat16)


def head_columns(head_major):
    return jnp.repeat(head_major.T, P_SIZE, axis=1)


def chain(earlier, later):
    return (earlier[0] * later[0], later[0][None, :] * earlier[1] + later[1])


def on_device(
    x_in,
    bc_in,
    dt_in,
    conv_x_weight,
    conv_x_bias,
    conv_bc_weight,
    conv_bc_bias,
    dt_bias,
    a_log,
    skip,
):
    n_tp = lax.axis_size("tp")
    tp_index = lax.axis_index("tp")
    rows = x_in.shape[0]
    local_heads = H // n_tp
    head_width = local_heads * P_SIZE
    my_group = tp_index * local_heads // (H // G)
    rim = CONV - 1
    prior_x, prior_bc = from_behind((x_in[rows - rim :], bc_in[rows - rim :]), ("ctx", "tp"), 1)
    x_part = conv_silu(x_in, prior_x, conv_x_weight, conv_x_bias)
    bc_part = conv_silu(bc_in, prior_bc, conv_bc_weight, conv_bc_bias)
    seg_x, seg_dt = (
        lax.all_to_all(x_part, "tp", split_axis=1, concat_axis=0, tiled=True),
        lax.all_to_all(dt_in, "tp", split_axis=1, concat_axis=0, tiled=True),
    )
    whole = lax.all_gather(bc_part, "tp", axis=0, tiled=True)
    seg_b = lax.dynamic_slice_in_dim(whole, my_group * N, N, 1)
    seg_c = lax.dynamic_slice_in_dim(whole, G * N + my_group * N, N, 1)
    seg_len = seg_x.shape[0]
    bias_local = lax.dynamic_slice_in_dim(dt_bias, tp_index * local_heads, local_heads, 0)
    rate_local = lax.dynamic_slice_in_dim(a_log, tp_index * local_heads, local_heads, 0)
    skip_local = lax.dynamic_slice_in_dim(skip, tp_index * local_heads, local_heads, 0)
    skip_cols = jnp.repeat(skip_local, P_SIZE)
    step_size = jax.nn.softplus(seg_dt.astype(jnp.float32) + bias_local[None, :])
    log_decay = -step_size * jnp.exp(rate_local)[None, :]
    blocks = seg_len // BLOCK
    lower_mask = jnp.tril(jnp.ones((BLOCK, BLOCK), dtype=bool))

    def block_step(state, blk):
        x_blk, b_blk, c_blk, dt_blk, log_blk = blk
        cum_log = jnp.cumsum(log_blk, axis=1)
        scores = jnp.einsum("in,jn->ij", c_blk, b_blk, preferred_element_type=jnp.float32)
        gap_log = cum_log[:, :, None] - cum_log[:, None, :]
        decay = jnp.where(lower_mask[None], jnp.exp(jnp.where(lower_mask[None], gap_log, 0.0)), 0.0)
        weights = (scores[None] * decay * dt_blk[:, None, :]).astype(jnp.bfloat16)
        intra = jnp.einsum(
            "hij,jhp->ihp",
            weights,
            x_blk.reshape(BLOCK, local_heads, P_SIZE),
            preferred_element_type=jnp.float32,
        ).reshape(BLOCK, head_width)
        last_log = cum_log[:, -1]
        x_float = x_blk.astype(jnp.float32)
        wx = (head_columns(jnp.exp(last_log[:, None] - cum_log) * dt_blk) * x_float).astype(
            jnp.bfloat16
        )
        fresh = jnp.einsum("jn,jk->nk", b_blk, wx, preferred_element_type=jnp.float32)
        inter = head_columns(jnp.exp(cum_log)) * jnp.dot(
            c_blk.astype(jnp.float32), state, precision=lax.Precision.HIGHEST
        )
        partial_value = intra + inter + skip_cols[None, :] * x_float
        new_state = jnp.repeat(jnp.exp(last_log), P_SIZE)[None, :] * state + fresh
        return (new_state, partial_value)

    start = jnp.zeros((N, head_width), jnp.float32)
    final, partials = lax.scan(
        block_step,
        start,
        (
            seg_x.reshape(blocks, BLOCK, head_width),
            seg_b.reshape(blocks, BLOCK, N),
            seg_c.reshape(blocks, BLOCK, N),
            jnp.transpose(step_size.reshape(blocks, BLOCK, local_heads), (0, 2, 1)),
            jnp.transpose(log_decay.reshape(blocks, BLOCK, local_heads), (0, 2, 1)),
        ),
    )
    partials = partials.reshape(seg_len, head_width)
    segment_decay = jnp.repeat(jnp.exp(jnp.sum(log_decay, axis=0)), P_SIZE)
    earlier_decay, incoming = entering(
        (segment_decay, final), "ctx", chain, (jnp.ones_like(segment_decay), jnp.zeros_like(final))
    )
    reach = jnp.repeat(jnp.exp(jnp.cumsum(log_decay, axis=0)), P_SIZE, axis=1)
    carried = reach * jnp.dot(seg_c.astype(jnp.float32), incoming, precision=lax.Precision.HIGHEST)
    result = (partials + carried).astype(jnp.bfloat16)
    return lax.all_to_all(result, "tp", split_axis=0, concat_axis=1, tiled=True)


def solution(mesh):
    return jax.shard_map(
        on_device,
        mesh=mesh,
        in_specs=(
            P(("ctx", "tp"), None),
            P(("ctx", "tp"), None),
            P(("ctx", "tp"), None),
            P(),
            P(),
            P(),
            P(),
            P(),
            P(),
            P(),
        ),
        out_specs=P(("ctx", "tp"), None),
        check_vma=False,
    )
```

profile of v0, /device:TPU:25, one launch (start us, length us, event | category | flops | bytes accessed | tf_op | source)
XLA Modules:
  0.0 295.3 jit_solution(16272385171868117972)
XLA Ops:
  8.1 3.4 %all-to-all-start.1 = ((bf16[128,4,32]{0,2,1:T(8,128)(2,1)}), bf16[128,4,32]{0,2,1:T(8,128)(2,1)S(1)}, u32[]{:S(2)}, u32[]{:S(2)}) async-start(bf16[128,4,32]{0,2,1:T(8,128)(2,1)} %bitcast.12), calls=%async_computation.1 | async-start | bytes 65536 | tf_op jit(solution)/shard_map/all_to_all | solution.py:74
  12.5 3.4 %collective-permute-start = (bf16[3,8192]{1,0:T(4,128)(2,1)S(1)}, bf16[3,8192]{1,0:T(4,128)(2,1)S(1)}, u32[]{:S(2)}, u32[]{:S(2)}) collective-permute-start(bf16[3,8192]{1,0:T(4,128)(2,1)S(1)} %slice.71), channel_id=1, source_target_pairs={{0,1},{1,2},{2,3},{3,4},{4,5},{5,6},{6,7},{7,8},{8,9},{9,10},{10,1... | collective-permute-start | bytes 147464 | tf_op jit(solution)/shard_map/ppermute | solution.py:17
  16.7 3.1 %collective-permute-start.1 = (bf16[3,2048]{1,0:T(4,128)(2,1)S(1)}, bf16[3,2048]{1,0:T(4,128)(2,1)S(1)}, u32[]{:S(2)}, u32[]{:S(2)}) collective-permute-start(bf16[3,2048]{1,0:T(4,128)(2,1)S(1)} %slice.80), channel_id=1, source_target_pairs={{0,1},{1,2},{2,3},{3,4},{4,5},{5,6},{6,7},{7,8},{8,9},{9,10},{10,1... | collective-permute-start | bytes 36872 | tf_op jit(solution)/shard_map/ppermute | solution.py:17
  26.8 2.7 multiply_convert_fusion.2
  29.5 2.4 copy.47
  32.0 3.6 %all-to-all-start = ((bf16[128,4,2048]{0,2,1:T(8,128)(2,1)}), bf16[128,4,2048]{0,2,1:T(8,128)(2,1)S(1)}, u32[]{:S(2)}, u32[]{:S(2)}) async-start(bf16[128,4,2048]{0,2,1:T(8,128)(2,1)} %bitcast.124), calls=%async_computation | async-start | bytes 4194304 | tf_op jit(solution)/shard_map/all_to_all | solution.py:73
  37.9 2.5 broadcast_in_dim.74
  40.4 5.4 %copy.59 = f32[512,2048]{1,0:T(8,128)} copy(f32[512,2048]{0,1:T(8,128)} %bitcast.121) | data formatting | bytes 8388608 | tf_op jit(solution)/shard_map/while/body/eval_jaxpr/reshape | solution.py:43
  46.0 19.9 %all-to-all-done = bf16[128,4,2048]{0,2,1:T(8,128)(2,1)S(1)} async-done(((bf16[128,4,2048]{0,2,1:T(8,128)(2,1)}), bf16[128,4,2048]{0,2,1:T(8,128)(2,1)S(1)}, u32[]{:S(2)}, u32[]{:S(2)}) %all-to-all-start) | async-done | bytes 2097184 | tf_op jit(solution)/shard_map/all_to_all | solution.py:73
  68.1 5.4 %copy.55 = f32[4,128,2048]{2,1,0:T(8,128)} copy(f32[4,128,2048]{1,2,0:T(8,128)} %bitcast_convert_fusion) | data formatting | bytes 8388608 | tf_op jit(solution)/shard_map/while/body/eval_jaxpr/convert_element_type | solution.py:103
  73.4 5.4 %fusion.9 = bf16[512,2048]{1,0:T(8,128)(2,1)} fusion(f32[512,2048]{1,0:T(8,128)} %copy.59, f32[4,128,2048]{2,1,0:T(8,128)} %copy.55), kind=kLoop, calls=%fused_computation.18 | loop fusion | flops 2097152 | bytes 10485760 | tf_op jit(solution)/shard_map/while/body/eval_jaxpr/convert_element_type | solution.py:104
  78.9 3.7 %convolution_add_fusion = f32[256,2048]{1,0:T(8,128)} fusion(bf16[512,2048]{1,0:T(8,128)(2,1)} %fusion.9, f32[2048]{0:T(1024)S(1)} %mul.253, bf16[512,2048]{1,0:T(8,128)(2,1)} %all-gather.5.cloned.1.call-done, s32[]{:T(128)S(6)} %select_n.56), kind=kOutput, calls=%fused_computation.20 | convolution fusion | flops 537395200 | bytes 4464644 | tf_op jit(solution)/shard_map/while/body/eval_jaxpr/jn,jk->nk/dot_general | solution.py:107
  83.3 15.0 %all-gather.1 = f32[8,1,2048]{2,1,0:T(1,128)S(1)} all-gather(f32[1,1,2048]{2,1,0:T(1,128)S(1)} %reshape.244), channel_id=1, replica_groups=mesh['ctx'=8,'tp'=4] {'ctx'}, dimensions={0}, use_global_device_ids=true | all-gather | bytes 73728 | tf_op jit(solution)/shard_map/all_gather | solution.py:22
  98.3 2.5 broadcast_in_dim.69
  100.8 5.5 %copy.53 = f32[512,2048]{1,0:T(8,128)} copy(f32[512,2048]{0,1:T(8,128)} %bitcast.122) | data formatting | bytes 8388608 | tf_op jit(solution)/shard_map/while/body/eval_jaxpr/reshape | solution.py:43
  107.9 2.5 broadcast_in_dim.71
  110.4 5.4 %copy.60 = f32[512,2048]{1,0:T(8,128)} copy(f32[512,2048]{0,1:T(8,128)} %bitcast.123) | data formatting | bytes 8388608 | tf_op jit(solution)/shard_map/reshape | solution.py:132
  115.8 10.7 %copy.48 = bf16[4,128,2048]{1,0,2:T(4,128)(2,1)} copy(bf16[4,128,2048]{1,2,0:T(8,128)(2,1)S(1)} %bitcast.120) | data formatting | bytes 4194304 | tf_op jit(solution)/shard_map/all_to_all | solution.py:73
  126.5 2.7 reshape.231
  130.6 11.9 %fusion = f32[32,64,512]{2,1,0:T(8,128)} fusion(bf16[512,32,64]{0,2,1:T(8,128)(2,1)S(1)} %reshape.231, f32[32,512]{1,0:T(8,128)S(1)} %get-tuple-element.91, f32[32,512]{1,0:T(8,128)S(1)} %copy_bitcast_fusion, f32[512,512]{1,0:T(8,128)S(1)} %fusion.17, pred[512,512]{1,0:T(8,128)(4,1)S(1)} %iota_compare_fusion), kind=kOutput, calls=%fused_computation.3 | convolution fusion | flops 1124073472 | bytes 7733248 | tf_op jit(solution)/shard_map/while/body/eval_jaxpr/hij,jhp->ihp/dot_general | solution.py:96
  142.6 5.4 %copy.54 = f32[512,2048]{1,0:T(8,128)} copy(f32[512,2048]{0,1:T(8,128)} %bitcast.128) | data formatting | bytes 8388608 | tf_op jit(solution)/shard_map/while/body/eval_jaxpr/reshape | solution.py:101
  148.0 4.8 %fusion.14 = f32[512,2048]{1,0:T(8,128)} fusion(bf16[512,2048]{1,0:T(8,128)(2,1)} %all-gather.5.cloned.1.call-done, s32[]{:T(128)S(6)} %select_n.55), kind=kOutput, calls=%fused_computation.30 | convolution fusion | flops 3221225472 | bytes 4456452 | tf_op jit(solution)/shard_map/while/body/eval_jaxpr/dot_general | solution.py:108
  152.7 79.0 %all-gather.7.cloned.1.call-done = f32[2048,2048]{1,0:T(8,128)} async-done(((f32[256,2048]{1,0:T(8,128)}), f32[2048,2048]{1,0:T(8,128)}) %all-gather.7.cloned.1.call-update) | async-done | bytes 16777232 | tf_op jit(solution)/shard_map/all_gather | solution.py:22
  232.0 17.5 %while.3 = (s32[]{:T(128)}, f32[256,2048]{1,0:T(8,128)S(1)}, s32[]{:T(128)}, f32[8,2048]{1,0:T(8,128)S(1)}, f32[8,256,2048]{2,1,0:T(8,128)}, /*index=5*/s32[]{:T(128)}, s32[]{:T(128)}, s32[]{:T(128)}) while((s32[]{:T(128)}, f32[256,2048]{1,0:T(8,128)S(1)}, s32[]{:T(128)}, f32[8,2048]{1,0:T(8,128)S(1)}, f32[8,256,2048]{2,1,0:T(8,128)}, ...), condition=%wide.region_6.7_spmd, body=%wide.region_5.6_spmd.sunk | while | flops 1048581 | bytes 6316159 | solution.py:30
  232.0 2.4 bitcast_add_fusion.3
  234.5 2.4 bitcast_add_fusion.3
  237.0 2.4 bitcast_add_fusion.3
  239.4 2.4 bitcast_add_fusion.3
  241.9 2.4 bitcast_add_fusion.3
  244.3 2.4 bitcast_add_fusion.3
  249.5 10.0 %fusion.8 = bf16[512,2048]{1,0:T(8,128)(2,1)S(1)} fusion(f32[4,128,2048]{2,1,0:T(8,128)} %copy.55, f32[512,2048]{1,0:T(8,128)} %copy.60, f32[512,2048]{1,0:T(8,128)} %copy.54, f32[512,2048]{1,0:T(8,128)} %copy.53, f32[512,2048]{1,0:T(8,128)} %fusion.14, f32[256,2048]{1,0:T(8,128)S(1)} %get-tuple-element.79, f32[2048]{0:T(1024)S(1)} %mul.245, ...), kind=kOutput, calls=%fused_computation.17 | convolution fusion | flops 3228565504 | bytes 25436164 | tf_op jit(solution)/shard_map/dot_general | solution.py:133
  259.5 27.6 %all_to_all.48 = bf16[4,128,2048]{2,1,0:T(8,128)(2,1)S(1)} all-to-all(bf16[4,128,2048]{2,1,0:T(8,128)(2,1)S(1)} %bitcast.126), channel_id=1, replica_groups=mesh['ctx'=8,'tp'=4] {'tp'}, dimensions={0} | all-to-all | bytes 4194304 | tf_op jit(solution)/shard_map/all_to_all | solution.py:135
  (71 shorter events, 22.8 us)
Async XLA Ops:
  6.5 19.6 %copy-start = (bf16[128,8192]{1,0:T(8,128)(2,1)S(1)}, bf16[128,8192]{1,0:T(8,128)(2,1)}, u32[]{:S(2)}) copy-start(bf16[128,8192]{1,0:T(8,128)(2,1)} %param.12) | copy-start | bytes 6291460
  8.1 23.8 %all-to-all-start.1 = ((bf16[128,4,32]{0,2,1:T(8,128)(2,1)}), bf16[128,4,32]{0,2,1:T(8,128)(2,1)S(1)}, u32[]{:S(2)}, u32[]{:S(2)}) async-start(bf16[128,4,32]{0,2,1:T(8,128)(2,1)} %bitcast.12), calls=%async_computation.1 | async-start | bytes 65536 | tf_op jit(solution)/shard_map/all_to_all | solution.py:74
  11.6 67.3 %all-gather.5.cloned.1.call-start = ((), (), s32[]{:S(2)}) async-start(), calls=%async_computation.3 | async-start | bytes 2621440 | tf_op jit(solution)/shard_map/all_gather | solution.py:76
  12.5 13.6 %collective-permute-start = (bf16[3,8192]{1,0:T(4,128)(2,1)S(1)}, bf16[3,8192]{1,0:T(4,128)(2,1)S(1)}, u32[]{:S(2)}, u32[]{:S(2)}) collective-permute-start(bf16[3,8192]{1,0:T(4,128)(2,1)S(1)} %slice.71), channel_id=1, source_target_pairs={{0,1},{1,2},{2,3},{3,4},{4,5},{5,6},{6,7},{7,8},{8,9},{9,10},{10,1... | collective-permute-start | bytes 147464 | tf_op jit(solution)/shard_map/ppermute | solution.py:17
  16.7 6.0 %collective-permute-start.1 = (bf16[3,2048]{1,0:T(4,128)(2,1)S(1)}, bf16[3,2048]{1,0:T(4,128)(2,1)S(1)}, u32[]{:S(2)}, u32[]{:S(2)}) collective-permute-start(bf16[3,2048]{1,0:T(4,128)(2,1)S(1)} %slice.80), channel_id=1, source_target_pairs={{0,1},{1,2},{2,3},{3,4},{4,5},{5,6},{6,7},{7,8},{8,9},{9,10},{10,1... | collective-permute-start | bytes 36872 | tf_op jit(solution)/shard_map/ppermute | solution.py:17
  26.1 0.8 copy-start.1
  29.5 6.2 %copy-start.2 = (f32[128]{0:T(128)S(1)}, f32[128]{0:T(128)}, u32[]{:S(2)}) copy-start(f32[128]{0:T(128)} %param.19) | copy-start | bytes 1540
  29.5 6.3 %copy-start.3 = (f32[128]{0:T(128)S(1)}, f32[128]{0:T(128)}, u32[]{:S(2)}) copy-start(f32[128]{0:T(128)} %param.20) | copy-start | bytes 1540
  32.0 33.8 %all-to-all-start = ((bf16[128,4,2048]{0,2,1:T(8,128)(2,1)}), bf16[128,4,2048]{0,2,1:T(8,128)(2,1)S(1)}, u32[]{:S(2)}, u32[]{:S(2)}) async-start(bf16[128,4,2048]{0,2,1:T(8,128)(2,1)} %bitcast.124), calls=%async_computation | async-start | bytes 4194304 | tf_op jit(solution)/shard_map/all_to_all | solution.py:73
  35.6 196.1 %all-gather.7.cloned.1.call-start = ((), (), s32[]{:S(2)}) async-start(), calls=%async_computation.4 | async-start | bytes 18874368 | tf_op jit(solution)/shard_map/all_gather | solution.py:22
  78.8 3.8 %copy-start.4 = (f32[128]{0:T(128)S(1)}, f32[128]{0:T(128)}, u32[]{:S(2)}) copy-start(f32[128]{0:T(128)} %param.21) | copy-start | bytes 1540
Sparse Core Ops, SparseCore 0:
  26.2 52.0 all-gather.4
  82.7 148.9 all-gather.6
where the time goes:
time: 297 us; the launch traced here: 295 us
  waiting for transfers between devices  99.6 us (34%)
  local copies, waits for them, and re-layouts  59.1 us (20%)
  blocking collectives  42.5 us (14%)
  other arithmetic  34.5 us (12%)
  matrix products  31.8 us (11%)
  between operations  13.7 us (5%)
  starting transfers between devices  13.6 us (5%)
    all_gather x1, waiting for transfers between devices, entering(): gathered = jax.tree.map(lambda a: lax.all_gather(a, axis), part)  79 us
    all_to_all x1, blocking collectives, on_device(): return lax.all_to_all(result, 'tp', split_axis=0, concat_axis=1, tiled=True)  27.6 us
    all_to_all x1, waiting for transfers between devices, on_device(): lax.all_to_all(x_part, 'tp', split_axis=1, concat_axis=0, tiled=True)  19.9 us
    add x7, other arithmetic, chain(): return (earlier[0] * later[0], later[0][None, :] * earlier[1] + later[1])  16.9 us
    all_gather x1, blocking collectives, entering(): gathered = jax.tree.map(lambda a: lax.all_gather(a, axis), part)  15 us
    dot_general x1, matrix products, block_step(): jnp.einsum('hij,jhp->ihp', weights, x_blk.reshape(BLOCK, local_heads, P_S...  11.9 us
    reshape x2, local copies, waits for them, and re-layouts, head_columns(): return jnp.repeat(head_major.T, P_SIZE, axis=1)  10.8 us
    all_to_all x1, local copies, waits for them, and re-layouts, on_device(): lax.all_to_all(x_part, 'tp', split_axis=1, concat_axis=0, tiled=True)  10.7 us
  transfers between devices with their start and end apart: 6, of which 3 were waited for; matrix products, arithmetic and copies ran while one was open for 31% of the time, Pallas kernels for 0%

commit v1 on v0

v1 whole, which is shorter than its diff:
```python
import numpy as np
import jax
import jax.numpy as jnp
from jax import lax
from jax.sharding import PartitionSpec as P

H = 128
P_SIZE = 64
N = 256
G = 4
CONV = 4
BLOCK = 512


def from_behind(value, axis, steps):
    count = lax.axis_size(axis)
    initial, last = (max(0, -steps), min(count, count - steps))
    return lax.ppermute(value, axis, [(source, source + steps) for source in range(initial, last)])


def conv_silu(raw, prior, weight, bias):
    rows = raw.shape[0]
    full = jnp.concatenate([prior, raw], axis=0).astype(jnp.float32)
    total = bias[None, :] + weight[0][None, :] * full[0:rows]
    for k in range(1, CONV):
        total = total + weight[k][None, :] * full[k : k + rows]
    return jax.nn.silu(total).astype(jnp.bfloat16)


def head_columns(head_major):
    return jnp.repeat(head_major, P_SIZE, axis=-1)


def on_device(
    x_in,
    bc_in,
    dt_in,
    conv_x_weight,
    conv_x_bias,
    conv_bc_weight,
    conv_bc_bias,
    dt_bias,
    a_log,
    skip,
):
    n_tp = lax.axis_size("tp")
    tp_index = lax.axis_index("tp")
    n_ctx = lax.axis_size("ctx")
    ctx_index = lax.axis_index("ctx")
    rows = x_in.shape[0]
    local_heads = H // n_tp
    head_width = local_heads * P_SIZE
    per_group = H // G
    rim = CONV - 1

    prior_x, prior_bc = from_behind((x_in[rows - rim :], bc_in[rows - rim :]), ("ctx", "tp"), 1)
    x_part = conv_silu(x_in, prior_x, conv_x_weight, conv_x_bias)
    bc_part = conv_silu(bc_in, prior_bc, conv_bc_weight, conv_bc_bias)

    group_of = [(k * local_heads) // per_group for k in range(n_tp)]
    bc_groups = bc_part.reshape(rows, 2, G, N)
    if group_of != list(range(G)):
        bc_groups = jnp.take(bc_groups, np.array(group_of), axis=2)
    bc_groups = jnp.transpose(bc_groups, (2, 0, 1, 3))
    seg_bc = lax.all_to_all(bc_groups, "tp", split_axis=0, concat_axis=0, tiled=True)
    seg_bc = seg_bc.reshape(n_tp * rows, 2, N)
    seg_x = lax.all_to_all(x_part, "tp", split_axis=1, concat_axis=0, tiled=True)
    seg_dt = lax.all_to_all(dt_in, "tp", split_axis=1, concat_axis=0, tiled=True)
    seg_len = seg_x.shape[0]
    blocks = seg_len // BLOCK
    seg_b = seg_bc[:, 0].reshape(blocks, BLOCK, N)
    seg_c = seg_bc[:, 1].reshape(blocks, BLOCK, N)

    bias_local = lax.dynamic_slice_in_dim(dt_bias, tp_index * local_heads, local_heads, 0)
    rate_local = lax.dynamic_slice_in_dim(a_log, tp_index * local_heads, local_heads, 0)
    skip_local = lax.dynamic_slice_in_dim(skip, tp_index * local_heads, local_heads, 0)
    step_size = jax.nn.softplus(seg_dt.astype(jnp.float32) + bias_local[None, :])
    log_decay = -step_size * jnp.exp(rate_local)[None, :]

    dt_blk = step_size.reshape(blocks, BLOCK, local_heads)
    cum = jnp.cumsum(log_decay.reshape(blocks, BLOCK, local_heads), axis=1)
    last = cum[:, -1]
    x_blk = seg_x.reshape(blocks, BLOCK, head_width)
    x_float = x_blk.astype(jnp.float32)

    wx = (head_columns(jnp.exp(last[:, None, :] - cum) * dt_blk) * x_float).astype(jnp.bfloat16)
    fresh = jnp.einsum("bjn,bjk->bnk", seg_b, wx, preferred_element_type=jnp.float32)
    block_decay = jnp.exp(last)
    starts = [None]
    state = fresh[0]
    prefix = [jnp.ones((local_heads,), jnp.float32)]
    for b in range(1, blocks):
        starts.append(state)
        prefix.append(prefix[-1] * block_decay[b - 1])
        state = head_columns(block_decay[b])[None, :] * state + fresh[b]
    final = state
    segment_decay = prefix[-1] * block_decay[blocks - 1]

    core = ctx_index % 2
    chip = ctx_index // 2
    chips = n_ctx // 2
    half_width = head_width // 2
    half_heads = local_heads // 2
    decays = lax.all_gather(segment_decay, "ctx")
    mate_final = lax.ppermute(final, "ctx", [(i, i ^ 1) for i in range(n_ctx)])
    even_final = jnp.where(core == 0, final, mate_final)
    odd_final = jnp.where(core == 0, mate_final, final)
    odd_decay = lax.dynamic_index_in_dim(decays, chip * 2 + 1, 0, False)
    lo = core * half_width
    chip_half = head_columns(lax.dynamic_slice_in_dim(odd_decay, core * half_heads, half_heads, 0))[
        None, :
    ] * lax.dynamic_slice_in_dim(even_final, lo, half_width, 1) + lax.dynamic_slice_in_dim(
        odd_final, lo, half_width, 1
    )
    gathered = lax.all_gather(chip_half, "ctx")

    lower_mask = jnp.tril(jnp.ones((BLOCK, BLOCK), dtype=bool))
    cum_t = jnp.transpose(cum, (0, 2, 1))
    dt_t = jnp.transpose(dt_blk, (0, 2, 1))
    partials = []
    for b in range(blocks):
        scores = jnp.einsum("in,jn->ij", seg_c[b], seg_b[b], preferred_element_type=jnp.float32)
        gap_log = cum_t[b][:, :, None] - cum_t[b][:, None, :]
        decay = jnp.where(lower_mask[None], jnp.exp(jnp.where(lower_mask[None], gap_log, 0.0)), 0.0)
        weights = (scores[None] * decay * dt_t[b][:, None, :]).astype(jnp.bfloat16)
        intra = jnp.einsum(
            "hij,jhp->ihp",
            weights,
            x_blk[b].reshape(BLOCK, local_heads, P_SIZE),
            preferred_element_type=jnp.float32,
        ).reshape(BLOCK, head_width)
        partials.append(intra + head_columns(skip_local)[None, :] * x_float[b])

    seg_ids = jnp.arange(n_ctx)[None, :]
    chip_ids = jnp.arange(chips)[:, None]
    between = (seg_ids >= 2 * chip_ids + 2) & (seg_ids < ctx_index)
    chip_weight = jnp.prod(jnp.where(between[:, :, None], decays[None], 1.0), axis=1)
    chip_weight = jnp.where(chip_ids < chip, chip_weight, 0.0)
    halves = []
    for q in range(2):
        part = gathered[q::2]
        wq = head_columns(chip_weight[:, q * half_heads : (q + 1) * half_heads])
        halves.append(jnp.sum(wq[:, None, :] * part, axis=0))
    incoming = jnp.concatenate(halves, axis=1) + jnp.where(core == 1, 1.0, 0.0) * even_final

    results = []
    for b in range(blocks):
        carried_state = head_columns(prefix[b])[None, :] * incoming
        if starts[b] is not None:
            carried_state = starts[b] + carried_state
        inter = head_columns(jnp.exp(cum[b])) * jnp.dot(
            seg_c[b].astype(jnp.float32), carried_state, precision=lax.Precision.HIGHEST
        )
        results.append((partials[b] + inter).astype(jnp.bfloat16))
    result = jnp.concatenate(results, axis=0) if blocks > 1 else results[0]
    return lax.all_to_all(result, "tp", split_axis=0, concat_axis=1, tiled=True)


def solution(mesh):
    return jax.shard_map(
        on_device,
        mesh=mesh,
        in_specs=(
            P(("ctx", "tp"), None),
            P(("ctx", "tp"), None),
            P(("ctx", "tp"), None),
            P(),
            P(),
            P(),
            P(),
            P(),
            P(),
            P(),
        ),
        out_specs=P(("ctx", "tp"), None),
        check_vma=False,
    )
```

time: 297 us -> 252 us (0.85)
  the two profiles are of different devices: /device:TPU:25 before, /device:TPU:16 now
where the time goes in v1:
time: 252 us; the launch traced here: 248 us
  waiting for transfers between devices  70.2 us (28%)
  local copies, waits for them, and re-layouts  52.3 us (21%)
  blocking collectives  38.4 us (15%)
  other arithmetic  31.9 us (13%)
  matrix products  20.8 us (8%)
  starting transfers between devices  20.2 us (8%)
  between operations  13.7 us (5%)
    all_gather x1, waiting for transfers between devices, on_device(): gathered = lax.all_gather(chip_half, 'ctx')  44 us
    all_to_all x1, blocking collectives, on_device(): return lax.all_to_all(result, 'tp', split_axis=0, concat_axis=1, tiled=True)  29.2 us
    all_to_all x1, waiting for transfers between devices, on_device(): lax.all_to_all(x_part, 'tp', split_axis=1, concat_axis=0, tiled=True)  19.4 us
    dot_general x1, matrix products, on_device(): jnp.einsum('hij,jhp->ihp', weights, x_blk[b].reshape(BLOCK, local_heads,...  13.1 us
    all_to_all x1, local copies, waits for them, and re-layouts, on_device(): lax.all_to_all(x_part, 'tp', split_axis=1, concat_axis=0, tiled=True)  10.7 us
    convert_element_type x2, other arithmetic, conv_silu(): return jax.nn.silu(total).astype(jnp.bfloat16)  10.3 us
    all_gather x1, blocking collectives, on_device(): decays = lax.all_gather(segment_decay, 'ctx')  9.21 us
    ppermute x2, starting transfers between devices, from_behind(): lax.ppermute(value, axis, [(source, source + steps) for source in range(i...  7.3 us
  transfers between devices with their start and end apart: 7, of which 3 were waited for; matrix products, arithmetic and copies ran while one was open for 26% of the time, Pallas kernels for 0%

profile of v1, /device:TPU:16, one launch (start us, length us, event | category | flops | bytes accessed | tf_op | source)
XLA Modules:
  0.0 247.6 jit_solution(16872940111737145043)
XLA Ops:
  6.5 1.5 copy.88
  8.0 3.7 %all-to-all-start.2 = ((bf16[128,4,32]{0,2,1:T(8,128)(2,1)}), bf16[128,4,32]{0,2,1:T(8,128)(2,1)S(1)}, u32[]{:S(2)}, u32[]{:S(2)}) async-start(bf16[128,4,32]{0,2,1:T(8,128)(2,1)} %bitcast.15), calls=%async_computation.2 | async-start | bytes 65536 | tf_op jit(solution)/shard_map/all_to_all | solution.py:68
  12.7 3.9 %collective-permute-start = (bf16[3,8192]{1,0:T(4,128)(2,1)S(1)}, bf16[3,8192]{1,0:T(4,128)(2,1)S(1)}, u32[]{:S(2)}, u32[]{:S(2)}) collective-permute-start(bf16[3,8192]{1,0:T(4,128)(2,1)S(1)} %slice.82), channel_id=1, source_target_pairs={{0,1},{1,2},{2,3},{3,4},{4,5},{5,6},{6,7},{7,8},{8,9},{9,10},{10,1... | collective-permute-start | bytes 147464 | tf_op jit(solution)/shard_map/ppermute | solution.py:18
  17.7 3.4 %collective-permute-start.1 = (bf16[3,2048]{0,1:T(8,128)(2,1)S(1)}, bf16[3,2048]{0,1:T(8,128)(2,1)S(1)}, u32[]{:S(2)}, u32[]{:S(2)}) collective-permute-start(bf16[3,2048]{0,1:T(8,128)(2,1)S(1)} %copy.84), channel_id=1, source_target_pairs={{0,1},{1,2},{2,3},{3,4},{4,5},{5,6},{6,7},{7,8},{8,9},{9,10},{10,1... | collective-permute-start | bytes 36872 | tf_op jit(solution)/shard_map/ppermute | solution.py:18
  23.3 1.3 copy.85
  24.6 6.8 %collective-permute-done.1 = bf16[3,2048]{0,1:T(8,128)(2,1)S(1)} collective-permute-done((bf16[3,2048]{0,1:T(8,128)(2,1)S(1)}, bf16[3,2048]{0,1:T(8,128)(2,1)S(1)}, u32[]{:S(2)}, u32[]{:S(2)}) %collective-permute-start.1) | collective-permute-done | bytes 12320 | tf_op jit(solution)/shard_map/ppermute | solution.py:18
  31.8 2.6 %multiply_convert_fusion.4 = bf16[128,2048]{0,1:T(8,128)(2,1)S(1)} fusion(f32[131,2048]{0,1:T(8,128)S(1)} %maximum_convert_fusion.1, f32[2048]{0:T(1024)S(1)} %bitcast.116, f32[2048]{0:T(1024)S(1)} %bitcast.117, f32[2048]{0:T(1024)S(1)} %bitcast.115, f32[2048]{0:T(1024)S(1)} %bitcast.114, f32[2048]{0:T(1024)S(1)} %copy-done.8), kind=kLoop, calls=%fused_computation.37 | loop fusion | flops 3407872 | bytes 4759552 | tf_op jit(solution)/shard_map/convert_element_type | solution.py:27
  35.3 2.6 %maximum_convert_fusion = f32[131,8192]{1,0:T(8,128)} fusion(bf16[128,8192]{1,0:T(8,128)(2,1)S(1)} %copy-done.4, bf16[3,8192]{1,0:T(4,128)(2,1)S(1)} %collective-permute-done), kind=kLoop, calls=%fused_computation.19 | loop fusion | flops 4292608 | bytes 6438912 | tf_op jit(solution)/shard_map/convert_element_type | solution.py:23
  38.0 5.0 %all-to-all-start.1 = ((bf16[4,128,2,256]{1,3,2,0:T(8,128)(2,1)}), bf16[4,128,2,256]{1,3,2,0:T(8,128)(2,1)S(1)}, u32[]{:S(2)}, u32[]{:S(2)}) async-start(bf16[4,128,2,256]{1,3,2,0:T(8,128)(2,1)} %copy.86), calls=%async_computation.1 | async-start | bytes 1048576 | tf_op jit(solution)/shard_map/all_to_all | solution.py:65
  43.0 7.7 %multiply_convert_fusion.3 = bf16[128,8192]{1,0:T(8,128)(2,1)S(1)} fusion(f32[131,8192]{1,0:T(8,128)} %maximum_convert_fusion, f32[8192]{0:T(1024)S(1)} %bitcast.112, f32[8192]{0:T(1024)S(1)} %bitcast.113, f32[8192]{0:T(1024)S(1)} %bitcast.111, f32[8192]{0:T(1024)S(1)} %bitcast.110, f32[8192]{0:T(1024)S(1)} %copy-done.7), kind=kLoop, calls=%fused_computation.18 | loop fusion | flops 13631488 | bytes 19038208 | tf_op jit(solution)/shard_map/convert_element_type | solution.py:27
  50.8 2.4 copy.82
  53.2 4.2 %all-to-all-start = ((bf16[128,4,2048]{0,2,1:T(8,128)(2,1)}), bf16[128,4,2048]{0,2,1:T(8,128)(2,1)S(1)}, u32[]{:S(2)}, u32[]{:S(2)}) async-start(bf16[128,4,2048]{0,2,1:T(8,128)(2,1)} %bitcast.95), calls=%async_computation | async-start | bytes 4194304 | tf_op jit(solution)/shard_map/all_to_all | solution.py:67
  63.5 19.4 %all-to-all-done = bf16[128,4,2048]{0,2,1:T(8,128)(2,1)S(1)} async-done(((bf16[128,4,2048]{0,2,1:T(8,128)(2,1)}), bf16[128,4,2048]{0,2,1:T(8,128)(2,1)S(1)}, u32[]{:S(2)}, u32[]{:S(2)}) %all-to-all-start) | async-done | bytes 2097184 | tf_op jit(solution)/shard_map/all_to_all | solution.py:67
  82.9 10.7 %copy.83 = bf16[4,128,2048]{1,0,2:T(4,128)(2,1)} copy(bf16[4,128,2048]{1,2,0:T(8,128)(2,1)S(1)} %bitcast.91) | data formatting | bytes 4194304 | tf_op jit(solution)/shard_map/all_to_all | solution.py:67
  93.6 4.1 %reshape_squeeze_reshape.3 = bf16[512,32,64]{0,2,1:T(8,128)(2,1)} reshape(bf16[4,128,2048]{1,0,2:T(4,128)(2,1)} %copy.83) | data formatting | bytes 4194304 | tf_op jit(solution)/shard_map/reshape;squeeze;reshape | solution.py:129
  97.7 2.1 multiply_convert_fusion.2
  99.8 2.1 fusion.19
  101.9 9.2 %all-gather = f32[8,1,32]{2,1,0:T(1,128)S(1)} all-gather(f32[1,1,32]{2,1,0:T(1,128)S(1)} %get-tuple-element.11), channel_id=2, replica_groups=mesh['ctx'=8,'tp'=4] {'ctx'}, dimensions={0}, use_global_device_ids=true | all-gather | bytes 1152 | tf_op jit(solution)/shard_map/all_gather | solution.py:104
  111.3 1.9 broadcast_select_fusion
  113.2 1.4 copy-done.2
  114.5 2.9 %fusion.12 = f32[256,1024]{1,0:T(8,128)} fusion(f32[256,2048]{1,0:T(8,128)} %fusion.19, s32[]{:T(128)S(6)} %select_n.93, f32[256,2048]{1,0:T(8,128)} %collective-permute-done.2, f32[256,2048]{1,0:T(8,128)S(1)} %broadcast_select_fusion, f32[1024]{0:T(1024)S(1)} %mul.254, pred[]{:T(512)S(6)} %eq.9), kind=kLoop, calls=%fused_computation.25 | loop fusion | flops 786432 | bytes 4198405 | tf_op jit(solution)/shard_map/add | solution.py:110
  119.5 2.5 broadcast_in_dim.85
  122.0 5.6 %copy.101 = f32[512,2048]{1,0:T(8,128)} copy(f32[512,2048]{0,1:T(8,128)} %bitcast.92) | data formatting | bytes 8388608 | tf_op jit(solution)/shard_map/reshape | solution.py:31
  127.9 13.1 %fusion = f32[32,64,512]{2,1,0:T(8,128)} fusion(bf16[512,32,64]{0,2,1:T(8,128)(2,1)} %reshape_squeeze_reshape.3, f32[32,512]{1,0:T(8,128)S(1)} %copy.94, f32[32,512]{1,0:T(8,128)S(1)} %bitcast_add_fusion.2, f32[512,512]{1,0:T(8,128)S(1)} %fusion.18, pred[512,512]{1,0:T(8,128)(4,1)S(1)} %copy-done.6), kind=kOutput, calls=%fused_computation.1 | convolution fusion | flops 1124073472 | bytes 7733248 | tf_op jit(solution)/shard_map/hij,jhp->ihp/dot_general | solution.py:126
  141.0 5.4 %copy.96 = f32[512,2048]{1,0:T(8,128)} copy(f32[512,2048]{0,1:T(8,128)} %bitcast.101) | data formatting | bytes 8388608 | tf_op jit(solution)/shard_map/reshape | solution.py:131
  146.4 2.2 bitcast_convert_fusion
  148.7 5.5 %copy.95 = f32[4,128,2048]{2,1,0:T(8,128)} copy(f32[4,128,2048]{1,2,0:T(8,128)} %bitcast_convert_fusion) | data formatting | bytes 8388608 | tf_op jit(solution)/shard_map/convert_element_type | solution.py:84
  154.1 44.0 %all-gather.4.cloned.1.call-done = f32[2048,1024]{1,0:T(8,128)} async-done(((f32[256,1024]{1,0:T(8,128)}), f32[2048,1024]{1,0:T(8,128)}) %all-gather.4.cloned.1.call-update) | async-done | bytes 8388624 | tf_op jit(solution)/shard_map/all_gather | solution.py:115
  198.2 5.1 %multiply_reduce_fusion.1 = (f32[256,1024]{1,0:T(8,128)S(1)}, f32[256,1024]{1,0:T(8,128)S(1)}) fusion(f32[8,256,1024]{2,1,0:T(8,128)} %bitcast.93, f32[4,1024]{1,0:T(4,128)S(1)} %mul.250, f32[4,1024]{1,0:T(4,128)S(1)} %mul.262), kind=kLoop, calls=%fused_computation.16 | loop fusion | flops 3670016 | bytes 10518528 | tf_op jit(solution)/shard_map/reduce_sum | solution.py:143
  204.7 5.3 %fusion.8 = bf16[512,2048]{1,0:T(8,128)(2,1)S(1)} fusion(f32[512,2048]{1,0:T(8,128)S(1)} %copy-done.1, f32[4,128,2048]{2,1,0:T(8,128)} %copy.95, f32[512,2048]{1,0:T(8,128)S(1)} %copy-done, f32[256,1024]{1,0:T(8,128)S(1)} %get-tuple-element.6, f32[256,1024]{1,0:T(8,128)S(1)} %get-tuple-element.5, f32[256,2048]{1,0:T(8,128)S(1)} %copy-done.3, ...), kind=kOutput, calls=%fused_computation.14 | convolution fusion | flops 3228041216 | bytes 19144708 | tf_op jit(solution)/shard_map/dot_general | solution.py:151
  210.0 29.2 %all_to_all.53 = bf16[4,128,2048]{2,1,0:T(8,128)(2,1)S(1)} all-to-all(bf16[4,128,2048]{2,1,0:T(8,128)(2,1)S(1)} %bitcast.94), channel_id=1, replica_groups=mesh['ctx'=8,'tp'=4] {'tp'}, dimensions={0} | all-to-all | bytes 4194304 | tf_op jit(solution)/shard_map/all_to_all | solution.py:156
  239.2 1.6 copy.106
  (79 shorter events, 15.6 us)
Async XLA Ops:
  6.5 25.3 %copy-start.8 = (f32[2048]{0:T(1024)S(1)}, f32[2048]{0:T(1024)}, u32[]{:S(2)}) copy-start(f32[2048]{0:T(1024)} %param.16) | copy-start | bytes 24580
  8.0 29.9 %all-to-all-start.2 = ((bf16[128,4,32]{0,2,1:T(8,128)(2,1)}), bf16[128,4,32]{0,2,1:T(8,128)(2,1)S(1)}, u32[]{:S(2)}, u32[]{:S(2)}) async-start(bf16[128,4,32]{0,2,1:T(8,128)(2,1)} %bitcast.15), calls=%async_computation.2 | async-start | bytes 65536 | tf_op jit(solution)/shard_map/all_to_all | solution.py:68
  12.7 22.6 %collective-permute-start = (bf16[3,8192]{1,0:T(4,128)(2,1)S(1)}, bf16[3,8192]{1,0:T(4,128)(2,1)S(1)}, u32[]{:S(2)}, u32[]{:S(2)}) collective-permute-start(bf16[3,8192]{1,0:T(4,128)(2,1)S(1)} %slice.82), channel_id=1, source_target_pairs={{0,1},{1,2},{2,3},{3,4},{4,5},{5,6},{6,7},{7,8},{8,9},{9,10},{10,1... | collective-permute-start | bytes 147464 | tf_op jit(solution)/shard_map/ppermute | solution.py:18
  17.7 13.7 %collective-permute-start.1 = (bf16[3,2048]{0,1:T(8,128)(2,1)S(1)}, bf16[3,2048]{0,1:T(8,128)(2,1)S(1)}, u32[]{:S(2)}, u32[]{:S(2)}) collective-permute-start(bf16[3,2048]{0,1:T(8,128)(2,1)S(1)} %copy.84), channel_id=1, source_target_pairs={{0,1},{1,2},{2,3},{3,4},{4,5},{5,6},{6,7},{7,8},{8,9},{9,10},{10,1... | collective-permute-start | bytes 36872 | tf_op jit(solution)/shard_map/ppermute | solution.py:18
  24.6 10.7 %copy-start.4 = (bf16[128,8192]{1,0:T(8,128)(2,1)S(1)}, bf16[128,8192]{1,0:T(8,128)(2,1)}, u32[]{:S(2)}) copy-start(bf16[128,8192]{1,0:T(8,128)(2,1)} %param.10) | copy-start | bytes 6291460
  34.5 8.5 %copy-start.7 = (f32[8192]{0:T(1024)S(1)}, f32[8192]{0:T(1024)}, u32[]{:S(2)}) copy-start(f32[8192]{0:T(1024)} %param.14) | copy-start | bytes 98308
  38.0 15.2 %all-to-all-start.1 = ((bf16[4,128,2,256]{1,3,2,0:T(8,128)(2,1)}), bf16[4,128,2,256]{1,3,2,0:T(8,128)(2,1)S(1)}, u32[]{:S(2)}, u32[]{:S(2)}) async-start(bf16[4,128,2,256]{1,3,2,0:T(8,128)(2,1)} %copy.86), calls=%async_computation.1 | async-start | bytes 1048576 | tf_op jit(solution)/shard_map/all_to_all | solution.py:65
  50.7 6.7 %copy-start.9 = (f32[128]{0:T(128)S(1)}, f32[128]{0:T(128)}, u32[]{:S(2)}) copy-start(f32[128]{0:T(128)} %param.17) | copy-start | bytes 1540
  50.8 6.7 %copy-start.10 = (f32[128]{0:T(128)S(1)}, f32[128]{0:T(128)}, u32[]{:S(2)}) copy-start(f32[128]{0:T(128)} %param.18) | copy-start | bytes 1540
  53.2 29.7 %all-to-all-start = ((bf16[128,4,2048]{0,2,1:T(8,128)(2,1)}), bf16[128,4,2048]{0,2,1:T(8,128)(2,1)S(1)}, u32[]{:S(2)}, u32[]{:S(2)}) async-start(bf16[128,4,2048]{0,2,1:T(8,128)(2,1)} %bitcast.95), calls=%async_computation | async-start | bytes 4194304 | tf_op jit(solution)/shard_map/all_to_all | solution.py:67
  57.4 140.8 %all-gather.4.cloned.1.call-start = ((), (), s32[]{:S(2)}) async-start(), calls=%async_computation.4 | async-start | bytes 9437184 | tf_op jit(solution)/shard_map/all_gather | solution.py:115
  101.9 9.4 %collective-permute-start.2 = (f32[256,2048]{1,0:T(8,128)}, f32[256,2048]{1,0:T(8,128)}, u32[]{:S(2)}, u32[]{:S(2)}) collective-permute-start(f32[256,2048]{1,0:T(8,128)} %fusion.19), channel_id=1, source_target_pairs={{0,4},{4,0},{8,12},{12,8},{16,20},{20,16},{24,28},{28,24},{1,5},{5... | collective-permute-start | bytes 6291464 | tf_op jit(solution)/shard_map/ppermute | solution.py:105
  113.2 1.4 copy-start.2
  114.5 2.9 %copy-start.11 = (f32[128]{0:T(128)S(1)}, f32[128]{0:T(128)}, u32[]{:S(2)}) copy-start(f32[128]{0:T(128)} %param.19) | copy-start | bytes 1540
  114.5 4.6 %copy-start.5 = (f32[32,512]{0,1:T(8,128)S(1)}, f32[32,512]{0,1:T(8,128)}, u32[]{:S(2)}) copy-start(f32[32,512]{0,1:T(8,128)} %get-tuple-element.10) | copy-start | bytes 196612
  122.0 5.9 %copy-start.6 = (pred[512,512]{1,0:T(8,128)(4,1)S(1)}, pred[512,512]{1,0:T(8,128)(4,1)}, u32[]{:S(2)}) copy-start(pred[512,512]{1,0:T(8,128)(4,1)} %iota_compare_fusion) | copy-start | bytes 786436
  198.2 5.1 %copy-start = (f32[512,2048]{1,0:T(8,128)S(1)}, f32[512,2048]{1,0:T(8,128)}, u32[]{:S(2)}) copy-start(f32[512,2048]{1,0:T(8,128)} %copy.101) | copy-start | bytes 12582916
  198.2 5.9 %copy-start.1 = (f32[512,2048]{1,0:T(8,128)S(1)}, f32[512,2048]{1,0:T(8,128)}, u32[]{:S(2)}) copy-start(f32[512,2048]{1,0:T(8,128)} %copy.96) | copy-start | bytes 12582916
  198.2 6.5 %copy-start.3 = (f32[256,2048]{1,0:T(8,128)S(1)}, f32[256,2048]{1,0:T(8,128)}, u32[]{:S(2)}) copy-start(f32[256,2048]{1,0:T(8,128)} %copy-done.2) | copy-start | bytes 6291460
Sparse Core Ops, SparseCore 0:
  117.5 80.5 all-gather.3

commit v2 on v1

--- a/solution.py
+++ b/solution.py
@@ -3,6 +3,8 @@
 import jax.numpy as jnp
 from jax import lax
 from jax.sharding import PartitionSpec as P
+from jax.experimental import pallas as pl
+from jax.experimental.pallas import tpu as pltpu
 
 H = 128
 P_SIZE = 64
@@ -18,13 +20,80 @@
     return lax.ppermute(value, axis, [(source, source + steps) for source in range(initial, last)])
 
 
-def conv_silu(raw, prior, weight, bias):
-    rows = raw.shape[0]
-    full = jnp.concatenate([prior, raw], axis=0).astype(jnp.float32)
+def conv_rows(full, rows, weight, bias):
     total = bias[None, :] + weight[0][None, :] * full[0:rows]
     for k in range(1, CONV):
         total = total + weight[k][None, :] * full[k : k + rows]
     return jax.nn.silu(total).astype(jnp.bfloat16)
+
+
+def conv_silu(raw, prior, weight, bias):
+    rows = raw.shape[0]
+    rim = CONV - 1
+    zero_prior = jnp.zeros((rim, raw.shape[1]), jnp.float32)
+    body = conv_rows(jnp.concatenate([zero_prior, raw.astype(jnp.float32)], axis=0), rows, weight, bias)
+    edge = jnp.concatenate([prior, raw[:rim]], axis=0).astype(jnp.float32)
+    return lax.dynamic_update_slice_in_dim(body, conv_rows(edge, rim, weight, bias), 0, 0)
+
+
+def intra_kernel(x_ref, s_ref, cum_ref, cumt_ref, dtt_ref, skip_ref, o_ref):
+    tiles = BLOCK // 128
+    lane_head = lax.broadcasted_iota(jnp.int32, cum_ref.shape, 1)
+    row_head = lax.broadcasted_iota(jnp.int32, cumt_ref.shape, 0)
+    lane = lax.broadcasted_iota(jnp.int32, (128, 128), 1)
+
+    def pair(p, carry):
+        off = pl.multiple_of(p * 128, 128)
+        xp = x_ref[:, pl.ds(off, 128)]
+        cum_all = cum_ref[...]
+        cumt_all = cumt_ref[...]
+        dtt_all = dtt_ref[...]
+        cols, rows, dts = [], [], []
+        for k in range(2):
+            h = 2 * p + k
+            cols.append(jnp.sum(jnp.where(lane_head == h, cum_all, 0.0), axis=1, keepdims=True))
+            rows.append(jnp.sum(jnp.where(row_head == h, cumt_all, 0.0), axis=0, keepdims=True))
+            dts.append(jnp.sum(jnp.where(row_head == h, dtt_all, 0.0), axis=0, keepdims=True))
+        skip_p = skip_ref[:, pl.ds(off, 128)]
+        for r in range(tiles):
+            width = (r + 1) * 128
+            s_tile = s_ref[r * 128 : width, 0:width]
+            lower = lax.broadcasted_iota(jnp.int32, (128, width), 1) <= (
+                lax.broadcasted_iota(jnp.int32, (128, width), 0) + r * 128
+            )
+            res = []
+            for k in range(2):
+                gap = cols[k][r * 128 : width] - rows[k][:, 0:width]
+                decay = jnp.where(lower, jnp.exp(jnp.where(lower, gap, 0.0)), 0.0)
+                w = (s_tile * decay * dts[k][:, 0:width]).astype(jnp.bfloat16)
+                res.append(jnp.dot(w, xp[0:width], preferred_element_type=jnp.float32))
+            out = jnp.where(lane < P_SIZE, res[0], res[1])
+            o_ref[r * 128 : width, pl.ds(off, 128)] = out + skip_p * xp[r * 128 : width].astype(jnp.float32)
+        return carry
+
+    lax.fori_loop(0, x_ref.shape[1] // 128, pair, 0)
+
+
+def intra_block(x, scores, cum, dt, skip_cols):
+    heads = cum.shape[1]
+    width = x.shape[1]
+    cum_lanes = jnp.pad(cum, ((0, 0), (0, 128 - heads)))
+    pad_rows = (-heads) % 8
+    cum_rows = jnp.pad(cum.T, ((0, pad_rows), (0, 0)))
+    dt_rows = jnp.pad(dt.T, ((0, pad_rows), (0, 0)))
+    vmem = pl.BlockSpec(memory_space=pltpu.VMEM)
+    return pl.pallas_call(
+        intra_kernel,
+        out_shape=jax.ShapeDtypeStruct((BLOCK, width), jnp.float32),
+        in_specs=[vmem] * 6,
+        out_specs=vmem,
+        name="ssd_intra",
+        cost_estimate=pl.CostEstimate(
+            flops=2 * BLOCK * BLOCK * width * 2,
+            transcendentals=heads * BLOCK * BLOCK,
+            bytes_accessed=BLOCK * width * 6 + BLOCK * BLOCK * 4,
+        ),
+    )(x, scores, cum_lanes, cum_rows, dt_rows, skip_cols[None, :])
 
 
 def head_columns(head_major):
@@ -101,35 +170,30 @@
     chips = n_ctx // 2
     half_width = head_width // 2
     half_heads = local_heads // 2
-    decays = lax.all_gather(segment_decay, "ctx")
-    mate_final = lax.ppermute(final, "ctx", [(i, i ^ 1) for i in range(n_ctx)])
+    decay_slab = jnp.pad(segment_decay[None, :], ((0, 7), (0, head_width - local_heads)))
+    mate = lax.ppermute(
+        jnp.concatenate([final, decay_slab], axis=0), "ctx", [(i, i ^ 1) for i in range(n_ctx)]
+    )
+    mate_final = mate[:N]
     even_final = jnp.where(core == 0, final, mate_final)
     odd_final = jnp.where(core == 0, mate_final, final)
-    odd_decay = lax.dynamic_index_in_dim(decays, chip * 2 + 1, 0, False)
+    odd_decay = jnp.where(core == 0, mate[N, :local_heads], segment_decay)
     lo = core * half_width
     chip_half = head_columns(lax.dynamic_slice_in_dim(odd_decay, core * half_heads, half_heads, 0))[
         None, :
     ] * lax.dynamic_slice_in_dim(even_final, lo, half_width, 1) + lax.dynamic_slice_in_dim(
         odd_final, lo, half_width, 1
     )
-    gathered = lax.all_gather(chip_half, "ctx")
-
-    lower_mask = jnp.tril(jnp.ones((BLOCK, BLOCK), dtype=bool))
-    cum_t = jnp.transpose(cum, (0, 2, 1))
-    dt_t = jnp.transpose(dt_blk, (0, 2, 1))
+    gathered = lax.all_gather(
+        jnp.concatenate([chip_half, decay_slab[:, :half_width]], axis=0), "ctx"
+    )
+    decays = gathered[:, N, :local_heads]
+
+    skip_cols = head_columns(skip_local)
     partials = []
     for b in range(blocks):
         scores = jnp.einsum("in,jn->ij", seg_c[b], seg_b[b], preferred_element_type=jnp.float32)
-        gap_log = cum_t[b][:, :, None] - cum_t[b][:, None, :]
-        decay = jnp.where(lower_mask[None], jnp.exp(jnp.where(lower_mask[None], gap_log, 0.0)), 0.0)
-        weights = (scores[None] * decay * dt_t[b][:, None, :]).astype(jnp.bfloat16)
-        intra = jnp.einsum(
-            "hij,jhp->ihp",
-            weights,
-            x_blk[b].reshape(BLOCK, local_heads, P_SIZE),
-            preferred_element_type=jnp.float32,
-        ).reshape(BLOCK, head_width)
-        partials.append(intra + head_columns(skip_local)[None, :] * x_float[b])
+        partials.append(intra_block(x_blk[b], scores, cum[b], dt_blk[b], skip_cols))
 
     seg_ids = jnp.arange(n_ctx)[None, :]
     chip_ids = jnp.arange(chips)[:, None]
@@ -138,7 +202,7 @@
     chip_weight = jnp.where(chip_ids < chip, chip_weight, 0.0)
     halves = []
     for q in range(2):
-        part = gathered[q::2]
+        part = gathered[q::2, :N]
         wq = head_columns(chip_weight[:, q * half_heads : (q + 1) * half_heads])
         halves.append(jnp.sum(wq[:, None, :] * part, axis=0))
     incoming = jnp.concatenate(halves, axis=1) + jnp.where(core == 1, 1.0, 0.0) * even_final

time: 252 us -> 245 us (0.972)
  matrix products: 20.8 us -> 4.65 us
  waiting for transfers between devices: 70.2 us -> 85.4 us
  Pallas kernels: 0 us -> 13.3 us
  blocking collectives: 38.4 us -> 29.2 us
  local copies, waits for them, and re-layouts: 52.3 us -> 45.7 us
    pallas_call x0 -> x1, Pallas kernels: none -> 13.3 us  [intra_block(): pl.pallas_call(intra_kernel, out_shape=jax.ShapeDtypeStruct((BLOCK, width...]
    dot_general x1 -> x0, matrix products: 13.1 us -> none  [on_device(): jnp.einsum('hij,jhp->ihp', weights, x_blk[b].reshape(BLOCK, local_heads,...]
    all_gather x1, waiting for transfers between devices: 44 us -> 54.1 us  [on_device(): lax.all_gather(jnp.concatenate([chip_half, decay_slab[:, :half_width]], a...]
    convert_element_type x1 -> x2, local copies, waits for them, and re-layouts: 5.48 us -> 15.4 us  [on_device(): x_float = x_blk.astype(jnp.float32)]
    all_gather x1 -> x0, blocking collectives: 9.21 us -> none  [on_device(): decays = lax.all_gather(segment_decay, 'ctx')]
    all_to_all x1, local copies, waits for them, and re-layouts: 10.7 us -> 2.58 us  [on_device(): lax.all_to_all(x_part, 'tp', split_axis=1, concat_axis=0, tiled=True)]
    ppermute x2, waiting for transfers between devices: 6.77 us -> 0.01 us  [from_behind(): lax.ppermute(value, axis, [(source, source + steps) for source in range(i...]
    reshape x2 -> x0, local copies, waits for them, and re-layouts: 5.52 us -> none  [the longest x1 5.42 us: on_device(): intra = jnp.einsum('hij,jhp->ihp', weights, x_blk[b].reshape(BLOCK, local...]
  transfers between devices with their start and end apart: 7 -> 7, of which waited for: 3 -> 4; matrix products, arithmetic and copies ran while one was open for 26% -> 17% of each run, Pallas kernels for 0% -> 6%
where the time goes in v2:
time: 245 us; the launch traced here: 241 us
  waiting for transfers between devices  85.4 us (35%)
  local copies, waits for them, and re-layouts  45.7 us (19%)
  other arithmetic  30.8 us (13%)
  blocking collectives  29.2 us (12%)
  starting transfers between devices  18.5 us (8%)
  between operations  13.8 us (6%)
  Pallas kernels  13.3 us (5%)
  matrix products  4.65 us (2%)
    all_gather x1, waiting for transfers between devices, on_device(): lax.all_gather(jnp.concatenate([chip_half, decay_slab[:, :half_width]], a...  54.1 us
    all_to_all x1, blocking collectives, on_device(): return lax.all_to_all(result, 'tp', split_axis=0, concat_axis=1, tiled=True)  29.2 us
    all_to_all x1, waiting for transfers between devices, on_device(): lax.all_to_all(x_part, 'tp', split_axis=1, concat_axis=0, tiled=True)  21.8 us
    convert_element_type x2, local copies, waits for them, and re-layouts, on_device(): x_float = x_blk.astype(jnp.float32)  15.4 us
    pallas_call x1, Pallas kernels, intra_block(): pl.pallas_call(intra_kernel, out_shape=jax.ShapeDtypeStruct((BLOCK, width...  13.3 us
    convert_element_type x4, other arithmetic, conv_rows(): return jax.nn.silu(total).astype(jnp.bfloat16)  10.4 us
    ppermute x2, starting transfers between devices, from_behind(): lax.ppermute(value, axis, [(source, source + steps) for source in range(i...  7.43 us
    reshape x1, local copies, waits for them, and re-layouts, head_columns(): return jnp.repeat(head_major, P_SIZE, axis=-1)  5.74 us
  transfers between devices with their start and end apart: 7, of which 4 were waited for; matrix products, arithmetic and copies ran while one was open for 17% of the time, Pallas kernels for 6%

profile of v2, /device:TPU:16, one launch (start us, length us, event | category | flops | bytes accessed | tf_op | source)
XLA Modules:
  0.0 241.3 jit_solution(9909602000359701767)
XLA Ops:
  6.5 1.5 copy.84
  8.0 3.7 %all-to-all-start.2 = ((bf16[128,4,32]{0,2,1:T(8,128)(2,1)}), bf16[128,4,32]{0,2,1:T(8,128)(2,1)S(1)}, u32[]{:S(2)}, u32[]{:S(2)}) async-start(bf16[128,4,32]{0,2,1:T(8,128)(2,1)} %bitcast.16), calls=%async_computation.2 | async-start | bytes 65536 | tf_op jit(solution)/shard_map/all_to_all | solution.py:137
  12.7 3.9 %collective-permute-start = (bf16[3,8192]{1,0:T(4,128)(2,1)S(1)}, bf16[3,8192]{1,0:T(4,128)(2,1)S(1)}, u32[]{:S(2)}, u32[]{:S(2)}) collective-permute-start(bf16[3,8192]{1,0:T(4,128)(2,1)S(1)} %get-tuple-element.13), channel_id=1, source_target_pairs={{0,1},{1,2},{2,3},{3,4},{4,5},{5,6},{6,7},{7,8},{8,9},{9,10},{10,1... | collective-permute-start | bytes 147464 | tf_op jit(solution)/shard_map/ppermute | solution.py:20
  17.5 3.5 %collective-permute-start.1 = (bf16[3,2048]{1,0:T(4,128)(2,1)S(1)}, bf16[3,2048]{1,0:T(4,128)(2,1)S(1)}, u32[]{:S(2)}, u32[]{:S(2)}) collective-permute-start(bf16[3,2048]{1,0:T(4,128)(2,1)S(1)} %get-tuple-element.15), channel_id=1, source_target_pairs={{0,1},{1,2},{2,3},{3,4},{4,5},{5,6},{6,7},{7,8},{8,9},{9,10},{10,1... | collective-permute-start | bytes 36872 | tf_op jit(solution)/shard_map/ppermute | solution.py:20
  21.0 4.0 %convert_element_type.93 = f32[128,8192]{1,0:T(8,128)} convert(bf16[128,8192]{1,0:T(8,128)(2,1)} %param.10) | non-fusion elementwise | flops 1048576 | bytes 6291456 | tf_op jit(solution)/shard_map/convert_element_type | solution.py:34
  25.8 7.6 %multiply_convert_fusion.1 = bf16[128,8192]{1,0:T(8,128)(2,1)S(1)} fusion(f32[128,8192]{1,0:T(8,128)} %convert_element_type.93, f32[8192]{0:T(1024)S(1)} %bitcast.97, f32[8192]{0:T(1024)S(1)} %bitcast.99, f32[8192]{0:T(1024)S(1)} %bitcast.95, f32[8192]{0:T(1024)S(1)} %bitcast.93, f32[8192]{0:T(1024)S(1)} %copy-done.8), kind=kLoop, calls=%fused_computation.4 | loop fusion | flops 13631488 | bytes 6455296 | tf_op jit(solution)/shard_map/convert_element_type | solution.py:27
  33.3 2.6 %multiply_convert_fusion.2 = bf16[128,2048]{0,1:T(8,128)(2,1)S(1)} fusion(f32[128,2048]{0,1:T(8,128)S(1)} %convert_element_type.97, f32[2048]{0:T(1024)S(1)} %bitcast.105, f32[2048]{0:T(1024)S(1)} %bitcast.107, f32[2048]{0:T(1024)S(1)} %bitcast.103, f32[2048]{0:T(1024)S(1)} %bitcast.101, f32[2048]{0:T(1024)S(1)} %copy-done.10), kind=kLoop, calls=%fused_computation.27 | loop fusion | flops 3407872 | bytes 1613824 | tf_op jit(solution)/shard_map/convert_element_type | solution.py:27
  36.4 2.0 dynamic_update_slice.7
  39.3 3.5 %all-to-all-start.1 = ((bf16[4,128,2,256]{1,3,2,0:T(8,128)(2,1)}), bf16[4,128,2,256]{1,3,2,0:T(8,128)(2,1)S(1)}, u32[]{:S(2)}, u32[]{:S(2)}) async-start(bf16[4,128,2,256]{1,3,2,0:T(8,128)(2,1)} %copy.82), calls=%async_computation.1 | async-start | bytes 1048576 | tf_op jit(solution)/shard_map/all_to_all | solution.py:134
  43.9 2.4 %copy.78 = bf16[128,8192]{0,1:T(8,128)(2,1)} copy(bf16[128,8192]{1,0:T(8,128)(2,1)S(1)} %dynamic_update_slice.6) | data formatting | bytes 4194304 | tf_op jit(solution)/shard_map/dynamic_update_slice | solution.py:36
  46.4 5.0 %all-to-all-done.1 = bf16[4,128,2,256]{1,3,2,0:T(8,128)(2,1)S(1)} async-done(((bf16[4,128,2,256]{1,3,2,0:T(8,128)(2,1)}), bf16[4,128,2,256]{1,3,2,0:T(8,128)(2,1)S(1)}, u32[]{:S(2)}, u32[]{:S(2)}) %all-to-all-start.1) | async-done | bytes 524320 | tf_op jit(solution)/shard_map/all_to_all | solution.py:134
  51.3 3.6 %all-to-all-start = ((bf16[128,4,2048]{0,2,1:T(8,128)(2,1)}), bf16[128,4,2048]{0,2,1:T(8,128)(2,1)S(1)}, u32[]{:S(2)}, u32[]{:S(2)}) async-start(bf16[128,4,2048]{0,2,1:T(8,128)(2,1)} %bitcast.80), calls=%async_computation | async-start | bytes 4194304 | tf_op jit(solution)/shard_map/all_to_all | solution.py:136
  55.6 1.2 reduce-window.6
  57.8 21.8 %all-to-all-done = bf16[128,4,2048]{0,2,1:T(8,128)(2,1)S(1)} async-done(((bf16[128,4,2048]{0,2,1:T(8,128)(2,1)}), bf16[128,4,2048]{0,2,1:T(8,128)(2,1)S(1)}, u32[]{:S(2)}, u32[]{:S(2)}) %all-to-all-start) | async-done | bytes 2097184 | tf_op jit(solution)/shard_map/all_to_all | solution.py:136
  80.8 9.9 %copy.91 = f32[4,128,2048]{1,0,2:T(4,128)} copy(f32[4,128,2048]{1,2,0:T(8,128)S(1)} %bitcast_convert_fusion) | data formatting | bytes 8388608 | tf_op jit(solution)/shard_map/convert_element_type | solution.py:153
  90.8 5.5 %reshape.292 = f32[512,32,64]{0,2,1:T(8,128)} reshape(f32[4,128,2048]{1,0,2:T(4,128)} %copy.91) | data formatting | bytes 8388608 | tf_op jit(solution)/shard_map/convert_element_type | solution.py:153
  96.3 2.8 %multiply_convert_fusion = bf16[512,32,64]{0,2,1:T(8,128)(2,1)S(1)} fusion(f32[512,32,64]{0,2,1:T(8,128)} %reshape.292, f32[512,32]{0,1:T(8,128)S(1)} %multiply_bitcast_fusion), kind=kLoop, calls=%fused_computation.3 | loop fusion | flops 2097152 | bytes 6356992 | tf_op jit(solution)/shard_map/convert_element_type | solution.py:155
  99.9 1.5 pad_maximum_fusion
  101.4 4.6 %collective-permute-done.2 = f32[264,2048]{1,0:T(8,128)} collective-permute-done((f32[264,2048]{1,0:T(8,128)}, f32[264,2048]{1,0:T(8,128)}, u32[]{:S(2)}, u32[]{:S(2)}) %collective-permute-start.2) | collective-permute-done | bytes 2162720 | tf_op jit(solution)/shard_map/ppermute | solution.py:174
  106.9 2.0 broadcast_select_fusion
  110.2 1.1 pad_maximum_fusion.1
  113.2 2.5 %broadcast_in_dim.64 = f32[512,32,64]{0,2,1:T(8,128)} broadcast(f32[512,32]{0,1:T(8,128)S(1)} %get-tuple-element.9), dimensions={0,1} | broadcast | bytes 4259840 | tf_op jit(solution)/shard_map/broadcast_in_dim | solution.py:100
  115.6 5.7 %copy.92 = f32[512,2048]{1,0:T(8,128)} copy(f32[512,2048]{0,1:T(8,128)} %bitcast.78) | data formatting | bytes 8388608 | tf_op jit(solution)/shard_map/reshape | solution.py:100
  122.1 1.3 fusion.14.s_ref
  123.4 2.6 %copy.79 = bf16[4,128,2048]{2,1,0:T(8,128)(2,1)} copy(bf16[4,128,2048]{1,2,0:T(8,128)(2,1)S(1)} %bitcast.77) | data formatting | bytes 4194304 | tf_op jit(solution)/shard_map/all_to_all | solution.py:136
  126.0 13.3 %ssd_intra.1 = f32[512,2048]{1,0:T(8,128)} custom-call(bf16[512,2048]{1,0:T(8,128)(2,1)} %bitcast.89, f32[512,512]{1,0:T(8,128)} %fusion.14.s_ref, f32[512,128]{1,0:T(8,128)} %pad.10.clone.cum_ref, f32[32,512]{1,0:T(8,128)} %bitcast.92, f32[32,512]{1,0:T(8,128)} %fusion.21.dtt_ref, f32[1,2048]{1,0:T(1,128)} %broadcast_in_dim_reshape.2.skip_ref), custom_call_target="tpu_custom_call" | custom-call | flops 2147483648 | bytes 7340032 | tf_op jit(solution)/shard_map/ssd_intra/pallas_call | solution.py:85
  139.3 54.1 %all-gather.3.cloned.1.call-done = f32[2112,1024]{1,0:T(8,128)} async-done(((f32[264,1024]{1,0:T(8,128)}), f32[2112,1024]{1,0:T(8,128)}) %all-gather.3.cloned.1.call-update) | async-done | bytes 8650768 | tf_op jit(solution)/shard_map/all_gather | solution.py:187
  194.7 5.1 %multiply_reduce_fusion.1 = (f32[256,1024]{1,0:T(8,128)S(1)}, f32[256,1024]{1,0:T(8,128)S(1)}) fusion(f32[8,264,1024]{2,1,0:T(8,128)} %bitcast.84, f32[4,1024]{1,0:T(4,128)S(1)} %mul.309, f32[4,1024]{1,0:T(4,128)S(1)} %mul.312), kind=kLoop, calls=%fused_computation.2 | loop fusion | flops 3670016 | bytes 10518528 | tf_op jit(solution)/shard_map/reduce_sum | solution.py:207
  200.0 1.2 copy-done.5
  201.2 2.6 %add_convert_fusion = bf16[512,2048]{1,0:T(8,128)(2,1)S(1)} fusion(f32[512,2048]{1,0:T(8,128)S(1)} %copy-done.5, f32[512,2048]{1,0:T(8,128)S(1)} %copy-done.2, f32[256,1024]{1,0:T(8,128)S(1)} %get-tuple-element.6, f32[256,1024]{1,0:T(8,128)S(1)} %get-tuple-element.5, f32[256,2048]{1,0:T(8,128)S(1)} %copy-done.4, f32[]{:T(128)S(6)} %select_n.86, ...), kind=kOutput, calls=%fused_computation | convolution fusion | flops 3225944064 | bytes 14942212 | tf_op jit(solution)/shard_map/dot_general | solution.py:215
  203.8 29.2 %all_to_all.56 = bf16[4,128,2048]{2,1,0:T(8,128)(2,1)S(1)} all-to-all(bf16[4,128,2048]{2,1,0:T(8,128)(2,1)S(1)} %bitcast.82), channel_id=1, replica_groups=mesh['ctx'=8,'tp'=4] {'tp'}, dimensions={0} | all-to-all | bytes 4194304 | tf_op jit(solution)/shard_map/all_to_all | solution.py:220
  233.0 1.5 copy.98
  (91 shorter events, 14.9 us)
Async XLA Ops:
  8.0 31.3 %all-to-all-start.2 = ((bf16[128,4,32]{0,2,1:T(8,128)(2,1)}), bf16[128,4,32]{0,2,1:T(8,128)(2,1)S(1)}, u32[]{:S(2)}, u32[]{:S(2)}) async-start(bf16[128,4,32]{0,2,1:T(8,128)(2,1)} %bitcast.16), calls=%async_computation.2 | async-start | bytes 65536 | tf_op jit(solution)/shard_map/all_to_all | solution.py:137
  12.7 26.4 %collective-permute-start = (bf16[3,8192]{1,0:T(4,128)(2,1)S(1)}, bf16[3,8192]{1,0:T(4,128)(2,1)S(1)}, u32[]{:S(2)}, u32[]{:S(2)}) collective-permute-start(bf16[3,8192]{1,0:T(4,128)(2,1)S(1)} %get-tuple-element.13), channel_id=1, source_target_pairs={{0,1},{1,2},{2,3},{3,4},{4,5},{5,6},{6,7},{7,8},{8,9},{9,10},{10,1... | collective-permute-start | bytes 147464 | tf_op jit(solution)/shard_map/ppermute | solution.py:20
  17.5 7.5 %copy-start.7 = (bf16[128,2048]{1,0:T(8,128)(2,1)S(1)}, bf16[128,2048]{1,0:T(8,128)(2,1)}, u32[]{:S(2)}) copy-start(bf16[128,2048]{1,0:T(8,128)(2,1)} %param.11) | copy-start | bytes 1572868
  17.5 7.8 %copy-start.9 = (f32[4,8192]{1,0:T(4,128)S(1)}, f32[4,8192]{1,0:T(4,128)}, u32[]{:S(2)}) copy-start(f32[4,8192]{1,0:T(4,128)} %param.13) | copy-start | bytes 393220
  17.5 7.9 %copy-start.11 = (f32[4,2048]{1,0:T(4,128)S(1)}, f32[4,2048]{1,0:T(4,128)}, u32[]{:S(2)}) copy-start(f32[4,2048]{1,0:T(4,128)} %param.15) | copy-start | bytes 98308
  17.5 18.4 %collective-permute-start.1 = (bf16[3,2048]{1,0:T(4,128)(2,1)S(1)}, bf16[3,2048]{1,0:T(4,128)(2,1)S(1)}, u32[]{:S(2)}, u32[]{:S(2)}) collective-permute-start(bf16[3,2048]{1,0:T(4,128)(2,1)S(1)} %get-tuple-element.15), channel_id=1, source_target_pairs={{0,1},{1,2},{2,3},{3,4},{4,5},{5,6},{6,7},{7,8},{8,9},{9,10},{10,1... | collective-permute-start | bytes 36872 | tf_op jit(solution)/shard_map/ppermute | solution.py:20
  25.0 0.8 copy-start.8
  25.8 7.6 %copy-start.10 = (f32[2048]{0:T(1024)S(1)}, f32[2048]{0:T(1024)}, u32[]{:S(2)}) copy-start(f32[2048]{0:T(1024)} %param.16) | copy-start | bytes 24580
  39.3 12.1 %all-to-all-start.1 = ((bf16[4,128,2,256]{1,3,2,0:T(8,128)(2,1)}), bf16[4,128,2,256]{1,3,2,0:T(8,128)(2,1)S(1)}, u32[]{:S(2)}, u32[]{:S(2)}) async-start(bf16[4,128,2,256]{1,3,2,0:T(8,128)(2,1)} %copy.82), calls=%async_computation.1 | async-start | bytes 1048576 | tf_op jit(solution)/shard_map/all_to_all | solution.py:134
  46.4 8.8 %copy-start.12 = (f32[128]{0:T(128)S(1)}, f32[128]{0:T(128)}, u32[]{:S(2)}) copy-start(f32[128]{0:T(128)} %param.17) | copy-start | bytes 1540
  46.4 8.9 %copy-start.13 = (f32[128]{0:T(128)S(1)}, f32[128]{0:T(128)}, u32[]{:S(2)}) copy-start(f32[128]{0:T(128)} %param.18) | copy-start | bytes 1540
  51.3 28.2 %all-to-all-start = ((bf16[128,4,2048]{0,2,1:T(8,128)(2,1)}), bf16[128,4,2048]{0,2,1:T(8,128)(2,1)S(1)}, u32[]{:S(2)}, u32[]{:S(2)}) async-start(bf16[128,4,2048]{0,2,1:T(8,128)(2,1)} %bitcast.80), calls=%async_computation | async-start | bytes 4194304 | tf_op jit(solution)/shard_map/all_to_all | solution.py:136
  54.9 138.4 %all-gather.3.cloned.1.call-start = ((), (), s32[]{:S(2)}) async-start(), calls=%async_computation.4 | async-start | bytes 9732096 | tf_op jit(solution)/shard_map/all_gather | solution.py:187
  57.2 55.1 %copy-start.6 = (f32[1,32,512]{2,1,0:T(8,128)}, f32[1,32,512]{2,1,0:T(8,128)S(1)}, u32[]{:S(2)}) copy-start(f32[1,32,512]{2,1,0:T(8,128)S(1)} %get-tuple-element.10) | copy-start | bytes 196612
  79.5 1.3 copy-start
  101.4 4.6 %collective-permute-start.2 = (f32[264,2048]{1,0:T(8,128)}, f32[264,2048]{1,0:T(8,128)}, u32[]{:S(2)}, u32[]{:S(2)}) collective-permute-start(f32[264,2048]{1,0:T(8,128)} %pad_maximum_fusion), channel_id=1, source_target_pairs={{0,4},{4,0},{8,12},{12,8},{16,20},{20,16},{24,28},{28,24},{1,5},{5... | collective-permute-start | bytes 6488072 | tf_op jit(solution)/shard_map/ppermute | solution.py:174
  108.9 1.3 copy-start.3
  110.2 1.1 copy-start.14
  115.6 7.8 %copy-start.1 = (bf16[128,4,2048]{0,2,1:T(8,128)(2,1)S(1)}, bf16[128,4,2048]{0,2,1:T(8,128)(2,1)}, u32[]{:S(2)}) copy-start(bf16[128,4,2048]{0,2,1:T(8,128)(2,1)} %copy-done) | copy-start | bytes 6291460
  194.7 5.1 %copy-start.2 = (f32[512,2048]{1,0:T(8,128)S(1)}, f32[512,2048]{1,0:T(8,128)}, u32[]{:S(2)}) copy-start(f32[512,2048]{1,0:T(8,128)} %copy.92) | copy-start | bytes 12582916
  194.7 5.3 %copy-start.4 = (f32[256,2048]{1,0:T(8,128)S(1)}, f32[256,2048]{1,0:T(8,128)}, u32[]{:S(2)}) copy-start(f32[256,2048]{1,0:T(8,128)} %copy-done.3) | copy-start | bytes 6291460
  194.7 6.5 %copy-start.5 = (f32[512,2048]{1,0:T(8,128)S(1)}, f32[512,2048]{1,0:T(8,128)}, u32[]{:S(2)}) copy-start(f32[512,2048]{1,0:T(8,128)} %ssd_intra.1) | copy-start | bytes 12582916
Sparse Core Ops, SparseCore 0:
  111.5 81.8 all-gather.2

commit v3 on v2

--- a/solution.py
+++ b/solution.py
@@ -96,6 +96,48 @@
     )(x, scores, cum_lanes, cum_rows, dt_rows, skip_cols[None, :])
 
 
+def fresh_kernel(x_ref, bt_ref, cum_ref, dtl_ref, o_ref):
+    lane_head = lax.broadcasted_iota(jnp.int32, cum_ref.shape, 1)
+    lane = lax.broadcasted_iota(jnp.int32, (BLOCK, 128), 1)
+
+    def pair(p, carry):
+        off = pl.multiple_of(p * 128, 128)
+        xp = x_ref[:, pl.ds(off, 128)].astype(jnp.float32)
+        cum_all = cum_ref[...]
+        dt_all = dtl_ref[...]
+        factors = []
+        for k in range(2):
+            h = 2 * p + k
+            c = jnp.sum(jnp.where(lane_head == h, cum_all, 0.0), axis=1, keepdims=True)
+            d = jnp.sum(jnp.where(lane_head == h, dt_all, 0.0), axis=1, keepdims=True)
+            factors.append(jnp.exp(c[BLOCK - 1 : BLOCK] - c) * d)
+        wx = (jnp.where(lane < P_SIZE, factors[0], factors[1]) * xp).astype(jnp.bfloat16)
+        o_ref[:, pl.ds(off, 128)] = jnp.dot(bt_ref[...], wx, preferred_element_type=jnp.float32)
+        return carry
+
+    lax.fori_loop(0, x_ref.shape[1] // 128, pair, 0)
+
+
+def fresh_block(x, b, cum, dt):
+    heads = cum.shape[1]
+    width = x.shape[1]
+    cum_lanes = jnp.pad(cum, ((0, 0), (0, 128 - heads)))
+    dt_lanes = jnp.pad(dt, ((0, 0), (0, 128 - heads)))
+    vmem = pl.BlockSpec(memory_space=pltpu.VMEM)
+    return pl.pallas_call(
+        fresh_kernel,
+        out_shape=jax.ShapeDtypeStruct((N, width), jnp.float32),
+        in_specs=[vmem] * 4,
+        out_specs=vmem,
+        name="ssd_fresh",
+        cost_estimate=pl.CostEstimate(
+            flops=2 * BLOCK * N * width,
+            transcendentals=heads * BLOCK,
+            bytes_accessed=BLOCK * width * 2 + N * width * 4 + BLOCK * N * 2,
+        ),
+    )(x, b.T, cum_lanes, dt_lanes)
+
+
 def head_columns(head_major):
     return jnp.repeat(head_major, P_SIZE, axis=-1)
 
@@ -150,10 +192,8 @@
     cum = jnp.cumsum(log_decay.reshape(blocks, BLOCK, local_heads), axis=1)
     last = cum[:, -1]
     x_blk = seg_x.reshape(blocks, BLOCK, head_width)
-    x_float = x_blk.astype(jnp.float32)
-
-    wx = (head_columns(jnp.exp(last[:, None, :] - cum) * dt_blk) * x_float).astype(jnp.bfloat16)
-    fresh = jnp.einsum("bjn,bjk->bnk", seg_b, wx, preferred_element_type=jnp.float32)
+
+    fresh = [fresh_block(x_blk[b], seg_b[b], cum[b], dt_blk[b]) for b in range(blocks)]
     block_decay = jnp.exp(last)
     starts = [None]
     state = fresh[0]

time: 245 us -> 242 us (0.988)
  local copies, waits for them, and re-layouts: 45.7 us -> 31.4 us
  Pallas kernels: 13.3 us -> 25 us
    convert_element_type x2 -> x0, local copies, waits for them, and re-layouts: 15.4 us -> none  [on_device(): x_float = x_blk.astype(jnp.float32)]
    pallas_call x0 -> x1, Pallas kernels: none -> 11.9 us  [fresh_block(): pl.pallas_call(fresh_kernel, out_shape=jax.ShapeDtypeStruct((N, width), j...]
    convert_element_type x2 -> x1, other arithmetic: 3.12 us -> 0.01 us  [on_device(): seg_dt.astype(jnp.float32) + bias_local[None, :]]
    all_gather x1, waiting for transfers between devices: 54.1 us -> 56.9 us  [on_device(): lax.all_gather(jnp.concatenate([chip_half, decay_slab[:, :half_width]], a...]
    dynamic_update_slice x3 -> x2, local copies, waits for them, and re-layouts: 5.37 us -> 2.93 us  [conv_silu(): lax.dynamic_update_slice_in_dim(body, conv_rows(edge, rim, weight, bias),...]
    unnamed x33 -> x36, local copies, waits for them, and re-layouts: 5.62 us -> 6.59 us
where the time goes in v3:
time: 242 us; the launch traced here: 238 us
  waiting for transfers between devices  87.4 us (36%)
  local copies, waits for them, and re-layouts  31.4 us (13%)
  blocking collectives  29.2 us (12%)
  other arithmetic  28.8 us (12%)
  Pallas kernels  25 us (10%)
  starting transfers between devices  18.5 us (8%)
  between operations  13.8 us (6%)
  matrix products  3.96 us (2%)
    all_gather x1, waiting for transfers between devices, on_device(): lax.all_gather(jnp.concatenate([chip_half, decay_slab[:, :half_width]], a...  56.9 us
    all_to_all x1, blocking collectives, on_device(): return lax.all_to_all(result, 'tp', split_axis=0, concat_axis=1, tiled=True)  29.2 us
    all_to_all x1, waiting for transfers between devices, on_device(): lax.all_to_all(x_part, 'tp', split_axis=1, concat_axis=0, tiled=True)  19.9 us
    pallas_call x1, Pallas kernels, intra_block(): pl.pallas_call(intra_kernel, out_shape=jax.ShapeDtypeStruct((BLOCK, width...  13.1 us
    pallas_call x1, Pallas kernels, fresh_block(): pl.pallas_call(fresh_kernel, out_shape=jax.ShapeDtypeStruct((N, width), j...  11.9 us
    convert_element_type x4, other arithmetic, conv_rows(): return jax.nn.silu(total).astype(jnp.bfloat16)  10.4 us
    ppermute x2, starting transfers between devices, from_behind(): lax.ppermute(value, axis, [(source, source + steps) for source in range(i...  7.3 us
    unnamed x36, local copies, waits for them, and re-layouts  6.59 us
  transfers between devices with their start and end apart: 7, of which 4 were waited for; matrix products, arithmetic and copies ran while one was open for 17% of the time, Pallas kernels for 6%

profile of v3, /device:TPU:16, one launch (start us, length us, event | category | flops | bytes accessed | tf_op | source)
XLA Modules:
  0.0 238.1 jit_solution(9740253816302109936)
XLA Ops:
  6.5 1.5 copy.104
  8.0 3.7 %all-to-all-start.2 = ((bf16[128,4,32]{0,2,1:T(8,128)(2,1)}), bf16[128,4,32]{0,2,1:T(8,128)(2,1)S(1)}, u32[]{:S(2)}, u32[]{:S(2)}) async-start(bf16[128,4,32]{0,2,1:T(8,128)(2,1)} %bitcast.14), calls=%async_computation.2 | async-start | bytes 65536 | tf_op jit(solution)/shard_map/all_to_all | solution.py:179
  12.5 3.9 %collective-permute-start.1 = (bf16[3,2048]{1,0:T(4,128)(2,1)S(1)}, bf16[3,2048]{1,0:T(4,128)(2,1)S(1)}, u32[]{:S(2)}, u32[]{:S(2)}) collective-permute-start(bf16[3,2048]{1,0:T(4,128)(2,1)S(1)} %get-tuple-element.13), channel_id=1, source_target_pairs={{0,1},{1,2},{2,3},{3,4},{4,5},{5,6},{6,7},{7,8},{8,9},{9,10},{10,1... | collective-permute-start | bytes 36872 | tf_op jit(solution)/shard_map/ppermute | solution.py:20
  16.5 1.0 fusion.33
  17.5 3.4 %collective-permute-start = (bf16[3,8192]{1,0:T(4,128)(2,1)S(1)}, bf16[3,8192]{1,0:T(4,128)(2,1)S(1)}, u32[]{:S(2)}, u32[]{:S(2)}) collective-permute-start(bf16[3,8192]{1,0:T(4,128)(2,1)S(1)} %get-tuple-element.11), channel_id=1, source_target_pairs={{0,1},{1,2},{2,3},{3,4},{4,5},{5,6},{6,7},{7,8},{8,9},{9,10},{10,1... | collective-permute-start | bytes 147464 | tf_op jit(solution)/shard_map/ppermute | solution.py:20
  20.9 1.3 copy.100
  22.2 4.0 %convert_element_type.56 = f32[128,8192]{1,0:T(8,128)} convert(bf16[128,8192]{1,0:T(8,128)(2,1)} %param.10) | non-fusion elementwise | flops 1048576 | bytes 6291456 | tf_op jit(solution)/shard_map/convert_element_type | solution.py:34
  26.5 2.6 %multiply_convert_fusion.1 = bf16[128,2048]{0,1:T(8,128)(2,1)S(1)} fusion(f32[128,2048]{0,1:T(8,128)S(1)} %convert_element_type.60, f32[2048]{0:T(1024)S(1)} %bitcast.102, f32[2048]{0:T(1024)S(1)} %bitcast.104, f32[2048]{0:T(1024)S(1)} %bitcast.100, f32[2048]{0:T(1024)S(1)} %bitcast.98, f32[2048]{0:T(1024)S(1)} %copy-done.10), kind=kLoop, calls=%fused_computation.27 | loop fusion | flops 3407872 | bytes 1613824 | tf_op jit(solution)/shard_map/convert_element_type | solution.py:27
  29.1 7.5 %multiply_convert_fusion = bf16[128,8192]{1,0:T(8,128)(2,1)S(1)} fusion(f32[128,8192]{1,0:T(8,128)} %convert_element_type.56, f32[8192]{0:T(1024)S(1)} %bitcast.94, f32[8192]{0:T(1024)S(1)} %bitcast.96, f32[8192]{0:T(1024)S(1)} %bitcast.92, f32[8192]{0:T(1024)S(1)} %bitcast.90, f32[8192]{0:T(1024)S(1)} %copy-done.8), kind=kLoop, calls=%fused_computation.3 | loop fusion | flops 13631488 | bytes 6455296 | tf_op jit(solution)/shard_map/convert_element_type | solution.py:27
  38.3 2.0 dynamic_update_slice.7
  41.2 3.5 %all-to-all-start.1 = ((bf16[4,128,2,256]{1,3,2,0:T(8,128)(2,1)}), bf16[4,128,2,256]{1,3,2,0:T(8,128)(2,1)S(1)}, u32[]{:S(2)}, u32[]{:S(2)}) async-start(bf16[4,128,2,256]{1,3,2,0:T(8,128)(2,1)} %copy.102), calls=%async_computation.1 | async-start | bytes 1048576 | tf_op jit(solution)/shard_map/all_to_all | solution.py:176
  45.9 1.5 copy.119
  47.3 5.9 %all-to-all-done.1 = bf16[4,128,2,256]{1,3,2,0:T(8,128)(2,1)S(1)} async-done(((bf16[4,128,2,256]{1,3,2,0:T(8,128)(2,1)}), bf16[4,128,2,256]{1,3,2,0:T(8,128)(2,1)S(1)}, u32[]{:S(2)}, u32[]{:S(2)}) %all-to-all-start.1) | async-done | bytes 524320 | tf_op jit(solution)/shard_map/all_to_all | solution.py:176
  53.3 3.7 %all-to-all-start = ((bf16[128,4,2048]{2,0,1:T(8,128)(2,1)}), bf16[128,4,2048]{2,0,1:T(8,128)(2,1)S(1)}, u32[]{:S(2)}, u32[]{:S(2)}) async-start(bf16[128,4,2048]{2,0,1:T(8,128)(2,1)} %bitcast.79), calls=%async_computation | async-start | bytes 4194304 | tf_op jit(solution)/shard_map/all_to_all | solution.py:178
  57.7 1.2 reduce-window.6
  61.7 19.9 %all-to-all-done = bf16[128,4,2048]{2,0,1:T(8,128)(2,1)S(1)} async-done(((bf16[128,4,2048]{2,0,1:T(8,128)(2,1)}), bf16[128,4,2048]{2,0,1:T(8,128)(2,1)S(1)}, u32[]{:S(2)}, u32[]{:S(2)}) %all-to-all-start) | async-done | bytes 2097184 | tf_op jit(solution)/shard_map/all_to_all | solution.py:178
  81.6 1.3 copy-done.4
  82.9 11.9 %ssd_fresh.1 = f32[256,2048]{1,0:T(8,128)} custom-call(bf16[512,2048]{1,0:T(8,128)(2,1)} %bitcast.77, bf16[256,512]{1,0:T(8,128)(2,1)} %slice_bitcast_fusion.3.bt_ref, f32[512,128]{1,0:T(8,128)} %pad.14.cum_ref, f32[512,128]{1,0:T(8,128)} %pad.15.dtl_ref), custom_call_target="tpu_custom_call" | custom-call | flops 536870912 | bytes 4456448 | tf_op jit(solution)/shard_map/ssd_fresh/pallas_call | solution.py:127
  94.8 3.3 %pad_maximum_fusion = f32[264,2048]{1,0:T(8,128)} fusion(f32[8,2048]{1,0:T(8,128)S(1)} %pad.16, f32[256,2048]{1,0:T(8,128)} %ssd_fresh.1), kind=kLoop, calls=%fused_computation.10 | loop fusion | flops 540672 | bytes 4325376 | tf_op jit(solution)/shard_map/concatenate | solution.py:215
  98.1 4.6 %collective-permute-done.2 = f32[264,2048]{1,0:T(8,128)} collective-permute-done((f32[264,2048]{1,0:T(8,128)}, f32[264,2048]{1,0:T(8,128)}, u32[]{:S(2)}, u32[]{:S(2)}) %collective-permute-start.2) | collective-permute-done | bytes 2162720 | tf_op jit(solution)/shard_map/ppermute | solution.py:214
  103.6 2.0 broadcast_select_fusion
  107.0 1.1 pad_maximum_fusion.1
  110.6 2.5 %broadcast_in_dim.61 = f32[512,32,64]{0,2,1:T(8,128)} broadcast(f32[512,32]{0,1:T(8,128)S(1)} %copy.111), dimensions={0,1} | broadcast | bytes 4259840 | tf_op jit(solution)/shard_map/broadcast_in_dim | solution.py:142
  113.0 5.6 %copy.112 = f32[512,2048]{1,0:T(8,128)} copy(f32[512,2048]{0,1:T(8,128)} %bitcast.75) | data formatting | bytes 8388608 | tf_op jit(solution)/shard_map/reshape | solution.py:142
  118.7 1.3 fusion.14.s_ref
  120.0 13.1 %ssd_intra.1 = f32[512,2048]{1,0:T(8,128)} custom-call(bf16[512,2048]{1,0:T(8,128)(2,1)} %bitcast.78, f32[512,512]{1,0:T(8,128)} %fusion.14.s_ref, f32[512,128]{1,0:T(8,128)} %pad.14.cum_ref, f32[32,512]{1,0:T(8,128)} %copy.109.cumt_ref, f32[32,512]{1,0:T(8,128)} %copy.110.dtt_ref, f32[1,2048]{1,0:T(1,128)} %broadcast_in_dim_reshape.2.skip_ref), custom_call_target="tpu_custom_call" | custom-call | flops 2147483648 | bytes 7340032 | tf_op jit(solution)/shard_map/ssd_intra/pallas_call | solution.py:85
  133.1 56.9 %all-gather.3.cloned.1.call-done = f32[2112,1024]{1,0:T(8,128)} async-done(((f32[264,1024]{1,0:T(8,128)}), f32[2112,1024]{1,0:T(8,128)}) %all-gather.3.cloned.1.call-update) | async-done | bytes 8650768 | tf_op jit(solution)/shard_map/all_gather | solution.py:227
  191.4 5.1 %multiply_reduce_fusion.1 = (f32[256,1024]{1,0:T(8,128)S(1)}, f32[256,1024]{1,0:T(8,128)S(1)}) fusion(f32[8,264,1024]{2,1,0:T(8,128)} %bitcast.83, f32[4,1024]{1,0:T(4,128)S(1)} %mul.286, f32[4,1024]{1,0:T(4,128)S(1)} %mul.289), kind=kLoop, calls=%fused_computation.2 | loop fusion | flops 3670016 | bytes 10518528 | tf_op jit(solution)/shard_map/reduce_sum | solution.py:247
  196.7 1.2 copy-done.5
  197.9 2.7 %add_convert_fusion = bf16[512,2048]{1,0:T(8,128)(2,1)S(1)} fusion(f32[512,2048]{1,0:T(8,128)S(1)} %copy-done.5, f32[512,2048]{1,0:T(8,128)S(1)} %copy-done.1, f32[256,1024]{1,0:T(8,128)S(1)} %get-tuple-element.6, f32[256,1024]{1,0:T(8,128)S(1)} %get-tuple-element.5, f32[256,2048]{1,0:T(8,128)S(1)} %copy-done.3, f32[]{:T(128)S(6)} %select_n.82, ...), kind=kOutput, calls=%fused_computation | convolution fusion | flops 3225944064 | bytes 14942212 | tf_op jit(solution)/shard_map/dot_general | solution.py:255
  200.6 29.2 %all_to_all.56 = bf16[4,128,2048]{2,1,0:T(8,128)(2,1)S(1)} all-to-all(bf16[4,128,2048]{2,1,0:T(8,128)(2,1)S(1)} %bitcast.81), channel_id=1, replica_groups=mesh['ctx'=8,'tp'=4] {'tp'}, dimensions={0} | all-to-all | bytes 4194304 | tf_op jit(solution)/shard_map/all_to_all | solution.py:260
  229.8 1.5 copy.116
  (94 shorter events, 14.3 us)
Async XLA Ops:
  8.0 33.2 %all-to-all-start.2 = ((bf16[128,4,32]{0,2,1:T(8,128)(2,1)}), bf16[128,4,32]{0,2,1:T(8,128)(2,1)S(1)}, u32[]{:S(2)}, u32[]{:S(2)}) async-start(bf16[128,4,32]{0,2,1:T(8,128)(2,1)} %bitcast.14), calls=%async_computation.2 | async-start | bytes 65536 | tf_op jit(solution)/shard_map/all_to_all | solution.py:179
  12.5 25.4 %collective-permute-start.1 = (bf16[3,2048]{1,0:T(4,128)(2,1)S(1)}, bf16[3,2048]{1,0:T(4,128)(2,1)S(1)}, u32[]{:S(2)}, u32[]{:S(2)}) collective-permute-start(bf16[3,2048]{1,0:T(4,128)(2,1)S(1)} %get-tuple-element.13), channel_id=1, source_target_pairs={{0,1},{1,2},{2,3},{3,4},{4,5},{5,6},{6,7},{7,8},{8,9},{9,10},{10,1... | collective-permute-start | bytes 36872 | tf_op jit(solution)/shard_map/ppermute | solution.py:20
  17.5 23.6 %collective-permute-start = (bf16[3,8192]{1,0:T(4,128)(2,1)S(1)}, bf16[3,8192]{1,0:T(4,128)(2,1)S(1)}, u32[]{:S(2)}, u32[]{:S(2)}) collective-permute-start(bf16[3,8192]{1,0:T(4,128)(2,1)S(1)} %get-tuple-element.11), channel_id=1, source_target_pairs={{0,1},{1,2},{2,3},{3,4},{4,5},{5,6},{6,7},{7,8},{8,9},{9,10},{10,1... | collective-permute-start | bytes 147464 | tf_op jit(solution)/shard_map/ppermute | solution.py:20
  22.2 4.1 %copy-start.11 = (f32[4,2048]{1,0:T(4,128)S(1)}, f32[4,2048]{1,0:T(4,128)}, u32[]{:S(2)}) copy-start(f32[4,2048]{1,0:T(4,128)} %param.15) | copy-start | bytes 98308
  22.2 4.1 %copy-start.9 = (f32[4,8192]{1,0:T(4,128)S(1)}, f32[4,8192]{1,0:T(4,128)}, u32[]{:S(2)}) copy-start(f32[4,8192]{1,0:T(4,128)} %param.13) | copy-start | bytes 393220
  22.2 4.2 %copy-start.10 = (f32[2048]{0:T(1024)S(1)}, f32[2048]{0:T(1024)}, u32[]{:S(2)}) copy-start(f32[2048]{0:T(1024)} %param.16) | copy-start | bytes 24580
  26.2 2.9 %copy-start.8 = (f32[8192]{0:T(1024)S(1)}, f32[8192]{0:T(1024)}, u32[]{:S(2)}) copy-start(f32[8192]{0:T(1024)} %param.14) | copy-start | bytes 98308
  29.1 7.5 %copy-start.14 = (f32[128]{0:T(128)S(1)}, f32[128]{0:T(128)}, u32[]{:S(2)}) copy-start(f32[128]{0:T(128)} %param.18) | copy-start | bytes 1540
  29.1 8.2 %copy-start.15 = (f32[128]{0:T(128)S(1)}, f32[128]{0:T(128)}, u32[]{:S(2)}) copy-start(f32[128]{0:T(128)} %param.17) | copy-start | bytes 1540
  41.2 12.1 %all-to-all-start.1 = ((bf16[4,128,2,256]{1,3,2,0:T(8,128)(2,1)}), bf16[4,128,2,256]{1,3,2,0:T(8,128)(2,1)S(1)}, u32[]{:S(2)}, u32[]{:S(2)}) async-start(bf16[4,128,2,256]{1,3,2,0:T(8,128)(2,1)} %copy.102), calls=%async_computation.1 | async-start | bytes 1048576 | tf_op jit(solution)/shard_map/all_to_all | solution.py:176
  53.3 4.1 %copy-start.6 = (bf16[4,128,2,256]{1,3,2,0:T(8,128)(2,1)}, bf16[4,128,2,256]{1,3,2,0:T(8,128)(2,1)S(1)}, u32[]{:S(2)}) copy-start(bf16[4,128,2,256]{1,3,2,0:T(8,128)(2,1)S(1)} %all-to-all-done.1) | copy-start | bytes 1572868
  53.3 4.2 %copy-start.12 = (f32[32]{0:T(128)S(1)}, f32[32]{0:T(128)}, u32[]{:S(2)}) copy-start(f32[32]{0:T(128)} %dynamic_slice.18) | copy-start | bytes 388
  53.3 4.2 %copy-start.13 = (f32[32]{0:T(128)S(1)}, f32[32]{0:T(128)}, u32[]{:S(2)}) copy-start(f32[32]{0:T(128)} %dynamic-slice_exponential_fusion) | copy-start | bytes 388
  53.3 28.3 %all-to-all-start = ((bf16[128,4,2048]{2,0,1:T(8,128)(2,1)}), bf16[128,4,2048]{2,0,1:T(8,128)(2,1)S(1)}, u32[]{:S(2)}, u32[]{:S(2)}) async-start(bf16[128,4,2048]{2,0,1:T(8,128)(2,1)} %bitcast.79), calls=%async_computation | async-start | bytes 4194304 | tf_op jit(solution)/shard_map/all_to_all | solution.py:178
  57.0 133.0 %all-gather.3.cloned.1.call-start = ((), (), s32[]{:S(2)}) async-start(), calls=%async_computation.4 | async-start | bytes 9732096 | tf_op jit(solution)/shard_map/all_gather | solution.py:227
  59.2 1.7 copy-start.7
  81.6 1.3 copy-start.4
  94.8 8.8 %copy-start = (f32[256,2048]{1,0:T(8,128)S(1)}, f32[256,2048]{1,0:T(8,128)}, u32[]{:S(2)}) copy-start(f32[256,2048]{1,0:T(8,128)} %ssd_fresh.1) | copy-start | bytes 6291460
  98.1 4.6 %collective-permute-start.2 = (f32[264,2048]{1,0:T(8,128)}, f32[264,2048]{1,0:T(8,128)}, u32[]{:S(2)}, u32[]{:S(2)}) collective-permute-start(f32[264,2048]{1,0:T(8,128)} %pad_maximum_fusion), channel_id=1, source_target_pairs={{0,4},{4,0},{8,12},{12,8},{16,20},{20,16},{24,28},{28,24},{1,5},{5... | collective-permute-start | bytes 6488072 | tf_op jit(solution)/shard_map/ppermute | solution.py:214
  105.6 1.3 copy-start.2
  107.0 1.1 copy-start.16
  191.4 5.1 %copy-start.1 = (f32[512,2048]{1,0:T(8,128)S(1)}, f32[512,2048]{1,0:T(8,128)}, u32[]{:S(2)}) copy-start(f32[512,2048]{1,0:T(8,128)} %copy.112) | copy-start | bytes 12582916
  191.4 5.3 %copy-start.3 = (f32[256,2048]{1,0:T(8,128)S(1)}, f32[256,2048]{1,0:T(8,128)}, u32[]{:S(2)}) copy-start(f32[256,2048]{1,0:T(8,128)} %copy-done.2) | copy-start | bytes 6291460
  191.4 6.5 %copy-start.5 = (f32[512,2048]{1,0:T(8,128)S(1)}, f32[512,2048]{1,0:T(8,128)}, u32[]{:S(2)}) copy-start(f32[512,2048]{1,0:T(8,128)} %ssd_intra.1) | copy-start | bytes 12582916
Sparse Core Ops, SparseCore 0:
  108.2 81.8 all-gather.2

commit v4 on v3

--- a/solution.py
+++ b/solution.py
@@ -224,28 +224,33 @@
     ] * lax.dynamic_slice_in_dim(even_final, lo, half_width, 1) + lax.dynamic_slice_in_dim(
         odd_final, lo, half_width, 1
     )
-    gathered = lax.all_gather(
-        jnp.concatenate([chip_half, decay_slab[:, :half_width]], axis=0), "ctx"
-    )
-    decays = gathered[:, N, :local_heads]
-
     skip_cols = head_columns(skip_local)
     partials = []
     for b in range(blocks):
         scores = jnp.einsum("in,jn->ij", seg_c[b], seg_b[b], preferred_element_type=jnp.float32)
         partials.append(intra_block(x_blk[b], scores, cum[b], dt_blk[b], skip_cols))
 
-    seg_ids = jnp.arange(n_ctx)[None, :]
-    chip_ids = jnp.arange(chips)[:, None]
-    between = (seg_ids >= 2 * chip_ids + 2) & (seg_ids < ctx_index)
-    chip_weight = jnp.prod(jnp.where(between[:, :, None], decays[None], 1.0), axis=1)
-    chip_weight = jnp.where(chip_ids < chip, chip_weight, 0.0)
-    halves = []
-    for q in range(2):
-        part = gathered[q::2, :N]
-        wq = head_columns(chip_weight[:, q * half_heads : (q + 1) * half_heads])
-        halves.append(jnp.sum(wq[:, None, :] * part, axis=0))
-    incoming = jnp.concatenate(halves, axis=1) + jnp.where(core == 1, 1.0, 0.0) * even_final
+    mate_decay = mate[N, :local_heads]
+    chip_decay = head_columns(
+        lax.dynamic_slice_in_dim(segment_decay * mate_decay, core * half_heads, half_heads, 0)
+    )[None, :]
+    pieces = 4 if N % 32 == 0 else 1
+    piece_rows = N // pieces
+    acc = [jnp.zeros((piece_rows, half_width), jnp.float32) for _ in range(pieces)]
+    for r in range(chips - 1):
+        pairs = [(2 * r + q, 2 * r + 2 + q) for q in range(2)]
+        for k in range(pieces):
+            send = chip_decay * acc[k] + chip_half[k * piece_rows : (k + 1) * piece_rows]
+            acc[k] = acc[k] + lax.ppermute(send, "ctx", pairs)
+    prefix_half = jnp.concatenate(acc, axis=0) if pieces > 1 else acc[0]
+    mate_prefix = lax.ppermute(prefix_half, "ctx", [(i, i ^ 1) for i in range(n_ctx)])
+    chip_prefix = jnp.concatenate(
+        [jnp.where(core == 0, prefix_half, mate_prefix), jnp.where(core == 0, mate_prefix, prefix_half)],
+        axis=1,
+    )
+    incoming = jnp.where(
+        core == 1, head_columns(mate_decay)[None, :] * chip_prefix + mate_final, chip_prefix
+    )
 
     results = []
     for b in range(blocks):

time: 242 us -> 232 us (0.959)
  between operations: 13.8 us -> 0.52 us
  starting transfers between devices: 18.5 us -> 31.1 us
  waiting for transfers between devices: 87.4 us -> 78.8 us
  other arithmetic: 28.8 us -> 23.6 us
  local copies, waits for them, and re-layouts: 31.4 us -> 35.3 us
  matrix products: 3.96 us -> 6.85 us
    all_gather x1 -> x0, waiting for transfers between devices: 56.9 us -> none  [on_device(): lax.all_gather(jnp.concatenate([chip_half, decay_slab[:, :half_width]], a...]
    ppermute x0 -> x13, waiting for transfers between devices: none -> 49.5 us  [the longest x12 49.5 us: on_device(): acc[k] = acc[k] + lax.ppermute(send, 'ctx', pairs)]
    ppermute x0 -> x13, starting transfers between devices: none -> 13.3 us  [the longest x12 13.3 us: on_device(): acc[k] = acc[k] + lax.ppermute(send, 'ctx', pairs)]
    reduce_sum x1 -> x0, other arithmetic: 5.09 us -> none  [on_device(): halves.append(jnp.sum(wq[:, None, :] * part, axis=0))]
    dynamic_update_slice x2, local copies, waits for them, and re-layouts: 2.93 us -> 5.95 us  [conv_silu(): lax.dynamic_update_slice_in_dim(body, conv_rows(edge, rim, weight, bias),...]
    dot_general x1, matrix products: 2.66 us -> 5.51 us  [on_device(): jnp.dot(seg_c[b].astype(jnp.float32), carried_state, precision=lax.Precis...]
    select_n x3 -> x1, other arithmetic: 2.74 us -> 0.17 us  [on_device(): jnp.where(core == 0, prefix_half, mate_prefix)]
    unnamed x36 -> x30, local copies, waits for them, and re-layouts: 6.59 us -> 5.4 us
  transfers between devices with their start and end apart: 7 -> 19, of which waited for: 4 -> 10; matrix products, arithmetic and copies ran while one was open for 17% -> 20% of each run, Pallas kernels for 6% -> 6%
where the time goes in v4:
time: 232 us; the launch traced here: 230 us
  waiting for transfers between devices  78.8 us (34%)
  local copies, waits for them, and re-layouts  35.3 us (15%)
  starting transfers between devices  31.1 us (13%)
  blocking collectives  28.8 us (12%)
  Pallas kernels  25 us (11%)
  other arithmetic  23.6 us (10%)
  matrix products  6.85 us (3%)
    ppermute x12, waiting for transfers between devices, on_device(): acc[k] = acc[k] + lax.ppermute(send, 'ctx', pairs)  49.5 us
    all_to_all x1, blocking collectives, on_device(): return lax.all_to_all(result, 'tp', split_axis=0, concat_axis=1, tiled=True)  28.8 us
    all_to_all x1, waiting for transfers between devices, on_device(): lax.all_to_all(x_part, 'tp', split_axis=1, concat_axis=0, tiled=True)  19.1 us
    ppermute x12, starting transfers between devices, on_device(): acc[k] = acc[k] + lax.ppermute(send, 'ctx', pairs)  13.3 us
    pallas_call x1, Pallas kernels, intra_block(): pl.pallas_call(intra_kernel, out_shape=jax.ShapeDtypeStruct((BLOCK, width...  13.2 us
    pallas_call x1, Pallas kernels, fresh_block(): pl.pallas_call(fresh_kernel, out_shape=jax.ShapeDtypeStruct((N, width), j...  11.9 us
    convert_element_type x4, other arithmetic, conv_rows(): return jax.nn.silu(total).astype(jnp.bfloat16)  11.2 us
    ppermute x2, starting transfers between devices, from_behind(): lax.ppermute(value, axis, [(source, source + steps) for source in range(i...  6.79 us
  transfers between devices with their start and end apart: 19, of which 10 were waited for; matrix products, arithmetic and copies ran while one was open for 20% of the time, Pallas kernels for 6%

profile of v4, /device:TPU:16, one launch (start us, length us, event | category | flops | bytes accessed | tf_op | source)
XLA Modules:
  0.0 230.1 jit_solution(18384717144485391418)
XLA Ops:
  0.0 1.6 fusion.33
  1.6 3.4 %collective-permute-start = (bf16[3,8192]{1,0:T(4,128)(2,1)}, bf16[3,8192]{1,0:T(4,128)(2,1)S(1)}, u32[]{:S(2)}, u32[]{:S(2)}) collective-permute-start(bf16[3,8192]{1,0:T(4,128)(2,1)} %get-tuple-element.19), channel_id=1, source_target_pairs={{0,1},{1,2},{2,3},{3,4},{4,5},{5,6},{6,7},{7,8},{8,9},{9,10},{10,1... | collective-permute-start | bytes 147464 | tf_op jit(solution)/shard_map/ppermute | solution.py:20
  5.8 3.4 %collective-permute-start.1 = (bf16[3,2048]{1,0:T(4,128)(2,1)S(1)}, bf16[3,2048]{1,0:T(4,128)(2,1)S(1)}, u32[]{:S(2)}, u32[]{:S(2)}) collective-permute-start(bf16[3,2048]{1,0:T(4,128)(2,1)S(1)} %get-tuple-element.32), channel_id=1, source_target_pairs={{0,1},{1,2},{2,3},{3,4},{4,5},{5,6},{6,7},{7,8},{8,9},{9,10},{10,1... | collective-permute-start | bytes 36872 | tf_op jit(solution)/shard_map/ppermute | solution.py:20
  9.2 1.5 copy.89
  10.7 3.3 %all-to-all-start.2 = ((bf16[128,4,32]{0,2,1:T(8,128)(2,1)}), bf16[128,4,32]{0,2,1:T(8,128)(2,1)S(1)}, u32[]{:S(2)}, u32[]{:S(2)}) async-start(bf16[128,4,32]{0,2,1:T(8,128)(2,1)} %bitcast.14), calls=%async_computation.2 | async-start | bytes 65536 | tf_op jit(solution)/shard_map/all_to_all | solution.py:179
  14.0 4.1 %convert_element_type.56 = f32[128,8192]{1,0:T(8,128)} convert(bf16[128,8192]{1,0:T(8,128)(2,1)} %param.10) | non-fusion elementwise | flops 1048576 | bytes 6291456 | tf_op jit(solution)/shard_map/convert_element_type | solution.py:34
  18.9 7.7 %multiply_convert_fusion = bf16[128,8192]{1,0:T(8,128)(2,1)S(1)} fusion(f32[128,8192]{1,0:T(8,128)} %convert_element_type.56, f32[8192]{0:T(1024)S(1)} %bitcast.93, f32[8192]{0:T(1024)S(1)} %bitcast.95, f32[8192]{0:T(1024)S(1)} %bitcast.91, f32[8192]{0:T(1024)S(1)} %bitcast.89, f32[8192]{0:T(1024)S(1)} %copy-done.6), kind=kLoop, calls=%fused_computation.1 | loop fusion | flops 13631488 | bytes 6455296 | tf_op jit(solution)/shard_map/convert_element_type | solution.py:27
  26.6 3.2 %multiply_convert_fusion.1 = bf16[128,2048]{0,1:T(8,128)(2,1)} fusion(f32[128,2048]{0,1:T(8,128)S(1)} %convert_element_type.60, f32[2048]{0:T(1024)S(1)} %bitcast.101, f32[2048]{0:T(1024)S(1)} %bitcast.103, f32[2048]{0:T(1024)S(1)} %bitcast.99, f32[2048]{0:T(1024)S(1)} %bitcast.97, f32[2048]{0:T(1024)S(1)} %copy-done.8), kind=kLoop, calls=%fused_computation.25 | loop fusion | flops 3407872 | bytes 1613824 | tf_op jit(solution)/shard_map/convert_element_type | solution.py:27
  30.4 5.0 %dynamic_update_slice.7 = bf16[128,2048]{0,1:T(8,128)(2,1)} dynamic-update-slice(bf16[128,2048]{0,1:T(8,128)(2,1)} %multiply_convert_fusion.1, bf16[3,2048]{0,1:T(8,128)(2,1)S(1)} %copy.86, s32[]{:T(128)} %constant.26.clone.1, s32[]{:T(128)} %constant.26.clone.1) | dynamic-update-slice | bytes 24580 | tf_op jit(solution)/shard_map/dynamic_update_slice | solution.py:36
  35.4 1.9 copy.87
  37.3 4.2 %all-to-all-start.1 = ((bf16[4,128,2,256]{1,3,2,0:T(8,128)(2,1)}), bf16[4,128,2,256]{1,3,2,0:T(8,128)(2,1)S(1)}, u32[]{:S(2)}, u32[]{:S(2)}) async-start(bf16[4,128,2,256]{1,3,2,0:T(8,128)(2,1)} %copy.87), calls=%async_computation.1 | async-start | bytes 1048576 | tf_op jit(solution)/shard_map/all_to_all | solution.py:176
  44.1 5.6 %all-to-all-done.1 = bf16[4,128,2,256]{1,3,2,0:T(8,128)(2,1)S(1)} async-done(((bf16[4,128,2,256]{1,3,2,0:T(8,128)(2,1)}), bf16[4,128,2,256]{1,3,2,0:T(8,128)(2,1)S(1)}, u32[]{:S(2)}, u32[]{:S(2)}) %all-to-all-start.1) | async-done | bytes 524320 | tf_op jit(solution)/shard_map/all_to_all | solution.py:176
  49.7 3.6 %all-to-all-start = ((bf16[128,4,2048]{2,0,1:T(8,128)(2,1)}), bf16[128,4,2048]{2,0,1:T(8,128)(2,1)S(1)}, u32[]{:S(2)}, u32[]{:S(2)}) async-start(bf16[128,4,2048]{2,0,1:T(8,128)(2,1)} %bitcast.80), calls=%async_computation | async-start | bytes 4194304 | tf_op jit(solution)/shard_map/all_to_all | solution.py:178
  58.4 19.1 %all-to-all-done = bf16[128,4,2048]{2,0,1:T(8,128)(2,1)S(1)} async-done(((bf16[128,4,2048]{2,0,1:T(8,128)(2,1)}), bf16[128,4,2048]{2,0,1:T(8,128)(2,1)S(1)}, u32[]{:S(2)}, u32[]{:S(2)}) %all-to-all-start) | async-done | bytes 2097184 | tf_op jit(solution)/shard_map/all_to_all | solution.py:178
  78.8 11.9 %ssd_fresh.1 = f32[256,2048]{1,0:T(8,128)} custom-call(bf16[512,2048]{1,0:T(8,128)(2,1)} %bitcast.78, bf16[256,512]{1,0:T(8,128)(2,1)} %slice_bitcast_fusion.3.bt_ref, f32[512,128]{1,0:T(8,128)} %pad.14.cum_ref, f32[512,128]{1,0:T(8,128)} %pad.15.dtl_ref), custom_call_target="tpu_custom_call" | custom-call | flops 536870912 | bytes 4456448 | tf_op jit(solution)/shard_map/ssd_fresh/pallas_call | solution.py:127
  90.7 3.2 %select_maximum_fusion = f32[264,2048]{1,0:T(8,128)} fusion(f32[1,32]{1,0:T(1,128)S(1)} %fusion.31, f32[256,2048]{1,0:T(8,128)} %ssd_fresh.1), kind=kLoop, calls=%fused_computation.8 | loop fusion | flops 1622016 | bytes 4259968 | tf_op jit(solution)/shard_map/concatenate | solution.py:215
  93.9 4.6 %collective-permute-done.2 = f32[264,2048]{1,0:T(8,128)} collective-permute-done((f32[264,2048]{1,0:T(8,128)}, f32[264,2048]{1,0:T(8,128)}, u32[]{:S(2)}, u32[]{:S(2)}) %collective-permute-start.2) | collective-permute-done | bytes 2162720 | tf_op jit(solution)/shard_map/ppermute | solution.py:214
  99.6 1.7 slice.178
  105.9 13.7 %collective-permute-done.4 = f32[64,1024]{1,0:T(8,128)S(1)} collective-permute-done((f32[64,1024]{1,0:T(8,128)S(1)}, f32[64,1024]{1,0:T(8,128)S(1)}, u32[]{:S(2)}, u32[]{:S(2)}) %collective-permute-start.4) | collective-permute-done | bytes 262176 | tf_op jit(solution)/shard_map/ppermute | solution.py:244
  125.0 13.0 %collective-permute-done.7 = f32[64,1024]{1,0:T(8,128)S(1)} collective-permute-done((f32[64,1024]{1,0:T(8,128)S(1)}, f32[64,1024]{1,0:T(8,128)S(1)}, u32[]{:S(2)}, u32[]{:S(2)}) %collective-permute-start.7) | collective-permute-done | bytes 262176 | tf_op jit(solution)/shard_map/ppermute | solution.py:244
  138.0 5.6 %collective-permute-done.10 = f32[64,1024]{1,0:T(8,128)S(1)} collective-permute-done((f32[64,1024]{1,0:T(8,128)S(1)}, f32[64,1024]{1,0:T(8,128)S(1)}, u32[]{:S(2)}, u32[]{:S(2)}) %collective-permute-start.10) | collective-permute-done | bytes 262176 | tf_op jit(solution)/shard_map/ppermute | solution.py:244
  143.6 4.2 %collective-permute-done.13 = f32[64,1024]{1,0:T(8,128)S(1)} collective-permute-done((f32[64,1024]{1,0:T(8,128)S(1)}, f32[64,1024]{1,0:T(8,128)S(1)}, u32[]{:S(2)}, u32[]{:S(2)}) %collective-permute-start.13) | collective-permute-done | bytes 262176 | tf_op jit(solution)/shard_map/ppermute | solution.py:244
  150.7 1.5 collective-permute-start.8
  152.2 3.9 %collective-permute-done.14 = f32[64,1024]{1,0:T(8,128)S(1)} collective-permute-done((f32[64,1024]{1,0:T(8,128)S(1)}, f32[64,1024]{1,0:T(8,128)S(1)}, u32[]{:S(2)}, u32[]{:S(2)}) %collective-permute-start.14) | collective-permute-done | bytes 262176 | tf_op jit(solution)/shard_map/ppermute | solution.py:244
  156.1 5.6 %collective-permute-done.11 = f32[64,1024]{1,0:T(8,128)S(1)} collective-permute-done((f32[64,1024]{1,0:T(8,128)S(1)}, f32[64,1024]{1,0:T(8,128)S(1)}, u32[]{:S(2)}, u32[]{:S(2)}) %collective-permute-start.11) | collective-permute-done | bytes 262176 | tf_op jit(solution)/shard_map/ppermute | solution.py:244
  161.7 3.5 %collective-permute-done.8 = f32[64,1024]{1,0:T(8,128)S(1)} collective-permute-done((f32[64,1024]{1,0:T(8,128)S(1)}, f32[64,1024]{1,0:T(8,128)S(1)}, u32[]{:S(2)}, u32[]{:S(2)}) %collective-permute-start.8) | collective-permute-done | bytes 262176 | tf_op jit(solution)/shard_map/ppermute | solution.py:244
  168.7 2.6 %broadcast_in_dim.11 = f32[512,32,64]{0,2,1:T(8,128)} broadcast(f32[512,32]{0,1:T(8,128)S(1)} %copy.96), dimensions={0,1} | broadcast | bytes 4259840 | tf_op jit(solution)/shard_map/broadcast_in_dim | solution.py:142
  171.3 5.5 %copy.97 = f32[512,2048]{1,0:T(8,128)} copy(f32[512,2048]{0,1:T(8,128)} %bitcast.76) | data formatting | bytes 8388608 | tf_op jit(solution)/shard_map/reshape | solution.py:142
  178.1 13.2 %ssd_intra.1 = f32[512,2048]{1,0:T(8,128)} custom-call(bf16[512,2048]{1,0:T(8,128)(2,1)} %bitcast.79, f32[512,512]{1,0:T(8,128)} %fusion.14.s_ref, f32[512,128]{1,0:T(8,128)} %pad.14.cum_ref, f32[32,512]{1,0:T(8,128)} %copy.94.cumt_ref, f32[32,512]{1,0:T(8,128)} %copy.95.dtt_ref, f32[1,2048]{1,0:T(1,128)} %broadcast_in_dim_reshape.2.skip_ref), custom_call_target="tpu_custom_call" | custom-call | flops 2147483648 | bytes 7340032 | tf_op jit(solution)/shard_map/ssd_intra/pallas_call | solution.py:85
  192.3 2.0 copy-done
  194.3 5.5 %add_convert_fusion = bf16[512,2048]{1,0:T(8,128)(2,1)S(1)} fusion(f32[512,2048]{1,0:T(8,128)} %ssd_intra.1, f32[512,2048]{1,0:T(8,128)S(1)} %copy-done, f32[256,1024]{1,0:T(8,128)S(1)} %get-tuple-element.18, f32[256,1024]{1,0:T(8,128)S(1)} %get-tuple-element.17, f32[2048]{0:T(1024)S(1)} %mul.333, pred[]{:T(512)S(6)} %eq.6, ...), kind=kOutput, calls=%fused_computation | convolution fusion | flops 3226468352 | bytes 14950401 | tf_op jit(solution)/shard_map/dot_general | solution.py:260
  199.8 28.8 %all_to_all.56 = bf16[4,128,2048]{2,1,0:T(8,128)(2,1)S(1)} all-to-all(bf16[4,128,2048]{2,1,0:T(8,128)(2,1)S(1)} %bitcast.82), channel_id=1, replica_groups=mesh['ctx'=8,'tp'=4] {'tp'}, dimensions={0} | all-to-all | bytes 4194304 | tf_op jit(solution)/shard_map/all_to_all | solution.py:265
  (112 shorter events, 32.2 us)
Async XLA Ops:
  1.6 35.6 %collective-permute-start = (bf16[3,8192]{1,0:T(4,128)(2,1)}, bf16[3,8192]{1,0:T(4,128)(2,1)S(1)}, u32[]{:S(2)}, u32[]{:S(2)}) collective-permute-start(bf16[3,8192]{1,0:T(4,128)(2,1)} %get-tuple-element.19), channel_id=1, source_target_pairs={{0,1},{1,2},{2,3},{3,4},{4,5},{5,6},{6,7},{7,8},{8,9},{9,10},{10,1... | collective-permute-start | bytes 147464 | tf_op jit(solution)/shard_map/ppermute | solution.py:20
  5.8 24.1 %collective-permute-start.1 = (bf16[3,2048]{1,0:T(4,128)(2,1)S(1)}, bf16[3,2048]{1,0:T(4,128)(2,1)S(1)}, u32[]{:S(2)}, u32[]{:S(2)}) collective-permute-start(bf16[3,2048]{1,0:T(4,128)(2,1)S(1)} %get-tuple-element.32), channel_id=1, source_target_pairs={{0,1},{1,2},{2,3},{3,4},{4,5},{5,6},{6,7},{7,8},{8,9},{9,10},{10,1... | collective-permute-start | bytes 36872 | tf_op jit(solution)/shard_map/ppermute | solution.py:20
  10.7 26.6 %all-to-all-start.2 = ((bf16[128,4,32]{0,2,1:T(8,128)(2,1)}), bf16[128,4,32]{0,2,1:T(8,128)(2,1)S(1)}, u32[]{:S(2)}, u32[]{:S(2)}) async-start(bf16[128,4,32]{0,2,1:T(8,128)(2,1)} %bitcast.14), calls=%async_computation.2 | async-start | bytes 65536 | tf_op jit(solution)/shard_map/all_to_all | solution.py:179
  14.0 4.1 %copy-start.5 = (bf16[128,2048]{1,0:T(8,128)(2,1)S(1)}, bf16[128,2048]{1,0:T(8,128)(2,1)}, u32[]{:S(2)}) copy-start(bf16[128,2048]{1,0:T(8,128)(2,1)} %param.11) | copy-start | bytes 1572868
  14.0 4.4 %copy-start.7 = (f32[4,8192]{1,0:T(4,128)S(1)}, f32[4,8192]{1,0:T(4,128)}, u32[]{:S(2)}) copy-start(f32[4,8192]{1,0:T(4,128)} %param.13) | copy-start | bytes 393220
  18.1 0.8 copy-start.6
  18.9 7.7 %copy-start.8 = (f32[2048]{0:T(1024)S(1)}, f32[2048]{0:T(1024)}, u32[]{:S(2)}) copy-start(f32[2048]{0:T(1024)} %param.16) | copy-start | bytes 24580
  18.9 10.9 %copy-start.11 = (f32[128]{0:T(128)S(1)}, f32[128]{0:T(128)}, u32[]{:S(2)}) copy-start(f32[128]{0:T(128)} %param.18) | copy-start | bytes 1540
  18.9 11.0 %copy-start.12 = (f32[128]{0:T(128)S(1)}, f32[128]{0:T(128)}, u32[]{:S(2)}) copy-start(f32[128]{0:T(128)} %param.17) | copy-start | bytes 1540
  30.0 23.6 %copy-start.10 = (f32[32]{0:T(128)}, f32[32]{0:T(128)S(1)}, u32[]{:S(2)}) copy-start(f32[32]{0:T(128)S(1)} %dynamic_slice.21) | copy-start | bytes 388
  37.3 12.4 %all-to-all-start.1 = ((bf16[4,128,2,256]{1,3,2,0:T(8,128)(2,1)}), bf16[4,128,2,256]{1,3,2,0:T(8,128)(2,1)S(1)}, u32[]{:S(2)}, u32[]{:S(2)}) async-start(bf16[4,128,2,256]{1,3,2,0:T(8,128)(2,1)} %copy.87), calls=%async_computation.1 | async-start | bytes 1048576 | tf_op jit(solution)/shard_map/all_to_all | solution.py:176
  49.7 3.7 %copy-start.3 = (bf16[4,128,2,256]{1,3,2,0:T(8,128)(2,1)}, bf16[4,128,2,256]{1,3,2,0:T(8,128)(2,1)S(1)}, u32[]{:S(2)}) copy-start(bf16[4,128,2,256]{1,3,2,0:T(8,128)(2,1)S(1)} %all-to-all-done.1) | copy-start | bytes 1572868
  49.7 27.8 %all-to-all-start = ((bf16[128,4,2048]{2,0,1:T(8,128)(2,1)}), bf16[128,4,2048]{2,0,1:T(8,128)(2,1)S(1)}, u32[]{:S(2)}, u32[]{:S(2)}) async-start(bf16[128,4,2048]{2,0,1:T(8,128)(2,1)} %bitcast.80), calls=%async_computation | async-start | bytes 4194304 | tf_op jit(solution)/shard_map/all_to_all | solution.py:178
  55.2 2.4 %copy-start.4 = (bf16[4,128,2,256]{1,3,2,0:T(8,128)(2,1)S(1)}, bf16[4,128,2,256]{1,3,2,0:T(8,128)(2,1)}, u32[]{:S(2)}) copy-start(bf16[4,128,2,256]{1,3,2,0:T(8,128)(2,1)} %copy-done.3) | copy-start | bytes 1572868
  77.5 1.3 copy-start.2
  93.9 7.5 %copy-start.1 = (f32[256,2048]{1,0:T(8,128)S(1)}, f32[256,2048]{1,0:T(8,128)}, u32[]{:S(2)}) copy-start(f32[256,2048]{1,0:T(8,128)} %ssd_fresh.1) | copy-start | bytes 6291460
  93.9 4.6 %collective-permute-start.2 = (f32[264,2048]{1,0:T(8,128)}, f32[264,2048]{1,0:T(8,128)}, u32[]{:S(2)}, u32[]{:S(2)}) collective-permute-start(f32[264,2048]{1,0:T(8,128)} %select_maximum_fusion), channel_id=1, source_target_pairs={{0,4},{4,0},{8,12},{12,8},{16,20},{20,16},{24,28},{28,24},{1,5},{5... | collective-permute-start | bytes 6488072 | tf_op jit(solution)/shard_map/ppermute | solution.py:214
  101.8 2.7 %collective-permute-start.3 = (f32[64,1024]{1,0:T(8,128)S(1)}, f32[64,1024]{1,0:T(8,128)S(1)}, u32[]{:S(2)}, u32[]{:S(2)}) collective-permute-start(f32[64,1024]{1,0:T(8,128)S(1)} %get-tuple-element.24), channel_id=1, source_target_pairs={{0,8},{4,12},{1,9},{5,13},{2,10},{6,14},{3,11},{7,15}} | collective-permute-start | bytes 786440 | tf_op jit(solution)/shard_map/ppermute | solution.py:244
  102.5 3.4 %collective-permute-start.6 = (f32[64,1024]{1,0:T(8,128)S(1)}, f32[64,1024]{1,0:T(8,128)S(1)}, u32[]{:S(2)}, u32[]{:S(2)}) collective-permute-start(f32[64,1024]{1,0:T(8,128)S(1)} %get-tuple-element.27), channel_id=1, source_target_pairs={{0,8},{4,12},{1,9},{5,13},{2,10},{6,14},{3,11},{7,15}} | collective-permute-start | bytes 786440 | tf_op jit(solution)/shard_map/ppermute | solution.py:244
  103.1 2.7 %collective-permute-start.9 = (f32[64,1024]{1,0:T(8,128)S(1)}, f32[64,1024]{1,0:T(8,128)S(1)}, u32[]{:S(2)}, u32[]{:S(2)}) collective-permute-start(f32[64,1024]{1,0:T(8,128)S(1)} %get-tuple-element.26), channel_id=1, source_target_pairs={{0,8},{4,12},{1,9},{5,13},{2,10},{6,14},{3,11},{7,15}} | collective-permute-start | bytes 786440 | tf_op jit(solution)/shard_map/ppermute | solution.py:244
  103.8 2.1 collective-permute-start.12
  104.6 15.0 %collective-permute-start.4 = (f32[64,1024]{1,0:T(8,128)S(1)}, f32[64,1024]{1,0:T(8,128)S(1)}, u32[]{:S(2)}, u32[]{:S(2)}) collective-permute-start(f32[64,1024]{1,0:T(8,128)S(1)} %multiply_add_fusion.7), channel_id=1, source_target_pairs={{8,16},{12,20},{9,17},{13,21},{10,18},{14,22},{11,19},{15,23}} | collective-permute-start | bytes 786440 | tf_op jit(solution)/shard_map/ppermute | solution.py:244
  119.8 18.2 %collective-permute-start.7 = (f32[64,1024]{1,0:T(8,128)S(1)}, f32[64,1024]{1,0:T(8,128)S(1)}, u32[]{:S(2)}, u32[]{:S(2)}) collective-permute-start(f32[64,1024]{1,0:T(8,128)S(1)} %get-tuple-element.21), channel_id=1, source_target_pairs={{8,16},{12,20},{9,17},{13,21},{10,18},{14,22},{11,19},{15,23}} | collective-permute-start | bytes 786440 | tf_op jit(solution)/shard_map/ppermute | solution.py:244
  121.1 22.6 %collective-permute-start.10 = (f32[64,1024]{1,0:T(8,128)S(1)}, f32[64,1024]{1,0:T(8,128)S(1)}, u32[]{:S(2)}, u32[]{:S(2)}) collective-permute-start(f32[64,1024]{1,0:T(8,128)S(1)} %get-tuple-element.22), channel_id=1, source_target_pairs={{8,16},{12,20},{9,17},{13,21},{10,18},{14,22},{11,19},{15,23}} | collective-permute-start | bytes 786440 | tf_op jit(solution)/shard_map/ppermute | solution.py:244
  122.4 25.4 %collective-permute-start.13 = (f32[64,1024]{1,0:T(8,128)S(1)}, f32[64,1024]{1,0:T(8,128)S(1)}, u32[]{:S(2)}, u32[]{:S(2)}) collective-permute-start(f32[64,1024]{1,0:T(8,128)S(1)} %get-tuple-element.23), channel_id=1, source_target_pairs={{8,16},{12,20},{9,17},{13,21},{10,18},{14,22},{11,19},{15,23}} | collective-permute-start | bytes 786440 | tf_op jit(solution)/shard_map/ppermute | solution.py:244
  123.7 28.5 %collective-permute-start.5 = (f32[64,1024]{1,0:T(8,128)S(1)}, f32[64,1024]{1,0:T(8,128)S(1)}, u32[]{:S(2)}, u32[]{:S(2)}) collective-permute-start(f32[64,1024]{1,0:T(8,128)S(1)} %get-tuple-element.5), channel_id=1, source_target_pairs={{16,24},{20,28},{17,25},{21,29},{18,26},{22,30},{19,27},{23,31}} | collective-permute-start | bytes 786440 | tf_op jit(solution)/shard_map/ppermute | solution.py:244
  148.0 8.0 %collective-permute-start.14 = (f32[64,1024]{1,0:T(8,128)S(1)}, f32[64,1024]{1,0:T(8,128)S(1)}, u32[]{:S(2)}, u32[]{:S(2)}) collective-permute-start(f32[64,1024]{1,0:T(8,128)S(1)} %get-tuple-element.30), channel_id=1, source_target_pairs={{16,24},{20,28},{17,25},{21,29},{18,26},{22,30},{19,27},{23,31}} | collective-permute-start | bytes 786440 | tf_op jit(solution)/shard_map/ppermute | solution.py:244
  149.4 12.3 %collective-permute-start.11 = (f32[64,1024]{1,0:T(8,128)S(1)}, f32[64,1024]{1,0:T(8,128)S(1)}, u32[]{:S(2)}, u32[]{:S(2)}) collective-permute-start(f32[64,1024]{1,0:T(8,128)S(1)} %get-tuple-element.28), channel_id=1, source_target_pairs={{16,24},{20,28},{17,25},{21,29},{18,26},{22,30},{19,27},{23,31}} | collective-permute-start | bytes 786440 | tf_op jit(solution)/shard_map/ppermute | solution.py:244
  150.7 14.6 %collective-permute-start.8 = (f32[64,1024]{1,0:T(8,128)S(1)}, f32[64,1024]{1,0:T(8,128)S(1)}, u32[]{:S(2)}, u32[]{:S(2)}) collective-permute-start(f32[64,1024]{1,0:T(8,128)S(1)} %get-tuple-element.7), channel_id=1, source_target_pairs={{16,24},{20,28},{17,25},{21,29},{18,26},{22,30},{19,27},{23,31}} | collective-permute-start | bytes 786440 | tf_op jit(solution)/shard_map/ppermute | solution.py:244
  156.1 10.2 %copy-start.13 = (f32[128]{0:T(128)S(1)}, f32[128]{0:T(128)}, u32[]{:S(2)}) copy-start(f32[128]{0:T(128)} %param.19) | copy-start | bytes 1540
  166.3 25.8 %collective-permute-start.15 = (f32[256,1024]{1,0:T(8,128)}, f32[256,1024]{1,0:T(8,128)S(1)}, u32[]{:S(2)}, u32[]{:S(2)}) collective-permute-start(f32[256,1024]{1,0:T(8,128)} %pad_maximum_fusion.2), channel_id=1, source_target_pairs={{0,4},{4,0},{8,12},{12,8},{16,20},{20,16},{24,28},{28,24},{1,5},{5... | collective-permute-start | bytes 3145736 | tf_op jit(solution)/shard_map/ppermute | solution.py:246
  192.1 2.2 copy-start
  (1 other events, 0.8 us)

commit v5 on v4

--- a/solution.py
+++ b/solution.py
@@ -224,12 +224,6 @@
     ] * lax.dynamic_slice_in_dim(even_final, lo, half_width, 1) + lax.dynamic_slice_in_dim(
         odd_final, lo, half_width, 1
     )
-    skip_cols = head_columns(skip_local)
-    partials = []
-    for b in range(blocks):
-        scores = jnp.einsum("in,jn->ij", seg_c[b], seg_b[b], preferred_element_type=jnp.float32)
-        partials.append(intra_block(x_blk[b], scores, cum[b], dt_blk[b], skip_cols))
-
     mate_decay = mate[N, :local_heads]
     chip_decay = head_columns(
         lax.dynamic_slice_in_dim(segment_decay * mate_decay, core * half_heads, half_heads, 0)
@@ -237,12 +231,24 @@
     pieces = 4 if N % 32 == 0 else 1
     piece_rows = N // pieces
     acc = [jnp.zeros((piece_rows, half_width), jnp.float32) for _ in range(pieces)]
+    last_send = None
     for r in range(chips - 1):
         pairs = [(2 * r + q, 2 * r + 2 + q) for q in range(2)]
         for k in range(pieces):
             send = chip_decay * acc[k] + chip_half[k * piece_rows : (k + 1) * piece_rows]
             acc[k] = acc[k] + lax.ppermute(send, "ctx", pairs)
+            last_send = send
+    skip_cols = head_columns(skip_local)
+    partials = []
+    for b in range(blocks):
+        scores = jnp.einsum("in,jn->ij", seg_c[b], seg_b[b], preferred_element_type=jnp.float32)
+        operands = (x_blk[b], scores, cum[b], dt_blk[b])
+        if last_send is not None:
+            operands = lax.optimization_barrier(operands + (last_send,))[:4]
+        partials.append(intra_block(*operands, skip_cols))
+
     prefix_half = jnp.concatenate(acc, axis=0) if pieces > 1 else acc[0]
+    prefix_half = lax.optimization_barrier((prefix_half, partials))[0]
     mate_prefix = lax.ppermute(prefix_half, "ctx", [(i, i ^ 1) for i in range(n_ctx)])
     chip_prefix = jnp.concatenate(
         [jnp.where(core == 0, prefix_half, mate_prefix), jnp.where(core == 0, mate_prefix, prefix_half)],
@@ -257,9 +263,12 @@
         carried_state = head_columns(prefix[b])[None, :] * incoming
         if starts[b] is not None:
             carried_state = starts[b] + carried_state
-        inter = head_columns(jnp.exp(cum[b])) * jnp.dot(
-            seg_c[b].astype(jnp.float32), carried_state, precision=lax.Precision.HIGHEST
+        state_hi = carried_state.astype(jnp.bfloat16)
+        state_lo = (carried_state - state_hi.astype(jnp.float32)).astype(jnp.bfloat16)
+        projected = jnp.dot(seg_c[b], state_hi, preferred_element_type=jnp.float32) + jnp.dot(
+            seg_c[b], state_lo, preferred_element_type=jnp.float32
         )
+        inter = head_columns(jnp.exp(cum[b])) * projected
         results.append((partials[b] + inter).astype(jnp.bfloat16))
     result = jnp.concatenate(results, axis=0) if blocks > 1 else results[0]
     return lax.all_to_all(result, "tp", split_axis=0, concat_axis=1, tiled=True)

time: 232 us -> 223 us (0.961)
  waiting for transfers between devices: 78.8 us -> 61.8 us
  other arithmetic: 23.6 us -> 32.4 us
  matrix products: 6.85 us -> 3.33 us
  starting transfers between devices: 31.1 us -> 34.4 us
    ppermute x12, waiting for transfers between devices: 49.5 us -> 33.7 us  [on_device(): acc[k] = acc[k] + lax.ppermute(send, 'ctx', pairs)]
    unnamed x30 -> x53, local copies, waits for them, and re-layouts: 5.4 us -> 10.1 us
    add x4, other arithmetic: 0.58 us -> 4.74 us  [on_device(): send = chip_decay * acc[k] + chip_half[k * piece_rows:(k + 1) * piece_rows]]
    add x4, other arithmetic: 0.16 us -> 3.95 us  [on_device(): acc[k] = acc[k] + lax.ppermute(send, 'ctx', pairs)]
    dot_general x1 -> x2, matrix products: 5.51 us -> 2.01 us  [the longest x1 1.19 us: on_device(): jnp.dot(seg_c[b], state_hi, preferred_element_type=jnp.float32)]
    dynamic_update_slice x2, local copies, waits for them, and re-layouts: 5.95 us -> 2.93 us  [conv_silu(): lax.dynamic_update_slice_in_dim(body, conv_rows(edge, rim, weight, bias),...]
    ppermute x12, starting transfers between devices: 13.3 us -> 16.2 us  [on_device(): acc[k] = acc[k] + lax.ppermute(send, 'ctx', pairs)]
  transfers between devices with their start and end apart: 19 -> 19, of which waited for: 10 -> 7; matrix products, arithmetic and copies ran while one was open for 20% -> 22% of each run, Pallas kernels for 6% -> 6%
where the time goes in v5:
time: 223 us; the launch traced here: 222 us
  waiting for transfers between devices  61.8 us (28%)
  local copies, waits for them, and re-layouts  35.6 us (16%)
  starting transfers between devices  34.4 us (15%)
  other arithmetic  32.4 us (15%)
  blocking collectives  28.8 us (13%)
  Pallas kernels  25 us (11%)
  matrix products  3.33 us (1%)
    ppermute x12, waiting for transfers between devices, on_device(): acc[k] = acc[k] + lax.ppermute(send, 'ctx', pairs)  33.7 us
    all_to_all x1, blocking collectives, on_device(): return lax.all_to_all(result, 'tp', split_axis=0, concat_axis=1, tiled=True)  28.8 us
    all_to_all x1, waiting for transfers between devices, on_device(): lax.all_to_all(x_part, 'tp', split_axis=1, concat_axis=0, tiled=True)  19.9 us
    ppermute x12, starting transfers between devices, on_device(): acc[k] = acc[k] + lax.ppermute(send, 'ctx', pairs)  16.2 us
    pallas_call x1, Pallas kernels, intra_block(): pl.pallas_call(intra_kernel, out_shape=jax.ShapeDtypeStruct((BLOCK, width...  13.2 us
    pallas_call x1, Pallas kernels, fresh_block(): pl.pallas_call(fresh_kernel, out_shape=jax.ShapeDtypeStruct((N, width), j...  11.9 us
    convert_element_type x4, other arithmetic, conv_rows(): return jax.nn.silu(total).astype(jnp.bfloat16)  10.5 us
    unnamed x53, local copies, waits for them, and re-layouts  10.1 us
  transfers between devices with their start and end apart: 19, of which 7 were waited for; matrix products, arithmetic and copies ran while one was open for 22% of the time, Pallas kernels for 6%

profile of v5, /device:TPU:16, one launch (start us, length us, event | category | flops | bytes accessed | tf_op | source)
XLA Modules:
  0.0 221.9 jit_solution(528135822562084253)
XLA Ops:
  0.0 1.5 copy.97
  1.5 3.7 %all-to-all-start.2 = ((bf16[128,4,32]{0,2,1:T(8,128)(2,1)}), bf16[128,4,32]{0,2,1:T(8,128)(2,1)S(1)}, u32[]{:S(2)}, u32[]{:S(2)}) async-start(bf16[128,4,32]{0,2,1:T(8,128)(2,1)} %bitcast.14), calls=%async_computation.2 | async-start | bytes 65536 | tf_op jit(solution)/shard_map/all_to_all | solution.py:179
  6.0 3.9 %collective-permute-start.1 = (bf16[3,2048]{1,0:T(4,128)(2,1)S(1)}, bf16[3,2048]{1,0:T(4,128)(2,1)S(1)}, u32[]{:S(2)}, u32[]{:S(2)}) collective-permute-start(bf16[3,2048]{1,0:T(4,128)(2,1)S(1)} %get-tuple-element.42), channel_id=1, source_target_pairs={{0,1},{1,2},{2,3},{3,4},{4,5},{5,6},{6,7},{7,8},{8,9},{9,10},{10,1... | collective-permute-start | bytes 36872 | tf_op jit(solution)/shard_map/ppermute | solution.py:20
  9.9 1.7 fusion.38
  11.6 3.4 %collective-permute-start = (bf16[3,8192]{1,0:T(4,128)(2,1)}, bf16[3,8192]{1,0:T(4,128)(2,1)S(1)}, u32[]{:S(2)}, u32[]{:S(2)}) collective-permute-start(bf16[3,8192]{1,0:T(4,128)(2,1)} %get-tuple-element.29), channel_id=1, source_target_pairs={{0,1},{1,2},{2,3},{3,4},{4,5},{5,6},{6,7},{7,8},{8,9},{9,10},{10,1... | collective-permute-start | bytes 147464 | tf_op jit(solution)/shard_map/ppermute | solution.py:20
  16.3 4.0 %convert_element_type.64 = f32[128,8192]{1,0:T(8,128)} convert(bf16[128,8192]{1,0:T(8,128)(2,1)} %param.10) | non-fusion elementwise | flops 1048576 | bytes 6291456 | tf_op jit(solution)/shard_map/convert_element_type | solution.py:34
  20.5 2.6 %multiply_convert_fusion.1 = bf16[128,2048]{0,1:T(8,128)(2,1)S(1)} fusion(f32[128,2048]{0,1:T(8,128)S(1)} %convert_element_type.68, f32[2048]{0:T(1024)S(1)} %bitcast.104, f32[2048]{0:T(1024)S(1)} %bitcast.106, f32[2048]{0:T(1024)S(1)} %bitcast.102, f32[2048]{0:T(1024)S(1)} %bitcast.100, f32[2048]{0:T(1024)S(1)} %copy-done.18), kind=kLoop, calls=%fused_computation.24 | loop fusion | flops 3407872 | bytes 1613824 | tf_op jit(solution)/shard_map/convert_element_type | solution.py:27
  23.2 7.7 %multiply_convert_fusion = bf16[128,8192]{1,0:T(8,128)(2,1)S(1)} fusion(f32[128,8192]{1,0:T(8,128)} %convert_element_type.64, f32[8192]{0:T(1024)S(1)} %bitcast.95, f32[8192]{0:T(1024)S(1)} %bitcast.97, f32[8192]{0:T(1024)S(1)} %bitcast.93, f32[8192]{0:T(1024)S(1)} %bitcast.91, f32[8192]{0:T(1024)S(1)} %copy-done.16), kind=kLoop, calls=%fused_computation.1 | loop fusion | flops 13631488 | bytes 6455296 | tf_op jit(solution)/shard_map/convert_element_type | solution.py:27
  32.5 2.0 dynamic_update_slice.7
  35.3 3.5 %all-to-all-start.1 = ((bf16[4,128,2,256]{1,3,2,0:T(8,128)(2,1)}), bf16[4,128,2,256]{1,3,2,0:T(8,128)(2,1)S(1)}, u32[]{:S(2)}, u32[]{:S(2)}) async-start(bf16[4,128,2,256]{1,3,2,0:T(8,128)(2,1)} %copy.95), calls=%async_computation.1 | async-start | bytes 1048576 | tf_op jit(solution)/shard_map/all_to_all | solution.py:176
  42.0 1.6 copy.127
  43.6 3.7 %all-to-all-done.1 = bf16[4,128,2,256]{1,3,2,0:T(8,128)(2,1)S(1)} async-done(((bf16[4,128,2,256]{1,3,2,0:T(8,128)(2,1)}), bf16[4,128,2,256]{1,3,2,0:T(8,128)(2,1)S(1)}, u32[]{:S(2)}, u32[]{:S(2)}) %all-to-all-start.1) | async-done | bytes 524320 | tf_op jit(solution)/shard_map/all_to_all | solution.py:176
  47.3 3.7 %all-to-all-start = ((bf16[128,4,2048]{2,0,1:T(8,128)(2,1)}), bf16[128,4,2048]{2,0,1:T(8,128)(2,1)S(1)}, u32[]{:S(2)}, u32[]{:S(2)}) async-start(bf16[128,4,2048]{2,0,1:T(8,128)(2,1)} %bitcast.87), calls=%async_computation | async-start | bytes 4194304 | tf_op jit(solution)/shard_map/all_to_all | solution.py:178
  55.8 19.9 %all-to-all-done = bf16[128,4,2048]{2,0,1:T(8,128)(2,1)S(1)} async-done(((bf16[128,4,2048]{2,0,1:T(8,128)(2,1)}), bf16[128,4,2048]{2,0,1:T(8,128)(2,1)S(1)}, u32[]{:S(2)}, u32[]{:S(2)}) %all-to-all-start) | async-done | bytes 2097184 | tf_op jit(solution)/shard_map/all_to_all | solution.py:178
  77.0 11.9 %ssd_fresh.1 = f32[256,2048]{1,0:T(8,128)} custom-call(bf16[512,2048]{1,0:T(8,128)(2,1)} %bitcast.85, bf16[256,512]{1,0:T(8,128)(2,1)} %slice_bitcast_fusion.1.bt_ref, f32[512,128]{1,0:T(8,128)} %pad.16.clone.cum_ref, f32[512,128]{1,0:T(8,128)} %pad.17.clone.dtl_ref), custom_call_target="tpu_custom_call" | custom-call | flops 536870912 | bytes 4456448 | tf_op jit(solution)/shard_map/ssd_fresh/pallas_call | solution.py:127
  88.8 3.2 %select_maximum_fusion = f32[264,2048]{1,0:T(8,128)} fusion(f32[1,32]{1,0:T(1,128)S(1)} %bitcast.109, f32[256,2048]{1,0:T(8,128)} %ssd_fresh.1), kind=kLoop, calls=%fused_computation.8 | loop fusion | flops 1622016 | bytes 4259968 | tf_op jit(solution)/shard_map/concatenate | solution.py:215
  92.0 4.5 %collective-permute-done.2 = f32[264,2048]{1,0:T(8,128)S(1)} collective-permute-done((f32[264,2048]{1,0:T(8,128)}, f32[264,2048]{1,0:T(8,128)S(1)}, u32[]{:S(2)}, u32[]{:S(2)}) %collective-permute-start.2) | collective-permute-done | bytes 2162720 | tf_op jit(solution)/shard_map/ppermute | solution.py:214
  103.9 12.8 %collective-permute-done.6 = f32[64,1024]{1,0:T(8,128)S(1)} collective-permute-done((f32[64,1024]{1,0:T(8,128)S(1)}, f32[64,1024]{1,0:T(8,128)S(1)}, u32[]{:S(2)}, u32[]{:S(2)}) %collective-permute-start.6) | collective-permute-done | bytes 262176 | tf_op jit(solution)/shard_map/ppermute | solution.py:239
  116.7 2.1 multiply_add_fusion.4
  124.8 2.1 collective-permute-start.7
  127.0 11.1 %collective-permute-done.4 = f32[64,1024]{1,0:T(8,128)} collective-permute-done((f32[64,1024]{1,0:T(8,128)}, f32[64,1024]{1,0:T(8,128)}, u32[]{:S(2)}, u32[]{:S(2)}) %collective-permute-start.4) | collective-permute-done | bytes 262176 | tf_op jit(solution)/shard_map/ppermute | solution.py:239
  138.0 5.6 %collective-permute-done.9 = f32[64,1024]{1,0:T(8,128)} collective-permute-done((f32[64,1024]{1,0:T(8,128)}, f32[64,1024]{1,0:T(8,128)}, u32[]{:S(2)}, u32[]{:S(2)}) %collective-permute-start.9) | collective-permute-done | bytes 262176 | tf_op jit(solution)/shard_map/ppermute | solution.py:239
  143.6 4.2 %collective-permute-done.12 = f32[64,1024]{1,0:T(8,128)} collective-permute-done((f32[64,1024]{1,0:T(8,128)}, f32[64,1024]{1,0:T(8,128)}, u32[]{:S(2)}, u32[]{:S(2)}) %collective-permute-start.12) | collective-permute-done | bytes 262176 | tf_op jit(solution)/shard_map/ppermute | solution.py:239
  147.8 2.5 %multiply_add_fusion.2 = (f32[64,1024]{1,0:T(8,128)}, f32[64,1024]{1,0:T(8,128)}, f32[64,1024]{1,0:T(8,128)}, f32[64,1024]{1,0:T(8,128)}, f32[64,1024]{1,0:T(8,128)}, /*index=5*/f32[64,1024]{1,0:T(8,128)}) fusion(f32[256,1024]{1,0:T(8,128)S(1)} %select_add_fusion, f32[1024]{0:T(1024)S(1)} %mul.335, f32[64,1024]{1,0:T(8,128)} %collective-permute-done.8, ...), kind=kLoop, calls=%fused_computation.35 | loop fusion | flops 589824 | bytes 3936256 | tf_op jit(solution)/shard_map/add | solution.py:238
  151.8 2.0 collective-permute-start.13
  153.8 2.0 collective-permute-start.14
  158.9 13.2 %ssd_intra.1 = f32[512,2048]{1,0:T(8,128)} custom-call(bf16[512,2048]{1,0:T(8,128)(2,1)} %bitcast.86, f32[512,512]{1,0:T(8,128)} %fusion.12.s_ref, f32[512,128]{1,0:T(8,128)} %pad.19.clone.cum_ref, f32[32,512]{1,0:T(8,128)} %bitcast.90, f32[32,512]{1,0:T(8,128)} %bitcast.99, f32[1,2048]{1,0:T(1,128)} %broadcast_in_dim_reshape.2.skip_ref), custom_call_target="tpu_custom_call" | custom-call | flops 2147483648 | bytes 7340032 | tf_op jit(solution)/shard_map/ssd_intra/pallas_call | solution.py:85
  176.9 2.6 %broadcast_in_dim.26 = f32[512,32,64]{0,2,1:T(8,128)} broadcast(f32[512,32]{0,1:T(8,128)S(1)} %copy-done.13), dimensions={0,1} | broadcast | bytes 4259840 | tf_op jit(solution)/shard_map/broadcast_in_dim | solution.py:142
  179.5 5.4 %copy.106 = f32[512,2048]{1,0:T(8,128)} copy(f32[512,2048]{0,1:T(8,128)} %bitcast.82) | data formatting | bytes 8388608 | tf_op jit(solution)/shard_map/reshape | solution.py:142
  185.1 1.8 broadcast_select_fusion
  191.6 28.8 %all_to_all.56 = bf16[4,128,2048]{2,1,0:T(8,128)(2,1)S(1)} all-to-all(bf16[4,128,2048]{2,1,0:T(8,128)(2,1)S(1)} %bitcast.84), channel_id=1, replica_groups=mesh['ctx'=8,'tp'=4] {'tp'}, dimensions={0} | all-to-all | bytes 4194304 | tf_op jit(solution)/shard_map/all_to_all | solution.py:274
  220.4 1.6 copy.115
  (136 shorter events, 41.4 us)
Async XLA Ops:
  1.5 33.8 %all-to-all-start.2 = ((bf16[128,4,32]{0,2,1:T(8,128)(2,1)}), bf16[128,4,32]{0,2,1:T(8,128)(2,1)S(1)}, u32[]{:S(2)}, u32[]{:S(2)}) async-start(bf16[128,4,32]{0,2,1:T(8,128)(2,1)} %bitcast.14), calls=%async_computation.2 | async-start | bytes 65536 | tf_op jit(solution)/shard_map/all_to_all | solution.py:179
  6.0 26.1 %collective-permute-start.1 = (bf16[3,2048]{1,0:T(4,128)(2,1)S(1)}, bf16[3,2048]{1,0:T(4,128)(2,1)S(1)}, u32[]{:S(2)}, u32[]{:S(2)}) collective-permute-start(bf16[3,2048]{1,0:T(4,128)(2,1)S(1)} %get-tuple-element.42), channel_id=1, source_target_pairs={{0,1},{1,2},{2,3},{3,4},{4,5},{5,6},{6,7},{7,8},{8,9},{9,10},{10,1... | collective-permute-start | bytes 36872 | tf_op jit(solution)/shard_map/ppermute | solution.py:20
  11.6 29.2 %collective-permute-start = (bf16[3,8192]{1,0:T(4,128)(2,1)}, bf16[3,8192]{1,0:T(4,128)(2,1)S(1)}, u32[]{:S(2)}, u32[]{:S(2)}) collective-permute-start(bf16[3,8192]{1,0:T(4,128)(2,1)} %get-tuple-element.29), channel_id=1, source_target_pairs={{0,1},{1,2},{2,3},{3,4},{4,5},{5,6},{6,7},{7,8},{8,9},{9,10},{10,1... | collective-permute-start | bytes 147464 | tf_op jit(solution)/shard_map/ppermute | solution.py:20
  16.3 4.3 %copy-start.18 = (f32[2048]{0:T(1024)S(1)}, f32[2048]{0:T(1024)}, u32[]{:S(2)}) copy-start(f32[2048]{0:T(1024)} %param.16) | copy-start | bytes 24580
  23.2 7.7 %copy-start.21 = (f32[128]{0:T(128)S(1)}, f32[128]{0:T(128)}, u32[]{:S(2)}) copy-start(f32[128]{0:T(128)} %param.18) | copy-start | bytes 1540
  23.2 8.3 %copy-start.22 = (f32[128]{0:T(128)S(1)}, f32[128]{0:T(128)}, u32[]{:S(2)}) copy-start(f32[128]{0:T(128)} %param.17) | copy-start | bytes 1540
  35.3 12.0 %all-to-all-start.1 = ((bf16[4,128,2,256]{1,3,2,0:T(8,128)(2,1)}), bf16[4,128,2,256]{1,3,2,0:T(8,128)(2,1)S(1)}, u32[]{:S(2)}, u32[]{:S(2)}) async-start(bf16[4,128,2,256]{1,3,2,0:T(8,128)(2,1)} %copy.95), calls=%async_computation.1 | async-start | bytes 1048576 | tf_op jit(solution)/shard_map/all_to_all | solution.py:176
  47.3 5.7 %copy-start.20 = (f32[32]{0:T(128)S(1)}, f32[32]{0:T(128)}, u32[]{:S(2)}) copy-start(f32[32]{0:T(128)} %dynamic_slice.21) | copy-start | bytes 388
  47.3 28.3 %all-to-all-start = ((bf16[128,4,2048]{2,0,1:T(8,128)(2,1)}), bf16[128,4,2048]{2,0,1:T(8,128)(2,1)S(1)}, u32[]{:S(2)}, u32[]{:S(2)}) async-start(bf16[128,4,2048]{2,0,1:T(8,128)(2,1)} %bitcast.87), calls=%async_computation | async-start | bytes 4194304 | tf_op jit(solution)/shard_map/all_to_all | solution.py:178
  52.1 104.9 %copy-start.12 = (f32[512,32]{0,1:T(8,128)}, f32[512,32]{0,1:T(8,128)S(1)}, u32[]{:S(2)}) copy-start(f32[512,32]{0,1:T(8,128)S(1)} %get-tuple-element.12) | copy-start | bytes 196612
  53.1 35.7 %copy-start.15 = (f32[512,32]{0,1:T(8,128)}, f32[512,32]{0,1:T(8,128)S(1)}, u32[]{:S(2)}) copy-start(f32[512,32]{0,1:T(8,128)S(1)} %compare_select_fusion) | copy-start | bytes 196612
  92.0 4.5 %collective-permute-start.2 = (f32[264,2048]{1,0:T(8,128)}, f32[264,2048]{1,0:T(8,128)S(1)}, u32[]{:S(2)}, u32[]{:S(2)}) collective-permute-start(f32[264,2048]{1,0:T(8,128)} %select_maximum_fusion), channel_id=1, source_target_pairs={{0,4},{4,0},{8,12},{12,8},{16,20},{20,16},{24,28},{28,24},{1,5},{5... | collective-permute-start | bytes 6488072 | tf_op jit(solution)/shard_map/ppermute | solution.py:214
  98.9 3.6 %collective-permute-start.5 = (f32[64,1024]{1,0:T(8,128)S(1)}, f32[64,1024]{1,0:T(8,128)S(1)}, u32[]{:S(2)}, u32[]{:S(2)}) collective-permute-start(f32[64,1024]{1,0:T(8,128)S(1)} %get-tuple-element.34), channel_id=1, source_target_pairs={{0,8},{4,12},{1,9},{5,13},{2,10},{6,14},{3,11},{7,15}} | collective-permute-start | bytes 786440 | tf_op jit(solution)/shard_map/ppermute | solution.py:239
  99.6 4.2 %collective-permute-start.11 = (f32[64,1024]{1,0:T(8,128)S(1)}, f32[64,1024]{1,0:T(8,128)S(1)}, u32[]{:S(2)}, u32[]{:S(2)}) collective-permute-start(f32[64,1024]{1,0:T(8,128)S(1)} %get-tuple-element.35), channel_id=1, source_target_pairs={{0,8},{4,12},{1,9},{5,13},{2,10},{6,14},{3,11},{7,15}} | collective-permute-start | bytes 786440 | tf_op jit(solution)/shard_map/ppermute | solution.py:239
  100.3 3.6 %collective-permute-start.8 = (f32[64,1024]{1,0:T(8,128)S(1)}, f32[64,1024]{1,0:T(8,128)}, u32[]{:S(2)}, u32[]{:S(2)}) collective-permute-start(f32[64,1024]{1,0:T(8,128)S(1)} %get-tuple-element.36), channel_id=1, source_target_pairs={{0,8},{4,12},{1,9},{5,13},{2,10},{6,14},{3,11},{7,15}} | collective-permute-start | bytes 786440 | tf_op jit(solution)/shard_map/ppermute | solution.py:239
  101.7 21.0 %copy-start.23 = (f32[128]{0:T(128)S(1)}, f32[128]{0:T(128)}, u32[]{:S(2)}) copy-start(f32[128]{0:T(128)} %param.19) | copy-start | bytes 1540
  101.7 2.2 collective-permute-start.3
  102.5 14.2 %collective-permute-start.6 = (f32[64,1024]{1,0:T(8,128)S(1)}, f32[64,1024]{1,0:T(8,128)S(1)}, u32[]{:S(2)}, u32[]{:S(2)}) collective-permute-start(f32[64,1024]{1,0:T(8,128)S(1)} %multiply_add_fusion.5), channel_id=1, source_target_pairs={{8,16},{12,20},{9,17},{13,21},{10,18},{14,22},{11,19},{15,23}} | collective-permute-start | bytes 786440 | tf_op jit(solution)/shard_map/ppermute | solution.py:239
  103.9 12.8 %copy-start.7 = (f32[64,1024]{1,0:T(8,128)}, f32[64,1024]{1,0:T(8,128)S(1)}, u32[]{:S(2)}) copy-start(f32[64,1024]{1,0:T(8,128)S(1)} %collective-permute-done.3) | copy-start | bytes 786436
  118.8 19.2 %collective-permute-start.4 = (f32[64,1024]{1,0:T(8,128)}, f32[64,1024]{1,0:T(8,128)}, u32[]{:S(2)}, u32[]{:S(2)}) collective-permute-start(f32[64,1024]{1,0:T(8,128)} %get-tuple-element.31), channel_id=1, source_target_pairs={{8,16},{12,20},{9,17},{13,21},{10,18},{14,22},{11,19},{15,23}} | collective-permute-start | bytes 786440 | tf_op jit(solution)/shard_map/ppermute | solution.py:239
  120.1 23.6 %collective-permute-start.9 = (f32[64,1024]{1,0:T(8,128)}, f32[64,1024]{1,0:T(8,128)}, u32[]{:S(2)}, u32[]{:S(2)}) collective-permute-start(f32[64,1024]{1,0:T(8,128)} %get-tuple-element.32), channel_id=1, source_target_pairs={{8,16},{12,20},{9,17},{13,21},{10,18},{14,22},{11,19},{15,23}} | collective-permute-start | bytes 786440 | tf_op jit(solution)/shard_map/ppermute | solution.py:239
  121.4 26.5 %collective-permute-start.12 = (f32[64,1024]{1,0:T(8,128)}, f32[64,1024]{1,0:T(8,128)}, u32[]{:S(2)}, u32[]{:S(2)}) collective-permute-start(f32[64,1024]{1,0:T(8,128)} %get-tuple-element.33), channel_id=1, source_target_pairs={{8,16},{12,20},{9,17},{13,21},{10,18},{14,22},{11,19},{15,23}} | collective-permute-start | bytes 786440 | tf_op jit(solution)/shard_map/ppermute | solution.py:239
  124.8 30.9 %copy-start.4 = (bf16[512,2,256]{0,2,1:T(8,128)(2,1)S(1)}, bf16[512,2,256]{0,2,1:T(8,128)(2,1)}, u32[]{:S(2)}) copy-start(bf16[512,2,256]{0,2,1:T(8,128)(2,1)} %copy-done.3) | copy-start | bytes 1572868
  124.8 33.1 %collective-permute-start.7 = (f32[64,1024]{1,0:T(8,128)}, f32[64,1024]{1,0:T(8,128)}, u32[]{:S(2)}, u32[]{:S(2)}) collective-permute-start(f32[64,1024]{1,0:T(8,128)} %get-tuple-element.15), channel_id=1, source_target_pairs={{16,24},{20,28},{17,25},{21,29},{18,26},{22,30},{19,27},{23,31}} | collective-permute-start | bytes 786440 | tf_op jit(solution)/shard_map/ppermute | solution.py:239
  150.3 7.6 %copy-start.8 = (f32[64,1024]{1,0:T(8,128)S(1)}, f32[64,1024]{1,0:T(8,128)}, u32[]{:S(2)}) copy-start(f32[64,1024]{1,0:T(8,128)} %get-tuple-element.16) | copy-start | bytes 786436
  150.3 21.8 %collective-permute-start.10 = (f32[64,1024]{1,0:T(8,128)}, f32[64,1024]{1,0:T(8,128)S(1)}, u32[]{:S(2)}, u32[]{:S(2)}) collective-permute-start(f32[64,1024]{1,0:T(8,128)} %get-tuple-element.17), channel_id=1, source_target_pairs={{16,24},{20,28},{17,25},{21,29},{18,26},{22,30},{19,27},{23,31}} | collective-permute-start | bytes 786440 | tf_op jit(solution)/shard_map/ppermute | solution.py:239
  151.8 22.1 %collective-permute-start.13 = (f32[64,1024]{1,0:T(8,128)}, f32[64,1024]{1,0:T(8,128)}, u32[]{:S(2)}, u32[]{:S(2)}) collective-permute-start(f32[64,1024]{1,0:T(8,128)} %get-tuple-element.40), channel_id=1, source_target_pairs={{16,24},{20,28},{17,25},{21,29},{18,26},{22,30},{19,27},{23,31}} | collective-permute-start | bytes 786440 | tf_op jit(solution)/shard_map/ppermute | solution.py:239
  153.8 21.1 %collective-permute-start.14 = (f32[64,1024]{1,0:T(8,128)}, f32[64,1024]{1,0:T(8,128)}, u32[]{:S(2)}, u32[]{:S(2)}) collective-permute-start(f32[64,1024]{1,0:T(8,128)} %get-tuple-element.38), channel_id=1, source_target_pairs={{16,24},{20,28},{17,25},{21,29},{18,26},{22,30},{19,27},{23,31}} | collective-permute-start | bytes 786440 | tf_op jit(solution)/shard_map/ppermute | solution.py:239
  158.9 13.9 %copy-start.11 = (f32[64,1024]{1,0:T(8,128)S(1)}, f32[64,1024]{1,0:T(8,128)}, u32[]{:S(2)}) copy-start(f32[64,1024]{1,0:T(8,128)} %get-tuple-element.18) | copy-start | bytes 786436
  158.9 14.9 %copy-start.10 = (f32[64,1024]{1,0:T(8,128)S(1)}, f32[64,1024]{1,0:T(8,128)}, u32[]{:S(2)}) copy-start(f32[64,1024]{1,0:T(8,128)} %get-tuple-element.41) | copy-start | bytes 786436
  158.9 15.9 %copy-start.9 = (f32[64,1024]{1,0:T(8,128)S(1)}, f32[64,1024]{1,0:T(8,128)}, u32[]{:S(2)}) copy-start(f32[64,1024]{1,0:T(8,128)} %get-tuple-element.39) | copy-start | bytes 786436
  176.9 8.2 %collective-permute-start.15 = (f32[256,1024]{1,0:T(8,128)}, f32[256,1024]{1,0:T(8,128)}, u32[]{:S(2)}, u32[]{:S(2)}) collective-permute-start(f32[256,1024]{1,0:T(8,128)} %pad_maximum_fusion.1), channel_id=1, source_target_pairs={{0,4},{4,0},{8,12},{12,8},{16,20},{20,16},{24,28},{28,24},{1,5},{5... | collective-permute-start | bytes 3145736 | tf_op jit(solution)/shard_map/ppermute | solution.py:252
  (11 other events, 27.1 us)

commit v6 on v5

--- a/solution.py
+++ b/solution.py
@@ -263,11 +263,11 @@
         carried_state = head_columns(prefix[b])[None, :] * incoming
         if starts[b] is not None:
             carried_state = starts[b] + carried_state
-        state_hi = carried_state.astype(jnp.bfloat16)
-        state_lo = (carried_state - state_hi.astype(jnp.float32)).astype(jnp.bfloat16)
-        projected = jnp.dot(seg_c[b], state_hi, preferred_element_type=jnp.float32) + jnp.dot(
-            seg_c[b], state_lo, preferred_element_type=jnp.float32
-        )
+        state_hi = lax.reduce_precision(carried_state, exponent_bits=8, mantissa_bits=7)
+        state_lo = (carried_state - state_hi).astype(jnp.bfloat16)
+        projected = jnp.dot(
+            seg_c[b], state_hi.astype(jnp.bfloat16), preferred_element_type=jnp.float32
+        ) + jnp.dot(seg_c[b], state_lo, preferred_element_type=jnp.float32)
         inter = head_columns(jnp.exp(cum[b])) * projected
         results.append((partials[b] + inter).astype(jnp.bfloat16))
     result = jnp.concatenate(results, axis=0) if blocks > 1 else results[0]

time: 223 us -> 223 us (level)
  no operation moved by 1% of the time
where the time goes in v6:
time: 223 us; the launch traced here: 222 us
  waiting for transfers between devices  61.8 us (28%)
  local copies, waits for them, and re-layouts  35.6 us (16%)
  starting transfers between devices  34.4 us (15%)
  other arithmetic  32.4 us (15%)
  blocking collectives  28.8 us (13%)
  Pallas kernels  25 us (11%)
  matrix products  3.42 us (2%)
    ppermute x12, waiting for transfers between devices, on_device(): acc[k] = acc[k] + lax.ppermute(send, 'ctx', pairs)  33.7 us
    all_to_all x1, blocking collectives, on_device(): return lax.all_to_all(result, 'tp', split_axis=0, concat_axis=1, tiled=True)  28.8 us
    all_to_all x1, waiting for transfers between devices, on_device(): lax.all_to_all(x_part, 'tp', split_axis=1, concat_axis=0, tiled=True)  19.9 us
    ppermute x12, starting transfers between devices, on_device(): acc[k] = acc[k] + lax.ppermute(send, 'ctx', pairs)  16.2 us
    pallas_call x1, Pallas kernels, intra_block(): pl.pallas_call(intra_kernel, out_shape=jax.ShapeDtypeStruct((BLOCK, width...  13.2 us
    pallas_call x1, Pallas kernels, fresh_block(): pl.pallas_call(fresh_kernel, out_shape=jax.ShapeDtypeStruct((N, width), j...  11.9 us
    convert_element_type x4, other arithmetic, conv_rows(): return jax.nn.silu(total).astype(jnp.bfloat16)  10.5 us
    unnamed x53, local copies, waits for them, and re-layouts  10.1 us
  transfers between devices with their start and end apart: 19, of which 7 were waited for; matrix products, arithmetic and copies ran while one was open for 22% of the time, Pallas kernels for 6%

profile of v6, /device:TPU:16, one launch (start us, length us, event | category | flops | bytes accessed | tf_op | source)
XLA Modules:
  0.0 222.0 jit_solution(18309059727663982920)
XLA Ops:
  0.0 1.5 copy.97
  1.5 3.7 %all-to-all-start.2 = ((bf16[128,4,32]{0,2,1:T(8,128)(2,1)}), bf16[128,4,32]{0,2,1:T(8,128)(2,1)S(1)}, u32[]{:S(2)}, u32[]{:S(2)}) async-start(bf16[128,4,32]{0,2,1:T(8,128)(2,1)} %bitcast.14), calls=%async_computation.2 | async-start | bytes 65536 | tf_op jit(solution)/shard_map/all_to_all | solution.py:179
  6.0 3.9 %collective-permute-start.1 = (bf16[3,2048]{1,0:T(4,128)(2,1)S(1)}, bf16[3,2048]{1,0:T(4,128)(2,1)S(1)}, u32[]{:S(2)}, u32[]{:S(2)}) collective-permute-start(bf16[3,2048]{1,0:T(4,128)(2,1)S(1)} %get-tuple-element.42), channel_id=1, source_target_pairs={{0,1},{1,2},{2,3},{3,4},{4,5},{5,6},{6,7},{7,8},{8,9},{9,10},{10,1... | collective-permute-start | bytes 36872 | tf_op jit(solution)/shard_map/ppermute | solution.py:20
  9.9 1.7 fusion.38
  11.6 3.4 %collective-permute-start = (bf16[3,8192]{1,0:T(4,128)(2,1)}, bf16[3,8192]{1,0:T(4,128)(2,1)S(1)}, u32[]{:S(2)}, u32[]{:S(2)}) collective-permute-start(bf16[3,8192]{1,0:T(4,128)(2,1)} %get-tuple-element.29), channel_id=1, source_target_pairs={{0,1},{1,2},{2,3},{3,4},{4,5},{5,6},{6,7},{7,8},{8,9},{9,10},{10,1... | collective-permute-start | bytes 147464 | tf_op jit(solution)/shard_map/ppermute | solution.py:20
  16.3 4.0 %convert_element_type.61 = f32[128,8192]{1,0:T(8,128)} convert(bf16[128,8192]{1,0:T(8,128)(2,1)} %param.10) | non-fusion elementwise | flops 1048576 | bytes 6291456 | tf_op jit(solution)/shard_map/convert_element_type | solution.py:34
  20.5 2.6 %multiply_convert_fusion.1 = bf16[128,2048]{0,1:T(8,128)(2,1)S(1)} fusion(f32[128,2048]{0,1:T(8,128)S(1)} %convert_element_type.65, f32[2048]{0:T(1024)S(1)} %bitcast.104, f32[2048]{0:T(1024)S(1)} %bitcast.106, f32[2048]{0:T(1024)S(1)} %bitcast.102, f32[2048]{0:T(1024)S(1)} %bitcast.100, f32[2048]{0:T(1024)S(1)} %copy-done.18), kind=kLoop, calls=%fused_computation.26 | loop fusion | flops 3407872 | bytes 1613824 | tf_op jit(solution)/shard_map/convert_element_type | solution.py:27
  23.2 7.7 %multiply_convert_fusion = bf16[128,8192]{1,0:T(8,128)(2,1)S(1)} fusion(f32[128,8192]{1,0:T(8,128)} %convert_element_type.61, f32[8192]{0:T(1024)S(1)} %bitcast.95, f32[8192]{0:T(1024)S(1)} %bitcast.97, f32[8192]{0:T(1024)S(1)} %bitcast.93, f32[8192]{0:T(1024)S(1)} %bitcast.91, f32[8192]{0:T(1024)S(1)} %copy-done.16), kind=kLoop, calls=%fused_computation.1 | loop fusion | flops 13631488 | bytes 6455296 | tf_op jit(solution)/shard_map/convert_element_type | solution.py:27
  32.5 2.0 dynamic_update_slice.7
  35.3 3.5 %all-to-all-start.1 = ((bf16[4,128,2,256]{1,3,2,0:T(8,128)(2,1)}), bf16[4,128,2,256]{1,3,2,0:T(8,128)(2,1)S(1)}, u32[]{:S(2)}, u32[]{:S(2)}) async-start(bf16[4,128,2,256]{1,3,2,0:T(8,128)(2,1)} %copy.95), calls=%async_computation.1 | async-start | bytes 1048576 | tf_op jit(solution)/shard_map/all_to_all | solution.py:176
  42.0 1.6 copy.127
  43.6 3.7 %all-to-all-done.1 = bf16[4,128,2,256]{1,3,2,0:T(8,128)(2,1)S(1)} async-done(((bf16[4,128,2,256]{1,3,2,0:T(8,128)(2,1)}), bf16[4,128,2,256]{1,3,2,0:T(8,128)(2,1)S(1)}, u32[]{:S(2)}, u32[]{:S(2)}) %all-to-all-start.1) | async-done | bytes 524320 | tf_op jit(solution)/shard_map/all_to_all | solution.py:176
  47.3 3.7 %all-to-all-start = ((bf16[128,4,2048]{2,0,1:T(8,128)(2,1)}), bf16[128,4,2048]{2,0,1:T(8,128)(2,1)S(1)}, u32[]{:S(2)}, u32[]{:S(2)}) async-start(bf16[128,4,2048]{2,0,1:T(8,128)(2,1)} %bitcast.87), calls=%async_computation | async-start | bytes 4194304 | tf_op jit(solution)/shard_map/all_to_all | solution.py:178
  55.8 19.9 %all-to-all-done = bf16[128,4,2048]{2,0,1:T(8,128)(2,1)S(1)} async-done(((bf16[128,4,2048]{2,0,1:T(8,128)(2,1)}), bf16[128,4,2048]{2,0,1:T(8,128)(2,1)S(1)}, u32[]{:S(2)}, u32[]{:S(2)}) %all-to-all-start) | async-done | bytes 2097184 | tf_op jit(solution)/shard_map/all_to_all | solution.py:178
  77.0 11.9 %ssd_fresh.1 = f32[256,2048]{1,0:T(8,128)} custom-call(bf16[512,2048]{1,0:T(8,128)(2,1)} %bitcast.85, bf16[256,512]{1,0:T(8,128)(2,1)} %slice_bitcast_fusion.1.bt_ref, f32[512,128]{1,0:T(8,128)} %pad.16.clone.cum_ref, f32[512,128]{1,0:T(8,128)} %pad.17.clone.dtl_ref), custom_call_target="tpu_custom_call" | custom-call | flops 536870912 | bytes 4456448 | tf_op jit(solution)/shard_map/ssd_fresh/pallas_call | solution.py:127
  88.8 3.2 %select_maximum_fusion = f32[264,2048]{1,0:T(8,128)} fusion(f32[1,32]{1,0:T(1,128)S(1)} %bitcast.109, f32[256,2048]{1,0:T(8,128)} %ssd_fresh.1), kind=kLoop, calls=%fused_computation.10 | loop fusion | flops 1622016 | bytes 4259968 | tf_op jit(solution)/shard_map/concatenate | solution.py:215
  92.0 4.5 %collective-permute-done.2 = f32[264,2048]{1,0:T(8,128)S(1)} collective-permute-done((f32[264,2048]{1,0:T(8,128)}, f32[264,2048]{1,0:T(8,128)S(1)}, u32[]{:S(2)}, u32[]{:S(2)}) %collective-permute-start.2) | collective-permute-done | bytes 2162720 | tf_op jit(solution)/shard_map/ppermute | solution.py:214
  103.9 12.8 %collective-permute-done.6 = f32[64,1024]{1,0:T(8,128)S(1)} collective-permute-done((f32[64,1024]{1,0:T(8,128)S(1)}, f32[64,1024]{1,0:T(8,128)S(1)}, u32[]{:S(2)}, u32[]{:S(2)}) %collective-permute-start.6) | collective-permute-done | bytes 262176 | tf_op jit(solution)/shard_map/ppermute | solution.py:239
  116.7 2.1 multiply_add_fusion.4
  124.8 2.1 collective-permute-start.7
  127.0 11.1 %collective-permute-done.4 = f32[64,1024]{1,0:T(8,128)} collective-permute-done((f32[64,1024]{1,0:T(8,128)}, f32[64,1024]{1,0:T(8,128)}, u32[]{:S(2)}, u32[]{:S(2)}) %collective-permute-start.4) | collective-permute-done | bytes 262176 | tf_op jit(solution)/shard_map/ppermute | solution.py:239
  138.0 5.6 %collective-permute-done.9 = f32[64,1024]{1,0:T(8,128)} collective-permute-done((f32[64,1024]{1,0:T(8,128)}, f32[64,1024]{1,0:T(8,128)}, u32[]{:S(2)}, u32[]{:S(2)}) %collective-permute-start.9) | collective-permute-done | bytes 262176 | tf_op jit(solution)/shard_map/ppermute | solution.py:239
  143.6 4.2 %collective-permute-done.12 = f32[64,1024]{1,0:T(8,128)} collective-permute-done((f32[64,1024]{1,0:T(8,128)}, f32[64,1024]{1,0:T(8,128)}, u32[]{:S(2)}, u32[]{:S(2)}) %collective-permute-start.12) | collective-permute-done | bytes 262176 | tf_op jit(solution)/shard_map/ppermute | solution.py:239
  147.8 2.5 %multiply_add_fusion.2 = (f32[64,1024]{1,0:T(8,128)}, f32[64,1024]{1,0:T(8,128)}, f32[64,1024]{1,0:T(8,128)}, f32[64,1024]{1,0:T(8,128)}, f32[64,1024]{1,0:T(8,128)}, /*index=5*/f32[64,1024]{1,0:T(8,128)}) fusion(f32[256,1024]{1,0:T(8,128)S(1)} %select_add_fusion, f32[1024]{0:T(1024)S(1)} %mul.335, f32[64,1024]{1,0:T(8,128)} %collective-permute-done.8, ...), kind=kLoop, calls=%fused_computation.35 | loop fusion | flops 589824 | bytes 3936256 | tf_op jit(solution)/shard_map/add | solution.py:238
  151.8 2.0 collective-permute-start.13
  153.8 2.0 collective-permute-start.14
  158.9 13.2 %ssd_intra.1 = f32[512,2048]{1,0:T(8,128)} custom-call(bf16[512,2048]{1,0:T(8,128)(2,1)} %bitcast.86, f32[512,512]{1,0:T(8,128)} %fusion.12.s_ref, f32[512,128]{1,0:T(8,128)} %pad.19.clone.cum_ref, f32[32,512]{1,0:T(8,128)} %bitcast.90, f32[32,512]{1,0:T(8,128)} %bitcast.99, f32[1,2048]{1,0:T(1,128)} %broadcast_in_dim_reshape.2.skip_ref), custom_call_target="tpu_custom_call" | custom-call | flops 2147483648 | bytes 7340032 | tf_op jit(solution)/shard_map/ssd_intra/pallas_call | solution.py:85
  176.9 2.6 %broadcast_in_dim.26 = f32[512,32,64]{0,2,1:T(8,128)} broadcast(f32[512,32]{0,1:T(8,128)S(1)} %copy-done.13), dimensions={0,1} | broadcast | bytes 4259840 | tf_op jit(solution)/shard_map/broadcast_in_dim | solution.py:142
  179.5 5.4 %copy.106 = f32[512,2048]{1,0:T(8,128)} copy(f32[512,2048]{0,1:T(8,128)} %bitcast.82) | data formatting | bytes 8388608 | tf_op jit(solution)/shard_map/reshape | solution.py:142
  185.1 1.8 broadcast_select_fusion
  191.7 28.8 %all_to_all.56 = bf16[4,128,2048]{2,1,0:T(8,128)(2,1)S(1)} all-to-all(bf16[4,128,2048]{2,1,0:T(8,128)(2,1)S(1)} %bitcast.84), channel_id=1, replica_groups=mesh['ctx'=8,'tp'=4] {'tp'}, dimensions={0} | all-to-all | bytes 4194304 | tf_op jit(solution)/shard_map/all_to_all | solution.py:274
  220.4 1.6 copy.115
  (136 shorter events, 41.4 us)
Async XLA Ops:
  1.5 33.8 %all-to-all-start.2 = ((bf16[128,4,32]{0,2,1:T(8,128)(2,1)}), bf16[128,4,32]{0,2,1:T(8,128)(2,1)S(1)}, u32[]{:S(2)}, u32[]{:S(2)}) async-start(bf16[128,4,32]{0,2,1:T(8,128)(2,1)} %bitcast.14), calls=%async_computation.2 | async-start | bytes 65536 | tf_op jit(solution)/shard_map/all_to_all | solution.py:179
  6.0 26.1 %collective-permute-start.1 = (bf16[3,2048]{1,0:T(4,128)(2,1)S(1)}, bf16[3,2048]{1,0:T(4,128)(2,1)S(1)}, u32[]{:S(2)}, u32[]{:S(2)}) collective-permute-start(bf16[3,2048]{1,0:T(4,128)(2,1)S(1)} %get-tuple-element.42), channel_id=1, source_target_pairs={{0,1},{1,2},{2,3},{3,4},{4,5},{5,6},{6,7},{7,8},{8,9},{9,10},{10,1... | collective-permute-start | bytes 36872 | tf_op jit(solution)/shard_map/ppermute | solution.py:20
  11.6 29.2 %collective-permute-start = (bf16[3,8192]{1,0:T(4,128)(2,1)}, bf16[3,8192]{1,0:T(4,128)(2,1)S(1)}, u32[]{:S(2)}, u32[]{:S(2)}) collective-permute-start(bf16[3,8192]{1,0:T(4,128)(2,1)} %get-tuple-element.29), channel_id=1, source_target_pairs={{0,1},{1,2},{2,3},{3,4},{4,5},{5,6},{6,7},{7,8},{8,9},{9,10},{10,1... | collective-permute-start | bytes 147464 | tf_op jit(solution)/shard_map/ppermute | solution.py:20
  16.3 4.3 %copy-start.18 = (f32[2048]{0:T(1024)S(1)}, f32[2048]{0:T(1024)}, u32[]{:S(2)}) copy-start(f32[2048]{0:T(1024)} %param.16) | copy-start | bytes 24580
  23.2 7.7 %copy-start.21 = (f32[128]{0:T(128)S(1)}, f32[128]{0:T(128)}, u32[]{:S(2)}) copy-start(f32[128]{0:T(128)} %param.18) | copy-start | bytes 1540
  23.2 8.3 %copy-start.22 = (f32[128]{0:T(128)S(1)}, f32[128]{0:T(128)}, u32[]{:S(2)}) copy-start(f32[128]{0:T(128)} %param.17) | copy-start | bytes 1540
  35.3 12.0 %all-to-all-start.1 = ((bf16[4,128,2,256]{1,3,2,0:T(8,128)(2,1)}), bf16[4,128,2,256]{1,3,2,0:T(8,128)(2,1)S(1)}, u32[]{:S(2)}, u32[]{:S(2)}) async-start(bf16[4,128,2,256]{1,3,2,0:T(8,128)(2,1)} %copy.95), calls=%async_computation.1 | async-start | bytes 1048576 | tf_op jit(solution)/shard_map/all_to_all | solution.py:176
  47.3 5.7 %copy-start.20 = (f32[32]{0:T(128)S(1)}, f32[32]{0:T(128)}, u32[]{:S(2)}) copy-start(f32[32]{0:T(128)} %dynamic_slice.21) | copy-start | bytes 388
  47.3 28.3 %all-to-all-start = ((bf16[128,4,2048]{2,0,1:T(8,128)(2,1)}), bf16[128,4,2048]{2,0,1:T(8,128)(2,1)S(1)}, u32[]{:S(2)}, u32[]{:S(2)}) async-start(bf16[128,4,2048]{2,0,1:T(8,128)(2,1)} %bitcast.87), calls=%async_computation | async-start | bytes 4194304 | tf_op jit(solution)/shard_map/all_to_all | solution.py:178
  52.1 104.9 %copy-start.12 = (f32[512,32]{0,1:T(8,128)}, f32[512,32]{0,1:T(8,128)S(1)}, u32[]{:S(2)}) copy-start(f32[512,32]{0,1:T(8,128)S(1)} %get-tuple-element.12) | copy-start | bytes 196612
  53.1 35.7 %copy-start.15 = (f32[512,32]{0,1:T(8,128)}, f32[512,32]{0,1:T(8,128)S(1)}, u32[]{:S(2)}) copy-start(f32[512,32]{0,1:T(8,128)S(1)} %compare_select_fusion) | copy-start | bytes 196612
  92.0 4.5 %collective-permute-start.2 = (f32[264,2048]{1,0:T(8,128)}, f32[264,2048]{1,0:T(8,128)S(1)}, u32[]{:S(2)}, u32[]{:S(2)}) collective-permute-start(f32[264,2048]{1,0:T(8,128)} %select_maximum_fusion), channel_id=1, source_target_pairs={{0,4},{4,0},{8,12},{12,8},{16,20},{20,16},{24,28},{28,24},{1,5},{5... | collective-permute-start | bytes 6488072 | tf_op jit(solution)/shard_map/ppermute | solution.py:214
  98.9 3.6 %collective-permute-start.5 = (f32[64,1024]{1,0:T(8,128)S(1)}, f32[64,1024]{1,0:T(8,128)S(1)}, u32[]{:S(2)}, u32[]{:S(2)}) collective-permute-start(f32[64,1024]{1,0:T(8,128)S(1)} %get-tuple-element.34), channel_id=1, source_target_pairs={{0,8},{4,12},{1,9},{5,13},{2,10},{6,14},{3,11},{7,15}} | collective-permute-start | bytes 786440 | tf_op jit(solution)/shard_map/ppermute | solution.py:239
  99.6 4.2 %collective-permute-start.11 = (f32[64,1024]{1,0:T(8,128)S(1)}, f32[64,1024]{1,0:T(8,128)S(1)}, u32[]{:S(2)}, u32[]{:S(2)}) collective-permute-start(f32[64,1024]{1,0:T(8,128)S(1)} %get-tuple-element.35), channel_id=1, source_target_pairs={{0,8},{4,12},{1,9},{5,13},{2,10},{6,14},{3,11},{7,15}} | collective-permute-start | bytes 786440 | tf_op jit(solution)/shard_map/ppermute | solution.py:239
  100.3 3.6 %collective-permute-start.8 = (f32[64,1024]{1,0:T(8,128)S(1)}, f32[64,1024]{1,0:T(8,128)}, u32[]{:S(2)}, u32[]{:S(2)}) collective-permute-start(f32[64,1024]{1,0:T(8,128)S(1)} %get-tuple-element.36), channel_id=1, source_target_pairs={{0,8},{4,12},{1,9},{5,13},{2,10},{6,14},{3,11},{7,15}} | collective-permute-start | bytes 786440 | tf_op jit(solution)/shard_map/ppermute | solution.py:239
  101.7 21.0 %copy-start.23 = (f32[128]{0:T(128)S(1)}, f32[128]{0:T(128)}, u32[]{:S(2)}) copy-start(f32[128]{0:T(128)} %param.19) | copy-start | bytes 1540
  101.7 2.2 collective-permute-start.3
  102.5 14.2 %collective-permute-start.6 = (f32[64,1024]{1,0:T(8,128)S(1)}, f32[64,1024]{1,0:T(8,128)S(1)}, u32[]{:S(2)}, u32[]{:S(2)}) collective-permute-start(f32[64,1024]{1,0:T(8,128)S(1)} %multiply_add_fusion.5), channel_id=1, source_target_pairs={{8,16},{12,20},{9,17},{13,21},{10,18},{14,22},{11,19},{15,23}} | collective-permute-start | bytes 786440 | tf_op jit(solution)/shard_map/ppermute | solution.py:239
  103.9 12.8 %copy-start.7 = (f32[64,1024]{1,0:T(8,128)}, f32[64,1024]{1,0:T(8,128)S(1)}, u32[]{:S(2)}) copy-start(f32[64,1024]{1,0:T(8,128)S(1)} %collective-permute-done.3) | copy-start | bytes 786436
  118.8 19.2 %collective-permute-start.4 = (f32[64,1024]{1,0:T(8,128)}, f32[64,1024]{1,0:T(8,128)}, u32[]{:S(2)}, u32[]{:S(2)}) collective-permute-start(f32[64,1024]{1,0:T(8,128)} %get-tuple-element.31), channel_id=1, source_target_pairs={{8,16},{12,20},{9,17},{13,21},{10,18},{14,22},{11,19},{15,23}} | collective-permute-start | bytes 786440 | tf_op jit(solution)/shard_map/ppermute | solution.py:239
  120.1 23.6 %collective-permute-start.9 = (f32[64,1024]{1,0:T(8,128)}, f32[64,1024]{1,0:T(8,128)}, u32[]{:S(2)}, u32[]{:S(2)}) collective-permute-start(f32[64,1024]{1,0:T(8,128)} %get-tuple-element.32), channel_id=1, source_target_pairs={{8,16},{12,20},{9,17},{13,21},{10,18},{14,22},{11,19},{15,23}} | collective-permute-start | bytes 786440 | tf_op jit(solution)/shard_map/ppermute | solution.py:239
  121.4 26.5 %collective-permute-start.12 = (f32[64,1024]{1,0:T(8,128)}, f32[64,1024]{1,0:T(8,128)}, u32[]{:S(2)}, u32[]{:S(2)}) collective-permute-start(f32[64,1024]{1,0:T(8,128)} %get-tuple-element.33), channel_id=1, source_target_pairs={{8,16},{12,20},{9,17},{13,21},{10,18},{14,22},{11,19},{15,23}} | collective-permute-start | bytes 786440 | tf_op jit(solution)/shard_map/ppermute | solution.py:239
  124.8 30.9 %copy-start.4 = (bf16[512,2,256]{0,2,1:T(8,128)(2,1)S(1)}, bf16[512,2,256]{0,2,1:T(8,128)(2,1)}, u32[]{:S(2)}) copy-start(bf16[512,2,256]{0,2,1:T(8,128)(2,1)} %copy-done.3) | copy-start | bytes 1572868
  124.8 33.1 %collective-permute-start.7 = (f32[64,1024]{1,0:T(8,128)}, f32[64,1024]{1,0:T(8,128)}, u32[]{:S(2)}, u32[]{:S(2)}) collective-permute-start(f32[64,1024]{1,0:T(8,128)} %get-tuple-element.15), channel_id=1, source_target_pairs={{16,24},{20,28},{17,25},{21,29},{18,26},{22,30},{19,27},{23,31}} | collective-permute-start | bytes 786440 | tf_op jit(solution)/shard_map/ppermute | solution.py:239
  150.3 7.6 %copy-start.8 = (f32[64,1024]{1,0:T(8,128)S(1)}, f32[64,1024]{1,0:T(8,128)}, u32[]{:S(2)}) copy-start(f32[64,1024]{1,0:T(8,128)} %get-tuple-element.16) | copy-start | bytes 786436
  150.3 21.8 %collective-permute-start.10 = (f32[64,1024]{1,0:T(8,128)}, f32[64,1024]{1,0:T(8,128)S(1)}, u32[]{:S(2)}, u32[]{:S(2)}) collective-permute-start(f32[64,1024]{1,0:T(8,128)} %get-tuple-element.17), channel_id=1, source_target_pairs={{16,24},{20,28},{17,25},{21,29},{18,26},{22,30},{19,27},{23,31}} | collective-permute-start | bytes 786440 | tf_op jit(solution)/shard_map/ppermute | solution.py:239
  151.8 22.1 %collective-permute-start.13 = (f32[64,1024]{1,0:T(8,128)}, f32[64,1024]{1,0:T(8,128)}, u32[]{:S(2)}, u32[]{:S(2)}) collective-permute-start(f32[64,1024]{1,0:T(8,128)} %get-tuple-element.40), channel_id=1, source_target_pairs={{16,24},{20,28},{17,25},{21,29},{18,26},{22,30},{19,27},{23,31}} | collective-permute-start | bytes 786440 | tf_op jit(solution)/shard_map/ppermute | solution.py:239
  153.8 21.1 %collective-permute-start.14 = (f32[64,1024]{1,0:T(8,128)}, f32[64,1024]{1,0:T(8,128)}, u32[]{:S(2)}, u32[]{:S(2)}) collective-permute-start(f32[64,1024]{1,0:T(8,128)} %get-tuple-element.38), channel_id=1, source_target_pairs={{16,24},{20,28},{17,25},{21,29},{18,26},{22,30},{19,27},{23,31}} | collective-permute-start | bytes 786440 | tf_op jit(solution)/shard_map/ppermute | solution.py:239
  158.9 13.9 %copy-start.11 = (f32[64,1024]{1,0:T(8,128)S(1)}, f32[64,1024]{1,0:T(8,128)}, u32[]{:S(2)}) copy-start(f32[64,1024]{1,0:T(8,128)} %get-tuple-element.18) | copy-start | bytes 786436
  158.9 14.9 %copy-start.10 = (f32[64,1024]{1,0:T(8,128)S(1)}, f32[64,1024]{1,0:T(8,128)}, u32[]{:S(2)}) copy-start(f32[64,1024]{1,0:T(8,128)} %get-tuple-element.41) | copy-start | bytes 786436
  158.9 15.9 %copy-start.9 = (f32[64,1024]{1,0:T(8,128)S(1)}, f32[64,1024]{1,0:T(8,128)}, u32[]{:S(2)}) copy-start(f32[64,1024]{1,0:T(8,128)} %get-tuple-element.39) | copy-start | bytes 786436
  176.9 8.2 %collective-permute-start.15 = (f32[256,1024]{1,0:T(8,128)}, f32[256,1024]{1,0:T(8,128)}, u32[]{:S(2)}, u32[]{:S(2)}) collective-permute-start(f32[256,1024]{1,0:T(8,128)} %pad_maximum_fusion.1), channel_id=1, source_target_pairs={{0,4},{4,0},{8,12},{12,8},{16,20},{20,16},{24,28},{28,24},{1,5},{5... | collective-permute-start | bytes 3145736 | tf_op jit(solution)/shard_map/ppermute | solution.py:252
  (11 other events, 27.1 us)

commit v7 on v6

--- a/solution.py
+++ b/solution.py
@@ -230,25 +230,41 @@
     )[None, :]
     pieces = 4 if N % 32 == 0 else 1
     piece_rows = N // pieces
-    acc = [jnp.zeros((piece_rows, half_width), jnp.float32) for _ in range(pieces)]
-    last_send = None
-    for r in range(chips - 1):
-        pairs = [(2 * r + q, 2 * r + 2 + q) for q in range(2)]
-        for k in range(pieces):
-            send = chip_decay * acc[k] + chip_half[k * piece_rows : (k + 1) * piece_rows]
-            acc[k] = acc[k] + lax.ppermute(send, "ctx", pairs)
-            last_send = send
+    own_pieces = chip_half.reshape(pieces, piece_rows, half_width)
+
     skip_cols = head_columns(skip_local)
-    partials = []
-    for b in range(blocks):
-        scores = jnp.einsum("in,jn->ij", seg_c[b], seg_b[b], preferred_element_type=jnp.float32)
-        operands = (x_blk[b], scores, cum[b], dt_blk[b])
-        if last_send is not None:
-            operands = lax.optimization_barrier(operands + (last_send,))[:4]
-        partials.append(intra_block(*operands, skip_cols))
-
-    prefix_half = jnp.concatenate(acc, axis=0) if pieces > 1 else acc[0]
-    prefix_half = lax.optimization_barrier((prefix_half, partials))[0]
+    scores = [
+        jnp.einsum("in,jn->ij", seg_c[b], seg_b[b], preferred_element_type=jnp.float32)
+        for b in range(blocks)
+    ]
+
+    def run_intra(_):
+        return [intra_block(x_blk[b], scores[b], cum[b], dt_blk[b], skip_cols) for b in range(blocks)]
+
+    def no_intra(_):
+        return [jnp.zeros((BLOCK, head_width), jnp.float32) for _ in range(blocks)]
+
+    early = chip >= 2
+    ahead = lax.cond(early, run_intra, no_intra, 0)
+    own_pieces = lax.optimization_barrier((own_pieces, ahead))[0]
+
+    acc = jnp.zeros((pieces, piece_rows, half_width), jnp.float32)
+    for s in range(chips - 2 + pieces):
+        pairs = [
+            (2 * r + q, 2 * r + 2 + q) for r in range(chips - 1) if 0 <= s - r < pieces for q in range(2)
+        ]
+        send_piece = jnp.clip(s - chip, 0, pieces - 1)
+        send = chip_decay * lax.dynamic_index_in_dim(acc, send_piece, 0, False) + lax.dynamic_index_in_dim(
+            own_pieces, send_piece, 0, False
+        )
+        got = lax.ppermute(send, "ctx", pairs)
+        recv_piece = jnp.clip(s - chip + 1, 0, pieces - 1)
+        acc = lax.dynamic_update_index_in_dim(
+            acc, lax.dynamic_index_in_dim(acc, recv_piece, 0, False) + got, recv_piece, 0
+        )
+    acc, ahead = lax.optimization_barrier((acc, ahead))
+    partials = lax.cond(early, lambda a: a, run_intra, ahead)
+    prefix_half = acc.reshape(N, half_width)
     mate_prefix = lax.ppermute(prefix_half, "ctx", [(i, i ^ 1) for i in range(n_ctx)])
     chip_prefix = jnp.concatenate(
         [jnp.where(core == 0, prefix_half, mate_prefix), jnp.where(core == 0, mate_prefix, prefix_half)],

time: 223 us -> 235 us (1.054)
  the two profiles are of different devices: /device:TPU:16 before, /device:TPU:8 now
where the time goes in v7:
time: 235 us; the launch traced here: 233 us
  waiting for transfers between devices  55.4 us (24%)
  starting transfers between devices  42 us (18%)
  local copies, waits for them, and re-layouts  40.5 us (17%)
  other arithmetic  37.8 us (16%)
  blocking collectives  28.8 us (12%)
  Pallas kernels  24.9 us (11%)
  matrix products  3.42 us (1%)
    ppermute x6, waiting for transfers between devices, on_device(): got = lax.ppermute(send, 'ctx', pairs)  29.7 us
    all_to_all x1, blocking collectives, on_device(): return lax.all_to_all(result, 'tp', split_axis=0, concat_axis=1, tiled=True)  28.8 us
    ppermute x6, starting transfers between devices, on_device(): got = lax.ppermute(send, 'ctx', pairs)  23.8 us
    all_to_all x1, waiting for transfers between devices, on_device(): lax.all_to_all(x_part, 'tp', split_axis=1, concat_axis=0, tiled=True)  19.3 us
    pallas_call x1, Pallas kernels, intra_block(): pl.pallas_call(intra_kernel, out_shape=jax.ShapeDtypeStruct((BLOCK, width...  13.2 us
    pallas_call x1, Pallas kernels, fresh_block(): pl.pallas_call(fresh_kernel, out_shape=jax.ShapeDtypeStruct((N, width), j...  11.8 us
    convert_element_type x4, other arithmetic, conv_rows(): return jax.nn.silu(total).astype(jnp.bfloat16)  11.3 us
    add x6, other arithmetic, on_device(): chip_decay * lax.dynamic_index_in_dim(acc, send_piece, 0, False)  9.25 us
  transfers between devices with their start and end apart: 13, of which 8 were waited for; matrix products, arithmetic and copies ran while one was open for 22% of the time, Pallas kernels for 6%

profile of v7, /device:TPU:8, one launch (start us, length us, event | category | flops | bytes accessed | tf_op | source)
XLA Modules:
  0.0 233.4 jit_solution(8633267946846694737)
XLA Ops:
  1.5 3.7 %all-to-all-start = ((bf16[128,4,32]{0,2,1:T(8,128)(2,1)}), bf16[128,4,32]{0,2,1:T(8,128)(2,1)S(1)}, u32[]{:S(2)}, u32[]{:S(2)}) async-start(bf16[128,4,32]{0,2,1:T(8,128)(2,1)} %bitcast.6), calls=%async_computation | async-start | bytes 65536 | tf_op jit(solution)/shard_map/all_to_all | solution.py:179
  6.9 3.9 %collective-permute-start = (bf16[3,8192]{1,0:T(4,128)(2,1)}, bf16[3,8192]{1,0:T(4,128)(2,1)}, u32[]{:S(2)}, u32[]{:S(2)}) collective-permute-start(bf16[3,8192]{1,0:T(4,128)(2,1)} %get-tuple-element.124), channel_id=1, source_target_pairs={{0,1},{1,2},{2,3},{3,4},{4,5},{5,6},{6,7},{7,8},{8,9},{9,10},{10,1... | collective-permute-start | bytes 147464 | tf_op jit(solution)/shard_map/ppermute | solution.py:20
  11.6 3.4 %collective-permute-start.1 = (bf16[3,2048]{1,0:T(4,128)(2,1)S(1)}, bf16[3,2048]{1,0:T(4,128)(2,1)S(1)}, u32[]{:S(2)}, u32[]{:S(2)}) collective-permute-start(bf16[3,2048]{1,0:T(4,128)(2,1)S(1)} %get-tuple-element.126), channel_id=1, source_target_pairs={{0,1},{1,2},{2,3},{3,4},{4,5},{5,6},{6,7},{7,8},{8,9},{9,10},{10,1... | collective-permute-start | bytes 36872 | tf_op jit(solution)/shard_map/ppermute | solution.py:20
  15.0 4.0 %convert_element_type.72 = f32[128,8192]{1,0:T(8,128)} convert(bf16[128,8192]{1,0:T(8,128)(2,1)} %param.14) | non-fusion elementwise | flops 1048576 | bytes 6291456 | tf_op jit(solution)/shard_map/convert_element_type | solution.py:34
  19.9 7.8 %multiply_convert_fusion = bf16[128,8192]{1,0:T(8,128)(2,1)S(1)} fusion(f32[128,8192]{1,0:T(8,128)} %convert_element_type.72, f32[8192]{0:T(1024)S(1)} %bitcast.179, f32[8192]{0:T(1024)S(1)} %bitcast.181, f32[8192]{0:T(1024)S(1)} %bitcast.177, f32[8192]{0:T(1024)S(1)} %bitcast.175, f32[8192]{0:T(1024)S(1)} %copy-done.11), kind=kLoop, calls=%fused_computation.1 | loop fusion | flops 13631488 | bytes 6455296 | tf_op jit(solution)/shard_map/convert_element_type | solution.py:27
  27.6 3.2 %multiply_convert_fusion.1 = bf16[128,2048]{0,1:T(8,128)(2,1)} fusion(f32[128,2048]{0,1:T(8,128)S(1)} %convert_element_type.76, f32[2048]{0:T(1024)S(1)} %bitcast.187, f32[2048]{0:T(1024)S(1)} %bitcast.189, f32[2048]{0:T(1024)S(1)} %bitcast.185, f32[2048]{0:T(1024)S(1)} %bitcast.183, f32[2048]{0:T(1024)S(1)} %copy-done.13), kind=kLoop, calls=%fused_computation.25 | loop fusion | flops 3407872 | bytes 1613824 | tf_op jit(solution)/shard_map/convert_element_type | solution.py:27
  31.5 5.0 %dynamic_update_slice.26 = bf16[128,2048]{0,1:T(8,128)(2,1)} dynamic-update-slice(bf16[128,2048]{0,1:T(8,128)(2,1)} %multiply_convert_fusion.1, bf16[3,2048]{0,1:T(8,128)(2,1)S(1)} %copy.117, s32[]{:T(128)} %constant.133.clone.1, s32[]{:T(128)} %constant.133.clone.1) | dynamic-update-slice | bytes 24580 | tf_op jit(solution)/shard_map/dynamic_update_slice | solution.py:36
  36.4 1.9 copy.118
  39.2 3.5 %all-to-all-start.2 = ((bf16[4,128,2,256]{1,3,2,0:T(8,128)(2,1)}), bf16[4,128,2,256]{1,3,2,0:T(8,128)(2,1)S(1)}, u32[]{:S(2)}, u32[]{:S(2)}) async-start(bf16[4,128,2,256]{1,3,2,0:T(8,128)(2,1)} %copy.118), calls=%async_computation.2 | async-start | bytes 1048576 | tf_op jit(solution)/shard_map/all_to_all | solution.py:176
  45.5 5.8 %all-to-all-done.2 = bf16[4,128,2,256]{1,3,2,0:T(8,128)(2,1)S(1)} async-done(((bf16[4,128,2,256]{1,3,2,0:T(8,128)(2,1)}), bf16[4,128,2,256]{1,3,2,0:T(8,128)(2,1)S(1)}, u32[]{:S(2)}, u32[]{:S(2)}) %all-to-all-start.2) | async-done | bytes 524320 | tf_op jit(solution)/shard_map/all_to_all | solution.py:176
  51.3 3.6 %all-to-all-start.1 = ((bf16[128,4,2048]{2,0,1:T(8,128)(2,1)}), bf16[128,4,2048]{2,0,1:T(8,128)(2,1)S(1)}, u32[]{:S(2)}, u32[]{:S(2)}) async-start(bf16[128,4,2048]{2,0,1:T(8,128)(2,1)} %bitcast.166), calls=%async_computation.1 | async-start | bytes 4194304 | tf_op jit(solution)/shard_map/all_to_all | solution.py:178
  60.2 19.3 %all-to-all-done.1 = bf16[128,4,2048]{2,0,1:T(8,128)(2,1)S(1)} async-done(((bf16[128,4,2048]{2,0,1:T(8,128)(2,1)}), bf16[128,4,2048]{2,0,1:T(8,128)(2,1)S(1)}, u32[]{:S(2)}, u32[]{:S(2)}) %all-to-all-start.1) | async-done | bytes 2097184 | tf_op jit(solution)/shard_map/all_to_all | solution.py:178
  79.5 11.8 %ssd_fresh.1 = f32[256,2048]{1,0:T(8,128)} custom-call(bf16[512,2048]{1,0:T(8,128)(2,1)S(1)} %bitcast.163, bf16[256,512]{1,0:T(8,128)(2,1)} %slice_bitcast_fusion.1.bt_ref, f32[512,128]{1,0:T(8,128)} %pad.19.cum_ref, f32[512,128]{1,0:T(8,128)} %pad.20.dtl_ref), custom_call_target="tpu_custom_call" | custom-call | flops 536870912 | bytes 4456448 | tf_op jit(solution)/shard_map/ssd_fresh/pallas_call | solution.py:127
  91.3 3.2 %select_maximum_fusion = f32[264,2048]{1,0:T(8,128)} fusion(f32[1,32]{1,0:T(1,128)S(1)} %fusion.30, f32[256,2048]{1,0:T(8,128)} %ssd_fresh.1), kind=kLoop, calls=%fused_computation.10 | loop fusion | flops 1622016 | bytes 4259968 | tf_op jit(solution)/shard_map/concatenate | solution.py:215
  96.0 2.5 %conditional.2 = (f32[512,2048]{1,0:T(8,128)}) conditional(s32[]{:T(128)} %convert_element_type.66, () %tuple.20, (f32[1,512,32]{2,1,0:T(8,128)S(1)}, f32[512,32]{1,0:T(8,128)S(1)}, f32[32,64]{1,0:T(8,128)S(1)}, bf16[512,2048]{1,0:T(8,128)(2,1)}, f32[512,512]{1,0:T(8,128)}) %tuple.54), branch_computations={%region_2.3_spmd, %region_3.4_spmd} | conditional | flops 2147483648 | bytes 7946252 | solution.py:248
  96.0 2.5 %broadcast.81 = f32[512,2048]{1,0:T(8,128)} broadcast(f32[]{:T(128)} %constant.127.clone), dimensions={} | broadcast | bytes 4194308 | tf_op jit(solution)/shard_map/broadcast.9
  103.4 9.2 %collective-permute-done.3 = f32[64,1024]{1,0:T(8,128)} collective-permute-done((f32[64,1024]{1,0:T(8,128)}, f32[64,1024]{1,0:T(8,128)}, u32[]{:S(2)}, u32[]{:S(2)}) %collective-permute-start.3) | collective-permute-done | bytes 262176 | tf_op jit(solution)/shard_map/ppermute | solution.py:260
  113.8 1.7 bitcast_add_fusion.8
  115.5 7.3 %collective-permute-start.4 = (f32[64,1024]{1,0:T(8,128)}, f32[64,1024]{1,0:T(8,128)}, u32[]{:S(2)}, u32[]{:S(2)}) collective-permute-start(f32[64,1024]{1,0:T(8,128)} %bitcast_add_fusion.8), channel_id=1, source_target_pairs={{0,8},{4,12},{8,16},{12,20},{1,9},{5,13},{9,17},{13,21},{2,10},{6,... | collective-permute-start | bytes 786440 | tf_op jit(solution)/shard_map/ppermute | solution.py:260
  122.8 6.5 %collective-permute-done.4 = f32[64,1024]{1,0:T(8,128)} collective-permute-done((f32[64,1024]{1,0:T(8,128)}, f32[64,1024]{1,0:T(8,128)}, u32[]{:S(2)}, u32[]{:S(2)}) %collective-permute-start.4) | collective-permute-done | bytes 262176 | tf_op jit(solution)/shard_map/ppermute | solution.py:260
  132.0 4.4 %collective-permute-start.5 = (f32[64,1024]{1,0:T(8,128)}, f32[64,1024]{1,0:T(8,128)}, u32[]{:S(2)}, u32[]{:S(2)}) collective-permute-start(f32[64,1024]{1,0:T(8,128)} %bitcast_add_fusion.6), channel_id=1, source_target_pairs={{0,8},{4,12},{8,16},{12,20},{16,24},{20,28},{1,9},{5,13},{9,17},{1... | collective-permute-start | bytes 786440 | tf_op jit(solution)/shard_map/ppermute | solution.py:260
  136.4 5.7 %collective-permute-done.5 = f32[64,1024]{1,0:T(8,128)} collective-permute-done((f32[64,1024]{1,0:T(8,128)}, f32[64,1024]{1,0:T(8,128)}, u32[]{:S(2)}, u32[]{:S(2)}) %collective-permute-start.5) | collective-permute-done | bytes 262176 | tf_op jit(solution)/shard_map/ppermute | solution.py:260
  144.8 4.4 %collective-permute-start.6 = (f32[64,1024]{1,0:T(8,128)}, f32[64,1024]{1,0:T(8,128)}, u32[]{:S(2)}, u32[]{:S(2)}) collective-permute-start(f32[64,1024]{1,0:T(8,128)} %bitcast_add_fusion.4), channel_id=1, source_target_pairs={{0,8},{4,12},{8,16},{12,20},{16,24},{20,28},{1,9},{5,13},{9,17},{1... | collective-permute-start | bytes 786440 | tf_op jit(solution)/shard_map/ppermute | solution.py:260
  149.2 4.8 %collective-permute-done.6 = f32[64,1024]{1,0:T(8,128)} collective-permute-done((f32[64,1024]{1,0:T(8,128)}, f32[64,1024]{1,0:T(8,128)}, u32[]{:S(2)}, u32[]{:S(2)}) %collective-permute-start.6) | collective-permute-done | bytes 262176 | tf_op jit(solution)/shard_map/ppermute | solution.py:260
  156.7 5.1 %collective-permute-start.7 = (f32[64,1024]{1,0:T(8,128)}, f32[64,1024]{1,0:T(8,128)}, u32[]{:S(2)}, u32[]{:S(2)}) collective-permute-start(f32[64,1024]{1,0:T(8,128)} %bitcast_add_fusion.2), channel_id=1, source_target_pairs={{8,16},{12,20},{16,24},{20,28},{9,17},{13,21},{17,25},{21,29},{10,... | collective-permute-start | bytes 786440 | tf_op jit(solution)/shard_map/ppermute | solution.py:260
  161.9 3.5 %collective-permute-done.7 = f32[64,1024]{1,0:T(8,128)} collective-permute-done((f32[64,1024]{1,0:T(8,128)}, f32[64,1024]{1,0:T(8,128)}, u32[]{:S(2)}, u32[]{:S(2)}) %collective-permute-start.7) | collective-permute-done | bytes 262176 | tf_op jit(solution)/shard_map/ppermute | solution.py:260
  171.5 2.6 %broadcast_in_dim.55 = f32[512,32,64]{0,2,1:T(8,128)} broadcast(f32[512,32]{0,1:T(8,128)S(1)} %copy.124), dimensions={0,1} | broadcast | bytes 4259840 | tf_op jit(solution)/shard_map/broadcast_in_dim | solution.py:142
  174.1 5.4 %copy.125 = f32[512,2048]{1,0:T(8,128)} copy(f32[512,2048]{0,1:T(8,128)} %bitcast.153) | data formatting | bytes 8388608 | tf_op jit(solution)/shard_map/reshape | solution.py:142
  179.6 17.0 %conditional.3 = (f32[512,2048]{1,0:T(8,128)}) conditional(s32[]{:T(128)} %convert_element_type.66, (f32[1,512,32]{2,1,0:T(8,128)S(1)}, f32[512,32]{1,0:T(8,128)}, f32[32,64]{1,0:T(8,128)S(1)}, bf16[512,2048]{1,0:T(8,128)(2,1)}, f32[512,512]{1,0:T(8,128)}) %tuple.56, f32[512,2048]{1,0:T(8,128)} %get-tuple-element.136), branch_computations={%region_4.5_spmd, %region_5.6_spmd} | conditional | flops 2147483648 | bytes 7946252 | solution.py:266
  181.1 1.7 copy.123
  183.5 13.2 %ssd_intra.3 = f32[512,2048]{1,0:T(8,128)} custom-call(bf16[512,2048]{1,0:T(8,128)(2,1)} %get-tuple-element.37.x_ref, f32[512,512]{1,0:T(8,128)} %get-tuple-element.38.s_ref, f32[512,128]{1,0:T(8,128)} %pad.15.clone.cum_ref, f32[32,512]{1,0:T(8,128)} %bitcast.191, f32[32,512]{1,0:T(8,128)} %bitcast.192, f32[1,2048]{1,0:T(1,128)} %broadcast_in_dim_reshape.4.skip_ref), custom_call_target="tpu_custom_call" | custom-call | flops 2147483648 | bytes 7340032 | tf_op jit(solution)/shard_map/cond/branch_0_fun/ssd_intra/pallas_call | solution.py:85
  203.0 28.8 %all_to_all.56 = bf16[4,128,2048]{2,1,0:T(8,128)(2,1)S(1)} all-to-all(bf16[4,128,2048]{2,1,0:T(8,128)(2,1)S(1)} %bitcast.162), channel_id=1, replica_groups=mesh['ctx'=8,'tp'=4] {'tp'}, dimensions={0} | all-to-all | bytes 4194304 | tf_op jit(solution)/shard_map/all_to_all | solution.py:290
  (122 shorter events, 45.9 us)
Async XLA Ops:
  1.5 37.7 %all-to-all-start = ((bf16[128,4,32]{0,2,1:T(8,128)(2,1)}), bf16[128,4,32]{0,2,1:T(8,128)(2,1)S(1)}, u32[]{:S(2)}, u32[]{:S(2)}) async-start(bf16[128,4,32]{0,2,1:T(8,128)(2,1)} %bitcast.6), calls=%async_computation | async-start | bytes 65536 | tf_op jit(solution)/shard_map/all_to_all | solution.py:179
  6.9 31.5 %collective-permute-start = (bf16[3,8192]{1,0:T(4,128)(2,1)}, bf16[3,8192]{1,0:T(4,128)(2,1)}, u32[]{:S(2)}, u32[]{:S(2)}) collective-permute-start(bf16[3,8192]{1,0:T(4,128)(2,1)} %get-tuple-element.124), channel_id=1, source_target_pairs={{0,1},{1,2},{2,3},{3,4},{4,5},{5,6},{6,7},{7,8},{8,9},{9,10},{10,1... | collective-permute-start | bytes 147464 | tf_op jit(solution)/shard_map/ppermute | solution.py:20
  11.6 19.5 %collective-permute-start.1 = (bf16[3,2048]{1,0:T(4,128)(2,1)S(1)}, bf16[3,2048]{1,0:T(4,128)(2,1)S(1)}, u32[]{:S(2)}, u32[]{:S(2)}) collective-permute-start(bf16[3,2048]{1,0:T(4,128)(2,1)S(1)} %get-tuple-element.126), channel_id=1, source_target_pairs={{0,1},{1,2},{2,3},{3,4},{4,5},{5,6},{6,7},{7,8},{8,9},{9,10},{10,1... | collective-permute-start | bytes 36872 | tf_op jit(solution)/shard_map/ppermute | solution.py:20
  15.0 4.1 %copy-start.10 = (bf16[128,2048]{1,0:T(8,128)(2,1)S(1)}, bf16[128,2048]{1,0:T(8,128)(2,1)}, u32[]{:S(2)}) copy-start(bf16[128,2048]{1,0:T(8,128)(2,1)} %param.15) | copy-start | bytes 1572868
  15.0 4.3 %copy-start.12 = (f32[4,8192]{1,0:T(4,128)S(1)}, f32[4,8192]{1,0:T(4,128)}, u32[]{:S(2)}) copy-start(f32[4,8192]{1,0:T(4,128)} %param.17) | copy-start | bytes 393220
  19.0 0.8 copy-start.14
  19.0 0.8 copy-start.11
  19.8 7.8 %copy-start.13 = (f32[2048]{0:T(1024)S(1)}, f32[2048]{0:T(1024)}, u32[]{:S(2)}) copy-start(f32[2048]{0:T(1024)} %param.20) | copy-start | bytes 24580
  19.8 11.0 %copy-start.15 = (f32[128]{0:T(128)S(1)}, f32[128]{0:T(128)}, u32[]{:S(2)}) copy-start(f32[128]{0:T(128)} %param.22) | copy-start | bytes 1540
  19.9 11.1 %copy-start.16 = (f32[128]{0:T(128)S(1)}, f32[128]{0:T(128)}, u32[]{:S(2)}) copy-start(f32[128]{0:T(128)} %param.21) | copy-start | bytes 1540
  39.2 12.1 %all-to-all-start.2 = ((bf16[4,128,2,256]{1,3,2,0:T(8,128)(2,1)}), bf16[4,128,2,256]{1,3,2,0:T(8,128)(2,1)S(1)}, u32[]{:S(2)}, u32[]{:S(2)}) async-start(bf16[4,128,2,256]{1,3,2,0:T(8,128)(2,1)} %copy.118), calls=%async_computation.2 | async-start | bytes 1048576 | tf_op jit(solution)/shard_map/all_to_all | solution.py:176
  51.3 3.7 %copy-start.8 = (bf16[4,128,2,256]{1,3,2,0:T(8,128)(2,1)}, bf16[4,128,2,256]{1,3,2,0:T(8,128)(2,1)S(1)}, u32[]{:S(2)}) copy-start(bf16[4,128,2,256]{1,3,2,0:T(8,128)(2,1)S(1)} %all-to-all-done.2) | copy-start | bytes 1572868
  51.3 28.2 %all-to-all-start.1 = ((bf16[128,4,2048]{2,0,1:T(8,128)(2,1)}), bf16[128,4,2048]{2,0,1:T(8,128)(2,1)S(1)}, u32[]{:S(2)}, u32[]{:S(2)}) async-start(bf16[128,4,2048]{2,0,1:T(8,128)(2,1)} %bitcast.166), calls=%async_computation.1 | async-start | bytes 4194304 | tf_op jit(solution)/shard_map/all_to_all | solution.py:178
  56.8 2.5 %copy-start.9 = (bf16[4,128,2,256]{1,3,2,0:T(8,128)(2,1)S(1)}, bf16[4,128,2,256]{1,3,2,0:T(8,128)(2,1)}, u32[]{:S(2)}) copy-start(bf16[4,128,2,256]{1,3,2,0:T(8,128)(2,1)} %copy-done.8) | copy-start | bytes 1572868
  58.5 37.5 %copy-start.7 = (f32[512,32]{1,0:T(8,128)}, f32[512,32]{1,0:T(8,128)S(1)}, u32[]{:S(2)}) copy-start(f32[512,32]{1,0:T(8,128)S(1)} %compare_select_fusion) | copy-start | bytes 196612
  59.4 35.2 %copy-start.4 = (bf16[512,2,256]{0,2,1:T(8,128)(2,1)}, bf16[512,2,256]{0,2,1:T(8,128)(2,1)S(1)}, u32[]{:S(2)}) copy-start(bf16[512,2,256]{0,2,1:T(8,128)(2,1)S(1)} %copy_bitcast_fusion.1) | copy-start | bytes 1572868
  79.5 11.8 %copy-start.3 = (bf16[128,4,2048]{2,0,1:T(8,128)(2,1)}, bf16[128,4,2048]{2,0,1:T(8,128)(2,1)S(1)}, u32[]{:S(2)}) copy-start(bf16[128,4,2048]{2,0,1:T(8,128)(2,1)S(1)} %all-to-all-done.1) | copy-start | bytes 6291460
  91.3 3.3 %copy-start.17 = (f32[128]{0:T(128)S(1)}, f32[128]{0:T(128)}, u32[]{:S(2)}) copy-start(f32[128]{0:T(128)} %param.23) | copy-start | bytes 1540
  94.5 4.5 %collective-permute-start.2 = (f32[264,2048]{1,0:T(8,128)}, f32[264,2048]{1,0:T(8,128)S(1)}, u32[]{:S(2)}, u32[]{:S(2)}) collective-permute-start(f32[264,2048]{1,0:T(8,128)} %select_maximum_fusion), channel_id=1, source_target_pairs={{0,4},{4,0},{8,12},{12,8},{16,20},{20,16},{24,28},{28,24},{1,5},{5... | collective-permute-start | bytes 6488072 | tf_op jit(solution)/shard_map/ppermute | solution.py:214
  99.2 1.6 copy-start.2
  101.1 2.4 %copy-start.6 = (f32[256,1024]{1,0:T(8,128)}, f32[256,1024]{1,0:T(8,128)S(1)}, u32[]{:S(2)}) copy-start(f32[256,1024]{1,0:T(8,128)S(1)} %select_add_fusion) | copy-start | bytes 3145732
  102.1 10.5 %collective-permute-start.3 = (f32[64,1024]{1,0:T(8,128)}, f32[64,1024]{1,0:T(8,128)}, u32[]{:S(2)}, u32[]{:S(2)}) collective-permute-start(f32[64,1024]{1,0:T(8,128)} %bitcast_add_fusion.10), channel_id=1, source_target_pairs={{0,8},{4,12},{1,9},{5,13},{2,10},{6,14},{3,11},{7,15}} | collective-permute-start | bytes 786440 | tf_op jit(solution)/shard_map/ppermute | solution.py:260
  115.5 13.9 %collective-permute-start.4 = (f32[64,1024]{1,0:T(8,128)}, f32[64,1024]{1,0:T(8,128)}, u32[]{:S(2)}, u32[]{:S(2)}) collective-permute-start(f32[64,1024]{1,0:T(8,128)} %bitcast_add_fusion.8), channel_id=1, source_target_pairs={{0,8},{4,12},{8,16},{12,20},{1,9},{5,13},{9,17},{13,21},{2,10},{6,... | collective-permute-start | bytes 786440 | tf_op jit(solution)/shard_map/ppermute | solution.py:260
  132.0 10.1 %collective-permute-start.5 = (f32[64,1024]{1,0:T(8,128)}, f32[64,1024]{1,0:T(8,128)}, u32[]{:S(2)}, u32[]{:S(2)}) collective-permute-start(f32[64,1024]{1,0:T(8,128)} %bitcast_add_fusion.6), channel_id=1, source_target_pairs={{0,8},{4,12},{8,16},{12,20},{16,24},{20,28},{1,9},{5,13},{9,17},{1... | collective-permute-start | bytes 786440 | tf_op jit(solution)/shard_map/ppermute | solution.py:260
  144.8 9.3 %collective-permute-start.6 = (f32[64,1024]{1,0:T(8,128)}, f32[64,1024]{1,0:T(8,128)}, u32[]{:S(2)}, u32[]{:S(2)}) collective-permute-start(f32[64,1024]{1,0:T(8,128)} %bitcast_add_fusion.4), channel_id=1, source_target_pairs={{0,8},{4,12},{8,16},{12,20},{16,24},{20,28},{1,9},{5,13},{9,17},{1... | collective-permute-start | bytes 786440 | tf_op jit(solution)/shard_map/ppermute | solution.py:260
  156.7 8.6 %collective-permute-start.7 = (f32[64,1024]{1,0:T(8,128)}, f32[64,1024]{1,0:T(8,128)}, u32[]{:S(2)}, u32[]{:S(2)}) collective-permute-start(f32[64,1024]{1,0:T(8,128)} %bitcast_add_fusion.2), channel_id=1, source_target_pairs={{8,16},{12,20},{16,24},{20,28},{9,17},{13,21},{17,25},{21,29},{10,... | collective-permute-start | bytes 786440 | tf_op jit(solution)/shard_map/ppermute | solution.py:260
  168.0 1.4 collective-permute-start.8
  170.4 26.3 %collective-permute-start.9 = (f32[256,1024]{1,0:T(8,128)S(1)}, f32[256,1024]{1,0:T(8,128)}, u32[]{:S(2)}, u32[]{:S(2)}) collective-permute-start(f32[256,1024]{1,0:T(8,128)S(1)} %bitcast.152), channel_id=1, source_target_pairs={{0,4},{4,0},{8,12},{12,8},{16,20},{20,16},{24,28},{28,24},{1,5},{5... | collective-permute-start | bytes 3145736 | tf_op jit(solution)/shard_map/ppermute | solution.py:268
  196.6 1.6 copy-start.5
  198.2 2.2 copy-start
  198.2 3.5 %copy-start.1 = (f32[512,2048]{1,0:T(8,128)S(1)}, f32[512,2048]{1,0:T(8,128)}, u32[]{:S(2)}) copy-start(f32[512,2048]{1,0:T(8,128)} %get-tuple-element.137) | copy-start | bytes 12582916

commit v8 on v6

--- a/solution.py
+++ b/solution.py
@@ -96,22 +96,11 @@
     )(x, scores, cum_lanes, cum_rows, dt_rows, skip_cols[None, :])
 
 
-def fresh_kernel(x_ref, bt_ref, cum_ref, dtl_ref, o_ref):
-    lane_head = lax.broadcasted_iota(jnp.int32, cum_ref.shape, 1)
-    lane = lax.broadcasted_iota(jnp.int32, (BLOCK, 128), 1)
-
+def fresh_kernel(x_ref, bt_ref, fac_ref, o_ref):
     def pair(p, carry):
         off = pl.multiple_of(p * 128, 128)
         xp = x_ref[:, pl.ds(off, 128)].astype(jnp.float32)
-        cum_all = cum_ref[...]
-        dt_all = dtl_ref[...]
-        factors = []
-        for k in range(2):
-            h = 2 * p + k
-            c = jnp.sum(jnp.where(lane_head == h, cum_all, 0.0), axis=1, keepdims=True)
-            d = jnp.sum(jnp.where(lane_head == h, dt_all, 0.0), axis=1, keepdims=True)
-            factors.append(jnp.exp(c[BLOCK - 1 : BLOCK] - c) * d)
-        wx = (jnp.where(lane < P_SIZE, factors[0], factors[1]) * xp).astype(jnp.bfloat16)
+        wx = (fac_ref[:, pl.ds(off, 128)] * xp).astype(jnp.bfloat16)
         o_ref[:, pl.ds(off, 128)] = jnp.dot(bt_ref[...], wx, preferred_element_type=jnp.float32)
         return carry
 
@@ -121,21 +110,20 @@
 def fresh_block(x, b, cum, dt):
     heads = cum.shape[1]
     width = x.shape[1]
-    cum_lanes = jnp.pad(cum, ((0, 0), (0, 128 - heads)))
-    dt_lanes = jnp.pad(dt, ((0, 0), (0, 128 - heads)))
+    factors = head_columns(jnp.exp(cum[BLOCK - 1 :] - cum) * dt)
     vmem = pl.BlockSpec(memory_space=pltpu.VMEM)
     return pl.pallas_call(
         fresh_kernel,
         out_shape=jax.ShapeDtypeStruct((N, width), jnp.float32),
-        in_specs=[vmem] * 4,
+        in_specs=[vmem] * 3,
         out_specs=vmem,
         name="ssd_fresh",
         cost_estimate=pl.CostEstimate(
             flops=2 * BLOCK * N * width,
-            transcendentals=heads * BLOCK,
-            bytes_accessed=BLOCK * width * 2 + N * width * 4 + BLOCK * N * 2,
+            transcendentals=0,
+            bytes_accessed=BLOCK * width * 6 + N * width * 4 + BLOCK * N * 2,
         ),
-    )(x, b.T, cum_lanes, dt_lanes)
+    )(x, b.T, factors)
 
 
 def head_columns(head_major):
@@ -231,24 +219,35 @@
     pieces = 4 if N % 32 == 0 else 1
     piece_rows = N // pieces
     acc = [jnp.zeros((piece_rows, half_width), jnp.float32) for _ in range(pieces)]
+    skip_cols = head_columns(skip_local)
+    scores = [
+        jnp.einsum("in,jn->ij", seg_c[b], seg_b[b], preferred_element_type=jnp.float32)
+        for b in range(blocks)
+    ]
+
+    def intra_after(tie):
+        parts = []
+        for b in range(blocks):
+            operands = (x_blk[b], scores[b], cum[b], dt_blk[b])
+            if tie is not None:
+                operands = lax.optimization_barrier(operands + (tie,))[:4]
+            parts.append(intra_block(*operands, skip_cols))
+        return parts
+
+    partials = None
     last_send = None
     for r in range(chips - 1):
+        if r == chips - 2 and r >= 1:
+            partials = intra_after(last_send)
+            acc = list(lax.optimization_barrier((tuple(acc), partials))[0])
         pairs = [(2 * r + q, 2 * r + 2 + q) for q in range(2)]
         for k in range(pieces):
             send = chip_decay * acc[k] + chip_half[k * piece_rows : (k + 1) * piece_rows]
             acc[k] = acc[k] + lax.ppermute(send, "ctx", pairs)
             last_send = send
-    skip_cols = head_columns(skip_local)
-    partials = []
-    for b in range(blocks):
-        scores = jnp.einsum("in,jn->ij", seg_c[b], seg_b[b], preferred_element_type=jnp.float32)
-        operands = (x_blk[b], scores, cum[b], dt_blk[b])
-        if last_send is not None:
-            operands = lax.optimization_barrier(operands + (last_send,))[:4]
-        partials.append(intra_block(*operands, skip_cols))
-
+    if partials is None:
+        partials = intra_after(last_send)
     prefix_half = jnp.concatenate(acc, axis=0) if pieces > 1 else acc[0]
-    prefix_half = lax.optimization_barrier((prefix_half, partials))[0]
     mate_prefix = lax.ppermute(prefix_half, "ctx", [(i, i ^ 1) for i in range(n_ctx)])
     chip_prefix = jnp.concatenate(
         [jnp.where(core == 0, prefix_half, mate_prefix), jnp.where(core == 0, mate_prefix, prefix_half)],

time: 223 us -> 222 us (level)
  local copies, waits for them, and re-layouts: 35.6 us -> 41.5 us
  Pallas kernels: 25 us -> 21.8 us
  waiting for transfers between devices: 61.8 us -> 59 us
    all_to_all x1, waiting for transfers between devices: 19.9 us -> 13 us  [on_device(): lax.all_to_all(x_part, 'tp', split_axis=1, concat_axis=0, tiled=True)]
    reshape x1 -> x2, local copies, waits for them, and re-layouts: 5.43 us -> 10.9 us  [head_columns(): return jnp.repeat(head_major, P_SIZE, axis=-1)]
    ppermute x12, waiting for transfers between devices: 33.7 us -> 37.1 us  [on_device(): acc[k] = acc[k] + lax.ppermute(send, 'ctx', pairs)]
    pallas_call x1, Pallas kernels: 11.9 us -> 8.71 us  [fresh_block(): pl.pallas_call(fresh_kernel, out_shape=jax.ShapeDtypeStruct((N, width), j...]
    broadcast_in_dim x5 -> x6, local copies, waits for them, and re-layouts: 3.46 us -> 5.98 us  [head_columns(): return jnp.repeat(head_major, P_SIZE, axis=-1)]
    add x4 -> x3, other arithmetic: 4.74 us -> 3.43 us  [on_device(): send = chip_decay * acc[k] + chip_half[k * piece_rows:(k + 1) * piece_rows]]
    unnamed x53 -> x37, local copies, waits for them, and re-layouts: 10.1 us -> 9.74 us
  transfers between devices with their start and end apart: 19 -> 19, of which waited for: 7 -> 11; matrix products, arithmetic and copies ran while one was open for 22% -> 24% of each run, Pallas kernels for 6% -> 6%
where the time goes in v8:
time: 222 us; the launch traced here: 220 us
  waiting for transfers between devices  59 us (27%)
  local copies, waits for them, and re-layouts  41.5 us (19%)
  starting transfers between devices  33.4 us (15%)
  other arithmetic  31.2 us (14%)
  blocking collectives  28.8 us (13%)
  Pallas kernels  21.8 us (10%)
  matrix products  3.45 us (2%)
    ppermute x12, waiting for transfers between devices, on_device(): acc[k] = acc[k] + lax.ppermute(send, 'ctx', pairs)  37.1 us
    all_to_all x1, blocking collectives, on_device(): return lax.all_to_all(result, 'tp', split_axis=0, concat_axis=1, tiled=True)  28.8 us
    ppermute x12, starting transfers between devices, on_device(): acc[k] = acc[k] + lax.ppermute(send, 'ctx', pairs)  15.3 us
    pallas_call x1, Pallas kernels, intra_block(): pl.pallas_call(intra_kernel, out_shape=jax.ShapeDtypeStruct((BLOCK, width...  13.1 us
    all_to_all x1, waiting for transfers between devices, on_device(): lax.all_to_all(x_part, 'tp', split_axis=1, concat_axis=0, tiled=True)  13 us
    reshape x2, local copies, waits for them, and re-layouts, head_columns(): return jnp.repeat(head_major, P_SIZE, axis=-1)  10.9 us
    convert_element_type x4, other arithmetic, conv_rows(): return jax.nn.silu(total).astype(jnp.bfloat16)  10.5 us
    unnamed x37, local copies, waits for them, and re-layouts  9.74 us
  transfers between devices with their start and end apart: 19, of which 11 were waited for; matrix products, arithmetic and copies ran while one was open for 24% of the time, Pallas kernels for 6%

profile of v8, /device:TPU:16, one launch (start us, length us, event | category | flops | bytes accessed | tf_op | source)
XLA Modules:
  0.0 219.6 jit_solution(7056809827805778375)
XLA Ops:
  1.5 3.7 %all-to-all-start.2 = ((bf16[128,4,32]{0,2,1:T(8,128)(2,1)}), bf16[128,4,32]{0,2,1:T(8,128)(2,1)S(1)}, u32[]{:S(2)}, u32[]{:S(2)}) async-start(bf16[128,4,32]{0,2,1:T(8,128)(2,1)} %bitcast.14), calls=%async_computation.2 | async-start | bytes 65536 | tf_op jit(solution)/shard_map/all_to_all | solution.py:167
  6.0 3.9 %collective-permute-start.1 = (bf16[3,2048]{1,0:T(4,128)(2,1)S(1)}, bf16[3,2048]{1,0:T(4,128)(2,1)S(1)}, u32[]{:S(2)}, u32[]{:S(2)}) collective-permute-start(bf16[3,2048]{1,0:T(4,128)(2,1)S(1)} %get-tuple-element.45), channel_id=1, source_target_pairs={{0,1},{1,2},{2,3},{3,4},{4,5},{5,6},{6,7},{7,8},{8,9},{9,10},{10,1... | collective-permute-start | bytes 36872 | tf_op jit(solution)/shard_map/ppermute | solution.py:20
  9.9 1.7 fusion.36
  11.6 3.4 %collective-permute-start = (bf16[3,8192]{1,0:T(4,128)(2,1)}, bf16[3,8192]{1,0:T(4,128)(2,1)S(1)}, u32[]{:S(2)}, u32[]{:S(2)}) collective-permute-start(bf16[3,8192]{1,0:T(4,128)(2,1)} %get-tuple-element.31), channel_id=1, source_target_pairs={{0,1},{1,2},{2,3},{3,4},{4,5},{5,6},{6,7},{7,8},{8,9},{9,10},{10,1... | collective-permute-start | bytes 147464 | tf_op jit(solution)/shard_map/ppermute | solution.py:20
  16.3 4.0 %convert_element_type.59 = f32[128,8192]{1,0:T(8,128)} convert(bf16[128,8192]{1,0:T(8,128)(2,1)} %param.10) | non-fusion elementwise | flops 1048576 | bytes 6291456 | tf_op jit(solution)/shard_map/convert_element_type | solution.py:34
  20.6 2.6 %multiply_convert_fusion.1 = bf16[128,2048]{0,1:T(8,128)(2,1)S(1)} fusion(f32[128,2048]{0,1:T(8,128)S(1)} %convert_element_type.63, f32[2048]{0:T(1024)S(1)} %bitcast.106, f32[2048]{0:T(1024)S(1)} %bitcast.108, f32[2048]{0:T(1024)S(1)} %bitcast.104, f32[2048]{0:T(1024)S(1)} %bitcast.102, f32[2048]{0:T(1024)S(1)} %copy-done.12), kind=kLoop, calls=%fused_computation.26 | loop fusion | flops 3407872 | bytes 1613824 | tf_op jit(solution)/shard_map/convert_element_type | solution.py:27
  23.2 7.7 %multiply_convert_fusion = bf16[128,8192]{1,0:T(8,128)(2,1)S(1)} fusion(f32[128,8192]{1,0:T(8,128)} %convert_element_type.59, f32[8192]{0:T(1024)S(1)} %bitcast.98, f32[8192]{0:T(1024)S(1)} %bitcast.100, f32[8192]{0:T(1024)S(1)} %bitcast.96, f32[8192]{0:T(1024)S(1)} %bitcast.94, f32[8192]{0:T(1024)S(1)} %copy-done.10), kind=kLoop, calls=%fused_computation.1 | loop fusion | flops 13631488 | bytes 6455296 | tf_op jit(solution)/shard_map/convert_element_type | solution.py:27
  31.5 2.0 dynamic_update_slice.7
  34.3 3.5 %all-to-all-start.1 = ((bf16[4,128,2,256]{1,3,2,0:T(8,128)(2,1)}), bf16[4,128,2,256]{1,3,2,0:T(8,128)(2,1)S(1)}, u32[]{:S(2)}, u32[]{:S(2)}) async-start(bf16[4,128,2,256]{1,3,2,0:T(8,128)(2,1)} %copy.89), calls=%async_computation.1 | async-start | bytes 1048576 | tf_op jit(solution)/shard_map/all_to_all | solution.py:164
  41.9 4.4 %all-to-all-done.1 = bf16[4,128,2,256]{1,3,2,0:T(8,128)(2,1)S(1)} async-done(((bf16[4,128,2,256]{1,3,2,0:T(8,128)(2,1)}), bf16[4,128,2,256]{1,3,2,0:T(8,128)(2,1)S(1)}, u32[]{:S(2)}, u32[]{:S(2)}) %all-to-all-start.1) | async-done | bytes 524320 | tf_op jit(solution)/shard_map/all_to_all | solution.py:164
  46.3 3.6 %all-to-all-start = ((bf16[128,4,2048]{2,0,1:T(8,128)(2,1)}), bf16[128,4,2048]{2,0,1:T(8,128)(2,1)S(1)}, u32[]{:S(2)}, u32[]{:S(2)}) async-start(bf16[128,4,2048]{2,0,1:T(8,128)(2,1)} %bitcast.88), calls=%async_computation | async-start | bytes 4194304 | tf_op jit(solution)/shard_map/all_to_all | solution.py:166
  52.0 2.6 %broadcast_in_dim.12 = f32[512,32,64]{0,2,1:T(8,128)} broadcast(f32[512,32]{0,1:T(8,128)S(1)} %get-tuple-element.25), dimensions={0,1} | broadcast | bytes 4259840 | tf_op jit(solution)/shard_map/broadcast_in_dim | solution.py:130
  54.5 5.5 %copy.97.fac_ref = f32[512,2048]{1,0:T(8,128)} copy(f32[512,2048]{0,1:T(8,128)} %bitcast.84) | data formatting | bytes 8388608 | tf_op jit(solution)/shard_map/reshape | solution.py:130
  61.6 13.0 %all-to-all-done = bf16[128,4,2048]{2,0,1:T(8,128)(2,1)S(1)} async-done(((bf16[128,4,2048]{2,0,1:T(8,128)(2,1)}), bf16[128,4,2048]{2,0,1:T(8,128)(2,1)S(1)}, u32[]{:S(2)}, u32[]{:S(2)}) %all-to-all-start) | async-done | bytes 2097184 | tf_op jit(solution)/shard_map/all_to_all | solution.py:166
  75.8 8.7 %ssd_fresh.1 = f32[256,2048]{1,0:T(8,128)} custom-call(bf16[512,2048]{1,0:T(8,128)(2,1)} %bitcast.90, bf16[256,512]{1,0:T(8,128)(2,1)} %slice_bitcast_fusion.1.bt_ref, f32[512,2048]{1,0:T(8,128)} %copy.97.fac_ref), custom_call_target="tpu_custom_call" | custom-call | flops 536870912 | bytes 8650752 | tf_op jit(solution)/shard_map/ssd_fresh/pallas_call | solution.py:115
  84.6 3.2 %select_maximum_fusion = f32[264,2048]{1,0:T(8,128)} fusion(f32[1,32]{1,0:T(1,128)S(1)} %bitcast.112, f32[256,2048]{1,0:T(8,128)} %ssd_fresh.1), kind=kLoop, calls=%fused_computation.10 | loop fusion | flops 1622016 | bytes 4259968 | tf_op jit(solution)/shard_map/concatenate | solution.py:203
  87.8 4.5 %collective-permute-done.2 = f32[264,2048]{1,0:T(8,128)S(1)} collective-permute-done((f32[264,2048]{1,0:T(8,128)}, f32[264,2048]{1,0:T(8,128)S(1)}, u32[]{:S(2)}, u32[]{:S(2)}) %collective-permute-start.2) | collective-permute-done | bytes 2162720 | tf_op jit(solution)/shard_map/ppermute | solution.py:202
  102.4 2.2 %multiply_add_fusion.4 = (f32[64,1024]{1,0:T(8,128)}, f32[64,1024]{1,0:T(8,128)}, f32[64,1024]{1,0:T(8,128)}, f32[64,1024]{1,0:T(8,128)}) fusion(f32[64,1024]{1,0:T(8,128)} %collective-permute-done.8, f32[256,1024]{1,0:T(8,128)S(1)} %select_add_fusion, f32[1024]{0:T(1024)S(1)} %mul.339, f32[64,1024]{1,0:T(8,128)} %collective-permute-done.3, ...), kind=kLoop, calls=%fused_computation.37 | loop fusion | flops 524288 | bytes 3149824 | tf_op jit(solution)/shard_map/add | solution.py:245
  112.0 1.7 pad.11.clone.cum_ref
  113.7 13.1 %ssd_intra.1 = f32[512,2048]{1,0:T(8,128)} custom-call(bf16[512,2048]{1,0:T(8,128)(2,1)} %bitcast.91, f32[512,512]{1,0:T(8,128)} %fusion.12.s_ref, f32[512,128]{1,0:T(8,128)} %pad.11.clone.cum_ref, f32[32,512]{1,0:T(8,128)} %bitcast.93, f32[32,512]{1,0:T(8,128)} %bitcast.110, f32[1,2048]{1,0:T(1,128)} %broadcast_in_dim_reshape.2.skip_ref), custom_call_target="tpu_custom_call" | custom-call | flops 2147483648 | bytes 7340032 | tf_op jit(solution)/shard_map/ssd_intra/pallas_call | solution.py:85
  126.8 7.5 %collective-permute-done.9 = f32[64,1024]{1,0:T(8,128)} collective-permute-done((f32[64,1024]{1,0:T(8,128)}, f32[64,1024]{1,0:T(8,128)}, u32[]{:S(2)}, u32[]{:S(2)}) %collective-permute-start.9) | collective-permute-done | bytes 262176 | tf_op jit(solution)/shard_map/ppermute | solution.py:246
  135.4 4.6 %collective-permute-done.5 = f32[64,1024]{1,0:T(8,128)} collective-permute-done((f32[64,1024]{1,0:T(8,128)}, f32[64,1024]{1,0:T(8,128)}, u32[]{:S(2)}, u32[]{:S(2)}) %collective-permute-start.5) | collective-permute-done | bytes 262176 | tf_op jit(solution)/shard_map/ppermute | solution.py:246
  141.0 4.6 %collective-permute-done.7 = f32[64,1024]{1,0:T(8,128)} collective-permute-done((f32[64,1024]{1,0:T(8,128)}, f32[64,1024]{1,0:T(8,128)}, u32[]{:S(2)}, u32[]{:S(2)}) %collective-permute-start.7) | collective-permute-done | bytes 262176 | tf_op jit(solution)/shard_map/ppermute | solution.py:246
  146.5 3.2 %collective-permute-done.10 = f32[64,1024]{1,0:T(8,128)} collective-permute-done((f32[64,1024]{1,0:T(8,128)}, f32[64,1024]{1,0:T(8,128)}, u32[]{:S(2)}, u32[]{:S(2)}) %collective-permute-start.10) | collective-permute-done | bytes 262176 | tf_op jit(solution)/shard_map/ppermute | solution.py:246
  156.5 2.6 %collective-permute-done.11 = f32[64,1024]{1,0:T(8,128)S(1)} collective-permute-done((f32[64,1024]{1,0:T(8,128)S(1)}, f32[64,1024]{1,0:T(8,128)S(1)}, u32[]{:S(2)}, u32[]{:S(2)}) %collective-permute-start.11) | collective-permute-done | bytes 262176 | tf_op jit(solution)/shard_map/ppermute | solution.py:246
  159.1 5.6 %collective-permute-done.14 = f32[64,1024]{1,0:T(8,128)S(1)} collective-permute-done((f32[64,1024]{1,0:T(8,128)S(1)}, f32[64,1024]{1,0:T(8,128)S(1)}, u32[]{:S(2)}, u32[]{:S(2)}) %collective-permute-start.14) | collective-permute-done | bytes 262176 | tf_op jit(solution)/shard_map/ppermute | solution.py:246
  164.8 5.6 %collective-permute-done.12 = f32[64,1024]{1,0:T(8,128)S(1)} collective-permute-done((f32[64,1024]{1,0:T(8,128)S(1)}, f32[64,1024]{1,0:T(8,128)S(1)}, u32[]{:S(2)}, u32[]{:S(2)}) %collective-permute-start.12) | collective-permute-done | bytes 262176 | tf_op jit(solution)/shard_map/ppermute | solution.py:246
  170.4 3.5 %collective-permute-done.13 = f32[64,1024]{1,0:T(8,128)S(1)} collective-permute-done((f32[64,1024]{1,0:T(8,128)S(1)}, f32[64,1024]{1,0:T(8,128)S(1)}, u32[]{:S(2)}, u32[]{:S(2)}) %collective-permute-start.13) | collective-permute-done | bytes 262176 | tf_op jit(solution)/shard_map/ppermute | solution.py:246
  175.0 2.5 %broadcast_in_dim.30 = f32[512,32,64]{0,2,1:T(8,128)} broadcast(f32[512,32]{0,1:T(8,128)S(1)} %copy-done.9), dimensions={0,1} | broadcast | bytes 4259840 | tf_op jit(solution)/shard_map/broadcast_in_dim | solution.py:130
  177.5 5.4 %copy.99 = f32[512,2048]{1,0:T(8,128)} copy(f32[512,2048]{0,1:T(8,128)} %bitcast.85) | data formatting | bytes 8388608 | tf_op jit(solution)/shard_map/reshape | solution.py:130
  183.1 1.5 broadcast_select_fusion
  189.4 28.8 %all_to_all.56 = bf16[4,128,2048]{2,1,0:T(8,128)(2,1)S(1)} all-to-all(bf16[4,128,2048]{2,1,0:T(8,128)(2,1)S(1)} %bitcast.87), channel_id=1, replica_groups=mesh['ctx'=8,'tp'=4] {'tp'}, dimensions={0} | all-to-all | bytes 4194304 | tf_op jit(solution)/shard_map/all_to_all | solution.py:273
  (123 shorter events, 48.9 us)
Async XLA Ops:
  1.5 32.8 %all-to-all-start.2 = ((bf16[128,4,32]{0,2,1:T(8,128)(2,1)}), bf16[128,4,32]{0,2,1:T(8,128)(2,1)S(1)}, u32[]{:S(2)}, u32[]{:S(2)}) async-start(bf16[128,4,32]{0,2,1:T(8,128)(2,1)} %bitcast.14), calls=%async_computation.2 | async-start | bytes 65536 | tf_op jit(solution)/shard_map/all_to_all | solution.py:167
  6.0 25.1 %collective-permute-start.1 = (bf16[3,2048]{1,0:T(4,128)(2,1)S(1)}, bf16[3,2048]{1,0:T(4,128)(2,1)S(1)}, u32[]{:S(2)}, u32[]{:S(2)}) collective-permute-start(bf16[3,2048]{1,0:T(4,128)(2,1)S(1)} %get-tuple-element.45), channel_id=1, source_target_pairs={{0,1},{1,2},{2,3},{3,4},{4,5},{5,6},{6,7},{7,8},{8,9},{9,10},{10,1... | collective-permute-start | bytes 36872 | tf_op jit(solution)/shard_map/ppermute | solution.py:20
  11.6 27.6 %collective-permute-start = (bf16[3,8192]{1,0:T(4,128)(2,1)}, bf16[3,8192]{1,0:T(4,128)(2,1)S(1)}, u32[]{:S(2)}, u32[]{:S(2)}) collective-permute-start(bf16[3,8192]{1,0:T(4,128)(2,1)} %get-tuple-element.31), channel_id=1, source_target_pairs={{0,1},{1,2},{2,3},{3,4},{4,5},{5,6},{6,7},{7,8},{8,9},{9,10},{10,1... | collective-permute-start | bytes 147464 | tf_op jit(solution)/shard_map/ppermute | solution.py:20
  16.3 4.1 %copy-start.13 = (f32[4,2048]{1,0:T(4,128)S(1)}, f32[4,2048]{1,0:T(4,128)}, u32[]{:S(2)}) copy-start(f32[4,2048]{1,0:T(4,128)} %param.15) | copy-start | bytes 98308
  16.3 4.1 %copy-start.11 = (f32[4,8192]{1,0:T(4,128)S(1)}, f32[4,8192]{1,0:T(4,128)}, u32[]{:S(2)}) copy-start(f32[4,8192]{1,0:T(4,128)} %param.13) | copy-start | bytes 393220
  16.3 4.3 %copy-start.12 = (f32[2048]{0:T(1024)S(1)}, f32[2048]{0:T(1024)}, u32[]{:S(2)}) copy-start(f32[2048]{0:T(1024)} %param.16) | copy-start | bytes 24580
  20.3 2.9 %copy-start.10 = (f32[8192]{0:T(1024)S(1)}, f32[8192]{0:T(1024)}, u32[]{:S(2)}) copy-start(f32[8192]{0:T(1024)} %param.14) | copy-start | bytes 98308
  23.2 7.7 %copy-start.14 = (f32[128]{0:T(128)S(1)}, f32[128]{0:T(128)}, u32[]{:S(2)}) copy-start(f32[128]{0:T(128)} %param.18) | copy-start | bytes 1540
  23.2 7.8 %copy-start.15 = (f32[128]{0:T(128)S(1)}, f32[128]{0:T(128)}, u32[]{:S(2)}) copy-start(f32[128]{0:T(128)} %param.17) | copy-start | bytes 1540
  34.3 12.0 %all-to-all-start.1 = ((bf16[4,128,2,256]{1,3,2,0:T(8,128)(2,1)}), bf16[4,128,2,256]{1,3,2,0:T(8,128)(2,1)S(1)}, u32[]{:S(2)}, u32[]{:S(2)}) async-start(bf16[4,128,2,256]{1,3,2,0:T(8,128)(2,1)} %copy.89), calls=%async_computation.1 | async-start | bytes 1048576 | tf_op jit(solution)/shard_map/all_to_all | solution.py:164
  46.3 28.2 %all-to-all-start = ((bf16[128,4,2048]{2,0,1:T(8,128)(2,1)}), bf16[128,4,2048]{2,0,1:T(8,128)(2,1)S(1)}, u32[]{:S(2)}, u32[]{:S(2)}) async-start(bf16[128,4,2048]{2,0,1:T(8,128)(2,1)} %bitcast.88), calls=%async_computation | async-start | bytes 4194304 | tf_op jit(solution)/shard_map/all_to_all | solution.py:166
  51.2 60.0 %copy-start.8 = (f32[512,32]{0,1:T(8,128)}, f32[512,32]{0,1:T(8,128)S(1)}, u32[]{:S(2)}) copy-start(f32[512,32]{0,1:T(8,128)S(1)} %get-tuple-element.15) | copy-start | bytes 196612
  87.8 4.5 %collective-permute-start.2 = (f32[264,2048]{1,0:T(8,128)}, f32[264,2048]{1,0:T(8,128)S(1)}, u32[]{:S(2)}, u32[]{:S(2)}) collective-permute-start(f32[264,2048]{1,0:T(8,128)} %select_maximum_fusion), channel_id=1, source_target_pairs={{0,4},{4,0},{8,12},{12,8},{16,20},{20,16},{24,28},{28,24},{1,5},{5... | collective-permute-start | bytes 6488072 | tf_op jit(solution)/shard_map/ppermute | solution.py:202
  94.3 6.0 %copy-start.16 = (f32[128]{0:T(128)S(1)}, f32[128]{0:T(128)}, u32[]{:S(2)}) copy-start(f32[128]{0:T(128)} %param.19) | copy-start | bytes 1540
  95.5 6.9 %collective-permute-start.8 = (f32[64,1024]{1,0:T(8,128)}, f32[64,1024]{1,0:T(8,128)}, u32[]{:S(2)}, u32[]{:S(2)}) collective-permute-start(f32[64,1024]{1,0:T(8,128)} %get-tuple-element.41), channel_id=1, source_target_pairs={{0,8},{4,12},{1,9},{5,13},{2,10},{6,14},{3,11},{7,15}} | collective-permute-start | bytes 786440 | tf_op jit(solution)/shard_map/ppermute | solution.py:246
  96.9 5.5 %collective-permute-start.6 = (f32[64,1024]{1,0:T(8,128)}, f32[64,1024]{1,0:T(8,128)S(1)}, u32[]{:S(2)}, u32[]{:S(2)}) collective-permute-start(f32[64,1024]{1,0:T(8,128)} %get-tuple-element.42), channel_id=1, source_target_pairs={{0,8},{4,12},{1,9},{5,13},{2,10},{6,14},{3,11},{7,15}} | collective-permute-start | bytes 786440 | tf_op jit(solution)/shard_map/ppermute | solution.py:246
  97.6 4.9 %collective-permute-start.4 = (f32[64,1024]{1,0:T(8,128)}, f32[64,1024]{1,0:T(8,128)}, u32[]{:S(2)}, u32[]{:S(2)}) collective-permute-start(f32[64,1024]{1,0:T(8,128)} %get-tuple-element.43), channel_id=1, source_target_pairs={{0,8},{4,12},{1,9},{5,13},{2,10},{6,14},{3,11},{7,15}} | collective-permute-start | bytes 786440 | tf_op jit(solution)/shard_map/ppermute | solution.py:246
  98.9 3.5 %collective-permute-start.3 = (f32[64,1024]{1,0:T(8,128)}, f32[64,1024]{1,0:T(8,128)}, u32[]{:S(2)}, u32[]{:S(2)}) collective-permute-start(f32[64,1024]{1,0:T(8,128)} %get-tuple-element.44), channel_id=1, source_target_pairs={{0,8},{4,12},{1,9},{5,13},{2,10},{6,14},{3,11},{7,15}} | collective-permute-start | bytes 786440 | tf_op jit(solution)/shard_map/ppermute | solution.py:246
  102.4 7.4 %copy-start.4 = (bf16[512,2,256]{0,2,1:T(8,128)(2,1)S(1)}, bf16[512,2,256]{0,2,1:T(8,128)(2,1)}, u32[]{:S(2)}) copy-start(bf16[512,2,256]{0,2,1:T(8,128)(2,1)} %copy-done.3) | copy-start | bytes 1572868
  104.6 29.7 %collective-permute-start.9 = (f32[64,1024]{1,0:T(8,128)}, f32[64,1024]{1,0:T(8,128)}, u32[]{:S(2)}, u32[]{:S(2)}) collective-permute-start(f32[64,1024]{1,0:T(8,128)} %get-tuple-element.37), channel_id=1, source_target_pairs={{8,16},{12,20},{9,17},{13,21},{10,18},{14,22},{11,19},{15,23}} | collective-permute-start | bytes 786440 | tf_op jit(solution)/shard_map/ppermute | solution.py:246
  105.9 34.0 %collective-permute-start.5 = (f32[64,1024]{1,0:T(8,128)}, f32[64,1024]{1,0:T(8,128)}, u32[]{:S(2)}, u32[]{:S(2)}) collective-permute-start(f32[64,1024]{1,0:T(8,128)} %get-tuple-element.39), channel_id=1, source_target_pairs={{8,16},{12,20},{9,17},{13,21},{10,18},{14,22},{11,19},{15,23}} | collective-permute-start | bytes 786440 | tf_op jit(solution)/shard_map/ppermute | solution.py:246
  107.2 38.3 %collective-permute-start.7 = (f32[64,1024]{1,0:T(8,128)}, f32[64,1024]{1,0:T(8,128)}, u32[]{:S(2)}, u32[]{:S(2)}) collective-permute-start(f32[64,1024]{1,0:T(8,128)} %get-tuple-element.40), channel_id=1, source_target_pairs={{8,16},{12,20},{9,17},{13,21},{10,18},{14,22},{11,19},{15,23}} | collective-permute-start | bytes 786440 | tf_op jit(solution)/shard_map/ppermute | solution.py:246
  108.5 41.2 %collective-permute-start.10 = (f32[64,1024]{1,0:T(8,128)}, f32[64,1024]{1,0:T(8,128)}, u32[]{:S(2)}, u32[]{:S(2)}) collective-permute-start(f32[64,1024]{1,0:T(8,128)} %get-tuple-element.38), channel_id=1, source_target_pairs={{8,16},{12,20},{9,17},{13,21},{10,18},{14,22},{11,19},{15,23}} | collective-permute-start | bytes 786440 | tf_op jit(solution)/shard_map/ppermute | solution.py:246
  151.1 8.0 %collective-permute-start.11 = (f32[64,1024]{1,0:T(8,128)S(1)}, f32[64,1024]{1,0:T(8,128)S(1)}, u32[]{:S(2)}, u32[]{:S(2)}) collective-permute-start(f32[64,1024]{1,0:T(8,128)S(1)} %get-tuple-element.33), channel_id=1, source_target_pairs={{16,24},{20,28},{17,25},{21,29},{18,26},{22,30},{19,27},{23,31}} | collective-permute-start | bytes 786440 | tf_op jit(solution)/shard_map/ppermute | solution.py:246
  152.4 12.3 %collective-permute-start.14 = (f32[64,1024]{1,0:T(8,128)S(1)}, f32[64,1024]{1,0:T(8,128)S(1)}, u32[]{:S(2)}, u32[]{:S(2)}) collective-permute-start(f32[64,1024]{1,0:T(8,128)S(1)} %get-tuple-element.34), channel_id=1, source_target_pairs={{16,24},{20,28},{17,25},{21,29},{18,26},{22,30},{19,27},{23,31}} | collective-permute-start | bytes 786440 | tf_op jit(solution)/shard_map/ppermute | solution.py:246
  153.7 16.6 %collective-permute-start.12 = (f32[64,1024]{1,0:T(8,128)S(1)}, f32[64,1024]{1,0:T(8,128)S(1)}, u32[]{:S(2)}, u32[]{:S(2)}) collective-permute-start(f32[64,1024]{1,0:T(8,128)S(1)} %get-tuple-element.35), channel_id=1, source_target_pairs={{16,24},{20,28},{17,25},{21,29},{18,26},{22,30},{19,27},{23,31}} | collective-permute-start | bytes 786440 | tf_op jit(solution)/shard_map/ppermute | solution.py:246
  155.0 18.9 %collective-permute-start.13 = (f32[64,1024]{1,0:T(8,128)S(1)}, f32[64,1024]{1,0:T(8,128)S(1)}, u32[]{:S(2)}, u32[]{:S(2)}) collective-permute-start(f32[64,1024]{1,0:T(8,128)S(1)} %get-tuple-element.36), channel_id=1, source_target_pairs={{16,24},{20,28},{17,25},{21,29},{18,26},{22,30},{19,27},{23,31}} | collective-permute-start | bytes 786440 | tf_op jit(solution)/shard_map/ppermute | solution.py:246
  159.1 15.9 %copy-start.9 = (f32[512,32]{0,1:T(8,128)S(1)}, f32[512,32]{0,1:T(8,128)}, u32[]{:S(2)}) copy-start(f32[512,32]{0,1:T(8,128)} %get-tuple-element.23) | copy-start | bytes 196612
  173.9 3.6 %copy-start.7 = (f32[64,1024]{1,0:T(8,128)}, f32[64,1024]{1,0:T(8,128)S(1)}, u32[]{:S(2)}) copy-start(f32[64,1024]{1,0:T(8,128)S(1)} %add.265) | copy-start | bytes 786436
  175.0 8.1 %collective-permute-start.15 = (f32[256,1024]{1,0:T(8,128)}, f32[256,1024]{1,0:T(8,128)}, u32[]{:S(2)}, u32[]{:S(2)}) collective-permute-start(f32[256,1024]{1,0:T(8,128)} %pad_maximum_fusion.1), channel_id=1, source_target_pairs={{0,4},{4,0},{8,12},{12,8},{16,20},{20,16},{24,28},{28,24},{1,5},{5... | collective-permute-start | bytes 3145736 | tf_op jit(solution)/shard_map/ppermute | solution.py:251
  184.6 2.2 copy-start
  184.6 3.5 %copy-start.6 = (f32[512,2048]{1,0:T(8,128)S(1)}, f32[512,2048]{1,0:T(8,128)}, u32[]{:S(2)}) copy-start(f32[512,2048]{1,0:T(8,128)} %ssd_intra.1) | copy-start | bytes 12582916
  (4 other events, 5.4 us)

commit v9 on v8

--- a/solution.py
+++ b/solution.py
@@ -226,27 +226,28 @@
     ]
 
     def intra_after(tie):
-        parts = []
+        parts, reach = [], []
         for b in range(blocks):
-            operands = (x_blk[b], scores[b], cum[b], dt_blk[b])
+            operands = (x_blk[b], scores[b], cum[b], dt_blk[b], head_columns(jnp.exp(cum[b])))
             if tie is not None:
-                operands = lax.optimization_barrier(operands + (tie,))[:4]
-            parts.append(intra_block(*operands, skip_cols))
-        return parts
+                operands = lax.optimization_barrier(operands + (tie,))[:5]
+            parts.append(intra_block(*operands[:4], skip_cols))
+            reach.append(operands[4])
+        return parts, reach
 
     partials = None
     last_send = None
     for r in range(chips - 1):
         if r == chips - 2 and r >= 1:
-            partials = intra_after(last_send)
-            acc = list(lax.optimization_barrier((tuple(acc), partials))[0])
+            partials, reach = intra_after(last_send)
+            acc = list(lax.optimization_barrier((tuple(acc), partials, reach))[0])
         pairs = [(2 * r + q, 2 * r + 2 + q) for q in range(2)]
         for k in range(pieces):
             send = chip_decay * acc[k] + chip_half[k * piece_rows : (k + 1) * piece_rows]
             acc[k] = acc[k] + lax.ppermute(send, "ctx", pairs)
             last_send = send
     if partials is None:
-        partials = intra_after(last_send)
+        partials, reach = intra_after(last_send)
     prefix_half = jnp.concatenate(acc, axis=0) if pieces > 1 else acc[0]
     mate_prefix = lax.ppermute(prefix_half, "ctx", [(i, i ^ 1) for i in range(n_ctx)])
     chip_prefix = jnp.concatenate(
@@ -267,7 +268,7 @@
         projected = jnp.dot(
             seg_c[b], state_hi.astype(jnp.bfloat16), preferred_element_type=jnp.float32
         ) + jnp.dot(seg_c[b], state_lo, preferred_element_type=jnp.float32)
-        inter = head_columns(jnp.exp(cum[b])) * projected
+        inter = reach[b] * projected
         results.append((partials[b] + inter).astype(jnp.bfloat16))
     result = jnp.concatenate(results, axis=0) if blocks > 1 else results[0]
     return lax.all_to_all(result, "tp", split_axis=0, concat_axis=1, tiled=True)

time: 222 us -> 222 us (level)
  waiting for transfers between devices: 59 us -> 55.2 us
  local copies, waits for them, and re-layouts: 41.5 us -> 45 us
    reshape x2 -> x1, local copies, waits for them, and re-layouts: 10.9 us -> 5.38 us  [head_columns(): return jnp.repeat(head_major, P_SIZE, axis=-1)]
    optimization_barrier x0 -> x1, local copies, waits for them, and re-layouts: none -> 5.39 us  [intra_after(): operands = lax.optimization_barrier(operands + (tie,))[:5]]
    dynamic_update_slice x2, local copies, waits for them, and re-layouts: 2.93 us -> 5.95 us  [conv_silu(): lax.dynamic_update_slice_in_dim(body, conv_rows(edge, rim, weight, bias),...]
    ppermute x12, waiting for transfers between devices: 37.1 us -> 34.3 us  [on_device(): acc[k] = acc[k] + lax.ppermute(send, 'ctx', pairs)]
    unnamed x37 -> x35, local copies, waits for them, and re-layouts: 9.74 us -> 9.07 us
  transfers between devices with their start and end apart: 19 -> 19, of which waited for: 11 -> 11; matrix products, arithmetic and copies ran while one was open for 24% -> 26% of each run, Pallas kernels for 6% -> 6%
where the time goes in v9:
time: 222 us; the launch traced here: 220 us
  waiting for transfers between devices  55.2 us (25%)
  local copies, waits for them, and re-layouts  45 us (20%)
  starting transfers between devices  33.1 us (15%)
  other arithmetic  32.2 us (15%)
  blocking collectives  28.8 us (13%)
  Pallas kernels  21.8 us (10%)
  matrix products  3.46 us (2%)
    ppermute x12, waiting for transfers between devices, on_device(): acc[k] = acc[k] + lax.ppermute(send, 'ctx', pairs)  34.3 us
    all_to_all x1, blocking collectives, on_device(): return lax.all_to_all(result, 'tp', split_axis=0, concat_axis=1, tiled=True)  28.8 us
    ppermute x12, starting transfers between devices, on_device(): acc[k] = acc[k] + lax.ppermute(send, 'ctx', pairs)  15.3 us
    pallas_call x1, Pallas kernels, intra_block(): pl.pallas_call(intra_kernel, out_shape=jax.ShapeDtypeStruct((BLOCK, width...  13.1 us
    all_to_all x1, waiting for transfers between devices, on_device(): lax.all_to_all(x_part, 'tp', split_axis=1, concat_axis=0, tiled=True)  12 us
    convert_element_type x4, other arithmetic, conv_rows(): return jax.nn.silu(total).astype(jnp.bfloat16)  11.4 us
    unnamed x35, local copies, waits for them, and re-layouts  9.07 us
    pallas_call x1, Pallas kernels, fresh_block(): pl.pallas_call(fresh_kernel, out_shape=jax.ShapeDtypeStruct((N, width), j...  8.7 us
  transfers between devices with their start and end apart: 19, of which 11 were waited for; matrix products, arithmetic and copies ran while one was open for 26% of the time, Pallas kernels for 6%

profile of v9, /device:TPU:16, one launch (start us, length us, event | category | flops | bytes accessed | tf_op | source)
XLA Modules:
  0.0 220.1 jit_solution(10562227945606331831)
XLA Ops:
  0.0 1.6 fusion.35
  1.6 3.4 %collective-permute-start = (bf16[3,8192]{1,0:T(4,128)(2,1)}, bf16[3,8192]{1,0:T(4,128)(2,1)}, u32[]{:S(2)}, u32[]{:S(2)}) collective-permute-start(bf16[3,8192]{1,0:T(4,128)(2,1)} %get-tuple-element.32), channel_id=1, source_target_pairs={{0,1},{1,2},{2,3},{3,4},{4,5},{5,6},{6,7},{7,8},{8,9},{9,10},{10,1... | collective-permute-start | bytes 147464 | tf_op jit(solution)/shard_map/ppermute | solution.py:20
  5.8 3.4 %collective-permute-start.1 = (bf16[3,2048]{1,0:T(4,128)(2,1)S(1)}, bf16[3,2048]{1,0:T(4,128)(2,1)S(1)}, u32[]{:S(2)}, u32[]{:S(2)}) collective-permute-start(bf16[3,2048]{1,0:T(4,128)(2,1)S(1)} %get-tuple-element.46), channel_id=1, source_target_pairs={{0,1},{1,2},{2,3},{3,4},{4,5},{5,6},{6,7},{7,8},{8,9},{9,10},{10,1... | collective-permute-start | bytes 36872 | tf_op jit(solution)/shard_map/ppermute | solution.py:20
  10.7 3.3 %all-to-all-start.2 = ((bf16[128,4,32]{0,2,1:T(8,128)(2,1)}), bf16[128,4,32]{0,2,1:T(8,128)(2,1)S(1)}, u32[]{:S(2)}, u32[]{:S(2)}) async-start(bf16[128,4,32]{0,2,1:T(8,128)(2,1)} %bitcast.14), calls=%async_computation.2 | async-start | bytes 65536 | tf_op jit(solution)/shard_map/all_to_all | solution.py:167
  14.0 4.0 %convert_element_type.59 = f32[128,8192]{1,0:T(8,128)} convert(bf16[128,8192]{1,0:T(8,128)(2,1)} %param.10) | non-fusion elementwise | flops 1048576 | bytes 6291456 | tf_op jit(solution)/shard_map/convert_element_type | solution.py:34
  18.9 7.9 %multiply_convert_fusion = bf16[128,8192]{1,0:T(8,128)(2,1)S(1)} fusion(f32[128,8192]{1,0:T(8,128)} %convert_element_type.59, f32[8192]{0:T(1024)S(1)} %bitcast.98, f32[8192]{0:T(1024)S(1)} %bitcast.100, f32[8192]{0:T(1024)S(1)} %bitcast.96, f32[8192]{0:T(1024)S(1)} %bitcast.94, f32[8192]{0:T(1024)S(1)} %copy-done.9), kind=kLoop, calls=%fused_computation.1 | loop fusion | flops 13631488 | bytes 6455296 | tf_op jit(solution)/shard_map/convert_element_type | solution.py:27
  26.8 3.2 %multiply_convert_fusion.1 = bf16[128,2048]{0,1:T(8,128)(2,1)} fusion(f32[128,2048]{0,1:T(8,128)S(1)} %convert_element_type.63, f32[2048]{0:T(1024)S(1)} %bitcast.106, f32[2048]{0:T(1024)S(1)} %bitcast.108, f32[2048]{0:T(1024)S(1)} %bitcast.104, f32[2048]{0:T(1024)S(1)} %bitcast.102, f32[2048]{0:T(1024)S(1)} %copy-done.11), kind=kLoop, calls=%fused_computation.26 | loop fusion | flops 3407872 | bytes 1613824 | tf_op jit(solution)/shard_map/convert_element_type | solution.py:27
  30.6 5.0 %dynamic_update_slice.7 = bf16[128,2048]{0,1:T(8,128)(2,1)} dynamic-update-slice(bf16[128,2048]{0,1:T(8,128)(2,1)} %multiply_convert_fusion.1, bf16[3,2048]{0,1:T(8,128)(2,1)S(1)} %copy.88, s32[]{:T(128)} %constant.26.clone.1, s32[]{:T(128)} %constant.26.clone.1) | dynamic-update-slice | bytes 24580 | tf_op jit(solution)/shard_map/dynamic_update_slice | solution.py:36
  35.6 1.9 copy.89
  37.4 4.1 %all-to-all-start.1 = ((bf16[4,128,2,256]{1,3,2,0:T(8,128)(2,1)}), bf16[4,128,2,256]{1,3,2,0:T(8,128)(2,1)S(1)}, u32[]{:S(2)}, u32[]{:S(2)}) async-start(bf16[4,128,2,256]{1,3,2,0:T(8,128)(2,1)} %copy.89), calls=%async_computation.1 | async-start | bytes 1048576 | tf_op jit(solution)/shard_map/all_to_all | solution.py:164
  45.3 4.5 %all-to-all-done.1 = bf16[4,128,2,256]{1,3,2,0:T(8,128)(2,1)S(1)} async-done(((bf16[4,128,2,256]{1,3,2,0:T(8,128)(2,1)}), bf16[4,128,2,256]{1,3,2,0:T(8,128)(2,1)S(1)}, u32[]{:S(2)}, u32[]{:S(2)}) %all-to-all-start.1) | async-done | bytes 524320 | tf_op jit(solution)/shard_map/all_to_all | solution.py:164
  49.8 3.6 %all-to-all-start = ((bf16[128,4,2048]{2,0,1:T(8,128)(2,1)}), bf16[128,4,2048]{2,0,1:T(8,128)(2,1)S(1)}, u32[]{:S(2)}, u32[]{:S(2)}) async-start(bf16[128,4,2048]{2,0,1:T(8,128)(2,1)} %bitcast.88), calls=%async_computation | async-start | bytes 4194304 | tf_op jit(solution)/shard_map/all_to_all | solution.py:166
  56.1 2.5 %broadcast_in_dim.13 = f32[512,32,64]{0,2,1:T(8,128)} broadcast(f32[512,32]{0,1:T(8,128)S(1)} %get-tuple-element.25), dimensions={0,1} | broadcast | bytes 4259840 | tf_op jit(solution)/shard_map/broadcast_in_dim | solution.py:130
  58.7 5.4 %copy.97.fac_ref = f32[512,2048]{1,0:T(8,128)} copy(f32[512,2048]{0,1:T(8,128)} %bitcast.85) | data formatting | bytes 8388608 | tf_op jit(solution)/shard_map/reshape | solution.py:130
  65.6 12.0 %all-to-all-done = bf16[128,4,2048]{2,0,1:T(8,128)(2,1)S(1)} async-done(((bf16[128,4,2048]{2,0,1:T(8,128)(2,1)}), bf16[128,4,2048]{2,0,1:T(8,128)(2,1)S(1)}, u32[]{:S(2)}, u32[]{:S(2)}) %all-to-all-start) | async-done | bytes 2097184 | tf_op jit(solution)/shard_map/all_to_all | solution.py:166
  78.9 8.7 %ssd_fresh.1 = f32[256,2048]{1,0:T(8,128)} custom-call(bf16[512,2048]{1,0:T(8,128)(2,1)} %bitcast.90, bf16[256,512]{1,0:T(8,128)(2,1)} %slice_bitcast_fusion.1.bt_ref, f32[512,2048]{1,0:T(8,128)} %copy.97.fac_ref), custom_call_target="tpu_custom_call" | custom-call | flops 536870912 | bytes 8650752 | tf_op jit(solution)/shard_map/ssd_fresh/pallas_call | solution.py:115
  87.6 3.2 %select_maximum_fusion = f32[264,2048]{1,0:T(8,128)} fusion(f32[1,32]{1,0:T(1,128)S(1)} %bitcast.112, f32[256,2048]{1,0:T(8,128)} %ssd_fresh.1), kind=kLoop, calls=%fused_computation.10 | loop fusion | flops 1622016 | bytes 4259968 | tf_op jit(solution)/shard_map/concatenate | solution.py:203
  90.9 4.5 %collective-permute-done.2 = f32[264,2048]{1,0:T(8,128)S(1)} collective-permute-done((f32[264,2048]{1,0:T(8,128)}, f32[264,2048]{1,0:T(8,128)S(1)}, u32[]{:S(2)}, u32[]{:S(2)}) %collective-permute-start.2) | collective-permute-done | bytes 2162720 | tf_op jit(solution)/shard_map/ppermute | solution.py:202
  105.6 2.2 multiply_add_fusion.4
  114.3 2.5 %broadcast_in_dim.12 = f32[512,32,64]{0,2,1:T(8,128)} broadcast(f32[512,32]{0,1:T(8,128)S(1)} %exp.62), dimensions={0,1} | broadcast | bytes 4259840 | tf_op jit(solution)/shard_map/broadcast_in_dim | solution.py:130
  117.8 1.7 pad.11.clone.cum_ref
  119.4 13.1 %ssd_intra.1 = f32[512,2048]{1,0:T(8,128)} custom-call(bf16[512,2048]{1,0:T(8,128)(2,1)} %bitcast.91, f32[512,512]{1,0:T(8,128)} %fusion.12.s_ref, f32[512,128]{1,0:T(8,128)} %pad.11.clone.cum_ref, f32[32,512]{1,0:T(8,128)} %bitcast.93, f32[32,512]{1,0:T(8,128)} %bitcast.110, f32[1,2048]{1,0:T(1,128)} %broadcast_in_dim_reshape.2.skip_ref), custom_call_target="tpu_custom_call" | custom-call | flops 2147483648 | bytes 7340032 | tf_op jit(solution)/shard_map/ssd_intra/pallas_call | solution.py:85
  132.6 4.8 %collective-permute-done.5 = f32[64,1024]{1,0:T(8,128)} collective-permute-done((f32[64,1024]{1,0:T(8,128)}, f32[64,1024]{1,0:T(8,128)}, u32[]{:S(2)}, u32[]{:S(2)}) %collective-permute-start.5) | collective-permute-done | bytes 262176 | tf_op jit(solution)/shard_map/ppermute | solution.py:247
  138.5 4.6 %collective-permute-done.7 = f32[64,1024]{1,0:T(8,128)} collective-permute-done((f32[64,1024]{1,0:T(8,128)}, f32[64,1024]{1,0:T(8,128)}, u32[]{:S(2)}, u32[]{:S(2)}) %collective-permute-start.7) | collective-permute-done | bytes 262176 | tf_op jit(solution)/shard_map/ppermute | solution.py:247
  144.1 4.6 %collective-permute-done.9 = f32[64,1024]{1,0:T(8,128)} collective-permute-done((f32[64,1024]{1,0:T(8,128)}, f32[64,1024]{1,0:T(8,128)}, u32[]{:S(2)}, u32[]{:S(2)}) %collective-permute-start.9) | collective-permute-done | bytes 262176 | tf_op jit(solution)/shard_map/ppermute | solution.py:247
  149.7 3.1 %collective-permute-done.10 = f32[64,1024]{1,0:T(8,128)} collective-permute-done((f32[64,1024]{1,0:T(8,128)}, f32[64,1024]{1,0:T(8,128)}, u32[]{:S(2)}, u32[]{:S(2)}) %collective-permute-start.10) | collective-permute-done | bytes 262176 | tf_op jit(solution)/shard_map/ppermute | solution.py:247
  159.5 2.6 %collective-permute-done.14 = f32[64,1024]{1,0:T(8,128)S(1)} collective-permute-done((f32[64,1024]{1,0:T(8,128)S(1)}, f32[64,1024]{1,0:T(8,128)S(1)}, u32[]{:S(2)}, u32[]{:S(2)}) %collective-permute-start.14) | collective-permute-done | bytes 262176 | tf_op jit(solution)/shard_map/ppermute | solution.py:247
  162.1 5.6 %collective-permute-done.13 = f32[64,1024]{1,0:T(8,128)S(1)} collective-permute-done((f32[64,1024]{1,0:T(8,128)S(1)}, f32[64,1024]{1,0:T(8,128)S(1)}, u32[]{:S(2)}, u32[]{:S(2)}) %collective-permute-start.13) | collective-permute-done | bytes 262176 | tf_op jit(solution)/shard_map/ppermute | solution.py:247
  167.7 5.6 %collective-permute-done.12 = f32[64,1024]{1,0:T(8,128)S(1)} collective-permute-done((f32[64,1024]{1,0:T(8,128)S(1)}, f32[64,1024]{1,0:T(8,128)S(1)}, u32[]{:S(2)}, u32[]{:S(2)}) %collective-permute-start.12) | collective-permute-done | bytes 262176 | tf_op jit(solution)/shard_map/ppermute | solution.py:247
  173.4 3.5 %collective-permute-done.11 = f32[64,1024]{1,0:T(8,128)S(1)} collective-permute-done((f32[64,1024]{1,0:T(8,128)S(1)}, f32[64,1024]{1,0:T(8,128)S(1)}, u32[]{:S(2)}, u32[]{:S(2)}) %collective-permute-start.11) | collective-permute-done | bytes 262176 | tf_op jit(solution)/shard_map/ppermute | solution.py:247
  178.1 5.4 %copy.99 = f32[512,2048]{1,0:T(8,128)} copy(f32[512,2048]{0,1:T(8,128)} %bitcast.84) | data formatting | bytes 8388608 | tf_op jit(solution)/shard_map/optimization_barrier | solution.py:233
  189.8 28.8 %all_to_all.56 = bf16[4,128,2048]{2,1,0:T(8,128)(2,1)S(1)} all-to-all(bf16[4,128,2048]{2,1,0:T(8,128)(2,1)S(1)} %bitcast.87), channel_id=1, replica_groups=mesh['ctx'=8,'tp'=4] {'tp'}, dimensions={0} | all-to-all | bytes 4194304 | tf_op jit(solution)/shard_map/all_to_all | solution.py:274
  (121 shorter events, 49.4 us)
Async XLA Ops:
  1.6 40.0 %collective-permute-start = (bf16[3,8192]{1,0:T(4,128)(2,1)}, bf16[3,8192]{1,0:T(4,128)(2,1)}, u32[]{:S(2)}, u32[]{:S(2)}) collective-permute-start(bf16[3,8192]{1,0:T(4,128)(2,1)} %get-tuple-element.32), channel_id=1, source_target_pairs={{0,1},{1,2},{2,3},{3,4},{4,5},{5,6},{6,7},{7,8},{8,9},{9,10},{10,1... | collective-permute-start | bytes 147464 | tf_op jit(solution)/shard_map/ppermute | solution.py:20
  5.8 24.3 %collective-permute-start.1 = (bf16[3,2048]{1,0:T(4,128)(2,1)S(1)}, bf16[3,2048]{1,0:T(4,128)(2,1)S(1)}, u32[]{:S(2)}, u32[]{:S(2)}) collective-permute-start(bf16[3,2048]{1,0:T(4,128)(2,1)S(1)} %get-tuple-element.46), channel_id=1, source_target_pairs={{0,1},{1,2},{2,3},{3,4},{4,5},{5,6},{6,7},{7,8},{8,9},{9,10},{10,1... | collective-permute-start | bytes 36872 | tf_op jit(solution)/shard_map/ppermute | solution.py:20
  10.7 26.7 %all-to-all-start.2 = ((bf16[128,4,32]{0,2,1:T(8,128)(2,1)}), bf16[128,4,32]{0,2,1:T(8,128)(2,1)S(1)}, u32[]{:S(2)}, u32[]{:S(2)}) async-start(bf16[128,4,32]{0,2,1:T(8,128)(2,1)} %bitcast.14), calls=%async_computation.2 | async-start | bytes 65536 | tf_op jit(solution)/shard_map/all_to_all | solution.py:167
  14.0 4.1 %copy-start.7 = (bf16[128,2048]{1,0:T(8,128)(2,1)S(1)}, bf16[128,2048]{1,0:T(8,128)(2,1)}, u32[]{:S(2)}) copy-start(bf16[128,2048]{1,0:T(8,128)(2,1)} %param.11) | copy-start | bytes 1572868
  14.0 4.3 %copy-start.10 = (f32[4,8192]{1,0:T(4,128)S(1)}, f32[4,8192]{1,0:T(4,128)}, u32[]{:S(2)}) copy-start(f32[4,8192]{1,0:T(4,128)} %param.13) | copy-start | bytes 393220
  18.8 7.9 %copy-start.11 = (f32[2048]{0:T(1024)S(1)}, f32[2048]{0:T(1024)}, u32[]{:S(2)}) copy-start(f32[2048]{0:T(1024)} %param.16) | copy-start | bytes 24580
  18.9 11.2 %copy-start.13 = (f32[128]{0:T(128)S(1)}, f32[128]{0:T(128)}, u32[]{:S(2)}) copy-start(f32[128]{0:T(128)} %param.18) | copy-start | bytes 1540
  18.9 11.2 %copy-start.14 = (f32[128]{0:T(128)S(1)}, f32[128]{0:T(128)}, u32[]{:S(2)}) copy-start(f32[128]{0:T(128)} %param.17) | copy-start | bytes 1540
  37.4 12.4 %all-to-all-start.1 = ((bf16[4,128,2,256]{1,3,2,0:T(8,128)(2,1)}), bf16[4,128,2,256]{1,3,2,0:T(8,128)(2,1)S(1)}, u32[]{:S(2)}, u32[]{:S(2)}) async-start(bf16[4,128,2,256]{1,3,2,0:T(8,128)(2,1)} %copy.89), calls=%async_computation.1 | async-start | bytes 1048576 | tf_op jit(solution)/shard_map/all_to_all | solution.py:164
  49.8 27.8 %all-to-all-start = ((bf16[128,4,2048]{2,0,1:T(8,128)(2,1)}), bf16[128,4,2048]{2,0,1:T(8,128)(2,1)S(1)}, u32[]{:S(2)}, u32[]{:S(2)}) async-start(bf16[128,4,2048]{2,0,1:T(8,128)(2,1)} %bitcast.88), calls=%async_computation | async-start | bytes 4194304 | tf_op jit(solution)/shard_map/all_to_all | solution.py:166
  56.1 60.8 %copy-start.8 = (f32[512,32]{0,1:T(8,128)}, f32[512,32]{0,1:T(8,128)S(1)}, u32[]{:S(2)}) copy-start(f32[512,32]{0,1:T(8,128)S(1)} %get-tuple-element.16) | copy-start | bytes 196612
  77.6 1.3 copy-start.2
  90.9 4.5 %collective-permute-start.2 = (f32[264,2048]{1,0:T(8,128)}, f32[264,2048]{1,0:T(8,128)S(1)}, u32[]{:S(2)}, u32[]{:S(2)}) collective-permute-start(f32[264,2048]{1,0:T(8,128)} %select_maximum_fusion), channel_id=1, source_target_pairs={{0,4},{4,0},{8,12},{12,8},{16,20},{20,16},{24,28},{28,24},{1,5},{5... | collective-permute-start | bytes 6488072 | tf_op jit(solution)/shard_map/ppermute | solution.py:202
  95.8 1.6 copy-start.1
  97.4 6.0 %copy-start.15 = (f32[128]{0:T(128)S(1)}, f32[128]{0:T(128)}, u32[]{:S(2)}) copy-start(f32[128]{0:T(128)} %param.19) | copy-start | bytes 1540
  98.6 6.9 %collective-permute-start.8 = (f32[64,1024]{1,0:T(8,128)}, f32[64,1024]{1,0:T(8,128)}, u32[]{:S(2)}, u32[]{:S(2)}) collective-permute-start(f32[64,1024]{1,0:T(8,128)} %get-tuple-element.42), channel_id=1, source_target_pairs={{0,8},{4,12},{1,9},{5,13},{2,10},{6,14},{3,11},{7,15}} | collective-permute-start | bytes 786440 | tf_op jit(solution)/shard_map/ppermute | solution.py:247
  100.0 5.6 %collective-permute-start.3 = (f32[64,1024]{1,0:T(8,128)}, f32[64,1024]{1,0:T(8,128)S(1)}, u32[]{:S(2)}, u32[]{:S(2)}) collective-permute-start(f32[64,1024]{1,0:T(8,128)} %get-tuple-element.45), channel_id=1, source_target_pairs={{0,8},{4,12},{1,9},{5,13},{2,10},{6,14},{3,11},{7,15}} | collective-permute-start | bytes 786440 | tf_op jit(solution)/shard_map/ppermute | solution.py:247
  100.7 4.9 %collective-permute-start.4 = (f32[64,1024]{1,0:T(8,128)}, f32[64,1024]{1,0:T(8,128)}, u32[]{:S(2)}, u32[]{:S(2)}) collective-permute-start(f32[64,1024]{1,0:T(8,128)} %get-tuple-element.44), channel_id=1, source_target_pairs={{0,8},{4,12},{1,9},{5,13},{2,10},{6,14},{3,11},{7,15}} | collective-permute-start | bytes 786440 | tf_op jit(solution)/shard_map/ppermute | solution.py:247
  102.0 3.6 %collective-permute-start.6 = (f32[64,1024]{1,0:T(8,128)}, f32[64,1024]{1,0:T(8,128)}, u32[]{:S(2)}, u32[]{:S(2)}) collective-permute-start(f32[64,1024]{1,0:T(8,128)} %get-tuple-element.43), channel_id=1, source_target_pairs={{0,8},{4,12},{1,9},{5,13},{2,10},{6,14},{3,11},{7,15}} | collective-permute-start | bytes 786440 | tf_op jit(solution)/shard_map/ppermute | solution.py:247
  105.6 7.4 %copy-start.4 = (bf16[512,2,256]{0,2,1:T(8,128)(2,1)S(1)}, bf16[512,2,256]{0,2,1:T(8,128)(2,1)}, u32[]{:S(2)}) copy-start(bf16[512,2,256]{0,2,1:T(8,128)(2,1)} %copy-done.3) | copy-start | bytes 1572868
  107.8 29.6 %collective-permute-start.5 = (f32[64,1024]{1,0:T(8,128)}, f32[64,1024]{1,0:T(8,128)}, u32[]{:S(2)}, u32[]{:S(2)}) collective-permute-start(f32[64,1024]{1,0:T(8,128)} %get-tuple-element.40), channel_id=1, source_target_pairs={{8,16},{12,20},{9,17},{13,21},{10,18},{14,22},{11,19},{15,23}} | collective-permute-start | bytes 786440 | tf_op jit(solution)/shard_map/ppermute | solution.py:247
  109.1 33.9 %collective-permute-start.7 = (f32[64,1024]{1,0:T(8,128)}, f32[64,1024]{1,0:T(8,128)}, u32[]{:S(2)}, u32[]{:S(2)}) collective-permute-start(f32[64,1024]{1,0:T(8,128)} %get-tuple-element.41), channel_id=1, source_target_pairs={{8,16},{12,20},{9,17},{13,21},{10,18},{14,22},{11,19},{15,23}} | collective-permute-start | bytes 786440 | tf_op jit(solution)/shard_map/ppermute | solution.py:247
  110.4 38.2 %collective-permute-start.9 = (f32[64,1024]{1,0:T(8,128)}, f32[64,1024]{1,0:T(8,128)}, u32[]{:S(2)}, u32[]{:S(2)}) collective-permute-start(f32[64,1024]{1,0:T(8,128)} %get-tuple-element.38), channel_id=1, source_target_pairs={{8,16},{12,20},{9,17},{13,21},{10,18},{14,22},{11,19},{15,23}} | collective-permute-start | bytes 786440 | tf_op jit(solution)/shard_map/ppermute | solution.py:247
  111.7 41.1 %collective-permute-start.10 = (f32[64,1024]{1,0:T(8,128)}, f32[64,1024]{1,0:T(8,128)}, u32[]{:S(2)}, u32[]{:S(2)}) collective-permute-start(f32[64,1024]{1,0:T(8,128)} %get-tuple-element.39), channel_id=1, source_target_pairs={{8,16},{12,20},{9,17},{13,21},{10,18},{14,22},{11,19},{15,23}} | collective-permute-start | bytes 786440 | tf_op jit(solution)/shard_map/ppermute | solution.py:247
  154.0 8.0 %collective-permute-start.14 = (f32[64,1024]{1,0:T(8,128)S(1)}, f32[64,1024]{1,0:T(8,128)S(1)}, u32[]{:S(2)}, u32[]{:S(2)}) collective-permute-start(f32[64,1024]{1,0:T(8,128)S(1)} %get-tuple-element.35), channel_id=1, source_target_pairs={{16,24},{20,28},{17,25},{21,29},{18,26},{22,30},{19,27},{23,31}} | collective-permute-start | bytes 786440 | tf_op jit(solution)/shard_map/ppermute | solution.py:247
  155.4 12.3 %collective-permute-start.13 = (f32[64,1024]{1,0:T(8,128)S(1)}, f32[64,1024]{1,0:T(8,128)S(1)}, u32[]{:S(2)}, u32[]{:S(2)}) collective-permute-start(f32[64,1024]{1,0:T(8,128)S(1)} %get-tuple-element.37), channel_id=1, source_target_pairs={{16,24},{20,28},{17,25},{21,29},{18,26},{22,30},{19,27},{23,31}} | collective-permute-start | bytes 786440 | tf_op jit(solution)/shard_map/ppermute | solution.py:247
  156.7 16.6 %collective-permute-start.12 = (f32[64,1024]{1,0:T(8,128)S(1)}, f32[64,1024]{1,0:T(8,128)S(1)}, u32[]{:S(2)}, u32[]{:S(2)}) collective-permute-start(f32[64,1024]{1,0:T(8,128)S(1)} %get-tuple-element.36), channel_id=1, source_target_pairs={{16,24},{20,28},{17,25},{21,29},{18,26},{22,30},{19,27},{23,31}} | collective-permute-start | bytes 786440 | tf_op jit(solution)/shard_map/ppermute | solution.py:247
  158.0 18.9 %collective-permute-start.11 = (f32[64,1024]{1,0:T(8,128)S(1)}, f32[64,1024]{1,0:T(8,128)S(1)}, u32[]{:S(2)}, u32[]{:S(2)}) collective-permute-start(f32[64,1024]{1,0:T(8,128)S(1)} %get-tuple-element.34), channel_id=1, source_target_pairs={{16,24},{20,28},{17,25},{21,29},{18,26},{22,30},{19,27},{23,31}} | collective-permute-start | bytes 786440 | tf_op jit(solution)/shard_map/ppermute | solution.py:247
  178.0 5.5 %collective-permute-start.15 = (f32[256,1024]{1,0:T(8,128)}, f32[256,1024]{1,0:T(8,128)}, u32[]{:S(2)}, u32[]{:S(2)}) collective-permute-start(f32[256,1024]{1,0:T(8,128)} %pad_maximum_fusion.1), channel_id=1, source_target_pairs={{0,4},{4,0},{8,12},{12,8},{16,20},{20,16},{24,28},{28,24},{1,5},{5... | collective-permute-start | bytes 3145736 | tf_op jit(solution)/shard_map/ppermute | solution.py:252
  183.5 1.5 copy-start.5
  185.0 2.2 copy-start
  185.0 3.5 %copy-start.6 = (f32[512,2048]{1,0:T(8,128)S(1)}, f32[512,2048]{1,0:T(8,128)}, u32[]{:S(2)}) copy-start(f32[512,2048]{1,0:T(8,128)} %ssd_intra.1) | copy-start | bytes 12582916
  (3 other events, 2.3 us)

commit v10 on v9

--- a/solution.py
+++ b/solution.py
@@ -36,7 +36,7 @@
     return lax.dynamic_update_slice_in_dim(body, conv_rows(edge, rim, weight, bias), 0, 0)
 
 
-def intra_kernel(x_ref, s_ref, cum_ref, cumt_ref, dtt_ref, skip_ref, o_ref):
+def intra_kernel(x_ref, s_ref, cum_ref, cumt_ref, dtt_ref, skip_ref, o_ref, reach_ref):
     tiles = BLOCK // 128
     lane_head = lax.broadcasted_iota(jnp.int32, cum_ref.shape, 1)
     row_head = lax.broadcasted_iota(jnp.int32, cumt_ref.shape, 0)
@@ -55,6 +55,8 @@
             rows.append(jnp.sum(jnp.where(row_head == h, cumt_all, 0.0), axis=0, keepdims=True))
             dts.append(jnp.sum(jnp.where(row_head == h, dtt_all, 0.0), axis=0, keepdims=True))
         skip_p = skip_ref[:, pl.ds(off, 128)]
+        pair_lane = lax.broadcasted_iota(jnp.int32, (BLOCK, 128), 1)
+        reach_ref[:, pl.ds(off, 128)] = jnp.where(pair_lane < P_SIZE, jnp.exp(cols[0]), jnp.exp(cols[1]))
         for r in range(tiles):
             width = (r + 1) * 128
             s_tile = s_ref[r * 128 : width, 0:width]
@@ -84,9 +86,12 @@
     vmem = pl.BlockSpec(memory_space=pltpu.VMEM)
     return pl.pallas_call(
         intra_kernel,
-        out_shape=jax.ShapeDtypeStruct((BLOCK, width), jnp.float32),
+        out_shape=(
+            jax.ShapeDtypeStruct((BLOCK, width), jnp.float32),
+            jax.ShapeDtypeStruct((BLOCK, width), jnp.float32),
+        ),
         in_specs=[vmem] * 6,
-        out_specs=vmem,
+        out_specs=(vmem, vmem),
         name="ssd_intra",
         cost_estimate=pl.CostEstimate(
             flops=2 * BLOCK * BLOCK * width * 2,
@@ -228,11 +233,12 @@
     def intra_after(tie):
         parts, reach = [], []
         for b in range(blocks):
-            operands = (x_blk[b], scores[b], cum[b], dt_blk[b], head_columns(jnp.exp(cum[b])))
+            operands = (x_blk[b], scores[b], cum[b], dt_blk[b])
             if tie is not None:
-                operands = lax.optimization_barrier(operands + (tie,))[:5]
-            parts.append(intra_block(*operands[:4], skip_cols))
-            reach.append(operands[4])
+                operands = lax.optimization_barrier(operands + (tie,))[:4]
+            part, spread = intra_block(*operands, skip_cols)
+            parts.append(part)
+            reach.append(spread)
         return parts, reach
 
     partials = None

time: 222 us -> 217 us (0.977)
  local copies, waits for them, and re-layouts: 45 us -> 34.2 us
  waiting for transfers between devices: 55.2 us -> 60.3 us
    optimization_barrier x1 -> x0, local copies, waits for them, and re-layouts: 5.39 us -> none  [intra_after(): operands = lax.optimization_barrier(operands + (tie,))[:5]]
    dynamic_update_slice x2, local copies, waits for them, and re-layouts: 5.95 us -> 2.93 us  [conv_silu(): lax.dynamic_update_slice_in_dim(body, conv_rows(edge, rim, weight, bias),...]
    ppermute x1, waiting for transfers between devices: 0.01 us -> 2.85 us  [on_device(): lax.ppermute(prefix_half, 'ctx', [(i, i ^ 1) for i in range(n_ctx)])]
    broadcast_in_dim x6 -> x5, local copies, waits for them, and re-layouts: 6 us -> 3.45 us  [head_columns(): return jnp.repeat(head_major, P_SIZE, axis=-1)]
  transfers between devices with their start and end apart: 19 -> 19, of which waited for: 11 -> 12; matrix products, arithmetic and copies ran while one was open for 26% -> 21% of each run, Pallas kernels for 6% -> 7%
where the time goes in v10:
time: 217 us; the launch traced here: 215 us
  waiting for transfers between devices  60.3 us (28%)
  local copies, waits for them, and re-layouts  34.2 us (16%)
  starting transfers between devices  33.4 us (15%)
  other arithmetic  30.6 us (14%)
  blocking collectives  28.4 us (13%)
  Pallas kernels  24 us (11%)
  matrix products  3.44 us (2%)
    ppermute x12, waiting for transfers between devices, on_device(): acc[k] = acc[k] + lax.ppermute(send, 'ctx', pairs)  34.9 us
    all_to_all x1, blocking collectives, on_device(): return lax.all_to_all(result, 'tp', split_axis=0, concat_axis=1, tiled=True)  28.4 us
    ppermute x12, starting transfers between devices, on_device(): acc[k] = acc[k] + lax.ppermute(send, 'ctx', pairs)  15.3 us
    pallas_call x1, Pallas kernels, intra_block(): pl.pallas_call(intra_kernel, out_shape=(jax.ShapeDtypeStruct((BLOCK, widt...  15.2 us
    all_to_all x1, waiting for transfers between devices, on_device(): lax.all_to_all(x_part, 'tp', split_axis=1, concat_axis=0, tiled=True)  12.3 us
    convert_element_type x4, other arithmetic, conv_rows(): return jax.nn.silu(total).astype(jnp.bfloat16)  10.6 us
    unnamed x35, local copies, waits for them, and re-layouts  10.4 us
    pallas_call x1, Pallas kernels, fresh_block(): pl.pallas_call(fresh_kernel, out_shape=jax.ShapeDtypeStruct((N, width), j...  8.72 us
  transfers between devices with their start and end apart: 19, of which 12 were waited for; matrix products, arithmetic and copies ran while one was open for 21% of the time, Pallas kernels for 7%

profile of v10, /device:TPU:16, one launch (start us, length us, event | category | flops | bytes accessed | tf_op | source)
XLA Modules:
  0.0 214.9 jit_solution(4785494463437183189)
XLA Ops:
  1.5 3.7 %all-to-all-start.2 = ((bf16[128,4,32]{0,2,1:T(8,128)(2,1)}), bf16[128,4,32]{0,2,1:T(8,128)(2,1)S(1)}, u32[]{:S(2)}, u32[]{:S(2)}) async-start(bf16[128,4,32]{0,2,1:T(8,128)(2,1)} %bitcast.14), calls=%async_computation.2 | async-start | bytes 65536 | tf_op jit(solution)/shard_map/all_to_all | solution.py:172
  6.0 3.9 %collective-permute-start.1 = (bf16[3,2048]{1,0:T(4,128)(2,1)S(1)}, bf16[3,2048]{1,0:T(4,128)(2,1)S(1)}, u32[]{:S(2)}, u32[]{:S(2)}) collective-permute-start(bf16[3,2048]{1,0:T(4,128)(2,1)S(1)} %get-tuple-element.48), channel_id=1, source_target_pairs={{0,1},{1,2},{2,3},{3,4},{4,5},{5,6},{6,7},{7,8},{8,9},{9,10},{10,1... | collective-permute-start | bytes 36872 | tf_op jit(solution)/shard_map/ppermute | solution.py:20
  9.9 1.7 fusion.35
  11.6 3.4 %collective-permute-start = (bf16[3,8192]{1,0:T(4,128)(2,1)}, bf16[3,8192]{1,0:T(4,128)(2,1)S(1)}, u32[]{:S(2)}, u32[]{:S(2)}) collective-permute-start(bf16[3,8192]{1,0:T(4,128)(2,1)} %get-tuple-element.34), channel_id=1, source_target_pairs={{0,1},{1,2},{2,3},{3,4},{4,5},{5,6},{6,7},{7,8},{8,9},{9,10},{10,1... | collective-permute-start | bytes 147464 | tf_op jit(solution)/shard_map/ppermute | solution.py:20
  16.3 4.0 %convert_element_type.59 = f32[128,8192]{1,0:T(8,128)} convert(bf16[128,8192]{1,0:T(8,128)(2,1)} %param.10) | non-fusion elementwise | flops 1048576 | bytes 6291456 | tf_op jit(solution)/shard_map/convert_element_type | solution.py:34
  20.5 2.6 %multiply_convert_fusion.1 = bf16[128,2048]{0,1:T(8,128)(2,1)S(1)} fusion(f32[128,2048]{0,1:T(8,128)S(1)} %convert_element_type.63, f32[2048]{0:T(1024)S(1)} %bitcast.104, f32[2048]{0:T(1024)S(1)} %bitcast.106, f32[2048]{0:T(1024)S(1)} %bitcast.102, f32[2048]{0:T(1024)S(1)} %bitcast.100, f32[2048]{0:T(1024)S(1)} %copy-done.11), kind=kLoop, calls=%fused_computation.26 | loop fusion | flops 3407872 | bytes 1613824 | tf_op jit(solution)/shard_map/convert_element_type | solution.py:27
  23.2 7.8 %multiply_convert_fusion = bf16[128,8192]{1,0:T(8,128)(2,1)S(1)} fusion(f32[128,8192]{1,0:T(8,128)} %convert_element_type.59, f32[8192]{0:T(1024)S(1)} %bitcast.95, f32[8192]{0:T(1024)S(1)} %bitcast.97, f32[8192]{0:T(1024)S(1)} %bitcast.93, f32[8192]{0:T(1024)S(1)} %bitcast.91, f32[8192]{0:T(1024)S(1)} %copy-done.9), kind=kLoop, calls=%fused_computation.1 | loop fusion | flops 13631488 | bytes 6455296 | tf_op jit(solution)/shard_map/convert_element_type | solution.py:27
  31.6 2.0 dynamic_update_slice.7
  34.4 3.5 %all-to-all-start.1 = ((bf16[4,128,2,256]{1,3,2,0:T(8,128)(2,1)}), bf16[4,128,2,256]{1,3,2,0:T(8,128)(2,1)S(1)}, u32[]{:S(2)}, u32[]{:S(2)}) async-start(bf16[4,128,2,256]{1,3,2,0:T(8,128)(2,1)} %copy.83), calls=%async_computation.1 | async-start | bytes 1048576 | tf_op jit(solution)/shard_map/all_to_all | solution.py:169
  40.7 5.7 %all-to-all-done.1 = bf16[4,128,2,256]{1,3,2,0:T(8,128)(2,1)S(1)} async-done(((bf16[4,128,2,256]{1,3,2,0:T(8,128)(2,1)}), bf16[4,128,2,256]{1,3,2,0:T(8,128)(2,1)S(1)}, u32[]{:S(2)}, u32[]{:S(2)}) %all-to-all-start.1) | async-done | bytes 524320 | tf_op jit(solution)/shard_map/all_to_all | solution.py:169
  46.4 3.6 %all-to-all-start = ((bf16[128,4,2048]{2,0,1:T(8,128)(2,1)}), bf16[128,4,2048]{2,0,1:T(8,128)(2,1)S(1)}, u32[]{:S(2)}, u32[]{:S(2)}) async-start(bf16[128,4,2048]{2,0,1:T(8,128)(2,1)} %bitcast.86), calls=%async_computation | async-start | bytes 4194304 | tf_op jit(solution)/shard_map/all_to_all | solution.py:171
  52.8 2.6 %broadcast_in_dim.10 = f32[512,32,64]{0,2,1:T(8,128)} broadcast(f32[512,32]{0,1:T(8,128)S(1)} %get-tuple-element.27), dimensions={0,1} | broadcast | bytes 4259840 | tf_op jit(solution)/shard_map/broadcast_in_dim | solution.py:135
  55.3 5.4 %copy.91.fac_ref = f32[512,2048]{1,0:T(8,128)} copy(f32[512,2048]{0,1:T(8,128)} %bitcast.83) | data formatting | bytes 8388608 | tf_op jit(solution)/shard_map/reshape | solution.py:135
  62.3 12.3 %all-to-all-done = bf16[128,4,2048]{2,0,1:T(8,128)(2,1)S(1)} async-done(((bf16[128,4,2048]{2,0,1:T(8,128)(2,1)}), bf16[128,4,2048]{2,0,1:T(8,128)(2,1)S(1)}, u32[]{:S(2)}, u32[]{:S(2)}) %all-to-all-start) | async-done | bytes 2097184 | tf_op jit(solution)/shard_map/all_to_all | solution.py:171
  75.9 8.7 %ssd_fresh.1 = f32[256,2048]{1,0:T(8,128)} custom-call(bf16[512,2048]{1,0:T(8,128)(2,1)} %bitcast.88, bf16[256,512]{1,0:T(8,128)(2,1)} %slice_bitcast_fusion.1.bt_ref, f32[512,2048]{1,0:T(8,128)} %copy.91.fac_ref), custom_call_target="tpu_custom_call" | custom-call | flops 536870912 | bytes 8650752 | tf_op jit(solution)/shard_map/ssd_fresh/pallas_call | solution.py:120
  84.6 3.2 %select_maximum_fusion = f32[264,2048]{1,0:T(8,128)} fusion(f32[1,32]{1,0:T(1,128)S(1)} %bitcast.110, f32[256,2048]{1,0:T(8,128)} %ssd_fresh.1), kind=kLoop, calls=%fused_computation.10 | loop fusion | flops 1622016 | bytes 4259968 | tf_op jit(solution)/shard_map/concatenate | solution.py:208
  87.9 4.5 %collective-permute-done.2 = f32[264,2048]{1,0:T(8,128)S(1)} collective-permute-done((f32[264,2048]{1,0:T(8,128)}, f32[264,2048]{1,0:T(8,128)S(1)}, u32[]{:S(2)}, u32[]{:S(2)}) %collective-permute-start.2) | collective-permute-done | bytes 2162720 | tf_op jit(solution)/shard_map/ppermute | solution.py:207
  102.6 2.2 %multiply_add_fusion.4 = (f32[64,1024]{1,0:T(8,128)}, f32[64,1024]{1,0:T(8,128)}, f32[64,1024]{1,0:T(8,128)}, f32[64,1024]{1,0:T(8,128)}) fusion(f32[64,1024]{1,0:T(8,128)} %collective-permute-done.8, f32[256,1024]{1,0:T(8,128)S(1)} %select_add_fusion, f32[1024]{0:T(1024)S(1)} %mul.339, f32[64,1024]{1,0:T(8,128)} %collective-permute-done.3, ...), kind=kLoop, calls=%fused_computation.37 | loop fusion | flops 524288 | bytes 3149824 | tf_op jit(solution)/shard_map/add | solution.py:252
  112.1 1.7 pad.11.clone.cum_ref
  113.8 15.2 %ssd_intra.1 = (f32[512,2048]{1,0:T(8,128)}, f32[512,2048]{1,0:T(8,128)}) custom-call(bf16[512,2048]{1,0:T(8,128)(2,1)} %bitcast.89, f32[512,512]{1,0:T(8,128)} %fusion.12.s_ref, f32[512,128]{1,0:T(8,128)} %pad.11.clone.cum_ref, f32[32,512]{1,0:T(8,128)} %bitcast.99, f32[32,512]{1,0:T(8,128)} %bitcast.108, f32[1,2048]{1,0:T(1,128)} %broadcast_in_dim_reshape.2.skip_ref), custom_call_target="tpu_custom_call" | custom-call | flops 2147483648 | bytes 7340032 | tf_op jit(solution)/shard_map/ssd_intra/pallas_call | solution.py:87
  129.1 5.3 %collective-permute-done.9 = f32[64,1024]{1,0:T(8,128)} collective-permute-done((f32[64,1024]{1,0:T(8,128)}, f32[64,1024]{1,0:T(8,128)}, u32[]{:S(2)}, u32[]{:S(2)}) %collective-permute-start.9) | collective-permute-done | bytes 262176 | tf_op jit(solution)/shard_map/ppermute | solution.py:253
  135.5 4.6 %collective-permute-done.5 = f32[64,1024]{1,0:T(8,128)} collective-permute-done((f32[64,1024]{1,0:T(8,128)}, f32[64,1024]{1,0:T(8,128)}, u32[]{:S(2)}, u32[]{:S(2)}) %collective-permute-start.5) | collective-permute-done | bytes 262176 | tf_op jit(solution)/shard_map/ppermute | solution.py:253
  141.1 4.6 %collective-permute-done.7 = f32[64,1024]{1,0:T(8,128)} collective-permute-done((f32[64,1024]{1,0:T(8,128)}, f32[64,1024]{1,0:T(8,128)}, u32[]{:S(2)}, u32[]{:S(2)}) %collective-permute-start.7) | collective-permute-done | bytes 262176 | tf_op jit(solution)/shard_map/ppermute | solution.py:253
  146.6 3.2 %collective-permute-done.10 = f32[64,1024]{1,0:T(8,128)} collective-permute-done((f32[64,1024]{1,0:T(8,128)}, f32[64,1024]{1,0:T(8,128)}, u32[]{:S(2)}, u32[]{:S(2)}) %collective-permute-start.10) | collective-permute-done | bytes 262176 | tf_op jit(solution)/shard_map/ppermute | solution.py:253
  155.1 1.5 collective-permute-start.13
  156.6 2.6 %collective-permute-done.11 = f32[64,1024]{1,0:T(8,128)S(1)} collective-permute-done((f32[64,1024]{1,0:T(8,128)S(1)}, f32[64,1024]{1,0:T(8,128)S(1)}, u32[]{:S(2)}, u32[]{:S(2)}) %collective-permute-start.11) | collective-permute-done | bytes 262176 | tf_op jit(solution)/shard_map/ppermute | solution.py:253
  159.2 5.6 %collective-permute-done.14 = f32[64,1024]{1,0:T(8,128)S(1)} collective-permute-done((f32[64,1024]{1,0:T(8,128)S(1)}, f32[64,1024]{1,0:T(8,128)S(1)}, u32[]{:S(2)}, u32[]{:S(2)}) %collective-permute-start.14) | collective-permute-done | bytes 262176 | tf_op jit(solution)/shard_map/ppermute | solution.py:253
  164.8 5.6 %collective-permute-done.12 = f32[64,1024]{1,0:T(8,128)S(1)} collective-permute-done((f32[64,1024]{1,0:T(8,128)S(1)}, f32[64,1024]{1,0:T(8,128)S(1)}, u32[]{:S(2)}, u32[]{:S(2)}) %collective-permute-start.12) | collective-permute-done | bytes 262176 | tf_op jit(solution)/shard_map/ppermute | solution.py:253
  170.4 3.5 %collective-permute-done.13 = f32[64,1024]{1,0:T(8,128)S(1)} collective-permute-done((f32[64,1024]{1,0:T(8,128)S(1)}, f32[64,1024]{1,0:T(8,128)S(1)}, u32[]{:S(2)}, u32[]{:S(2)}) %collective-permute-start.13) | collective-permute-done | bytes 262176 | tf_op jit(solution)/shard_map/ppermute | solution.py:253
  175.9 2.9 %collective-permute-done.15 = f32[256,1024]{1,0:T(8,128)} collective-permute-done((f32[256,1024]{1,0:T(8,128)}, f32[256,1024]{1,0:T(8,128)}, u32[]{:S(2)}, u32[]{:S(2)}) %collective-permute-start.15) | collective-permute-done | bytes 1048608 | tf_op jit(solution)/shard_map/ppermute | solution.py:258
  178.7 1.5 broadcast_select_fusion
  185.0 28.4 %all_to_all.56 = bf16[4,128,2048]{2,1,0:T(8,128)(2,1)S(1)} all-to-all(bf16[4,128,2048]{2,1,0:T(8,128)(2,1)S(1)} %bitcast.85), channel_id=1, replica_groups=mesh['ctx'=8,'tp'=4] {'tp'}, dimensions={0} | all-to-all | bytes 4194304 | tf_op jit(solution)/shard_map/all_to_all | solution.py:280
  (118 shorter events, 47.5 us)
Async XLA Ops:
  1.5 32.9 %all-to-all-start.2 = ((bf16[128,4,32]{0,2,1:T(8,128)(2,1)}), bf16[128,4,32]{0,2,1:T(8,128)(2,1)S(1)}, u32[]{:S(2)}, u32[]{:S(2)}) async-start(bf16[128,4,32]{0,2,1:T(8,128)(2,1)} %bitcast.14), calls=%async_computation.2 | async-start | bytes 65536 | tf_op jit(solution)/shard_map/all_to_all | solution.py:172
  6.0 25.2 %collective-permute-start.1 = (bf16[3,2048]{1,0:T(4,128)(2,1)S(1)}, bf16[3,2048]{1,0:T(4,128)(2,1)S(1)}, u32[]{:S(2)}, u32[]{:S(2)}) collective-permute-start(bf16[3,2048]{1,0:T(4,128)(2,1)S(1)} %get-tuple-element.48), channel_id=1, source_target_pairs={{0,1},{1,2},{2,3},{3,4},{4,5},{5,6},{6,7},{7,8},{8,9},{9,10},{10,1... | collective-permute-start | bytes 36872 | tf_op jit(solution)/shard_map/ppermute | solution.py:20
  11.6 26.4 %collective-permute-start = (bf16[3,8192]{1,0:T(4,128)(2,1)}, bf16[3,8192]{1,0:T(4,128)(2,1)S(1)}, u32[]{:S(2)}, u32[]{:S(2)}) collective-permute-start(bf16[3,8192]{1,0:T(4,128)(2,1)} %get-tuple-element.34), channel_id=1, source_target_pairs={{0,1},{1,2},{2,3},{3,4},{4,5},{5,6},{6,7},{7,8},{8,9},{9,10},{10,1... | collective-permute-start | bytes 147464 | tf_op jit(solution)/shard_map/ppermute | solution.py:20
  16.3 4.1 %copy-start.12 = (f32[4,2048]{1,0:T(4,128)S(1)}, f32[4,2048]{1,0:T(4,128)}, u32[]{:S(2)}) copy-start(f32[4,2048]{1,0:T(4,128)} %param.15) | copy-start | bytes 98308
  16.3 4.1 %copy-start.10 = (f32[4,8192]{1,0:T(4,128)S(1)}, f32[4,8192]{1,0:T(4,128)}, u32[]{:S(2)}) copy-start(f32[4,8192]{1,0:T(4,128)} %param.13) | copy-start | bytes 393220
  16.3 4.3 %copy-start.11 = (f32[2048]{0:T(1024)S(1)}, f32[2048]{0:T(1024)}, u32[]{:S(2)}) copy-start(f32[2048]{0:T(1024)} %param.16) | copy-start | bytes 24580
  20.3 2.9 %copy-start.9 = (f32[8192]{0:T(1024)S(1)}, f32[8192]{0:T(1024)}, u32[]{:S(2)}) copy-start(f32[8192]{0:T(1024)} %param.14) | copy-start | bytes 98308
  23.2 7.8 %copy-start.13 = (f32[128]{0:T(128)S(1)}, f32[128]{0:T(128)}, u32[]{:S(2)}) copy-start(f32[128]{0:T(128)} %param.18) | copy-start | bytes 1540
  23.2 7.9 %copy-start.14 = (f32[128]{0:T(128)S(1)}, f32[128]{0:T(128)}, u32[]{:S(2)}) copy-start(f32[128]{0:T(128)} %param.17) | copy-start | bytes 1540
  34.4 12.0 %all-to-all-start.1 = ((bf16[4,128,2,256]{1,3,2,0:T(8,128)(2,1)}), bf16[4,128,2,256]{1,3,2,0:T(8,128)(2,1)S(1)}, u32[]{:S(2)}, u32[]{:S(2)}) async-start(bf16[4,128,2,256]{1,3,2,0:T(8,128)(2,1)} %copy.83), calls=%async_computation.1 | async-start | bytes 1048576 | tf_op jit(solution)/shard_map/all_to_all | solution.py:169
  46.4 28.2 %all-to-all-start = ((bf16[128,4,2048]{2,0,1:T(8,128)(2,1)}), bf16[128,4,2048]{2,0,1:T(8,128)(2,1)S(1)}, u32[]{:S(2)}, u32[]{:S(2)}) async-start(bf16[128,4,2048]{2,0,1:T(8,128)(2,1)} %bitcast.86), calls=%async_computation | async-start | bytes 4194304 | tf_op jit(solution)/shard_map/all_to_all | solution.py:171
  52.8 58.6 %copy-start.8 = (f32[512,32]{0,1:T(8,128)}, f32[512,32]{0,1:T(8,128)S(1)}, u32[]{:S(2)}) copy-start(f32[512,32]{0,1:T(8,128)S(1)} %get-tuple-element.17) | copy-start | bytes 196612
  87.9 4.5 %collective-permute-start.2 = (f32[264,2048]{1,0:T(8,128)}, f32[264,2048]{1,0:T(8,128)S(1)}, u32[]{:S(2)}, u32[]{:S(2)}) collective-permute-start(f32[264,2048]{1,0:T(8,128)} %select_maximum_fusion), channel_id=1, source_target_pairs={{0,4},{4,0},{8,12},{12,8},{16,20},{20,16},{24,28},{28,24},{1,5},{5... | collective-permute-start | bytes 6488072 | tf_op jit(solution)/shard_map/ppermute | solution.py:207
  92.8 1.6 copy-start
  94.4 6.0 %copy-start.15 = (f32[128]{0:T(128)S(1)}, f32[128]{0:T(128)}, u32[]{:S(2)}) copy-start(f32[128]{0:T(128)} %param.19) | copy-start | bytes 1540
  95.6 6.9 %collective-permute-start.8 = (f32[64,1024]{1,0:T(8,128)}, f32[64,1024]{1,0:T(8,128)}, u32[]{:S(2)}, u32[]{:S(2)}) collective-permute-start(f32[64,1024]{1,0:T(8,128)} %get-tuple-element.44), channel_id=1, source_target_pairs={{0,8},{4,12},{1,9},{5,13},{2,10},{6,14},{3,11},{7,15}} | collective-permute-start | bytes 786440 | tf_op jit(solution)/shard_map/ppermute | solution.py:253
  97.0 5.5 %collective-permute-start.6 = (f32[64,1024]{1,0:T(8,128)}, f32[64,1024]{1,0:T(8,128)S(1)}, u32[]{:S(2)}, u32[]{:S(2)}) collective-permute-start(f32[64,1024]{1,0:T(8,128)} %get-tuple-element.45), channel_id=1, source_target_pairs={{0,8},{4,12},{1,9},{5,13},{2,10},{6,14},{3,11},{7,15}} | collective-permute-start | bytes 786440 | tf_op jit(solution)/shard_map/ppermute | solution.py:253
  97.7 4.9 %collective-permute-start.4 = (f32[64,1024]{1,0:T(8,128)}, f32[64,1024]{1,0:T(8,128)}, u32[]{:S(2)}, u32[]{:S(2)}) collective-permute-start(f32[64,1024]{1,0:T(8,128)} %get-tuple-element.46), channel_id=1, source_target_pairs={{0,8},{4,12},{1,9},{5,13},{2,10},{6,14},{3,11},{7,15}} | collective-permute-start | bytes 786440 | tf_op jit(solution)/shard_map/ppermute | solution.py:253
  99.0 3.5 %collective-permute-start.3 = (f32[64,1024]{1,0:T(8,128)}, f32[64,1024]{1,0:T(8,128)}, u32[]{:S(2)}, u32[]{:S(2)}) collective-permute-start(f32[64,1024]{1,0:T(8,128)} %get-tuple-element.47), channel_id=1, source_target_pairs={{0,8},{4,12},{1,9},{5,13},{2,10},{6,14},{3,11},{7,15}} | collective-permute-start | bytes 786440 | tf_op jit(solution)/shard_map/ppermute | solution.py:253
  102.5 7.4 %copy-start.3 = (bf16[512,2,256]{0,2,1:T(8,128)(2,1)S(1)}, bf16[512,2,256]{0,2,1:T(8,128)(2,1)}, u32[]{:S(2)}) copy-start(bf16[512,2,256]{0,2,1:T(8,128)(2,1)} %copy-done.2) | copy-start | bytes 1572868
  104.8 29.6 %collective-permute-start.9 = (f32[64,1024]{1,0:T(8,128)}, f32[64,1024]{1,0:T(8,128)}, u32[]{:S(2)}, u32[]{:S(2)}) collective-permute-start(f32[64,1024]{1,0:T(8,128)} %get-tuple-element.40), channel_id=1, source_target_pairs={{8,16},{12,20},{9,17},{13,21},{10,18},{14,22},{11,19},{15,23}} | collective-permute-start | bytes 786440 | tf_op jit(solution)/shard_map/ppermute | solution.py:253
  106.1 34.0 %collective-permute-start.5 = (f32[64,1024]{1,0:T(8,128)}, f32[64,1024]{1,0:T(8,128)}, u32[]{:S(2)}, u32[]{:S(2)}) collective-permute-start(f32[64,1024]{1,0:T(8,128)} %get-tuple-element.42), channel_id=1, source_target_pairs={{8,16},{12,20},{9,17},{13,21},{10,18},{14,22},{11,19},{15,23}} | collective-permute-start | bytes 786440 | tf_op jit(solution)/shard_map/ppermute | solution.py:253
  107.4 38.3 %collective-permute-start.7 = (f32[64,1024]{1,0:T(8,128)}, f32[64,1024]{1,0:T(8,128)}, u32[]{:S(2)}, u32[]{:S(2)}) collective-permute-start(f32[64,1024]{1,0:T(8,128)} %get-tuple-element.43), channel_id=1, source_target_pairs={{8,16},{12,20},{9,17},{13,21},{10,18},{14,22},{11,19},{15,23}} | collective-permute-start | bytes 786440 | tf_op jit(solution)/shard_map/ppermute | solution.py:253
  108.7 41.2 %collective-permute-start.10 = (f32[64,1024]{1,0:T(8,128)}, f32[64,1024]{1,0:T(8,128)}, u32[]{:S(2)}, u32[]{:S(2)}) collective-permute-start(f32[64,1024]{1,0:T(8,128)} %get-tuple-element.41), channel_id=1, source_target_pairs={{8,16},{12,20},{9,17},{13,21},{10,18},{14,22},{11,19},{15,23}} | collective-permute-start | bytes 786440 | tf_op jit(solution)/shard_map/ppermute | solution.py:253
  151.1 8.0 %collective-permute-start.11 = (f32[64,1024]{1,0:T(8,128)S(1)}, f32[64,1024]{1,0:T(8,128)S(1)}, u32[]{:S(2)}, u32[]{:S(2)}) collective-permute-start(f32[64,1024]{1,0:T(8,128)S(1)} %get-tuple-element.36), channel_id=1, source_target_pairs={{16,24},{20,28},{17,25},{21,29},{18,26},{22,30},{19,27},{23,31}} | collective-permute-start | bytes 786440 | tf_op jit(solution)/shard_map/ppermute | solution.py:253
  152.5 12.3 %collective-permute-start.14 = (f32[64,1024]{1,0:T(8,128)S(1)}, f32[64,1024]{1,0:T(8,128)S(1)}, u32[]{:S(2)}, u32[]{:S(2)}) collective-permute-start(f32[64,1024]{1,0:T(8,128)S(1)} %get-tuple-element.37), channel_id=1, source_target_pairs={{16,24},{20,28},{17,25},{21,29},{18,26},{22,30},{19,27},{23,31}} | collective-permute-start | bytes 786440 | tf_op jit(solution)/shard_map/ppermute | solution.py:253
  153.8 16.6 %collective-permute-start.12 = (f32[64,1024]{1,0:T(8,128)S(1)}, f32[64,1024]{1,0:T(8,128)S(1)}, u32[]{:S(2)}, u32[]{:S(2)}) collective-permute-start(f32[64,1024]{1,0:T(8,128)S(1)} %get-tuple-element.38), channel_id=1, source_target_pairs={{16,24},{20,28},{17,25},{21,29},{18,26},{22,30},{19,27},{23,31}} | collective-permute-start | bytes 786440 | tf_op jit(solution)/shard_map/ppermute | solution.py:253
  155.1 18.9 %collective-permute-start.13 = (f32[64,1024]{1,0:T(8,128)S(1)}, f32[64,1024]{1,0:T(8,128)S(1)}, u32[]{:S(2)}, u32[]{:S(2)}) collective-permute-start(f32[64,1024]{1,0:T(8,128)S(1)} %get-tuple-element.39), channel_id=1, source_target_pairs={{16,24},{20,28},{17,25},{21,29},{18,26},{22,30},{19,27},{23,31}} | collective-permute-start | bytes 786440 | tf_op jit(solution)/shard_map/ppermute | solution.py:253
  175.7 4.5 %copy-start.4 = (bf16[512,2,256]{0,2,1:T(8,128)(2,1)S(1)}, bf16[512,2,256]{0,2,1:T(8,128)(2,1)}, u32[]{:S(2)}) copy-start(bf16[512,2,256]{0,2,1:T(8,128)(2,1)} %copy-done.2) | copy-start | bytes 1572868
  175.7 3.0 %collective-permute-start.15 = (f32[256,1024]{1,0:T(8,128)}, f32[256,1024]{1,0:T(8,128)}, u32[]{:S(2)}, u32[]{:S(2)}) collective-permute-start(f32[256,1024]{1,0:T(8,128)} %pad_maximum_fusion.1), channel_id=1, source_target_pairs={{0,4},{4,0},{8,12},{12,8},{16,20},{20,16},{24,28},{28,24},{1,5},{5... | collective-permute-start | bytes 3145736 | tf_op jit(solution)/shard_map/ppermute | solution.py:258
  180.2 2.2 %copy-start.5 = (f32[512,2048]{1,0:T(8,128)S(1)}, f32[512,2048]{1,0:T(8,128)}, u32[]{:S(2)}) copy-start(f32[512,2048]{1,0:T(8,128)} %get-tuple-element.19) | copy-start | bytes 12582916
  180.3 3.5 %copy-start.6 = (f32[512,2048]{1,0:T(8,128)S(1)}, f32[512,2048]{1,0:T(8,128)}, u32[]{:S(2)}) copy-start(f32[512,2048]{1,0:T(8,128)} %get-tuple-element.20) | copy-start | bytes 12582916
  (3 other events, 2.8 us)

commit v11 on v10

--- a/solution.py
+++ b/solution.py
@@ -102,26 +102,24 @@
 
 
 def fresh_kernel(x_ref, bt_ref, fac_ref, o_ref):
-    def pair(p, carry):
-        off = pl.multiple_of(p * 128, 128)
-        xp = x_ref[:, pl.ds(off, 128)].astype(jnp.float32)
-        wx = (fac_ref[:, pl.ds(off, 128)] * xp).astype(jnp.bfloat16)
-        o_ref[:, pl.ds(off, 128)] = jnp.dot(bt_ref[...], wx, preferred_element_type=jnp.float32)
-        return carry
-
-    lax.fori_loop(0, x_ref.shape[1] // 128, pair, 0)
+    wx = (fac_ref[...] * x_ref[...].astype(jnp.float32)).astype(jnp.bfloat16)
+    o_ref[...] = jnp.dot(bt_ref[...], wx, preferred_element_type=jnp.float32)
 
 
 def fresh_block(x, b, cum, dt):
     heads = cum.shape[1]
     width = x.shape[1]
     factors = head_columns(jnp.exp(cum[BLOCK - 1 :] - cum) * dt)
-    vmem = pl.BlockSpec(memory_space=pltpu.VMEM)
     return pl.pallas_call(
         fresh_kernel,
         out_shape=jax.ShapeDtypeStruct((N, width), jnp.float32),
-        in_specs=[vmem] * 3,
-        out_specs=vmem,
+        grid=(width // 128,),
+        in_specs=[
+            pl.BlockSpec((BLOCK, 128), lambda p: (0, p)),
+            pl.BlockSpec((N, BLOCK), lambda p: (0, 0)),
+            pl.BlockSpec((BLOCK, 128), lambda p: (0, p)),
+        ],
+        out_specs=pl.BlockSpec((N, 128), lambda p: (0, p)),
         name="ssd_fresh",
         cost_estimate=pl.CostEstimate(
             flops=2 * BLOCK * N * width,

time: 217 us -> 220 us (1.014)
  Pallas kernels: 24 us -> 27.2 us
    pallas_call x1, Pallas kernels: 8.72 us -> 12 us  [fresh_block(): pl.pallas_call(fresh_kernel, out_shape=jax.ShapeDtypeStruct((N, width), j...]
where the time goes in v11:
time: 220 us; the launch traced here: 218 us
  waiting for transfers between devices  60.3 us (27%)
  local copies, waits for them, and re-layouts  34.2 us (16%)
  starting transfers between devices  33.4 us (15%)
  other arithmetic  30.6 us (14%)
  blocking collectives  28.4 us (13%)
  Pallas kernels  27.2 us (12%)
  matrix products  3.44 us (2%)
    ppermute x12, waiting for transfers between devices, on_device(): acc[k] = acc[k] + lax.ppermute(send, 'ctx', pairs)  34.9 us
    all_to_all x1, blocking collectives, on_device(): return lax.all_to_all(result, 'tp', split_axis=0, concat_axis=1, tiled=True)  28.4 us
    ppermute x12, starting transfers between devices, on_device(): acc[k] = acc[k] + lax.ppermute(send, 'ctx', pairs)  15.3 us
    pallas_call x1, Pallas kernels, intra_block(): pl.pallas_call(intra_kernel, out_shape=(jax.ShapeDtypeStruct((BLOCK, widt...  15.2 us
    all_to_all x1, waiting for transfers between devices, on_device(): lax.all_to_all(x_part, 'tp', split_axis=1, concat_axis=0, tiled=True)  12.3 us
    pallas_call x1, Pallas kernels, fresh_block(): pl.pallas_call(fresh_kernel, out_shape=jax.ShapeDtypeStruct((N, width), j...  12 us
    convert_element_type x4, other arithmetic, conv_rows(): return jax.nn.silu(total).astype(jnp.bfloat16)  10.6 us
    unnamed x35, local copies, waits for them, and re-layouts  10.4 us
  transfers between devices with their start and end apart: 19, of which 12 were waited for; matrix products, arithmetic and copies ran while one was open for 21% of the time, Pallas kernels for 7%

profile of v11, /device:TPU:16, one launch (start us, length us, event | category | flops | bytes accessed | tf_op | source)
XLA Modules:
  0.0 218.1 jit_solution(3067623141406827883)
XLA Ops:
  1.5 3.7 %all-to-all-start.2 = ((bf16[128,4,32]{0,2,1:T(8,128)(2,1)}), bf16[128,4,32]{0,2,1:T(8,128)(2,1)S(1)}, u32[]{:S(2)}, u32[]{:S(2)}) async-start(bf16[128,4,32]{0,2,1:T(8,128)(2,1)} %bitcast.14), calls=%async_computation.2 | async-start | bytes 65536 | tf_op jit(solution)/shard_map/all_to_all | solution.py:170
  6.0 3.9 %collective-permute-start.1 = (bf16[3,2048]{1,0:T(4,128)(2,1)S(1)}, bf16[3,2048]{1,0:T(4,128)(2,1)S(1)}, u32[]{:S(2)}, u32[]{:S(2)}) collective-permute-start(bf16[3,2048]{1,0:T(4,128)(2,1)S(1)} %get-tuple-element.48), channel_id=1, source_target_pairs={{0,1},{1,2},{2,3},{3,4},{4,5},{5,6},{6,7},{7,8},{8,9},{9,10},{10,1... | collective-permute-start | bytes 36872 | tf_op jit(solution)/shard_map/ppermute | solution.py:20
  9.9 1.7 fusion.35
  11.6 3.4 %collective-permute-start = (bf16[3,8192]{1,0:T(4,128)(2,1)}, bf16[3,8192]{1,0:T(4,128)(2,1)S(1)}, u32[]{:S(2)}, u32[]{:S(2)}) collective-permute-start(bf16[3,8192]{1,0:T(4,128)(2,1)} %get-tuple-element.34), channel_id=1, source_target_pairs={{0,1},{1,2},{2,3},{3,4},{4,5},{5,6},{6,7},{7,8},{8,9},{9,10},{10,1... | collective-permute-start | bytes 147464 | tf_op jit(solution)/shard_map/ppermute | solution.py:20
  16.3 4.0 %convert_element_type.59 = f32[128,8192]{1,0:T(8,128)} convert(bf16[128,8192]{1,0:T(8,128)(2,1)} %param.10) | non-fusion elementwise | flops 1048576 | bytes 6291456 | tf_op jit(solution)/shard_map/convert_element_type | solution.py:34
  20.5 2.6 %multiply_convert_fusion.1 = bf16[128,2048]{0,1:T(8,128)(2,1)S(1)} fusion(f32[128,2048]{0,1:T(8,128)S(1)} %convert_element_type.63, f32[2048]{0:T(1024)S(1)} %bitcast.104, f32[2048]{0:T(1024)S(1)} %bitcast.106, f32[2048]{0:T(1024)S(1)} %bitcast.102, f32[2048]{0:T(1024)S(1)} %bitcast.100, f32[2048]{0:T(1024)S(1)} %copy-done.11), kind=kLoop, calls=%fused_computation.26 | loop fusion | flops 3407872 | bytes 1613824 | tf_op jit(solution)/shard_map/convert_element_type | solution.py:27
  23.2 7.8 %multiply_convert_fusion = bf16[128,8192]{1,0:T(8,128)(2,1)S(1)} fusion(f32[128,8192]{1,0:T(8,128)} %convert_element_type.59, f32[8192]{0:T(1024)S(1)} %bitcast.95, f32[8192]{0:T(1024)S(1)} %bitcast.97, f32[8192]{0:T(1024)S(1)} %bitcast.93, f32[8192]{0:T(1024)S(1)} %bitcast.91, f32[8192]{0:T(1024)S(1)} %copy-done.9), kind=kLoop, calls=%fused_computation.1 | loop fusion | flops 13631488 | bytes 6455296 | tf_op jit(solution)/shard_map/convert_element_type | solution.py:27
  31.6 2.0 dynamic_update_slice.7
  34.4 3.5 %all-to-all-start.1 = ((bf16[4,128,2,256]{1,3,2,0:T(8,128)(2,1)}), bf16[4,128,2,256]{1,3,2,0:T(8,128)(2,1)S(1)}, u32[]{:S(2)}, u32[]{:S(2)}) async-start(bf16[4,128,2,256]{1,3,2,0:T(8,128)(2,1)} %copy.83), calls=%async_computation.1 | async-start | bytes 1048576 | tf_op jit(solution)/shard_map/all_to_all | solution.py:167
  40.7 5.7 %all-to-all-done.1 = bf16[4,128,2,256]{1,3,2,0:T(8,128)(2,1)S(1)} async-done(((bf16[4,128,2,256]{1,3,2,0:T(8,128)(2,1)}), bf16[4,128,2,256]{1,3,2,0:T(8,128)(2,1)S(1)}, u32[]{:S(2)}, u32[]{:S(2)}) %all-to-all-start.1) | async-done | bytes 524320 | tf_op jit(solution)/shard_map/all_to_all | solution.py:167
  46.4 3.6 %all-to-all-start = ((bf16[128,4,2048]{2,0,1:T(8,128)(2,1)}), bf16[128,4,2048]{2,0,1:T(8,128)(2,1)S(1)}, u32[]{:S(2)}, u32[]{:S(2)}) async-start(bf16[128,4,2048]{2,0,1:T(8,128)(2,1)} %bitcast.86), calls=%async_computation | async-start | bytes 4194304 | tf_op jit(solution)/shard_map/all_to_all | solution.py:169
  52.8 2.6 %broadcast_in_dim.10 = f32[512,32,64]{0,2,1:T(8,128)} broadcast(f32[512,32]{0,1:T(8,128)S(1)} %get-tuple-element.27), dimensions={0,1} | broadcast | bytes 4259840 | tf_op jit(solution)/shard_map/broadcast_in_dim | solution.py:133
  55.3 5.4 %copy.91.fac_ref = f32[512,2048]{1,0:T(8,128)} copy(f32[512,2048]{0,1:T(8,128)} %bitcast.83) | data formatting | bytes 8388608 | tf_op jit(solution)/shard_map/reshape | solution.py:133
  62.3 12.3 %all-to-all-done = bf16[128,4,2048]{2,0,1:T(8,128)(2,1)S(1)} async-done(((bf16[128,4,2048]{2,0,1:T(8,128)(2,1)}), bf16[128,4,2048]{2,0,1:T(8,128)(2,1)S(1)}, u32[]{:S(2)}, u32[]{:S(2)}) %all-to-all-start) | async-done | bytes 2097184 | tf_op jit(solution)/shard_map/all_to_all | solution.py:169
  75.9 12.0 %ssd_fresh.1 = f32[256,2048]{1,0:T(8,128)} custom-call(bf16[512,2048]{1,0:T(8,128)(2,1)} %bitcast.88, bf16[256,512]{1,0:T(8,128)(2,1)} %slice_bitcast_fusion.1.bt_ref, f32[512,2048]{1,0:T(8,128)} %copy.91.fac_ref), custom_call_target="tpu_custom_call" | custom-call | flops 536870912 | bytes 8650752 | tf_op jit(solution)/shard_map/ssd_fresh/pallas_call | solution.py:113
  87.9 3.2 %select_maximum_fusion = f32[264,2048]{1,0:T(8,128)} fusion(f32[1,32]{1,0:T(1,128)S(1)} %bitcast.110, f32[256,2048]{1,0:T(8,128)} %ssd_fresh.1), kind=kLoop, calls=%fused_computation.10 | loop fusion | flops 1622016 | bytes 4259968 | tf_op jit(solution)/shard_map/concatenate | solution.py:206
  91.1 4.5 %collective-permute-done.2 = f32[264,2048]{1,0:T(8,128)S(1)} collective-permute-done((f32[264,2048]{1,0:T(8,128)}, f32[264,2048]{1,0:T(8,128)S(1)}, u32[]{:S(2)}, u32[]{:S(2)}) %collective-permute-start.2) | collective-permute-done | bytes 2162720 | tf_op jit(solution)/shard_map/ppermute | solution.py:205
  105.8 2.2 %multiply_add_fusion.4 = (f32[64,1024]{1,0:T(8,128)}, f32[64,1024]{1,0:T(8,128)}, f32[64,1024]{1,0:T(8,128)}, f32[64,1024]{1,0:T(8,128)}) fusion(f32[64,1024]{1,0:T(8,128)} %collective-permute-done.8, f32[256,1024]{1,0:T(8,128)S(1)} %select_add_fusion, f32[1024]{0:T(1024)S(1)} %mul.339, f32[64,1024]{1,0:T(8,128)} %collective-permute-done.3, ...), kind=kLoop, calls=%fused_computation.37 | loop fusion | flops 524288 | bytes 3149824 | tf_op jit(solution)/shard_map/add | solution.py:250
  115.4 1.7 pad.11.clone.cum_ref
  117.1 15.2 %ssd_intra.1 = (f32[512,2048]{1,0:T(8,128)}, f32[512,2048]{1,0:T(8,128)}) custom-call(bf16[512,2048]{1,0:T(8,128)(2,1)} %bitcast.89, f32[512,512]{1,0:T(8,128)} %fusion.12.s_ref, f32[512,128]{1,0:T(8,128)} %pad.11.clone.cum_ref, f32[32,512]{1,0:T(8,128)} %bitcast.99, f32[32,512]{1,0:T(8,128)} %bitcast.108, f32[1,2048]{1,0:T(1,128)} %broadcast_in_dim_reshape.2.skip_ref), custom_call_target="tpu_custom_call" | custom-call | flops 2147483648 | bytes 7340032 | tf_op jit(solution)/shard_map/ssd_intra/pallas_call | solution.py:87
  132.3 5.3 %collective-permute-done.9 = f32[64,1024]{1,0:T(8,128)} collective-permute-done((f32[64,1024]{1,0:T(8,128)}, f32[64,1024]{1,0:T(8,128)}, u32[]{:S(2)}, u32[]{:S(2)}) %collective-permute-start.9) | collective-permute-done | bytes 262176 | tf_op jit(solution)/shard_map/ppermute | solution.py:251
  138.7 4.6 %collective-permute-done.5 = f32[64,1024]{1,0:T(8,128)} collective-permute-done((f32[64,1024]{1,0:T(8,128)}, f32[64,1024]{1,0:T(8,128)}, u32[]{:S(2)}, u32[]{:S(2)}) %collective-permute-start.5) | collective-permute-done | bytes 262176 | tf_op jit(solution)/shard_map/ppermute | solution.py:251
  144.3 4.6 %collective-permute-done.7 = f32[64,1024]{1,0:T(8,128)} collective-permute-done((f32[64,1024]{1,0:T(8,128)}, f32[64,1024]{1,0:T(8,128)}, u32[]{:S(2)}, u32[]{:S(2)}) %collective-permute-start.7) | collective-permute-done | bytes 262176 | tf_op jit(solution)/shard_map/ppermute | solution.py:251
  149.9 3.2 %collective-permute-done.10 = f32[64,1024]{1,0:T(8,128)} collective-permute-done((f32[64,1024]{1,0:T(8,128)}, f32[64,1024]{1,0:T(8,128)}, u32[]{:S(2)}, u32[]{:S(2)}) %collective-permute-start.10) | collective-permute-done | bytes 262176 | tf_op jit(solution)/shard_map/ppermute | solution.py:251
  158.3 1.5 collective-permute-start.13
  159.8 2.6 %collective-permute-done.11 = f32[64,1024]{1,0:T(8,128)S(1)} collective-permute-done((f32[64,1024]{1,0:T(8,128)S(1)}, f32[64,1024]{1,0:T(8,128)S(1)}, u32[]{:S(2)}, u32[]{:S(2)}) %collective-permute-start.11) | collective-permute-done | bytes 262176 | tf_op jit(solution)/shard_map/ppermute | solution.py:251
  162.5 5.6 %collective-permute-done.14 = f32[64,1024]{1,0:T(8,128)S(1)} collective-permute-done((f32[64,1024]{1,0:T(8,128)S(1)}, f32[64,1024]{1,0:T(8,128)S(1)}, u32[]{:S(2)}, u32[]{:S(2)}) %collective-permute-start.14) | collective-permute-done | bytes 262176 | tf_op jit(solution)/shard_map/ppermute | solution.py:251
  168.1 5.6 %collective-permute-done.12 = f32[64,1024]{1,0:T(8,128)S(1)} collective-permute-done((f32[64,1024]{1,0:T(8,128)S(1)}, f32[64,1024]{1,0:T(8,128)S(1)}, u32[]{:S(2)}, u32[]{:S(2)}) %collective-permute-start.12) | collective-permute-done | bytes 262176 | tf_op jit(solution)/shard_map/ppermute | solution.py:251
  173.7 3.5 %collective-permute-done.13 = f32[64,1024]{1,0:T(8,128)S(1)} collective-permute-done((f32[64,1024]{1,0:T(8,128)S(1)}, f32[64,1024]{1,0:T(8,128)S(1)}, u32[]{:S(2)}, u32[]{:S(2)}) %collective-permute-start.13) | collective-permute-done | bytes 262176 | tf_op jit(solution)/shard_map/ppermute | solution.py:251
  179.2 2.9 %collective-permute-done.15 = f32[256,1024]{1,0:T(8,128)} collective-permute-done((f32[256,1024]{1,0:T(8,128)}, f32[256,1024]{1,0:T(8,128)}, u32[]{:S(2)}, u32[]{:S(2)}) %collective-permute-start.15) | collective-permute-done | bytes 1048608 | tf_op jit(solution)/shard_map/ppermute | solution.py:256
  182.0 1.5 broadcast_select_fusion
  188.3 28.4 %all_to_all.56 = bf16[4,128,2048]{2,1,0:T(8,128)(2,1)S(1)} all-to-all(bf16[4,128,2048]{2,1,0:T(8,128)(2,1)S(1)} %bitcast.85), channel_id=1, replica_groups=mesh['ctx'=8,'tp'=4] {'tp'}, dimensions={0} | all-to-all | bytes 4194304 | tf_op jit(solution)/shard_map/all_to_all | solution.py:278
  (118 shorter events, 47.5 us)
Async XLA Ops:
  1.5 32.9 %all-to-all-start.2 = ((bf16[128,4,32]{0,2,1:T(8,128)(2,1)}), bf16[128,4,32]{0,2,1:T(8,128)(2,1)S(1)}, u32[]{:S(2)}, u32[]{:S(2)}) async-start(bf16[128,4,32]{0,2,1:T(8,128)(2,1)} %bitcast.14), calls=%async_computation.2 | async-start | bytes 65536 | tf_op jit(solution)/shard_map/all_to_all | solution.py:170
  6.0 25.2 %collective-permute-start.1 = (bf16[3,2048]{1,0:T(4,128)(2,1)S(1)}, bf16[3,2048]{1,0:T(4,128)(2,1)S(1)}, u32[]{:S(2)}, u32[]{:S(2)}) collective-permute-start(bf16[3,2048]{1,0:T(4,128)(2,1)S(1)} %get-tuple-element.48), channel_id=1, source_target_pairs={{0,1},{1,2},{2,3},{3,4},{4,5},{5,6},{6,7},{7,8},{8,9},{9,10},{10,1... | collective-permute-start | bytes 36872 | tf_op jit(solution)/shard_map/ppermute | solution.py:20
  11.6 26.4 %collective-permute-start = (bf16[3,8192]{1,0:T(4,128)(2,1)}, bf16[3,8192]{1,0:T(4,128)(2,1)S(1)}, u32[]{:S(2)}, u32[]{:S(2)}) collective-permute-start(bf16[3,8192]{1,0:T(4,128)(2,1)} %get-tuple-element.34), channel_id=1, source_target_pairs={{0,1},{1,2},{2,3},{3,4},{4,5},{5,6},{6,7},{7,8},{8,9},{9,10},{10,1... | collective-permute-start | bytes 147464 | tf_op jit(solution)/shard_map/ppermute | solution.py:20
  16.3 4.1 %copy-start.12 = (f32[4,2048]{1,0:T(4,128)S(1)}, f32[4,2048]{1,0:T(4,128)}, u32[]{:S(2)}) copy-start(f32[4,2048]{1,0:T(4,128)} %param.15) | copy-start | bytes 98308
  16.3 4.1 %copy-start.10 = (f32[4,8192]{1,0:T(4,128)S(1)}, f32[4,8192]{1,0:T(4,128)}, u32[]{:S(2)}) copy-start(f32[4,8192]{1,0:T(4,128)} %param.13) | copy-start | bytes 393220
  16.3 4.3 %copy-start.11 = (f32[2048]{0:T(1024)S(1)}, f32[2048]{0:T(1024)}, u32[]{:S(2)}) copy-start(f32[2048]{0:T(1024)} %param.16) | copy-start | bytes 24580
  20.3 2.9 %copy-start.9 = (f32[8192]{0:T(1024)S(1)}, f32[8192]{0:T(1024)}, u32[]{:S(2)}) copy-start(f32[8192]{0:T(1024)} %param.14) | copy-start | bytes 98308
  23.2 7.8 %copy-start.13 = (f32[128]{0:T(128)S(1)}, f32[128]{0:T(128)}, u32[]{:S(2)}) copy-start(f32[128]{0:T(128)} %param.18) | copy-start | bytes 1540
  23.2 7.9 %copy-start.14 = (f32[128]{0:T(128)S(1)}, f32[128]{0:T(128)}, u32[]{:S(2)}) copy-start(f32[128]{0:T(128)} %param.17) | copy-start | bytes 1540
  34.4 12.0 %all-to-all-start.1 = ((bf16[4,128,2,256]{1,3,2,0:T(8,128)(2,1)}), bf16[4,128,2,256]{1,3,2,0:T(8,128)(2,1)S(1)}, u32[]{:S(2)}, u32[]{:S(2)}) async-start(bf16[4,128,2,256]{1,3,2,0:T(8,128)(2,1)} %copy.83), calls=%async_computation.1 | async-start | bytes 1048576 | tf_op jit(solution)/shard_map/all_to_all | solution.py:167
  46.4 28.2 %all-to-all-start = ((bf16[128,4,2048]{2,0,1:T(8,128)(2,1)}), bf16[128,4,2048]{2,0,1:T(8,128)(2,1)S(1)}, u32[]{:S(2)}, u32[]{:S(2)}) async-start(bf16[128,4,2048]{2,0,1:T(8,128)(2,1)} %bitcast.86), calls=%async_computation | async-start | bytes 4194304 | tf_op jit(solution)/shard_map/all_to_all | solution.py:169
  52.8 61.8 %copy-start.8 = (f32[512,32]{0,1:T(8,128)}, f32[512,32]{0,1:T(8,128)S(1)}, u32[]{:S(2)}) copy-start(f32[512,32]{0,1:T(8,128)S(1)} %get-tuple-element.17) | copy-start | bytes 196612
  91.1 4.5 %collective-permute-start.2 = (f32[264,2048]{1,0:T(8,128)}, f32[264,2048]{1,0:T(8,128)S(1)}, u32[]{:S(2)}, u32[]{:S(2)}) collective-permute-start(f32[264,2048]{1,0:T(8,128)} %select_maximum_fusion), channel_id=1, source_target_pairs={{0,4},{4,0},{8,12},{12,8},{16,20},{20,16},{24,28},{28,24},{1,5},{5... | collective-permute-start | bytes 6488072 | tf_op jit(solution)/shard_map/ppermute | solution.py:205
  96.0 1.6 copy-start
  97.6 6.0 %copy-start.15 = (f32[128]{0:T(128)S(1)}, f32[128]{0:T(128)}, u32[]{:S(2)}) copy-start(f32[128]{0:T(128)} %param.19) | copy-start | bytes 1540
  98.9 6.9 %collective-permute-start.8 = (f32[64,1024]{1,0:T(8,128)}, f32[64,1024]{1,0:T(8,128)}, u32[]{:S(2)}, u32[]{:S(2)}) collective-permute-start(f32[64,1024]{1,0:T(8,128)} %get-tuple-element.44), channel_id=1, source_target_pairs={{0,8},{4,12},{1,9},{5,13},{2,10},{6,14},{3,11},{7,15}} | collective-permute-start | bytes 786440 | tf_op jit(solution)/shard_map/ppermute | solution.py:251
  100.3 5.5 %collective-permute-start.6 = (f32[64,1024]{1,0:T(8,128)}, f32[64,1024]{1,0:T(8,128)S(1)}, u32[]{:S(2)}, u32[]{:S(2)}) collective-permute-start(f32[64,1024]{1,0:T(8,128)} %get-tuple-element.45), channel_id=1, source_target_pairs={{0,8},{4,12},{1,9},{5,13},{2,10},{6,14},{3,11},{7,15}} | collective-permute-start | bytes 786440 | tf_op jit(solution)/shard_map/ppermute | solution.py:251
  100.9 4.9 %collective-permute-start.4 = (f32[64,1024]{1,0:T(8,128)}, f32[64,1024]{1,0:T(8,128)}, u32[]{:S(2)}, u32[]{:S(2)}) collective-permute-start(f32[64,1024]{1,0:T(8,128)} %get-tuple-element.46), channel_id=1, source_target_pairs={{0,8},{4,12},{1,9},{5,13},{2,10},{6,14},{3,11},{7,15}} | collective-permute-start | bytes 786440 | tf_op jit(solution)/shard_map/ppermute | solution.py:251
  102.3 3.5 %collective-permute-start.3 = (f32[64,1024]{1,0:T(8,128)}, f32[64,1024]{1,0:T(8,128)}, u32[]{:S(2)}, u32[]{:S(2)}) collective-permute-start(f32[64,1024]{1,0:T(8,128)} %get-tuple-element.47), channel_id=1, source_target_pairs={{0,8},{4,12},{1,9},{5,13},{2,10},{6,14},{3,11},{7,15}} | collective-permute-start | bytes 786440 | tf_op jit(solution)/shard_map/ppermute | solution.py:251
  105.8 7.4 %copy-start.3 = (bf16[512,2,256]{0,2,1:T(8,128)(2,1)S(1)}, bf16[512,2,256]{0,2,1:T(8,128)(2,1)}, u32[]{:S(2)}) copy-start(bf16[512,2,256]{0,2,1:T(8,128)(2,1)} %copy-done.2) | copy-start | bytes 1572868
  108.0 29.6 %collective-permute-start.9 = (f32[64,1024]{1,0:T(8,128)}, f32[64,1024]{1,0:T(8,128)}, u32[]{:S(2)}, u32[]{:S(2)}) collective-permute-start(f32[64,1024]{1,0:T(8,128)} %get-tuple-element.40), channel_id=1, source_target_pairs={{8,16},{12,20},{9,17},{13,21},{10,18},{14,22},{11,19},{15,23}} | collective-permute-start | bytes 786440 | tf_op jit(solution)/shard_map/ppermute | solution.py:251
  109.3 34.0 %collective-permute-start.5 = (f32[64,1024]{1,0:T(8,128)}, f32[64,1024]{1,0:T(8,128)}, u32[]{:S(2)}, u32[]{:S(2)}) collective-permute-start(f32[64,1024]{1,0:T(8,128)} %get-tuple-element.42), channel_id=1, source_target_pairs={{8,16},{12,20},{9,17},{13,21},{10,18},{14,22},{11,19},{15,23}} | collective-permute-start | bytes 786440 | tf_op jit(solution)/shard_map/ppermute | solution.py:251
  110.6 38.3 %collective-permute-start.7 = (f32[64,1024]{1,0:T(8,128)}, f32[64,1024]{1,0:T(8,128)}, u32[]{:S(2)}, u32[]{:S(2)}) collective-permute-start(f32[64,1024]{1,0:T(8,128)} %get-tuple-element.43), channel_id=1, source_target_pairs={{8,16},{12,20},{9,17},{13,21},{10,18},{14,22},{11,19},{15,23}} | collective-permute-start | bytes 786440 | tf_op jit(solution)/shard_map/ppermute | solution.py:251
  111.9 41.2 %collective-permute-start.10 = (f32[64,1024]{1,0:T(8,128)}, f32[64,1024]{1,0:T(8,128)}, u32[]{:S(2)}, u32[]{:S(2)}) collective-permute-start(f32[64,1024]{1,0:T(8,128)} %get-tuple-element.41), channel_id=1, source_target_pairs={{8,16},{12,20},{9,17},{13,21},{10,18},{14,22},{11,19},{15,23}} | collective-permute-start | bytes 786440 | tf_op jit(solution)/shard_map/ppermute | solution.py:251
  154.4 8.0 %collective-permute-start.11 = (f32[64,1024]{1,0:T(8,128)S(1)}, f32[64,1024]{1,0:T(8,128)S(1)}, u32[]{:S(2)}, u32[]{:S(2)}) collective-permute-start(f32[64,1024]{1,0:T(8,128)S(1)} %get-tuple-element.36), channel_id=1, source_target_pairs={{16,24},{20,28},{17,25},{21,29},{18,26},{22,30},{19,27},{23,31}} | collective-permute-start | bytes 786440 | tf_op jit(solution)/shard_map/ppermute | solution.py:251
  155.7 12.3 %collective-permute-start.14 = (f32[64,1024]{1,0:T(8,128)S(1)}, f32[64,1024]{1,0:T(8,128)S(1)}, u32[]{:S(2)}, u32[]{:S(2)}) collective-permute-start(f32[64,1024]{1,0:T(8,128)S(1)} %get-tuple-element.37), channel_id=1, source_target_pairs={{16,24},{20,28},{17,25},{21,29},{18,26},{22,30},{19,27},{23,31}} | collective-permute-start | bytes 786440 | tf_op jit(solution)/shard_map/ppermute | solution.py:251
  157.0 16.6 %collective-permute-start.12 = (f32[64,1024]{1,0:T(8,128)S(1)}, f32[64,1024]{1,0:T(8,128)S(1)}, u32[]{:S(2)}, u32[]{:S(2)}) collective-permute-start(f32[64,1024]{1,0:T(8,128)S(1)} %get-tuple-element.38), channel_id=1, source_target_pairs={{16,24},{20,28},{17,25},{21,29},{18,26},{22,30},{19,27},{23,31}} | collective-permute-start | bytes 786440 | tf_op jit(solution)/shard_map/ppermute | solution.py:251
  158.3 18.9 %collective-permute-start.13 = (f32[64,1024]{1,0:T(8,128)S(1)}, f32[64,1024]{1,0:T(8,128)S(1)}, u32[]{:S(2)}, u32[]{:S(2)}) collective-permute-start(f32[64,1024]{1,0:T(8,128)S(1)} %get-tuple-element.39), channel_id=1, source_target_pairs={{16,24},{20,28},{17,25},{21,29},{18,26},{22,30},{19,27},{23,31}} | collective-permute-start | bytes 786440 | tf_op jit(solution)/shard_map/ppermute | solution.py:251
  179.0 4.5 %copy-start.4 = (bf16[512,2,256]{0,2,1:T(8,128)(2,1)S(1)}, bf16[512,2,256]{0,2,1:T(8,128)(2,1)}, u32[]{:S(2)}) copy-start(bf16[512,2,256]{0,2,1:T(8,128)(2,1)} %copy-done.2) | copy-start | bytes 1572868
  179.0 3.0 %collective-permute-start.15 = (f32[256,1024]{1,0:T(8,128)}, f32[256,1024]{1,0:T(8,128)}, u32[]{:S(2)}, u32[]{:S(2)}) collective-permute-start(f32[256,1024]{1,0:T(8,128)} %pad_maximum_fusion.1), channel_id=1, source_target_pairs={{0,4},{4,0},{8,12},{12,8},{16,20},{20,16},{24,28},{28,24},{1,5},{5... | collective-permute-start | bytes 3145736 | tf_op jit(solution)/shard_map/ppermute | solution.py:256
  183.5 2.2 %copy-start.5 = (f32[512,2048]{1,0:T(8,128)S(1)}, f32[512,2048]{1,0:T(8,128)}, u32[]{:S(2)}) copy-start(f32[512,2048]{1,0:T(8,128)} %get-tuple-element.19) | copy-start | bytes 12582916
  183.5 3.5 %copy-start.6 = (f32[512,2048]{1,0:T(8,128)S(1)}, f32[512,2048]{1,0:T(8,128)}, u32[]{:S(2)}) copy-start(f32[512,2048]{1,0:T(8,128)} %get-tuple-element.20) | copy-start | bytes 12582916
  (3 other events, 2.8 us)

commit v12 on v10

--- a/solution.py
+++ b/solution.py
@@ -157,7 +157,10 @@
     per_group = H // G
     rim = CONV - 1
 
-    prior_x, prior_bc = from_behind((x_in[rows - rim :], bc_in[rows - rim :]), ("ctx", "tp"), 1)
+    prior = from_behind(
+        jnp.concatenate([x_in[rows - rim :], bc_in[rows - rim :]], axis=1), ("ctx", "tp"), 1
+    )
+    prior_x, prior_bc = prior[:, : x_in.shape[1]], prior[:, x_in.shape[1] :]
     x_part = conv_silu(x_in, prior_x, conv_x_weight, conv_x_bias)
     bc_part = conv_silu(bc_in, prior_bc, conv_bc_weight, conv_bc_bias)
 

time: 217 us -> 213 us (0.982)
  starting transfers between devices: 33.4 us -> 30.1 us
    ppermute x2 -> x1, starting transfers between devices: 7.29 us -> 3.93 us  [from_behind(): lax.ppermute(value, axis, [(source, source + steps) for source in range(i...]
    unnamed x35 -> x37, local copies, waits for them, and re-layouts: 10.4 us -> 11 us
  transfers between devices with their start and end apart: 19 -> 18, of which waited for: 12 -> 12; matrix products, arithmetic and copies ran while one was open for 21% -> 20% of each run, Pallas kernels for 7% -> 7%
where the time goes in v12:
time: 213 us; the launch traced here: 211 us
  waiting for transfers between devices  58.4 us (27%)
  local copies, waits for them, and re-layouts  35 us (16%)
  other arithmetic  30.6 us (14%)
  starting transfers between devices  30.1 us (14%)
  blocking collectives  28.4 us (13%)
  Pallas kernels  24 us (11%)
  matrix products  3.44 us (2%)
    ppermute x12, waiting for transfers between devices, on_device(): acc[k] = acc[k] + lax.ppermute(send, 'ctx', pairs)  34.9 us
    all_to_all x1, blocking collectives, on_device(): return lax.all_to_all(result, 'tp', split_axis=0, concat_axis=1, tiled=True)  28.4 us
    ppermute x12, starting transfers between devices, on_device(): acc[k] = acc[k] + lax.ppermute(send, 'ctx', pairs)  15.3 us
    pallas_call x1, Pallas kernels, intra_block(): pl.pallas_call(intra_kernel, out_shape=(jax.ShapeDtypeStruct((BLOCK, widt...  15.2 us
    all_to_all x1, waiting for transfers between devices, on_device(): lax.all_to_all(x_part, 'tp', split_axis=1, concat_axis=0, tiled=True)  11.7 us
    unnamed x37, local copies, waits for them, and re-layouts  11 us
    convert_element_type x4, other arithmetic, conv_rows(): return jax.nn.silu(total).astype(jnp.bfloat16)  10.6 us
    pallas_call x1, Pallas kernels, fresh_block(): pl.pallas_call(fresh_kernel, out_shape=jax.ShapeDtypeStruct((N, width), j...  8.71 us
  transfers between devices with their start and end apart: 18, of which 12 were waited for; matrix products, arithmetic and copies ran while one was open for 20% of the time, Pallas kernels for 7%

profile of v12, /device:TPU:16, one launch (start us, length us, event | category | flops | bytes accessed | tf_op | source)
XLA Modules:
  0.0 210.5 jit_solution(4977043651417597890)
XLA Ops:
  0.0 1.5 copy.89
  1.5 3.7 %all-to-all-start.2 = ((bf16[128,4,32]{0,2,1:T(8,128)(2,1)}), bf16[128,4,32]{0,2,1:T(8,128)(2,1)S(1)}, u32[]{:S(2)}, u32[]{:S(2)}) async-start(bf16[128,4,32]{0,2,1:T(8,128)(2,1)} %bitcast.14), calls=%async_computation.2 | async-start | bytes 65536 | tf_op jit(solution)/shard_map/all_to_all | solution.py:175
  7.1 3.9 %collective-permute-start = (bf16[3,10240]{1,0:T(4,128)(2,1)S(1)}, bf16[3,10240]{1,0:T(4,128)(2,1)S(1)}, u32[]{:S(2)}, u32[]{:S(2)}) collective-permute-start(bf16[3,10240]{1,0:T(4,128)(2,1)S(1)} %pad_maximum_fusion.2), channel_id=1, source_target_pairs={{0,1},{1,2},{2,3},{3,4},{4,5},{5,6},{6,7},{7,8},{8,9},{9,10},{10,1... | collective-permute-start | bytes 184328 | tf_op jit(solution)/shard_map/ppermute | solution.py:20
  12.4 4.0 %convert_element_type.59 = f32[128,8192]{1,0:T(8,128)} convert(bf16[128,8192]{1,0:T(8,128)(2,1)} %param.10) | non-fusion elementwise | flops 1048576 | bytes 6291456 | tf_op jit(solution)/shard_map/convert_element_type | solution.py:34
  16.6 2.6 %multiply_convert_fusion.1 = bf16[128,2048]{0,1:T(8,128)(2,1)S(1)} fusion(f32[128,2048]{0,1:T(8,128)S(1)} %convert_element_type.63, f32[2048]{0:T(1024)S(1)} %bitcast.104, f32[2048]{0:T(1024)S(1)} %bitcast.106, f32[2048]{0:T(1024)S(1)} %bitcast.102, f32[2048]{0:T(1024)S(1)} %bitcast.100, f32[2048]{0:T(1024)S(1)} %copy-done.12), kind=kLoop, calls=%fused_computation.26 | loop fusion | flops 3407872 | bytes 1613824 | tf_op jit(solution)/shard_map/convert_element_type | solution.py:27
  19.3 7.8 %multiply_convert_fusion = bf16[128,8192]{1,0:T(8,128)(2,1)S(1)} fusion(f32[128,8192]{1,0:T(8,128)} %convert_element_type.59, f32[8192]{0:T(1024)S(1)} %bitcast.95, f32[8192]{0:T(1024)S(1)} %bitcast.97, f32[8192]{0:T(1024)S(1)} %bitcast.93, f32[8192]{0:T(1024)S(1)} %bitcast.91, f32[8192]{0:T(1024)S(1)} %copy-done.9), kind=kLoop, calls=%fused_computation.1 | loop fusion | flops 13631488 | bytes 6455296 | tf_op jit(solution)/shard_map/convert_element_type | solution.py:27
  28.3 2.0 dynamic_update_slice.7
  31.1 3.5 %all-to-all-start.1 = ((bf16[4,128,2,256]{1,3,2,0:T(8,128)(2,1)}), bf16[4,128,2,256]{1,3,2,0:T(8,128)(2,1)S(1)}, u32[]{:S(2)}, u32[]{:S(2)}) async-start(bf16[4,128,2,256]{1,3,2,0:T(8,128)(2,1)} %copy.87), calls=%async_computation.1 | async-start | bytes 1048576 | tf_op jit(solution)/shard_map/all_to_all | solution.py:172
  36.7 1.5 copy.116
  38.2 4.4 %all-to-all-done.1 = bf16[4,128,2,256]{1,3,2,0:T(8,128)(2,1)S(1)} async-done(((bf16[4,128,2,256]{1,3,2,0:T(8,128)(2,1)}), bf16[4,128,2,256]{1,3,2,0:T(8,128)(2,1)S(1)}, u32[]{:S(2)}, u32[]{:S(2)}) %all-to-all-start.1) | async-done | bytes 524320 | tf_op jit(solution)/shard_map/all_to_all | solution.py:172
  42.6 3.6 %all-to-all-start = ((bf16[128,4,2048]{2,0,1:T(8,128)(2,1)}), bf16[128,4,2048]{2,0,1:T(8,128)(2,1)S(1)}, u32[]{:S(2)}, u32[]{:S(2)}) async-start(bf16[128,4,2048]{2,0,1:T(8,128)(2,1)} %bitcast.86), calls=%async_computation | async-start | bytes 4194304 | tf_op jit(solution)/shard_map/all_to_all | solution.py:174
  49.0 2.6 %broadcast_in_dim.10 = f32[512,32,64]{0,2,1:T(8,128)} broadcast(f32[512,32]{0,1:T(8,128)S(1)} %get-tuple-element.27), dimensions={0,1} | broadcast | bytes 4259840 | tf_op jit(solution)/shard_map/broadcast_in_dim | solution.py:135
  51.5 5.4 %copy.95.fac_ref = f32[512,2048]{1,0:T(8,128)} copy(f32[512,2048]{0,1:T(8,128)} %bitcast.83) | data formatting | bytes 8388608 | tf_op jit(solution)/shard_map/reshape | solution.py:135
  58.5 11.7 %all-to-all-done = bf16[128,4,2048]{2,0,1:T(8,128)(2,1)S(1)} async-done(((bf16[128,4,2048]{2,0,1:T(8,128)(2,1)}), bf16[128,4,2048]{2,0,1:T(8,128)(2,1)S(1)}, u32[]{:S(2)}, u32[]{:S(2)}) %all-to-all-start) | async-done | bytes 2097184 | tf_op jit(solution)/shard_map/all_to_all | solution.py:174
  71.6 8.7 %ssd_fresh.1 = f32[256,2048]{1,0:T(8,128)} custom-call(bf16[512,2048]{1,0:T(8,128)(2,1)} %bitcast.88, bf16[256,512]{1,0:T(8,128)(2,1)} %slice_bitcast_fusion.1.bt_ref, f32[512,2048]{1,0:T(8,128)} %copy.95.fac_ref), custom_call_target="tpu_custom_call" | custom-call | flops 536870912 | bytes 8650752 | tf_op jit(solution)/shard_map/ssd_fresh/pallas_call | solution.py:120
  80.3 3.2 %select_maximum_fusion = f32[264,2048]{1,0:T(8,128)} fusion(f32[1,32]{1,0:T(1,128)S(1)} %bitcast.110, f32[256,2048]{1,0:T(8,128)} %ssd_fresh.1), kind=kLoop, calls=%fused_computation.10 | loop fusion | flops 1622016 | bytes 4259968 | tf_op jit(solution)/shard_map/concatenate | solution.py:211
  83.5 4.5 %collective-permute-done.1 = f32[264,2048]{1,0:T(8,128)S(1)} collective-permute-done((f32[264,2048]{1,0:T(8,128)}, f32[264,2048]{1,0:T(8,128)S(1)}, u32[]{:S(2)}, u32[]{:S(2)}) %collective-permute-start.1) | collective-permute-done | bytes 2162720 | tf_op jit(solution)/shard_map/ppermute | solution.py:210
  98.2 2.2 %multiply_add_fusion.4 = (f32[64,1024]{1,0:T(8,128)}, f32[64,1024]{1,0:T(8,128)}, f32[64,1024]{1,0:T(8,128)}, f32[64,1024]{1,0:T(8,128)}) fusion(f32[64,1024]{1,0:T(8,128)} %collective-permute-done.7, f32[256,1024]{1,0:T(8,128)S(1)} %select_add_fusion, f32[1024]{0:T(1024)S(1)} %mul.339, f32[64,1024]{1,0:T(8,128)} %collective-permute-done.2, ...), kind=kLoop, calls=%fused_computation.37 | loop fusion | flops 524288 | bytes 3149824 | tf_op jit(solution)/shard_map/add | solution.py:255
  107.8 1.7 pad.11.clone.cum_ref
  109.5 15.2 %ssd_intra.1 = (f32[512,2048]{1,0:T(8,128)}, f32[512,2048]{1,0:T(8,128)}) custom-call(bf16[512,2048]{1,0:T(8,128)(2,1)} %bitcast.89, f32[512,512]{1,0:T(8,128)} %fusion.12.s_ref, f32[512,128]{1,0:T(8,128)} %pad.11.clone.cum_ref, f32[32,512]{1,0:T(8,128)} %bitcast.99, f32[32,512]{1,0:T(8,128)} %bitcast.108, f32[1,2048]{1,0:T(1,128)} %broadcast_in_dim_reshape.2.skip_ref), custom_call_target="tpu_custom_call" | custom-call | flops 2147483648 | bytes 7340032 | tf_op jit(solution)/shard_map/ssd_intra/pallas_call | solution.py:87
  124.7 5.3 %collective-permute-done.8 = f32[64,1024]{1,0:T(8,128)} collective-permute-done((f32[64,1024]{1,0:T(8,128)}, f32[64,1024]{1,0:T(8,128)}, u32[]{:S(2)}, u32[]{:S(2)}) %collective-permute-start.8) | collective-permute-done | bytes 262176 | tf_op jit(solution)/shard_map/ppermute | solution.py:256
  131.1 4.6 %collective-permute-done.4 = f32[64,1024]{1,0:T(8,128)} collective-permute-done((f32[64,1024]{1,0:T(8,128)}, f32[64,1024]{1,0:T(8,128)}, u32[]{:S(2)}, u32[]{:S(2)}) %collective-permute-start.4) | collective-permute-done | bytes 262176 | tf_op jit(solution)/shard_map/ppermute | solution.py:256
  136.7 4.6 %collective-permute-done.6 = f32[64,1024]{1,0:T(8,128)} collective-permute-done((f32[64,1024]{1,0:T(8,128)}, f32[64,1024]{1,0:T(8,128)}, u32[]{:S(2)}, u32[]{:S(2)}) %collective-permute-start.6) | collective-permute-done | bytes 262176 | tf_op jit(solution)/shard_map/ppermute | solution.py:256
  142.3 3.2 %collective-permute-done.9 = f32[64,1024]{1,0:T(8,128)} collective-permute-done((f32[64,1024]{1,0:T(8,128)}, f32[64,1024]{1,0:T(8,128)}, u32[]{:S(2)}, u32[]{:S(2)}) %collective-permute-start.9) | collective-permute-done | bytes 262176 | tf_op jit(solution)/shard_map/ppermute | solution.py:256
  150.7 1.5 collective-permute-start.12
  152.2 2.6 %collective-permute-done.10 = f32[64,1024]{1,0:T(8,128)S(1)} collective-permute-done((f32[64,1024]{1,0:T(8,128)S(1)}, f32[64,1024]{1,0:T(8,128)S(1)}, u32[]{:S(2)}, u32[]{:S(2)}) %collective-permute-start.10) | collective-permute-done | bytes 262176 | tf_op jit(solution)/shard_map/ppermute | solution.py:256
  154.8 5.6 %collective-permute-done.13 = f32[64,1024]{1,0:T(8,128)S(1)} collective-permute-done((f32[64,1024]{1,0:T(8,128)S(1)}, f32[64,1024]{1,0:T(8,128)S(1)}, u32[]{:S(2)}, u32[]{:S(2)}) %collective-permute-start.13) | collective-permute-done | bytes 262176 | tf_op jit(solution)/shard_map/ppermute | solution.py:256
  160.5 5.6 %collective-permute-done.11 = f32[64,1024]{1,0:T(8,128)S(1)} collective-permute-done((f32[64,1024]{1,0:T(8,128)S(1)}, f32[64,1024]{1,0:T(8,128)S(1)}, u32[]{:S(2)}, u32[]{:S(2)}) %collective-permute-start.11) | collective-permute-done | bytes 262176 | tf_op jit(solution)/shard_map/ppermute | solution.py:256
  166.1 3.5 %collective-permute-done.12 = f32[64,1024]{1,0:T(8,128)S(1)} collective-permute-done((f32[64,1024]{1,0:T(8,128)S(1)}, f32[64,1024]{1,0:T(8,128)S(1)}, u32[]{:S(2)}, u32[]{:S(2)}) %collective-permute-start.12) | collective-permute-done | bytes 262176 | tf_op jit(solution)/shard_map/ppermute | solution.py:256
  171.5 2.9 %collective-permute-done.14 = f32[256,1024]{1,0:T(8,128)} collective-permute-done((f32[256,1024]{1,0:T(8,128)}, f32[256,1024]{1,0:T(8,128)}, u32[]{:S(2)}, u32[]{:S(2)}) %collective-permute-start.14) | collective-permute-done | bytes 1048608 | tf_op jit(solution)/shard_map/ppermute | solution.py:261
  174.4 1.5 broadcast_select_fusion
  180.6 28.4 %all_to_all.56 = bf16[4,128,2048]{2,1,0:T(8,128)(2,1)S(1)} all-to-all(bf16[4,128,2048]{2,1,0:T(8,128)(2,1)S(1)} %bitcast.85), channel_id=1, replica_groups=mesh['ctx'=8,'tp'=4] {'tp'}, dimensions={0} | all-to-all | bytes 4194304 | tf_op jit(solution)/shard_map/all_to_all | solution.py:283
  (121 shorter events, 47.1 us)
Async XLA Ops:
  1.5 25.7 %all-to-all-start.2 = ((bf16[128,4,32]{0,2,1:T(8,128)(2,1)}), bf16[128,4,32]{0,2,1:T(8,128)(2,1)S(1)}, u32[]{:S(2)}, u32[]{:S(2)}) async-start(bf16[128,4,32]{0,2,1:T(8,128)(2,1)} %bitcast.14), calls=%async_computation.2 | async-start | bytes 65536 | tf_op jit(solution)/shard_map/all_to_all | solution.py:175
  7.1 20.3 %collective-permute-start = (bf16[3,10240]{1,0:T(4,128)(2,1)S(1)}, bf16[3,10240]{1,0:T(4,128)(2,1)S(1)}, u32[]{:S(2)}, u32[]{:S(2)}) collective-permute-start(bf16[3,10240]{1,0:T(4,128)(2,1)S(1)} %pad_maximum_fusion.2), channel_id=1, source_target_pairs={{0,1},{1,2},{2,3},{3,4},{4,5},{5,6},{6,7},{7,8},{8,9},{9,10},{10,1... | collective-permute-start | bytes 184328 | tf_op jit(solution)/shard_map/ppermute | solution.py:20
  12.3 4.1 %copy-start.13 = (f32[4,2048]{1,0:T(4,128)S(1)}, f32[4,2048]{1,0:T(4,128)}, u32[]{:S(2)}) copy-start(f32[4,2048]{1,0:T(4,128)} %param.15) | copy-start | bytes 98308
  12.3 4.1 %copy-start.10 = (f32[4,8192]{1,0:T(4,128)S(1)}, f32[4,8192]{1,0:T(4,128)}, u32[]{:S(2)}) copy-start(f32[4,8192]{1,0:T(4,128)} %param.13) | copy-start | bytes 393220
  12.3 4.3 %copy-start.12 = (f32[2048]{0:T(1024)S(1)}, f32[2048]{0:T(1024)}, u32[]{:S(2)}) copy-start(f32[2048]{0:T(1024)} %param.16) | copy-start | bytes 24580
  16.4 2.9 %copy-start.9 = (f32[8192]{0:T(1024)S(1)}, f32[8192]{0:T(1024)}, u32[]{:S(2)}) copy-start(f32[8192]{0:T(1024)} %param.14) | copy-start | bytes 98308
  19.2 7.8 %copy-start.14 = (f32[128]{0:T(128)S(1)}, f32[128]{0:T(128)}, u32[]{:S(2)}) copy-start(f32[128]{0:T(128)} %param.18) | copy-start | bytes 1540
  19.3 7.9 %copy-start.15 = (f32[128]{0:T(128)S(1)}, f32[128]{0:T(128)}, u32[]{:S(2)}) copy-start(f32[128]{0:T(128)} %param.17) | copy-start | bytes 1540
  31.1 11.5 %all-to-all-start.1 = ((bf16[4,128,2,256]{1,3,2,0:T(8,128)(2,1)}), bf16[4,128,2,256]{1,3,2,0:T(8,128)(2,1)S(1)}, u32[]{:S(2)}, u32[]{:S(2)}) async-start(bf16[4,128,2,256]{1,3,2,0:T(8,128)(2,1)} %copy.87), calls=%async_computation.1 | async-start | bytes 1048576 | tf_op jit(solution)/shard_map/all_to_all | solution.py:172
  42.6 27.6 %all-to-all-start = ((bf16[128,4,2048]{2,0,1:T(8,128)(2,1)}), bf16[128,4,2048]{2,0,1:T(8,128)(2,1)S(1)}, u32[]{:S(2)}, u32[]{:S(2)}) async-start(bf16[128,4,2048]{2,0,1:T(8,128)(2,1)} %bitcast.86), calls=%async_computation | async-start | bytes 4194304 | tf_op jit(solution)/shard_map/all_to_all | solution.py:174
  49.0 58.0 %copy-start.8 = (f32[512,32]{0,1:T(8,128)}, f32[512,32]{0,1:T(8,128)S(1)}, u32[]{:S(2)}) copy-start(f32[512,32]{0,1:T(8,128)S(1)} %get-tuple-element.17) | copy-start | bytes 196612
  70.2 1.3 copy-start.1
  83.5 4.5 %collective-permute-start.1 = (f32[264,2048]{1,0:T(8,128)}, f32[264,2048]{1,0:T(8,128)S(1)}, u32[]{:S(2)}, u32[]{:S(2)}) collective-permute-start(f32[264,2048]{1,0:T(8,128)} %select_maximum_fusion), channel_id=1, source_target_pairs={{0,4},{4,0},{8,12},{12,8},{16,20},{20,16},{24,28},{28,24},{1,5},{5... | collective-permute-start | bytes 6488072 | tf_op jit(solution)/shard_map/ppermute | solution.py:210
  88.4 1.6 copy-start
  90.0 6.0 %copy-start.16 = (f32[128]{0:T(128)S(1)}, f32[128]{0:T(128)}, u32[]{:S(2)}) copy-start(f32[128]{0:T(128)} %param.19) | copy-start | bytes 1540
  91.3 6.9 %collective-permute-start.7 = (f32[64,1024]{1,0:T(8,128)}, f32[64,1024]{1,0:T(8,128)}, u32[]{:S(2)}, u32[]{:S(2)}) collective-permute-start(f32[64,1024]{1,0:T(8,128)} %get-tuple-element.44), channel_id=1, source_target_pairs={{0,8},{4,12},{1,9},{5,13},{2,10},{6,14},{3,11},{7,15}} | collective-permute-start | bytes 786440 | tf_op jit(solution)/shard_map/ppermute | solution.py:256
  92.6 5.5 %collective-permute-start.5 = (f32[64,1024]{1,0:T(8,128)}, f32[64,1024]{1,0:T(8,128)S(1)}, u32[]{:S(2)}, u32[]{:S(2)}) collective-permute-start(f32[64,1024]{1,0:T(8,128)} %get-tuple-element.45), channel_id=1, source_target_pairs={{0,8},{4,12},{1,9},{5,13},{2,10},{6,14},{3,11},{7,15}} | collective-permute-start | bytes 786440 | tf_op jit(solution)/shard_map/ppermute | solution.py:256
  93.3 4.9 %collective-permute-start.3 = (f32[64,1024]{1,0:T(8,128)}, f32[64,1024]{1,0:T(8,128)}, u32[]{:S(2)}, u32[]{:S(2)}) collective-permute-start(f32[64,1024]{1,0:T(8,128)} %get-tuple-element.46), channel_id=1, source_target_pairs={{0,8},{4,12},{1,9},{5,13},{2,10},{6,14},{3,11},{7,15}} | collective-permute-start | bytes 786440 | tf_op jit(solution)/shard_map/ppermute | solution.py:256
  94.7 3.5 %collective-permute-start.2 = (f32[64,1024]{1,0:T(8,128)}, f32[64,1024]{1,0:T(8,128)}, u32[]{:S(2)}, u32[]{:S(2)}) collective-permute-start(f32[64,1024]{1,0:T(8,128)} %get-tuple-element.47), channel_id=1, source_target_pairs={{0,8},{4,12},{1,9},{5,13},{2,10},{6,14},{3,11},{7,15}} | collective-permute-start | bytes 786440 | tf_op jit(solution)/shard_map/ppermute | solution.py:256
  98.2 7.4 %copy-start.3 = (bf16[512,2,256]{0,2,1:T(8,128)(2,1)S(1)}, bf16[512,2,256]{0,2,1:T(8,128)(2,1)}, u32[]{:S(2)}) copy-start(bf16[512,2,256]{0,2,1:T(8,128)(2,1)} %copy-done.2) | copy-start | bytes 1572868
  100.4 29.6 %collective-permute-start.8 = (f32[64,1024]{1,0:T(8,128)}, f32[64,1024]{1,0:T(8,128)}, u32[]{:S(2)}, u32[]{:S(2)}) collective-permute-start(f32[64,1024]{1,0:T(8,128)} %get-tuple-element.40), channel_id=1, source_target_pairs={{8,16},{12,20},{9,17},{13,21},{10,18},{14,22},{11,19},{15,23}} | collective-permute-start | bytes 786440 | tf_op jit(solution)/shard_map/ppermute | solution.py:256
  101.7 34.0 %collective-permute-start.4 = (f32[64,1024]{1,0:T(8,128)}, f32[64,1024]{1,0:T(8,128)}, u32[]{:S(2)}, u32[]{:S(2)}) collective-permute-start(f32[64,1024]{1,0:T(8,128)} %get-tuple-element.42), channel_id=1, source_target_pairs={{8,16},{12,20},{9,17},{13,21},{10,18},{14,22},{11,19},{15,23}} | collective-permute-start | bytes 786440 | tf_op jit(solution)/shard_map/ppermute | solution.py:256
  103.0 38.3 %collective-permute-start.6 = (f32[64,1024]{1,0:T(8,128)}, f32[64,1024]{1,0:T(8,128)}, u32[]{:S(2)}, u32[]{:S(2)}) collective-permute-start(f32[64,1024]{1,0:T(8,128)} %get-tuple-element.43), channel_id=1, source_target_pairs={{8,16},{12,20},{9,17},{13,21},{10,18},{14,22},{11,19},{15,23}} | collective-permute-start | bytes 786440 | tf_op jit(solution)/shard_map/ppermute | solution.py:256
  104.3 41.2 %collective-permute-start.9 = (f32[64,1024]{1,0:T(8,128)}, f32[64,1024]{1,0:T(8,128)}, u32[]{:S(2)}, u32[]{:S(2)}) collective-permute-start(f32[64,1024]{1,0:T(8,128)} %get-tuple-element.41), channel_id=1, source_target_pairs={{8,16},{12,20},{9,17},{13,21},{10,18},{14,22},{11,19},{15,23}} | collective-permute-start | bytes 786440 | tf_op jit(solution)/shard_map/ppermute | solution.py:256
  146.8 8.0 %collective-permute-start.10 = (f32[64,1024]{1,0:T(8,128)S(1)}, f32[64,1024]{1,0:T(8,128)S(1)}, u32[]{:S(2)}, u32[]{:S(2)}) collective-permute-start(f32[64,1024]{1,0:T(8,128)S(1)} %get-tuple-element.36), channel_id=1, source_target_pairs={{16,24},{20,28},{17,25},{21,29},{18,26},{22,30},{19,27},{23,31}} | collective-permute-start | bytes 786440 | tf_op jit(solution)/shard_map/ppermute | solution.py:256
  148.1 12.3 %collective-permute-start.13 = (f32[64,1024]{1,0:T(8,128)S(1)}, f32[64,1024]{1,0:T(8,128)S(1)}, u32[]{:S(2)}, u32[]{:S(2)}) collective-permute-start(f32[64,1024]{1,0:T(8,128)S(1)} %get-tuple-element.37), channel_id=1, source_target_pairs={{16,24},{20,28},{17,25},{21,29},{18,26},{22,30},{19,27},{23,31}} | collective-permute-start | bytes 786440 | tf_op jit(solution)/shard_map/ppermute | solution.py:256
  149.4 16.6 %collective-permute-start.11 = (f32[64,1024]{1,0:T(8,128)S(1)}, f32[64,1024]{1,0:T(8,128)S(1)}, u32[]{:S(2)}, u32[]{:S(2)}) collective-permute-start(f32[64,1024]{1,0:T(8,128)S(1)} %get-tuple-element.38), channel_id=1, source_target_pairs={{16,24},{20,28},{17,25},{21,29},{18,26},{22,30},{19,27},{23,31}} | collective-permute-start | bytes 786440 | tf_op jit(solution)/shard_map/ppermute | solution.py:256
  150.7 18.9 %collective-permute-start.12 = (f32[64,1024]{1,0:T(8,128)S(1)}, f32[64,1024]{1,0:T(8,128)S(1)}, u32[]{:S(2)}, u32[]{:S(2)}) collective-permute-start(f32[64,1024]{1,0:T(8,128)S(1)} %get-tuple-element.39), channel_id=1, source_target_pairs={{16,24},{20,28},{17,25},{21,29},{18,26},{22,30},{19,27},{23,31}} | collective-permute-start | bytes 786440 | tf_op jit(solution)/shard_map/ppermute | solution.py:256
  171.4 4.5 %copy-start.4 = (bf16[512,2,256]{0,2,1:T(8,128)(2,1)S(1)}, bf16[512,2,256]{0,2,1:T(8,128)(2,1)}, u32[]{:S(2)}) copy-start(bf16[512,2,256]{0,2,1:T(8,128)(2,1)} %copy-done.2) | copy-start | bytes 1572868
  171.4 3.0 %collective-permute-start.14 = (f32[256,1024]{1,0:T(8,128)}, f32[256,1024]{1,0:T(8,128)}, u32[]{:S(2)}, u32[]{:S(2)}) collective-permute-start(f32[256,1024]{1,0:T(8,128)} %pad_maximum_fusion.1), channel_id=1, source_target_pairs={{0,4},{4,0},{8,12},{12,8},{16,20},{20,16},{24,28},{28,24},{1,5},{5... | collective-permute-start | bytes 3145736 | tf_op jit(solution)/shard_map/ppermute | solution.py:261
  175.9 2.2 %copy-start.5 = (f32[512,2048]{1,0:T(8,128)S(1)}, f32[512,2048]{1,0:T(8,128)}, u32[]{:S(2)}) copy-start(f32[512,2048]{1,0:T(8,128)} %get-tuple-element.19) | copy-start | bytes 12582916
  175.9 3.5 %copy-start.6 = (f32[512,2048]{1,0:T(8,128)S(1)}, f32[512,2048]{1,0:T(8,128)}, u32[]{:S(2)}) copy-start(f32[512,2048]{1,0:T(8,128)} %get-tuple-element.20) | copy-start | bytes 12582916
  (3 other events, 2.1 us)

commit v13 on v12

--- a/solution.py
+++ b/solution.py
@@ -168,11 +168,20 @@
     bc_groups = bc_part.reshape(rows, 2, G, N)
     if group_of != list(range(G)):
         bc_groups = jnp.take(bc_groups, np.array(group_of), axis=2)
-    bc_groups = jnp.transpose(bc_groups, (2, 0, 1, 3))
-    seg_bc = lax.all_to_all(bc_groups, "tp", split_axis=0, concat_axis=0, tiled=True)
-    seg_bc = seg_bc.reshape(n_tp * rows, 2, N)
-    seg_x = lax.all_to_all(x_part, "tp", split_axis=1, concat_axis=0, tiled=True)
-    seg_dt = lax.all_to_all(dt_in, "tp", split_axis=1, concat_axis=0, tiled=True)
+    bc_groups = jnp.transpose(bc_groups, (2, 0, 1, 3)).reshape(n_tp, rows, 2 * N)
+    packed = jnp.concatenate(
+        [
+            jnp.transpose(x_part.reshape(rows, n_tp, head_width), (1, 0, 2)),
+            bc_groups,
+            jnp.transpose(dt_in.reshape(rows, n_tp, local_heads), (1, 0, 2)),
+        ],
+        axis=2,
+    )
+    packed = lax.all_to_all(packed, "tp", split_axis=0, concat_axis=0, tiled=True)
+    packed = packed.reshape(n_tp * rows, packed.shape[2])
+    seg_x = packed[:, :head_width]
+    seg_bc = packed[:, head_width : head_width + 2 * N].reshape(n_tp * rows, 2, N)
+    seg_dt = packed[:, head_width + 2 * N :]
     seg_len = seg_x.shape[0]
     blocks = seg_len // BLOCK
     seg_b = seg_bc[:, 0].reshape(blocks, BLOCK, N)

time: 213 us -> 213 us (level)
  waiting for transfers between devices: 58.4 us -> 73.2 us
  starting transfers between devices: 30.1 us -> 22.6 us
  local copies, waits for them, and re-layouts: 35 us -> 29.5 us
  other arithmetic: 30.6 us -> 26.4 us
  matrix products: 3.44 us -> 6.73 us
    all_to_all x3 -> x1, waiting for transfers between devices: 16.2 us -> 31 us  [on_device(): lax.all_to_all(packed, 'tp', split_axis=0, concat_axis=0, tiled=True)]
    unnamed x37 -> x34, local copies, waits for them, and re-layouts: 11 us -> 2.38 us
    all_to_all x3 -> x1, starting transfers between devices: 10.8 us -> 3.79 us  [on_device(): lax.all_to_all(packed, 'tp', split_axis=0, concat_axis=0, tiled=True)]
    convert_element_type x4, other arithmetic: 10.6 us -> 3.65 us  [conv_rows(): return jax.nn.silu(total).astype(jnp.bfloat16)]
    concatenate x0 -> x1, other arithmetic: none -> 3.27 us  [on_device(): jnp.concatenate([jnp.transpose(x_part.reshape(rows, n_tp, head_width), (1...]
    optimization_barrier x0 -> x1, local copies, waits for them, and re-layouts: none -> 2.36 us  [intra_after(): operands = lax.optimization_barrier(operands + (tie,))[:4]]
    slice x2 -> x5, local copies, waits for them, and re-layouts: 1.19 us -> 3.49 us  [the longest x2 2.5 us: on_device(): seg_x = packed[:, :head_width]]
  transfers between devices with their start and end apart: 18 -> 16, of which waited for: 12 -> 11; matrix products, arithmetic and copies ran while one was open for 20% -> 8% of each run, Pallas kernels for 7% -> 7%
where the time goes in v13:
time: 213 us; the launch traced here: 211 us
  waiting for transfers between devices  73.2 us (34%)
  local copies, waits for them, and re-layouts  29.5 us (14%)
  blocking collectives  28.4 us (13%)
  other arithmetic  26.4 us (12%)
  Pallas kernels  23.9 us (11%)
  starting transfers between devices  22.6 us (11%)
  matrix products  6.73 us (3%)
    ppermute x12, waiting for transfers between devices, on_device(): acc[k] = acc[k] + lax.ppermute(send, 'ctx', pairs)  35.6 us
    all_to_all x1, waiting for transfers between devices, on_device(): lax.all_to_all(packed, 'tp', split_axis=0, concat_axis=0, tiled=True)  31 us
    all_to_all x1, blocking collectives, on_device(): return lax.all_to_all(result, 'tp', split_axis=0, concat_axis=1, tiled=True)  28.4 us
    ppermute x12, starting transfers between devices, on_device(): acc[k] = acc[k] + lax.ppermute(send, 'ctx', pairs)  15.4 us
    pallas_call x1, Pallas kernels, intra_block(): pl.pallas_call(intra_kernel, out_shape=(jax.ShapeDtypeStruct((BLOCK, widt...  15.2 us
    pallas_call x1, Pallas kernels, fresh_block(): pl.pallas_call(fresh_kernel, out_shape=jax.ShapeDtypeStruct((N, width), j...  8.7 us
    reshape x1, local copies, waits for them, and re-layouts, head_columns(): return jnp.repeat(head_major, P_SIZE, axis=-1)  5.37 us
    ppermute x1, waiting for transfers between devices, on_device(): lax.ppermute(jnp.concatenate([final, decay_slab], axis=0), 'ctx', [(i, i...  4.59 us
  transfers between devices with their start and end apart: 16, of which 11 were waited for; matrix products, arithmetic and copies ran while one was open for 8% of the time, Pallas kernels for 7%

profile of v13, /device:TPU:16, one launch (start us, length us, event | category | flops | bytes accessed | tf_op | source)
XLA Modules:
  0.0 211.4 jit_solution(11882313238253420635)
XLA Ops:
  1.9 3.4 %collective-permute-start = (bf16[3,10240]{1,0:T(4,128)(2,1)S(1)}, bf16[3,10240]{1,0:T(4,128)(2,1)S(1)}, u32[]{:S(2)}, u32[]{:S(2)}) collective-permute-start(bf16[3,10240]{1,0:T(4,128)(2,1)S(1)} %pad_maximum_fusion.3), channel_id=1, source_target_pairs={{0,1},{1,2},{2,3},{3,4},{4,5},{5,6},{6,7},{7,8},{8,9},{9,10},{10,1... | collective-permute-start | bytes 184328 | tf_op jit(solution)/shard_map/ppermute | solution.py:20
  6.5 2.0 convert_element_type.40
  8.7 2.7 %multiply_convert_fusion = bf16[128,8192]{1,0:T(8,128)(2,1)S(1)} fusion(f32[128,8192]{1,0:T(8,128)S(1)} %convert_element_type.40, f32[8192]{0:T(1024)S(1)} %bitcast.90, f32[8192]{0:T(1024)S(1)} %bitcast.92, f32[8192]{0:T(1024)S(1)} %bitcast.88, f32[8192]{0:T(1024)S(1)} %bitcast.86, f32[8192]{0:T(1024)S(1)} %copy-done.8), kind=kLoop, calls=%fused_computation.1 | loop fusion | flops 13631488 | bytes 6455296 | tf_op jit(solution)/shard_map/convert_element_type | solution.py:27
  14.8 2.4 %copy.34 = bf16[128,8192]{0,1:T(8,128)(2,1)} copy(bf16[128,8192]{1,0:T(8,128)(2,1)S(1)} %dynamic_update_slice.6) | data formatting | bytes 4194304 | tf_op jit(solution)/shard_map/dynamic_update_slice | solution.py:36
  17.2 3.3 %pad_maximum_fusion = bf16[4,128,2592]{1,2,0:T(8,128)(2,1)} fusion(bf16[4,128,32]{1,2,0:T(8,128)(2,1)S(1)} %bitcast.96, bf16[4,128,512]{1,2,0:T(8,128)(2,1)S(1)} %bitcast.85, bf16[4,128,2048]{1,2,0:T(8,128)(2,1)} %bitcast.80), kind=kLoop, calls=%fused_computation.8 | loop fusion | flops 7962624 | bytes 5308416 | tf_op jit(solution)/shard_map/concatenate | solution.py:172
  20.5 3.8 %all-to-all-start = ((bf16[4,128,2592]{1,2,0:T(8,128)(2,1)}), bf16[4,128,2592]{1,2,0:T(8,128)(2,1)S(1)}, u32[]{:S(2)}, u32[]{:S(2)}) async-start(bf16[4,128,2592]{1,2,0:T(8,128)(2,1)} %pad_maximum_fusion), calls=%async_computation | async-start | bytes 5308416 | tf_op jit(solution)/shard_map/all_to_all | solution.py:180
  24.5 31.0 %all-to-all-done = bf16[4,128,2592]{1,2,0:T(8,128)(2,1)S(1)} async-done(((bf16[4,128,2592]{1,2,0:T(8,128)(2,1)}), bf16[4,128,2592]{1,2,0:T(8,128)(2,1)S(1)}, u32[]{:S(2)}, u32[]{:S(2)}) %all-to-all-start) | async-done | bytes 2654240 | tf_op jit(solution)/shard_map/all_to_all | solution.py:180
  60.7 2.4 %copy.41.x_ref = bf16[512,2048]{1,0:T(8,128)(2,1)} copy(bf16[512,2048]{0,1:T(8,128)(2,1)S(1)} %slice.197) | data formatting | bytes 4194304 | tf_op jit(solution)/shard_map/slice | solution.py:182
  63.0 2.5 %broadcast_in_dim.10 = f32[512,32,64]{0,2,1:T(8,128)} broadcast(f32[512,32]{0,1:T(8,128)S(1)} %get-tuple-element.27), dimensions={0,1} | broadcast | bytes 4259840 | tf_op jit(solution)/shard_map/broadcast_in_dim | solution.py:135
  65.6 5.4 %copy.42.fac_ref = f32[512,2048]{1,0:T(8,128)} copy(f32[512,2048]{0,1:T(8,128)} %bitcast.77) | data formatting | bytes 8388608 | tf_op jit(solution)/shard_map/reshape | solution.py:135
  71.0 8.7 %ssd_fresh.1 = f32[256,2048]{1,0:T(8,128)} custom-call(bf16[512,2048]{1,0:T(8,128)(2,1)} %copy.41.x_ref, bf16[256,512]{1,0:T(8,128)(2,1)} %slice_bitcast_fusion.1.bt_ref, f32[512,2048]{1,0:T(8,128)} %copy.42.fac_ref), custom_call_target="tpu_custom_call" | custom-call | flops 536870912 | bytes 8650752 | tf_op jit(solution)/shard_map/ssd_fresh/pallas_call | solution.py:120
  79.7 3.2 %select_maximum_fusion = f32[264,2048]{1,0:T(8,128)} fusion(f32[1,32]{1,0:T(1,128)S(1)} %bitcast.107, f32[256,2048]{1,0:T(8,128)} %ssd_fresh.1), kind=kLoop, calls=%fused_computation.9 | loop fusion | flops 1622016 | bytes 4259968 | tf_op jit(solution)/shard_map/concatenate | solution.py:220
  82.9 4.6 %collective-permute-done.1 = f32[264,2048]{1,0:T(8,128)} collective-permute-done((f32[264,2048]{1,0:T(8,128)}, f32[264,2048]{1,0:T(8,128)}, u32[]{:S(2)}, u32[]{:S(2)}) %collective-permute-start.1) | collective-permute-done | bytes 2162720 | tf_op jit(solution)/shard_map/ppermute | solution.py:219
  88.6 1.9 slice.205
  94.1 1.4 collective-permute-start.3
  97.7 2.2 %multiply_add_fusion.4 = (f32[64,1024]{1,0:T(8,128)}, f32[64,1024]{1,0:T(8,128)}, f32[64,1024]{1,0:T(8,128)}, f32[64,1024]{1,0:T(8,128)}) fusion(f32[64,1024]{1,0:T(8,128)} %collective-permute-done.7, f32[256,1024]{1,0:T(8,128)S(1)} %select_add_fusion, f32[1024]{0:T(1024)S(1)} %mul.332, f32[64,1024]{1,0:T(8,128)} %collective-permute-done.2, ...), kind=kLoop, calls=%fused_computation.30 | loop fusion | flops 524288 | bytes 3149824 | tf_op jit(solution)/shard_map/add | solution.py:264
  106.4 2.4 %copy.43.x_ref = bf16[512,2048]{1,0:T(8,128)(2,1)} copy(bf16[512,2048]{0,1:T(8,128)(2,1)S(1)} %slice.197) | data formatting | bytes 4194304 | tf_op jit(solution)/shard_map/optimization_barrier | solution.py:250
  109.6 15.2 %ssd_intra.1 = (f32[512,2048]{1,0:T(8,128)}, f32[512,2048]{1,0:T(8,128)}) custom-call(bf16[512,2048]{1,0:T(8,128)(2,1)} %copy.43.x_ref, f32[512,512]{1,0:T(8,128)} %fusion.7.s_ref, f32[512,128]{1,0:T(8,128)} %pad.11.clone.cum_ref, f32[32,512]{1,0:T(8,128)} %bitcast.94, f32[32,512]{1,0:T(8,128)} %bitcast.105, f32[1,2048]{1,0:T(1,128)} %broadcast_in_dim_reshape.2.skip_ref), custom_call_target="tpu_custom_call" | custom-call | flops 2147483648 | bytes 7340032 | tf_op jit(solution)/shard_map/ssd_intra/pallas_call | solution.py:87
  124.8 6.0 %collective-permute-done.8 = f32[64,1024]{1,0:T(8,128)} collective-permute-done((f32[64,1024]{1,0:T(8,128)}, f32[64,1024]{1,0:T(8,128)}, u32[]{:S(2)}, u32[]{:S(2)}) %collective-permute-start.8) | collective-permute-done | bytes 262176 | tf_op jit(solution)/shard_map/ppermute | solution.py:265
  131.9 4.6 %collective-permute-done.4 = f32[64,1024]{1,0:T(8,128)} collective-permute-done((f32[64,1024]{1,0:T(8,128)}, f32[64,1024]{1,0:T(8,128)}, u32[]{:S(2)}, u32[]{:S(2)}) %collective-permute-start.4) | collective-permute-done | bytes 262176 | tf_op jit(solution)/shard_map/ppermute | solution.py:265
  137.5 4.6 %collective-permute-done.6 = f32[64,1024]{1,0:T(8,128)} collective-permute-done((f32[64,1024]{1,0:T(8,128)}, f32[64,1024]{1,0:T(8,128)}, u32[]{:S(2)}, u32[]{:S(2)}) %collective-permute-start.6) | collective-permute-done | bytes 262176 | tf_op jit(solution)/shard_map/ppermute | solution.py:265
  143.0 3.2 %collective-permute-done.9 = f32[64,1024]{1,0:T(8,128)} collective-permute-done((f32[64,1024]{1,0:T(8,128)}, f32[64,1024]{1,0:T(8,128)}, u32[]{:S(2)}, u32[]{:S(2)}) %collective-permute-start.9) | collective-permute-done | bytes 262176 | tf_op jit(solution)/shard_map/ppermute | solution.py:265
  151.5 1.5 collective-permute-start.12
  153.0 2.6 %collective-permute-done.10 = f32[64,1024]{1,0:T(8,128)S(1)} collective-permute-done((f32[64,1024]{1,0:T(8,128)S(1)}, f32[64,1024]{1,0:T(8,128)S(1)}, u32[]{:S(2)}, u32[]{:S(2)}) %collective-permute-start.10) | collective-permute-done | bytes 262176 | tf_op jit(solution)/shard_map/ppermute | solution.py:265
  155.6 5.6 %collective-permute-done.13 = f32[64,1024]{1,0:T(8,128)S(1)} collective-permute-done((f32[64,1024]{1,0:T(8,128)S(1)}, f32[64,1024]{1,0:T(8,128)S(1)}, u32[]{:S(2)}, u32[]{:S(2)}) %collective-permute-start.13) | collective-permute-done | bytes 262176 | tf_op jit(solution)/shard_map/ppermute | solution.py:265
  161.2 5.6 %collective-permute-done.11 = f32[64,1024]{1,0:T(8,128)S(1)} collective-permute-done((f32[64,1024]{1,0:T(8,128)S(1)}, f32[64,1024]{1,0:T(8,128)S(1)}, u32[]{:S(2)}, u32[]{:S(2)}) %collective-permute-start.11) | collective-permute-done | bytes 262176 | tf_op jit(solution)/shard_map/ppermute | solution.py:265
  166.8 3.5 %collective-permute-done.12 = f32[64,1024]{1,0:T(8,128)S(1)} collective-permute-done((f32[64,1024]{1,0:T(8,128)S(1)}, f32[64,1024]{1,0:T(8,128)S(1)}, u32[]{:S(2)}, u32[]{:S(2)}) %collective-permute-start.12) | collective-permute-done | bytes 262176 | tf_op jit(solution)/shard_map/ppermute | solution.py:265
  172.3 2.0 collective-permute-done.14
  174.5 2.6 %fusion.4 = f32[512,2048]{1,0:T(8,128)S(1)} fusion(f32[256,1024]{1,0:T(8,128)S(1)} %get-tuple-element.34, f32[256,1024]{1,0:T(8,128)S(1)} %get-tuple-element.33, f32[2048]{0:T(1024)S(1)} %mul.341, pred[]{:T(512)S(6)} %eq.7, bf16[512,2,256]{0,2,1:T(8,128)(2,1)S(1)} %bitcast.83, f32[264,2048]{1,0:T(8,128)} %collective-permute-done.1), kind=kOutput, calls=%fused_computation.14 | convolution fusion | flops 540016640 | bytes 8658945 | tf_op jit(solution)/shard_map/dot_general | solution.py:286
  178.6 2.9 %add_convert_fusion = bf16[512,2048]{1,0:T(8,128)(2,1)S(1)} fusion(f32[512,2048]{1,0:T(8,128)S(1)} %copy-done.5, f32[512,2048]{1,0:T(8,128)S(1)} %copy-done.6, f32[512,2048]{1,0:T(8,128)S(1)} %fusion.4, f32[256,1024]{1,0:T(8,128)S(1)} %get-tuple-element.34, f32[256,1024]{1,0:T(8,128)S(1)} %get-tuple-element.33, f32[2048]{0:T(1024)S(1)} %mul.341, pred[]{:T(512)S(6)} %eq.7, ...), kind=kOutput, calls=%fused_computation | convolution fusion | flops 544735232 | bytes 19144704 | tf_op jit(solution)/shard_map/dot_general | solution.py:288
  181.5 28.4 %all_to_all.24 = bf16[4,128,2048]{2,1,0:T(8,128)(2,1)S(1)} all-to-all(bf16[4,128,2048]{2,1,0:T(8,128)(2,1)S(1)} %bitcast.78), channel_id=1, replica_groups=mesh['ctx'=8,'tp'=4] {'tp'}, dimensions={0} | all-to-all | bytes 4194304 | tf_op jit(solution)/shard_map/all_to_all | solution.py:292
  209.9 1.5 copy.50
  (115 shorter events, 37.9 us)
Async XLA Ops:
  1.9 10.4 %collective-permute-start = (bf16[3,10240]{1,0:T(4,128)(2,1)S(1)}, bf16[3,10240]{1,0:T(4,128)(2,1)S(1)}, u32[]{:S(2)}, u32[]{:S(2)}) collective-permute-start(bf16[3,10240]{1,0:T(4,128)(2,1)S(1)} %pad_maximum_fusion.3), channel_id=1, source_target_pairs={{0,1},{1,2},{2,3},{3,4},{4,5},{5,6},{6,7},{7,8},{8,9},{9,10},{10,1... | collective-permute-start | bytes 184328 | tf_op jit(solution)/shard_map/ppermute | solution.py:20
  6.4 2.1 copy-start.11
  6.4 2.1 %copy-start.9 = (f32[4,8192]{1,0:T(4,128)S(1)}, f32[4,8192]{1,0:T(4,128)}, u32[]{:S(2)}) copy-start(f32[4,8192]{1,0:T(4,128)} %param.13) | copy-start | bytes 393220
  6.4 2.2 %copy-start.8 = (f32[8192]{0:T(1024)S(1)}, f32[8192]{0:T(1024)}, u32[]{:S(2)}) copy-start(f32[8192]{0:T(1024)} %param.14) | copy-start | bytes 98308
  8.7 2.8 %copy-start.10 = (f32[2048]{0:T(1024)S(1)}, f32[2048]{0:T(1024)}, u32[]{:S(2)}) copy-start(f32[2048]{0:T(1024)} %param.16) | copy-start | bytes 24580
  8.7 3.4 %copy-start.12 = (bf16[128,128]{1,0:T(8,128)(2,1)S(1)}, bf16[128,128]{1,0:T(8,128)(2,1)}, u32[]{:S(2)}) copy-start(bf16[128,128]{1,0:T(8,128)(2,1)} %param.12) | copy-start | bytes 98308
  20.5 3.8 %copy-start.13 = (f32[128]{0:T(128)S(1)}, f32[128]{0:T(128)}, u32[]{:S(2)}) copy-start(f32[128]{0:T(128)} %param.17) | copy-start | bytes 1540
  20.5 3.9 %copy-start.14 = (f32[128]{0:T(128)S(1)}, f32[128]{0:T(128)}, u32[]{:S(2)}) copy-start(f32[128]{0:T(128)} %param.18) | copy-start | bytes 1540
  20.5 35.0 %all-to-all-start = ((bf16[4,128,2592]{1,2,0:T(8,128)(2,1)}), bf16[4,128,2592]{1,2,0:T(8,128)(2,1)S(1)}, u32[]{:S(2)}, u32[]{:S(2)}) async-start(bf16[4,128,2592]{1,2,0:T(8,128)(2,1)} %pad_maximum_fusion), calls=%async_computation | async-start | bytes 5308416 | tf_op jit(solution)/shard_map/all_to_all | solution.py:180
  55.7 1.5 copy-start.1
  55.7 4.2 %copy-start.2 = (bf16[512,512]{0,1:T(8,128)(2,1)}, bf16[512,512]{0,1:T(8,128)(2,1)S(1)}, u32[]{:S(2)}) copy-start(bf16[512,512]{0,1:T(8,128)(2,1)S(1)} %slice.198) | copy-start | bytes 1572868
  59.9 48.8 %copy-start.7 = (f32[512,32]{0,1:T(8,128)}, f32[512,32]{0,1:T(8,128)S(1)}, u32[]{:S(2)}) copy-start(f32[512,32]{0,1:T(8,128)S(1)} %get-tuple-element.17) | copy-start | bytes 196612
  82.9 4.6 %collective-permute-start.1 = (f32[264,2048]{1,0:T(8,128)}, f32[264,2048]{1,0:T(8,128)}, u32[]{:S(2)}, u32[]{:S(2)}) collective-permute-start(f32[264,2048]{1,0:T(8,128)} %select_maximum_fusion), channel_id=1, source_target_pairs={{0,4},{4,0},{8,12},{12,8},{16,20},{20,16},{24,28},{28,24},{1,5},{5... | collective-permute-start | bytes 6488072 | tf_op jit(solution)/shard_map/ppermute | solution.py:219
  88.6 2.2 %copy-start = (f32[256,2048]{1,0:T(8,128)S(1)}, f32[256,2048]{1,0:T(8,128)}, u32[]{:S(2)}) copy-start(f32[256,2048]{1,0:T(8,128)} %ssd_fresh.1) | copy-start | bytes 6291460
  90.8 6.0 %copy-start.15 = (f32[128]{0:T(128)S(1)}, f32[128]{0:T(128)}, u32[]{:S(2)}) copy-start(f32[128]{0:T(128)} %param.19) | copy-start | bytes 1540
  92.0 5.7 %collective-permute-start.7 = (f32[64,1024]{1,0:T(8,128)}, f32[64,1024]{1,0:T(8,128)}, u32[]{:S(2)}, u32[]{:S(2)}) collective-permute-start(f32[64,1024]{1,0:T(8,128)} %get-tuple-element.45), channel_id=1, source_target_pairs={{0,8},{4,12},{1,9},{5,13},{2,10},{6,14},{3,11},{7,15}} | collective-permute-start | bytes 786440 | tf_op jit(solution)/shard_map/ppermute | solution.py:265
  93.4 4.3 %collective-permute-start.5 = (f32[64,1024]{1,0:T(8,128)}, f32[64,1024]{1,0:T(8,128)S(1)}, u32[]{:S(2)}, u32[]{:S(2)}) collective-permute-start(f32[64,1024]{1,0:T(8,128)} %get-tuple-element.46), channel_id=1, source_target_pairs={{0,8},{4,12},{1,9},{5,13},{2,10},{6,14},{3,11},{7,15}} | collective-permute-start | bytes 786440 | tf_op jit(solution)/shard_map/ppermute | solution.py:265
  94.1 3.6 %collective-permute-start.3 = (f32[64,1024]{1,0:T(8,128)}, f32[64,1024]{1,0:T(8,128)}, u32[]{:S(2)}, u32[]{:S(2)}) collective-permute-start(f32[64,1024]{1,0:T(8,128)} %get-tuple-element.47), channel_id=1, source_target_pairs={{0,8},{4,12},{1,9},{5,13},{2,10},{6,14},{3,11},{7,15}} | collective-permute-start | bytes 786440 | tf_op jit(solution)/shard_map/ppermute | solution.py:265
  95.5 2.2 %collective-permute-start.2 = (f32[64,1024]{1,0:T(8,128)}, f32[64,1024]{1,0:T(8,128)}, u32[]{:S(2)}, u32[]{:S(2)}) collective-permute-start(f32[64,1024]{1,0:T(8,128)} %get-tuple-element.48), channel_id=1, source_target_pairs={{0,8},{4,12},{1,9},{5,13},{2,10},{6,14},{3,11},{7,15}} | collective-permute-start | bytes 786440 | tf_op jit(solution)/shard_map/ppermute | solution.py:265
  97.7 7.4 %copy-start.3 = (bf16[512,512]{0,1:T(8,128)(2,1)S(1)}, bf16[512,512]{0,1:T(8,128)(2,1)}, u32[]{:S(2)}) copy-start(bf16[512,512]{0,1:T(8,128)(2,1)} %copy-done.2) | copy-start | bytes 1572868
  99.9 30.9 %collective-permute-start.8 = (f32[64,1024]{1,0:T(8,128)}, f32[64,1024]{1,0:T(8,128)}, u32[]{:S(2)}, u32[]{:S(2)}) collective-permute-start(f32[64,1024]{1,0:T(8,128)} %get-tuple-element.41), channel_id=1, source_target_pairs={{8,16},{12,20},{9,17},{13,21},{10,18},{14,22},{11,19},{15,23}} | collective-permute-start | bytes 786440 | tf_op jit(solution)/shard_map/ppermute | solution.py:265
  101.2 35.2 %collective-permute-start.4 = (f32[64,1024]{1,0:T(8,128)}, f32[64,1024]{1,0:T(8,128)}, u32[]{:S(2)}, u32[]{:S(2)}) collective-permute-start(f32[64,1024]{1,0:T(8,128)} %get-tuple-element.43), channel_id=1, source_target_pairs={{8,16},{12,20},{9,17},{13,21},{10,18},{14,22},{11,19},{15,23}} | collective-permute-start | bytes 786440 | tf_op jit(solution)/shard_map/ppermute | solution.py:265
  102.5 39.5 %collective-permute-start.6 = (f32[64,1024]{1,0:T(8,128)}, f32[64,1024]{1,0:T(8,128)}, u32[]{:S(2)}, u32[]{:S(2)}) collective-permute-start(f32[64,1024]{1,0:T(8,128)} %get-tuple-element.44), channel_id=1, source_target_pairs={{8,16},{12,20},{9,17},{13,21},{10,18},{14,22},{11,19},{15,23}} | collective-permute-start | bytes 786440 | tf_op jit(solution)/shard_map/ppermute | solution.py:265
  103.8 42.4 %collective-permute-start.9 = (f32[64,1024]{1,0:T(8,128)}, f32[64,1024]{1,0:T(8,128)}, u32[]{:S(2)}, u32[]{:S(2)}) collective-permute-start(f32[64,1024]{1,0:T(8,128)} %get-tuple-element.42), channel_id=1, source_target_pairs={{8,16},{12,20},{9,17},{13,21},{10,18},{14,22},{11,19},{15,23}} | collective-permute-start | bytes 786440 | tf_op jit(solution)/shard_map/ppermute | solution.py:265
  147.5 8.0 %collective-permute-start.10 = (f32[64,1024]{1,0:T(8,128)S(1)}, f32[64,1024]{1,0:T(8,128)S(1)}, u32[]{:S(2)}, u32[]{:S(2)}) collective-permute-start(f32[64,1024]{1,0:T(8,128)S(1)} %get-tuple-element.37), channel_id=1, source_target_pairs={{16,24},{20,28},{17,25},{21,29},{18,26},{22,30},{19,27},{23,31}} | collective-permute-start | bytes 786440 | tf_op jit(solution)/shard_map/ppermute | solution.py:265
  148.8 12.3 %collective-permute-start.13 = (f32[64,1024]{1,0:T(8,128)S(1)}, f32[64,1024]{1,0:T(8,128)S(1)}, u32[]{:S(2)}, u32[]{:S(2)}) collective-permute-start(f32[64,1024]{1,0:T(8,128)S(1)} %get-tuple-element.38), channel_id=1, source_target_pairs={{16,24},{20,28},{17,25},{21,29},{18,26},{22,30},{19,27},{23,31}} | collective-permute-start | bytes 786440 | tf_op jit(solution)/shard_map/ppermute | solution.py:265
  150.2 16.6 %collective-permute-start.11 = (f32[64,1024]{1,0:T(8,128)S(1)}, f32[64,1024]{1,0:T(8,128)S(1)}, u32[]{:S(2)}, u32[]{:S(2)}) collective-permute-start(f32[64,1024]{1,0:T(8,128)S(1)} %get-tuple-element.39), channel_id=1, source_target_pairs={{16,24},{20,28},{17,25},{21,29},{18,26},{22,30},{19,27},{23,31}} | collective-permute-start | bytes 786440 | tf_op jit(solution)/shard_map/ppermute | solution.py:265
  151.5 18.9 %collective-permute-start.12 = (f32[64,1024]{1,0:T(8,128)S(1)}, f32[64,1024]{1,0:T(8,128)S(1)}, u32[]{:S(2)}, u32[]{:S(2)}) collective-permute-start(f32[64,1024]{1,0:T(8,128)S(1)} %get-tuple-element.40), channel_id=1, source_target_pairs={{16,24},{20,28},{17,25},{21,29},{18,26},{22,30},{19,27},{23,31}} | collective-permute-start | bytes 786440 | tf_op jit(solution)/shard_map/ppermute | solution.py:265
  170.4 4.1 %copy-start.4 = (bf16[512,512]{0,1:T(8,128)(2,1)S(1)}, bf16[512,512]{0,1:T(8,128)(2,1)}, u32[]{:S(2)}) copy-start(bf16[512,512]{0,1:T(8,128)(2,1)} %copy-done.2) | copy-start | bytes 1572868
  171.4 2.9 %collective-permute-start.14 = (f32[256,1024]{1,0:T(8,128)}, f32[256,1024]{1,0:T(8,128)S(1)}, u32[]{:S(2)}, u32[]{:S(2)}) collective-permute-start(f32[256,1024]{1,0:T(8,128)} %pad_maximum_fusion.2), channel_id=1, source_target_pairs={{0,4},{4,0},{8,12},{12,8},{16,20},{20,16},{24,28},{28,24},{1,5},{5... | collective-permute-start | bytes 3145736 | tf_op jit(solution)/shard_map/ppermute | solution.py:270
  174.5 2.8 %copy-start.5 = (f32[512,2048]{1,0:T(8,128)S(1)}, f32[512,2048]{1,0:T(8,128)}, u32[]{:S(2)}) copy-start(f32[512,2048]{1,0:T(8,128)} %get-tuple-element.19) | copy-start | bytes 12582916
  174.5 4.1 %copy-start.6 = (f32[512,2048]{1,0:T(8,128)S(1)}, f32[512,2048]{1,0:T(8,128)}, u32[]{:S(2)}) copy-start(f32[512,2048]{1,0:T(8,128)} %get-tuple-element.20) | copy-start | bytes 12582916

commit v14 on v12

--- a/solution.py
+++ b/solution.py
@@ -224,7 +224,7 @@
     chip_decay = head_columns(
         lax.dynamic_slice_in_dim(segment_decay * mate_decay, core * half_heads, half_heads, 0)
     )[None, :]
-    pieces = 4 if N % 32 == 0 else 1
+    pieces = 2 if N % 16 == 0 else 1
     piece_rows = N // pieces
     acc = [jnp.zeros((piece_rows, half_width), jnp.float32) for _ in range(pieces)]
     skip_cols = head_columns(skip_local)

time: 213 us -> 212 us (level)
  waiting for transfers between devices: 58.4 us -> 70.6 us
  starting transfers between devices: 30.1 us -> 21.5 us
  other arithmetic: 30.6 us -> 27.2 us
    ppermute x12 -> x6, waiting for transfers between devices: 34.9 us -> 47.1 us  [on_device(): acc[k] = acc[k] + lax.ppermute(send, 'ctx', pairs)]
    ppermute x12 -> x6, starting transfers between devices: 15.3 us -> 6.79 us  [on_device(): acc[k] = acc[k] + lax.ppermute(send, 'ctx', pairs)]
    add x8 -> x4, other arithmetic: 4.29 us -> 2.65 us  [on_device(): acc[k] = acc[k] + lax.ppermute(send, 'ctx', pairs)]
    unnamed x37 -> x39, local copies, waits for them, and re-layouts: 11 us -> 11.3 us
  transfers between devices with their start and end apart: 18 -> 12, of which waited for: 12 -> 8; matrix products, arithmetic and copies ran while one was open for 20% -> 18% of each run, Pallas kernels for 7% -> 7%
where the time goes in v14:
time: 212 us; the launch traced here: 210 us
  waiting for transfers between devices  70.6 us (33%)
  local copies, waits for them, and re-layouts  33 us (16%)
  blocking collectives  28.4 us (13%)
  other arithmetic  27.2 us (13%)
  Pallas kernels  23.9 us (11%)
  starting transfers between devices  21.5 us (10%)
  matrix products  4.49 us (2%)
    ppermute x6, waiting for transfers between devices, on_device(): acc[k] = acc[k] + lax.ppermute(send, 'ctx', pairs)  47.1 us
    all_to_all x1, blocking collectives, on_device(): return lax.all_to_all(result, 'tp', split_axis=0, concat_axis=1, tiled=True)  28.4 us
    pallas_call x1, Pallas kernels, intra_block(): pl.pallas_call(intra_kernel, out_shape=(jax.ShapeDtypeStruct((BLOCK, widt...  15.2 us
    all_to_all x1, waiting for transfers between devices, on_device(): lax.all_to_all(x_part, 'tp', split_axis=1, concat_axis=0, tiled=True)  11.8 us
    unnamed x39, local copies, waits for them, and re-layouts  11.3 us
    convert_element_type x4, other arithmetic, conv_rows(): return jax.nn.silu(total).astype(jnp.bfloat16)  10.7 us
    pallas_call x1, Pallas kernels, fresh_block(): pl.pallas_call(fresh_kernel, out_shape=jax.ShapeDtypeStruct((N, width), j...  8.71 us
    ppermute x6, starting transfers between devices, on_device(): acc[k] = acc[k] + lax.ppermute(send, 'ctx', pairs)  6.79 us
  transfers between devices with their start and end apart: 12, of which 8 were waited for; matrix products, arithmetic and copies ran while one was open for 18% of the time, Pallas kernels for 7%

profile of v14, /device:TPU:16, one launch (start us, length us, event | category | flops | bytes accessed | tf_op | source)
XLA Modules:
  0.0 209.7 jit_solution(13587065339928627080)
XLA Ops:
  0.0 1.5 copy.89
  1.5 3.7 %all-to-all-start.2 = ((bf16[128,4,32]{0,2,1:T(8,128)(2,1)}), bf16[128,4,32]{0,2,1:T(8,128)(2,1)S(1)}, u32[]{:S(2)}, u32[]{:S(2)}) async-start(bf16[128,4,32]{0,2,1:T(8,128)(2,1)} %bitcast.14), calls=%async_computation.2 | async-start | bytes 65536 | tf_op jit(solution)/shard_map/all_to_all | solution.py:175
  7.1 3.9 %collective-permute-start = (bf16[3,10240]{1,0:T(4,128)(2,1)S(1)}, bf16[3,10240]{1,0:T(4,128)(2,1)S(1)}, u32[]{:S(2)}, u32[]{:S(2)}) collective-permute-start(bf16[3,10240]{1,0:T(4,128)(2,1)S(1)} %pad_maximum_fusion.2), channel_id=1, source_target_pairs={{0,1},{1,2},{2,3},{3,4},{4,5},{5,6},{6,7},{7,8},{8,9},{9,10},{10,1... | collective-permute-start | bytes 184328 | tf_op jit(solution)/shard_map/ppermute | solution.py:20
  12.4 4.0 %convert_element_type.59 = f32[128,8192]{1,0:T(8,128)} convert(bf16[128,8192]{1,0:T(8,128)(2,1)} %param.10) | non-fusion elementwise | flops 1048576 | bytes 6291456 | tf_op jit(solution)/shard_map/convert_element_type | solution.py:34
  16.6 2.6 %multiply_convert_fusion.1 = bf16[128,2048]{0,1:T(8,128)(2,1)S(1)} fusion(f32[128,2048]{0,1:T(8,128)S(1)} %convert_element_type.63, f32[2048]{0:T(1024)S(1)} %bitcast.104, f32[2048]{0:T(1024)S(1)} %bitcast.106, f32[2048]{0:T(1024)S(1)} %bitcast.102, f32[2048]{0:T(1024)S(1)} %bitcast.100, f32[2048]{0:T(1024)S(1)} %copy-done.13), kind=kLoop, calls=%fused_computation.26 | loop fusion | flops 3407872 | bytes 1613824 | tf_op jit(solution)/shard_map/convert_element_type | solution.py:27
  19.3 7.8 %multiply_convert_fusion = bf16[128,8192]{1,0:T(8,128)(2,1)S(1)} fusion(f32[128,8192]{1,0:T(8,128)} %convert_element_type.59, f32[8192]{0:T(1024)S(1)} %bitcast.95, f32[8192]{0:T(1024)S(1)} %bitcast.97, f32[8192]{0:T(1024)S(1)} %bitcast.93, f32[8192]{0:T(1024)S(1)} %bitcast.91, f32[8192]{0:T(1024)S(1)} %copy-done.10), kind=kLoop, calls=%fused_computation.1 | loop fusion | flops 13631488 | bytes 6455296 | tf_op jit(solution)/shard_map/convert_element_type | solution.py:27
  28.4 2.0 dynamic_update_slice.7
  31.2 3.5 %all-to-all-start.1 = ((bf16[4,128,2,256]{1,3,2,0:T(8,128)(2,1)}), bf16[4,128,2,256]{1,3,2,0:T(8,128)(2,1)S(1)}, u32[]{:S(2)}, u32[]{:S(2)}) async-start(bf16[4,128,2,256]{1,3,2,0:T(8,128)(2,1)} %copy.87), calls=%async_computation.1 | async-start | bytes 1048576 | tf_op jit(solution)/shard_map/all_to_all | solution.py:172
  36.8 1.5 copy.116
  38.3 4.4 %all-to-all-done.1 = bf16[4,128,2,256]{1,3,2,0:T(8,128)(2,1)S(1)} async-done(((bf16[4,128,2,256]{1,3,2,0:T(8,128)(2,1)}), bf16[4,128,2,256]{1,3,2,0:T(8,128)(2,1)S(1)}, u32[]{:S(2)}, u32[]{:S(2)}) %all-to-all-start.1) | async-done | bytes 524320 | tf_op jit(solution)/shard_map/all_to_all | solution.py:172
  42.7 3.6 %all-to-all-start = ((bf16[128,4,2048]{2,0,1:T(8,128)(2,1)}), bf16[128,4,2048]{2,0,1:T(8,128)(2,1)S(1)}, u32[]{:S(2)}, u32[]{:S(2)}) async-start(bf16[128,4,2048]{2,0,1:T(8,128)(2,1)} %bitcast.86), calls=%async_computation | async-start | bytes 4194304 | tf_op jit(solution)/shard_map/all_to_all | solution.py:174
  49.0 2.5 %broadcast_in_dim.10 = f32[512,32,64]{0,2,1:T(8,128)} broadcast(f32[512,32]{0,1:T(8,128)S(1)} %get-tuple-element.23), dimensions={0,1} | broadcast | bytes 4259840 | tf_op jit(solution)/shard_map/broadcast_in_dim | solution.py:135
  51.6 5.4 %copy.95.fac_ref = f32[512,2048]{1,0:T(8,128)} copy(f32[512,2048]{0,1:T(8,128)} %bitcast.83) | data formatting | bytes 8388608 | tf_op jit(solution)/shard_map/reshape | solution.py:135
  58.5 11.8 %all-to-all-done = bf16[128,4,2048]{2,0,1:T(8,128)(2,1)S(1)} async-done(((bf16[128,4,2048]{2,0,1:T(8,128)(2,1)}), bf16[128,4,2048]{2,0,1:T(8,128)(2,1)S(1)}, u32[]{:S(2)}, u32[]{:S(2)}) %all-to-all-start) | async-done | bytes 2097184 | tf_op jit(solution)/shard_map/all_to_all | solution.py:174
  70.3 1.3 copy-done.1
  71.6 8.7 %ssd_fresh.1 = f32[256,2048]{1,0:T(8,128)} custom-call(bf16[512,2048]{1,0:T(8,128)(2,1)} %bitcast.88, bf16[256,512]{1,0:T(8,128)(2,1)} %slice_bitcast_fusion.1.bt_ref, f32[512,2048]{1,0:T(8,128)} %copy.95.fac_ref), custom_call_target="tpu_custom_call" | custom-call | flops 536870912 | bytes 8650752 | tf_op jit(solution)/shard_map/ssd_fresh/pallas_call | solution.py:120
  80.3 3.2 %select_maximum_fusion = f32[264,2048]{1,0:T(8,128)} fusion(f32[1,32]{1,0:T(1,128)S(1)} %bitcast.110, f32[256,2048]{1,0:T(8,128)} %ssd_fresh.1), kind=kLoop, calls=%fused_computation.10 | loop fusion | flops 1622016 | bytes 4259968 | tf_op jit(solution)/shard_map/concatenate | solution.py:211
  83.6 4.5 %collective-permute-done.1 = f32[264,2048]{1,0:T(8,128)S(1)} collective-permute-done((f32[264,2048]{1,0:T(8,128)}, f32[264,2048]{1,0:T(8,128)S(1)}, u32[]{:S(2)}, u32[]{:S(2)}) %collective-permute-start.1) | collective-permute-done | bytes 2162720 | tf_op jit(solution)/shard_map/ppermute | solution.py:210
  88.7 1.4 copy-done
  97.4 2.4 %fusion.12.s_ref = f32[512,512]{1,0:T(8,128)} fusion(bf16[512,2,256]{0,2,1:T(8,128)(2,1)} %copy-done.2), kind=kOutput, calls=%fused_computation.37 | convolution fusion | flops 134217728 | bytes 1572864 | tf_op jit(solution)/shard_map/in,jn->ij/dot_general | solution.py:232
  100.6 15.2 %ssd_intra.1 = (f32[512,2048]{1,0:T(8,128)}, f32[512,2048]{1,0:T(8,128)}) custom-call(bf16[512,2048]{1,0:T(8,128)(2,1)} %bitcast.89, f32[512,512]{1,0:T(8,128)} %fusion.12.s_ref, f32[512,128]{1,0:T(8,128)} %pad.11.clone.cum_ref, f32[32,512]{1,0:T(8,128)} %bitcast.99, f32[32,512]{1,0:T(8,128)} %bitcast.108, f32[1,2048]{1,0:T(1,128)} %broadcast_in_dim_reshape.2.skip_ref), custom_call_target="tpu_custom_call" | custom-call | flops 2147483648 | bytes 7340032 | tf_op jit(solution)/shard_map/ssd_intra/pallas_call | solution.py:87
  115.8 18.6 %collective-permute-done.4 = f32[128,1024]{1,0:T(8,128)} collective-permute-done((f32[128,1024]{1,0:T(8,128)}, f32[128,1024]{1,0:T(8,128)}, u32[]{:S(2)}, u32[]{:S(2)}) %collective-permute-start.4) | collective-permute-done | bytes 524320 | tf_op jit(solution)/shard_map/ppermute | solution.py:256
  135.7 8.5 %collective-permute-done.5 = f32[128,1024]{1,0:T(8,128)} collective-permute-done((f32[128,1024]{1,0:T(8,128)}, f32[128,1024]{1,0:T(8,128)}, u32[]{:S(2)}, u32[]{:S(2)}) %collective-permute-start.5) | collective-permute-done | bytes 524320 | tf_op jit(solution)/shard_map/ppermute | solution.py:256
  145.7 1.3 collective-permute-start.6
  147.0 1.5 collective-permute-start.7
  148.6 10.8 %collective-permute-done.6 = f32[128,1024]{1,0:T(8,128)S(1)} collective-permute-done((f32[128,1024]{1,0:T(8,128)S(1)}, f32[128,1024]{1,0:T(8,128)S(1)}, u32[]{:S(2)}, u32[]{:S(2)}) %collective-permute-start.6) | collective-permute-done | bytes 524320 | tf_op jit(solution)/shard_map/ppermute | solution.py:256
  159.5 9.1 %collective-permute-done.7 = f32[128,1024]{1,0:T(8,128)S(1)} collective-permute-done((f32[128,1024]{1,0:T(8,128)S(1)}, f32[128,1024]{1,0:T(8,128)S(1)}, u32[]{:S(2)}, u32[]{:S(2)}) %collective-permute-start.7) | collective-permute-done | bytes 524320 | tf_op jit(solution)/shard_map/ppermute | solution.py:256
  170.6 2.9 %collective-permute-done.8 = f32[256,1024]{1,0:T(8,128)} collective-permute-done((f32[256,1024]{1,0:T(8,128)}, f32[256,1024]{1,0:T(8,128)}, u32[]{:S(2)}, u32[]{:S(2)}) %collective-permute-start.8) | collective-permute-done | bytes 1048608 | tf_op jit(solution)/shard_map/ppermute | solution.py:261
  173.5 1.6 broadcast_select_fusion
  175.9 1.3 copy-done.5
  179.8 28.4 %all_to_all.56 = bf16[4,128,2048]{2,1,0:T(8,128)(2,1)S(1)} all-to-all(bf16[4,128,2048]{2,1,0:T(8,128)(2,1)S(1)} %bitcast.85), channel_id=1, replica_groups=mesh['ctx'=8,'tp'=4] {'tp'}, dimensions={0} | all-to-all | bytes 4194304 | tf_op jit(solution)/shard_map/all_to_all | solution.py:283
  208.3 1.5 copy.103
  (107 shorter events, 28.8 us)
Async XLA Ops:
  1.5 25.8 %all-to-all-start.2 = ((bf16[128,4,32]{0,2,1:T(8,128)(2,1)}), bf16[128,4,32]{0,2,1:T(8,128)(2,1)S(1)}, u32[]{:S(2)}, u32[]{:S(2)}) async-start(bf16[128,4,32]{0,2,1:T(8,128)(2,1)} %bitcast.14), calls=%async_computation.2 | async-start | bytes 65536 | tf_op jit(solution)/shard_map/all_to_all | solution.py:175
  7.1 20.3 %collective-permute-start = (bf16[3,10240]{1,0:T(4,128)(2,1)S(1)}, bf16[3,10240]{1,0:T(4,128)(2,1)S(1)}, u32[]{:S(2)}, u32[]{:S(2)}) collective-permute-start(bf16[3,10240]{1,0:T(4,128)(2,1)S(1)} %pad_maximum_fusion.2), channel_id=1, source_target_pairs={{0,1},{1,2},{2,3},{3,4},{4,5},{5,6},{6,7},{7,8},{8,9},{9,10},{10,1... | collective-permute-start | bytes 184328 | tf_op jit(solution)/shard_map/ppermute | solution.py:20
  12.3 4.1 %copy-start.14 = (f32[4,2048]{1,0:T(4,128)S(1)}, f32[4,2048]{1,0:T(4,128)}, u32[]{:S(2)}) copy-start(f32[4,2048]{1,0:T(4,128)} %param.15) | copy-start | bytes 98308
  12.3 4.1 %copy-start.11 = (f32[4,8192]{1,0:T(4,128)S(1)}, f32[4,8192]{1,0:T(4,128)}, u32[]{:S(2)}) copy-start(f32[4,8192]{1,0:T(4,128)} %param.13) | copy-start | bytes 393220
  12.3 4.3 %copy-start.13 = (f32[2048]{0:T(1024)S(1)}, f32[2048]{0:T(1024)}, u32[]{:S(2)}) copy-start(f32[2048]{0:T(1024)} %param.16) | copy-start | bytes 24580
  16.4 2.9 %copy-start.10 = (f32[8192]{0:T(1024)S(1)}, f32[8192]{0:T(1024)}, u32[]{:S(2)}) copy-start(f32[8192]{0:T(1024)} %param.14) | copy-start | bytes 98308
  19.2 7.8 %copy-start.15 = (f32[128]{0:T(128)S(1)}, f32[128]{0:T(128)}, u32[]{:S(2)}) copy-start(f32[128]{0:T(128)} %param.18) | copy-start | bytes 1540
  19.3 7.9 %copy-start.16 = (f32[128]{0:T(128)S(1)}, f32[128]{0:T(128)}, u32[]{:S(2)}) copy-start(f32[128]{0:T(128)} %param.17) | copy-start | bytes 1540
  27.4 0.6 copy-start.12
  31.2 11.5 %all-to-all-start.1 = ((bf16[4,128,2,256]{1,3,2,0:T(8,128)(2,1)}), bf16[4,128,2,256]{1,3,2,0:T(8,128)(2,1)S(1)}, u32[]{:S(2)}, u32[]{:S(2)}) async-start(bf16[4,128,2,256]{1,3,2,0:T(8,128)(2,1)} %copy.87), calls=%async_computation.1 | async-start | bytes 1048576 | tf_op jit(solution)/shard_map/all_to_all | solution.py:172
  42.7 27.6 %all-to-all-start = ((bf16[128,4,2048]{2,0,1:T(8,128)(2,1)}), bf16[128,4,2048]{2,0,1:T(8,128)(2,1)S(1)}, u32[]{:S(2)}, u32[]{:S(2)}) async-start(bf16[128,4,2048]{2,0,1:T(8,128)(2,1)} %bitcast.86), calls=%async_computation | async-start | bytes 4194304 | tf_op jit(solution)/shard_map/all_to_all | solution.py:174
  49.0 50.7 %copy-start.9 = (f32[512,32]{0,1:T(8,128)}, f32[512,32]{0,1:T(8,128)S(1)}, u32[]{:S(2)}) copy-start(f32[512,32]{0,1:T(8,128)S(1)} %get-tuple-element.15) | copy-start | bytes 196612
  57.0 0.8 copy-start.2
  70.3 1.3 copy-start.1
  83.6 4.5 %collective-permute-start.1 = (f32[264,2048]{1,0:T(8,128)}, f32[264,2048]{1,0:T(8,128)S(1)}, u32[]{:S(2)}, u32[]{:S(2)}) collective-permute-start(f32[264,2048]{1,0:T(8,128)} %select_maximum_fusion), channel_id=1, source_target_pairs={{0,4},{4,0},{8,12},{12,8},{16,20},{20,16},{24,28},{28,24},{1,5},{5... | collective-permute-start | bytes 6488072 | tf_op jit(solution)/shard_map/ppermute | solution.py:210
  88.5 1.6 copy-start
  90.3 6.2 %copy-start.17 = (f32[128]{0:T(128)S(1)}, f32[128]{0:T(128)}, u32[]{:S(2)}) copy-start(f32[128]{0:T(128)} %param.19) | copy-start | bytes 1540
  90.4 1.4 collective-permute-start.3
  91.1 0.7 collective-permute-start.2
  91.9 2.1 copy-start.8
  91.9 0.9 copy-start.7
  93.9 40.5 %collective-permute-start.4 = (f32[128,1024]{1,0:T(8,128)}, f32[128,1024]{1,0:T(8,128)}, u32[]{:S(2)}, u32[]{:S(2)}) collective-permute-start(f32[128,1024]{1,0:T(8,128)} %get-tuple-element.34), channel_id=1, source_target_pairs={{8,16},{12,20},{9,17},{13,21},{10,18},{14,22},{11,19},{15,23}} | collective-permute-start | bytes 1572872 | tf_op jit(solution)/shard_map/ppermute | solution.py:256
  95.2 49.0 %collective-permute-start.5 = (f32[128,1024]{1,0:T(8,128)}, f32[128,1024]{1,0:T(8,128)}, u32[]{:S(2)}, u32[]{:S(2)}) collective-permute-start(f32[128,1024]{1,0:T(8,128)} %get-tuple-element.35), channel_id=1, source_target_pairs={{8,16},{12,20},{9,17},{13,21},{10,18},{14,22},{11,19},{15,23}} | collective-permute-start | bytes 1572872 | tf_op jit(solution)/shard_map/ppermute | solution.py:256
  145.7 13.7 %collective-permute-start.6 = (f32[128,1024]{1,0:T(8,128)S(1)}, f32[128,1024]{1,0:T(8,128)S(1)}, u32[]{:S(2)}, u32[]{:S(2)}) collective-permute-start(f32[128,1024]{1,0:T(8,128)S(1)} %get-tuple-element.32), channel_id=1, source_target_pairs={{16,24},{20,28},{17,25},{21,29},{18,26},{22,30},{19,27},{23,31}} | collective-permute-start | bytes 1572872 | tf_op jit(solution)/shard_map/ppermute | solution.py:256
  147.0 21.5 %collective-permute-start.7 = (f32[128,1024]{1,0:T(8,128)S(1)}, f32[128,1024]{1,0:T(8,128)S(1)}, u32[]{:S(2)}, u32[]{:S(2)}) collective-permute-start(f32[128,1024]{1,0:T(8,128)S(1)} %get-tuple-element.33), channel_id=1, source_target_pairs={{16,24},{20,28},{17,25},{21,29},{18,26},{22,30},{19,27},{23,31}} | collective-permute-start | bytes 1572872 | tf_op jit(solution)/shard_map/ppermute | solution.py:256
  168.6 0.8 copy-start.4
  170.5 4.6 %copy-start.3 = (bf16[512,2,256]{0,2,1:T(8,128)(2,1)S(1)}, bf16[512,2,256]{0,2,1:T(8,128)(2,1)}, u32[]{:S(2)}) copy-start(bf16[512,2,256]{0,2,1:T(8,128)(2,1)} %copy-done.2) | copy-start | bytes 1572868
  170.5 3.0 %collective-permute-start.8 = (f32[256,1024]{1,0:T(8,128)}, f32[256,1024]{1,0:T(8,128)}, u32[]{:S(2)}, u32[]{:S(2)}) collective-permute-start(f32[256,1024]{1,0:T(8,128)} %pad_maximum_fusion.1), channel_id=1, source_target_pairs={{0,4},{4,0},{8,12},{12,8},{16,20},{20,16},{24,28},{28,24},{1,5},{5... | collective-permute-start | bytes 3145736 | tf_op jit(solution)/shard_map/ppermute | solution.py:261
  175.1 2.2 %copy-start.5 = (f32[512,2048]{1,0:T(8,128)S(1)}, f32[512,2048]{1,0:T(8,128)}, u32[]{:S(2)}) copy-start(f32[512,2048]{1,0:T(8,128)} %get-tuple-element.17) | copy-start | bytes 12582916
  175.1 3.5 %copy-start.6 = (f32[512,2048]{1,0:T(8,128)S(1)}, f32[512,2048]{1,0:T(8,128)}, u32[]{:S(2)}) copy-start(f32[512,2048]{1,0:T(8,128)} %get-tuple-element.18) | copy-start | bytes 12582916

commit v15 on v14

--- a/solution.py
+++ b/solution.py
@@ -224,7 +224,7 @@
     chip_decay = head_columns(
         lax.dynamic_slice_in_dim(segment_decay * mate_decay, core * half_heads, half_heads, 0)
     )[None, :]
-    pieces = 2 if N % 16 == 0 else 1
+    pieces = 1
     piece_rows = N // pieces
     acc = [jnp.zeros((piece_rows, half_width), jnp.float32) for _ in range(pieces)]
     skip_cols = head_columns(skip_local)

time: 212 us -> 211 us (level)
  waiting for transfers between devices: 70.6 us -> 75.2 us
  starting transfers between devices: 21.5 us -> 18.3 us
    ppermute x6 -> x3, waiting for transfers between devices: 47.1 us -> 51.7 us  [on_device(): acc[k] = acc[k] + lax.ppermute(send, 'ctx', pairs)]
    ppermute x6 -> x3, starting transfers between devices: 6.79 us -> 3.54 us  [on_device(): acc[k] = acc[k] + lax.ppermute(send, 'ctx', pairs)]
    unnamed x39 -> x35, local copies, waits for them, and re-layouts: 11.3 us -> 10.7 us
  transfers between devices with their start and end apart: 12 -> 9, of which waited for: 8 -> 6; matrix products, arithmetic and copies ran while one was open for 18% -> 18% of each run, Pallas kernels for 7% -> 7%
where the time goes in v15:
time: 211 us; the launch traced here: 209 us
  waiting for transfers between devices  75.2 us (36%)
  local copies, waits for them, and re-layouts  32.5 us (15%)
  blocking collectives  28.4 us (13%)
  other arithmetic  26.2 us (12%)
  Pallas kernels  23.9 us (11%)
  starting transfers between devices  18.3 us (9%)
  matrix products  4.47 us (2%)
    ppermute x3, waiting for transfers between devices, on_device(): acc[k] = acc[k] + lax.ppermute(send, 'ctx', pairs)  51.7 us
    all_to_all x1, blocking collectives, on_device(): return lax.all_to_all(result, 'tp', split_axis=0, concat_axis=1, tiled=True)  28.4 us
    pallas_call x1, Pallas kernels, intra_block(): pl.pallas_call(intra_kernel, out_shape=(jax.ShapeDtypeStruct((BLOCK, widt...  15.2 us
    all_to_all x1, waiting for transfers between devices, on_device(): lax.all_to_all(x_part, 'tp', split_axis=1, concat_axis=0, tiled=True)  11.7 us
    unnamed x35, local copies, waits for them, and re-layouts  10.7 us
    convert_element_type x4, other arithmetic, conv_rows(): return jax.nn.silu(total).astype(jnp.bfloat16)  10.4 us
    pallas_call x1, Pallas kernels, fresh_block(): pl.pallas_call(fresh_kernel, out_shape=jax.ShapeDtypeStruct((N, width), j...  8.67 us
    reshape x1, local copies, waits for them, and re-layouts, head_columns(): return jnp.repeat(head_major, P_SIZE, axis=-1)  5.41 us
  transfers between devices with their start and end apart: 9, of which 6 were waited for; matrix products, arithmetic and copies ran while one was open for 18% of the time, Pallas kernels for 7%

profile of v15, /device:TPU:16, one launch (start us, length us, event | category | flops | bytes accessed | tf_op | source)
XLA Modules:
  0.0 209.4 jit_solution(467554100186647778)
XLA Ops:
  0.0 1.5 copy.89
  1.5 3.7 %all-to-all-start.2 = ((bf16[128,4,32]{0,2,1:T(8,128)(2,1)}), bf16[128,4,32]{0,2,1:T(8,128)(2,1)S(1)}, u32[]{:S(2)}, u32[]{:S(2)}) async-start(bf16[128,4,32]{0,2,1:T(8,128)(2,1)} %bitcast.14), calls=%async_computation.2 | async-start | bytes 65536 | tf_op jit(solution)/shard_map/all_to_all | solution.py:175
  7.1 3.9 %collective-permute-start = (bf16[3,10240]{1,0:T(4,128)(2,1)S(1)}, bf16[3,10240]{1,0:T(4,128)(2,1)S(1)}, u32[]{:S(2)}, u32[]{:S(2)}) collective-permute-start(bf16[3,10240]{1,0:T(4,128)(2,1)S(1)} %pad_maximum_fusion.1), channel_id=1, source_target_pairs={{0,1},{1,2},{2,3},{3,4},{4,5},{5,6},{6,7},{7,8},{8,9},{9,10},{10,1... | collective-permute-start | bytes 184328 | tf_op jit(solution)/shard_map/ppermute | solution.py:20
  11.0 1.3 copy.85
  12.4 4.0 %convert_element_type.59 = f32[128,8192]{1,0:T(8,128)} convert(bf16[128,8192]{1,0:T(8,128)(2,1)} %param.10) | non-fusion elementwise | flops 1048576 | bytes 6291456 | tf_op jit(solution)/shard_map/convert_element_type | solution.py:34
  16.6 2.6 %multiply_convert_fusion.1 = bf16[128,2048]{0,1:T(8,128)(2,1)S(1)} fusion(f32[128,2048]{0,1:T(8,128)S(1)} %convert_element_type.63, f32[2048]{0:T(1024)S(1)} %bitcast.104, f32[2048]{0:T(1024)S(1)} %bitcast.106, f32[2048]{0:T(1024)S(1)} %bitcast.102, f32[2048]{0:T(1024)S(1)} %bitcast.100, f32[2048]{0:T(1024)S(1)} %copy-done.11), kind=kLoop, calls=%fused_computation.27 | loop fusion | flops 3407872 | bytes 1613824 | tf_op jit(solution)/shard_map/convert_element_type | solution.py:27
  19.3 7.6 %multiply_convert_fusion = bf16[128,8192]{1,0:T(8,128)(2,1)S(1)} fusion(f32[128,8192]{1,0:T(8,128)} %convert_element_type.59, f32[8192]{0:T(1024)S(1)} %bitcast.95, f32[8192]{0:T(1024)S(1)} %bitcast.97, f32[8192]{0:T(1024)S(1)} %bitcast.93, f32[8192]{0:T(1024)S(1)} %bitcast.91, f32[8192]{0:T(1024)S(1)} %copy-done.8), kind=kLoop, calls=%fused_computation.1 | loop fusion | flops 13631488 | bytes 6455296 | tf_op jit(solution)/shard_map/convert_element_type | solution.py:27
  28.1 2.0 dynamic_update_slice.7
  31.0 3.5 %all-to-all-start.1 = ((bf16[4,128,2,256]{1,3,2,0:T(8,128)(2,1)}), bf16[4,128,2,256]{1,3,2,0:T(8,128)(2,1)S(1)}, u32[]{:S(2)}, u32[]{:S(2)}) async-start(bf16[4,128,2,256]{1,3,2,0:T(8,128)(2,1)} %copy.87), calls=%async_computation.1 | async-start | bytes 1048576 | tf_op jit(solution)/shard_map/all_to_all | solution.py:172
  36.5 1.5 copy.116
  38.0 4.4 %all-to-all-done.1 = bf16[4,128,2,256]{1,3,2,0:T(8,128)(2,1)S(1)} async-done(((bf16[4,128,2,256]{1,3,2,0:T(8,128)(2,1)}), bf16[4,128,2,256]{1,3,2,0:T(8,128)(2,1)S(1)}, u32[]{:S(2)}, u32[]{:S(2)}) %all-to-all-start.1) | async-done | bytes 524320 | tf_op jit(solution)/shard_map/all_to_all | solution.py:172
  42.4 3.6 %all-to-all-start = ((bf16[128,4,2048]{2,0,1:T(8,128)(2,1)}), bf16[128,4,2048]{2,0,1:T(8,128)(2,1)S(1)}, u32[]{:S(2)}, u32[]{:S(2)}) async-start(bf16[128,4,2048]{2,0,1:T(8,128)(2,1)} %bitcast.86), calls=%async_computation | async-start | bytes 4194304 | tf_op jit(solution)/shard_map/all_to_all | solution.py:174
  48.8 2.5 %broadcast_in_dim.12 = f32[512,32,64]{0,2,1:T(8,128)} broadcast(f32[512,32]{0,1:T(8,128)S(1)} %get-tuple-element.23), dimensions={0,1} | broadcast | bytes 4259840 | tf_op jit(solution)/shard_map/broadcast_in_dim | solution.py:135
  51.3 5.4 %copy.95.fac_ref = f32[512,2048]{1,0:T(8,128)} copy(f32[512,2048]{0,1:T(8,128)} %bitcast.83) | data formatting | bytes 8388608 | tf_op jit(solution)/shard_map/reshape | solution.py:135
  58.3 11.7 %all-to-all-done = bf16[128,4,2048]{2,0,1:T(8,128)(2,1)S(1)} async-done(((bf16[128,4,2048]{2,0,1:T(8,128)(2,1)}), bf16[128,4,2048]{2,0,1:T(8,128)(2,1)S(1)}, u32[]{:S(2)}, u32[]{:S(2)}) %all-to-all-start) | async-done | bytes 2097184 | tf_op jit(solution)/shard_map/all_to_all | solution.py:174
  70.0 1.3 copy-done.1
  71.4 8.7 %ssd_fresh.1 = f32[256,2048]{1,0:T(8,128)} custom-call(bf16[512,2048]{1,0:T(8,128)(2,1)} %bitcast.88, bf16[256,512]{1,0:T(8,128)(2,1)} %slice_bitcast_fusion.1.bt_ref, f32[512,2048]{1,0:T(8,128)} %copy.95.fac_ref), custom_call_target="tpu_custom_call" | custom-call | flops 536870912 | bytes 8650752 | tf_op jit(solution)/shard_map/ssd_fresh/pallas_call | solution.py:120
  80.0 3.2 %select_maximum_fusion = f32[264,2048]{1,0:T(8,128)} fusion(f32[1,32]{1,0:T(1,128)S(1)} %bitcast.110, f32[256,2048]{1,0:T(8,128)} %ssd_fresh.1), kind=kLoop, calls=%fused_computation.10 | loop fusion | flops 1622016 | bytes 4259968 | tf_op jit(solution)/shard_map/concatenate | solution.py:211
  83.2 4.5 %collective-permute-done.1 = f32[264,2048]{1,0:T(8,128)S(1)} collective-permute-done((f32[264,2048]{1,0:T(8,128)}, f32[264,2048]{1,0:T(8,128)S(1)}, u32[]{:S(2)}, u32[]{:S(2)}) %collective-permute-start.1) | collective-permute-done | bytes 2162720 | tf_op jit(solution)/shard_map/ppermute | solution.py:210
  88.4 1.4 copy-done
  93.0 1.3 collective-permute-start.3
  95.2 2.4 %fusion.12.s_ref = f32[512,512]{1,0:T(8,128)} fusion(bf16[512,2,256]{0,2,1:T(8,128)(2,1)} %copy-done.2), kind=kOutput, calls=%fused_computation.33 | convolution fusion | flops 134217728 | bytes 1572864 | tf_op jit(solution)/shard_map/in,jn->ij/dot_general | solution.py:232
  98.4 15.2 %ssd_intra.1 = (f32[512,2048]{1,0:T(8,128)}, f32[512,2048]{1,0:T(8,128)}) custom-call(bf16[512,2048]{1,0:T(8,128)(2,1)} %bitcast.89, f32[512,512]{1,0:T(8,128)} %fusion.12.s_ref, f32[512,128]{1,0:T(8,128)} %pad.11.clone.cum_ref, f32[32,512]{1,0:T(8,128)} %bitcast.99, f32[32,512]{1,0:T(8,128)} %bitcast.108, f32[1,2048]{1,0:T(1,128)} %broadcast_in_dim_reshape.2.skip_ref), custom_call_target="tpu_custom_call" | custom-call | flops 2147483648 | bytes 7340032 | tf_op jit(solution)/shard_map/ssd_intra/pallas_call | solution.py:87
  113.6 30.5 %collective-permute-done.3 = f32[256,1024]{1,0:T(8,128)} collective-permute-done((f32[256,1024]{1,0:T(8,128)}, f32[256,1024]{1,0:T(8,128)}, u32[]{:S(2)}, u32[]{:S(2)}) %collective-permute-start.3) | collective-permute-done | bytes 1048608 | tf_op jit(solution)/shard_map/ppermute | solution.py:256
  144.1 1.7 add.205
  146.0 1.5 collective-permute-start.4
  147.5 21.3 %collective-permute-done.4 = f32[256,1024]{1,0:T(8,128)S(1)} collective-permute-done((f32[256,1024]{1,0:T(8,128)S(1)}, f32[256,1024]{1,0:T(8,128)S(1)}, u32[]{:S(2)}, u32[]{:S(2)}) %collective-permute-start.4) | collective-permute-done | bytes 1048608 | tf_op jit(solution)/shard_map/ppermute | solution.py:256
  170.1 2.9 %collective-permute-done.5 = f32[256,1024]{1,0:T(8,128)} collective-permute-done((f32[256,1024]{1,0:T(8,128)}, f32[256,1024]{1,0:T(8,128)}, u32[]{:S(2)}, u32[]{:S(2)}) %collective-permute-start.5) | collective-permute-done | bytes 1048608 | tf_op jit(solution)/shard_map/ppermute | solution.py:261
  172.9 1.8 broadcast_select_fusion
  175.6 1.3 copy-done.4
  179.5 28.4 %all_to_all.56 = bf16[4,128,2048]{2,1,0:T(8,128)(2,1)S(1)} all-to-all(bf16[4,128,2048]{2,1,0:T(8,128)(2,1)S(1)} %bitcast.85), channel_id=1, replica_groups=mesh['ctx'=8,'tp'=4] {'tp'}, dimensions={0} | all-to-all | bytes 4194304 | tf_op jit(solution)/shard_map/all_to_all | solution.py:283
  207.9 1.5 copy.103
  (93 shorter events, 21.0 us)
Async XLA Ops:
  1.5 25.5 %all-to-all-start.2 = ((bf16[128,4,32]{0,2,1:T(8,128)(2,1)}), bf16[128,4,32]{0,2,1:T(8,128)(2,1)S(1)}, u32[]{:S(2)}, u32[]{:S(2)}) async-start(bf16[128,4,32]{0,2,1:T(8,128)(2,1)} %bitcast.14), calls=%async_computation.2 | async-start | bytes 65536 | tf_op jit(solution)/shard_map/all_to_all | solution.py:175
  7.1 20.1 %collective-permute-start = (bf16[3,10240]{1,0:T(4,128)(2,1)S(1)}, bf16[3,10240]{1,0:T(4,128)(2,1)S(1)}, u32[]{:S(2)}, u32[]{:S(2)}) collective-permute-start(bf16[3,10240]{1,0:T(4,128)(2,1)S(1)} %pad_maximum_fusion.1), channel_id=1, source_target_pairs={{0,1},{1,2},{2,3},{3,4},{4,5},{5,6},{6,7},{7,8},{8,9},{9,10},{10,1... | collective-permute-start | bytes 184328 | tf_op jit(solution)/shard_map/ppermute | solution.py:20
  12.3 4.0 %copy-start.12 = (f32[4,2048]{1,0:T(4,128)S(1)}, f32[4,2048]{1,0:T(4,128)}, u32[]{:S(2)}) copy-start(f32[4,2048]{1,0:T(4,128)} %param.15) | copy-start | bytes 98308
  12.3 4.1 %copy-start.9 = (f32[4,8192]{1,0:T(4,128)S(1)}, f32[4,8192]{1,0:T(4,128)}, u32[]{:S(2)}) copy-start(f32[4,8192]{1,0:T(4,128)} %param.13) | copy-start | bytes 393220
  12.3 4.2 %copy-start.11 = (f32[2048]{0:T(1024)S(1)}, f32[2048]{0:T(1024)}, u32[]{:S(2)}) copy-start(f32[2048]{0:T(1024)} %param.16) | copy-start | bytes 24580
  16.4 2.9 %copy-start.8 = (f32[8192]{0:T(1024)S(1)}, f32[8192]{0:T(1024)}, u32[]{:S(2)}) copy-start(f32[8192]{0:T(1024)} %param.14) | copy-start | bytes 98308
  19.2 7.6 %copy-start.13 = (f32[128]{0:T(128)S(1)}, f32[128]{0:T(128)}, u32[]{:S(2)}) copy-start(f32[128]{0:T(128)} %param.18) | copy-start | bytes 1540
  19.2 7.7 %copy-start.14 = (f32[128]{0:T(128)S(1)}, f32[128]{0:T(128)}, u32[]{:S(2)}) copy-start(f32[128]{0:T(128)} %param.17) | copy-start | bytes 1540
  27.1 0.6 copy-start.10
  31.0 11.5 %all-to-all-start.1 = ((bf16[4,128,2,256]{1,3,2,0:T(8,128)(2,1)}), bf16[4,128,2,256]{1,3,2,0:T(8,128)(2,1)S(1)}, u32[]{:S(2)}, u32[]{:S(2)}) async-start(bf16[4,128,2,256]{1,3,2,0:T(8,128)(2,1)} %copy.87), calls=%async_computation.1 | async-start | bytes 1048576 | tf_op jit(solution)/shard_map/all_to_all | solution.py:172
  42.4 27.6 %all-to-all-start = ((bf16[128,4,2048]{2,0,1:T(8,128)(2,1)}), bf16[128,4,2048]{2,0,1:T(8,128)(2,1)S(1)}, u32[]{:S(2)}, u32[]{:S(2)}) async-start(bf16[128,4,2048]{2,0,1:T(8,128)(2,1)} %bitcast.86), calls=%async_computation | async-start | bytes 4194304 | tf_op jit(solution)/shard_map/all_to_all | solution.py:174
  48.8 48.8 %copy-start.7 = (f32[512,32]{0,1:T(8,128)}, f32[512,32]{0,1:T(8,128)S(1)}, u32[]{:S(2)}) copy-start(f32[512,32]{0,1:T(8,128)S(1)} %get-tuple-element.14) | copy-start | bytes 196612
  56.8 0.8 copy-start.2
  70.0 1.3 copy-start.1
  83.2 4.5 %collective-permute-start.1 = (f32[264,2048]{1,0:T(8,128)}, f32[264,2048]{1,0:T(8,128)S(1)}, u32[]{:S(2)}, u32[]{:S(2)}) collective-permute-start(f32[264,2048]{1,0:T(8,128)} %select_maximum_fusion), channel_id=1, source_target_pairs={{0,4},{4,0},{8,12},{12,8},{16,20},{20,16},{24,28},{28,24},{1,5},{5... | collective-permute-start | bytes 6488072 | tf_op jit(solution)/shard_map/ppermute | solution.py:210
  88.2 1.6 copy-start
  90.1 4.3 %copy-start.15 = (f32[128]{0:T(128)S(1)}, f32[128]{0:T(128)}, u32[]{:S(2)}) copy-start(f32[128]{0:T(128)} %param.19) | copy-start | bytes 1540
  90.1 0.7 collective-permute-start.2
  90.8 1.0 copy-start.6
  93.0 51.0 %collective-permute-start.3 = (f32[256,1024]{1,0:T(8,128)}, f32[256,1024]{1,0:T(8,128)}, u32[]{:S(2)}, u32[]{:S(2)}) collective-permute-start(f32[256,1024]{1,0:T(8,128)} %multiply_add_fusion.1), channel_id=1, source_target_pairs={{8,16},{12,20},{9,17},{13,21},{10,18},{14,22},{11,19},{15,23}} | collective-permute-start | bytes 3145736 | tf_op jit(solution)/shard_map/ppermute | solution.py:256
  146.0 22.8 %collective-permute-start.4 = (f32[256,1024]{1,0:T(8,128)S(1)}, f32[256,1024]{1,0:T(8,128)S(1)}, u32[]{:S(2)}, u32[]{:S(2)}) collective-permute-start(f32[256,1024]{1,0:T(8,128)S(1)} %multiply_add_fusion), channel_id=1, source_target_pairs={{16,24},{20,28},{17,25},{21,29},{18,26},{22,30},{19,27},{23,31}} | collective-permute-start | bytes 3145736 | tf_op jit(solution)/shard_map/ppermute | solution.py:256
  169.9 4.8 %copy-start.3 = (bf16[512,2,256]{0,2,1:T(8,128)(2,1)S(1)}, bf16[512,2,256]{0,2,1:T(8,128)(2,1)}, u32[]{:S(2)}) copy-start(bf16[512,2,256]{0,2,1:T(8,128)(2,1)} %copy-done.2) | copy-start | bytes 1572868
  169.9 3.0 %collective-permute-start.5 = (f32[256,1024]{1,0:T(8,128)}, f32[256,1024]{1,0:T(8,128)}, u32[]{:S(2)}, u32[]{:S(2)}) collective-permute-start(f32[256,1024]{1,0:T(8,128)} %add.207), channel_id=1, source_target_pairs={{0,4},{4,0},{8,12},{12,8},{16,20},{20,16},{24,28},{28,24},{1,5},{5... | collective-permute-start | bytes 3145736 | tf_op jit(solution)/shard_map/ppermute | solution.py:261
  174.7 2.2 %copy-start.4 = (f32[512,2048]{1,0:T(8,128)S(1)}, f32[512,2048]{1,0:T(8,128)}, u32[]{:S(2)}) copy-start(f32[512,2048]{1,0:T(8,128)} %get-tuple-element.16) | copy-start | bytes 12582916
  174.8 3.5 %copy-start.5 = (f32[512,2048]{1,0:T(8,128)S(1)}, f32[512,2048]{1,0:T(8,128)}, u32[]{:S(2)}) copy-start(f32[512,2048]{1,0:T(8,128)} %get-tuple-element.17) | copy-start | bytes 12582916
